TPU v7x, 128 devices: a whole 4x4x4 slice. The times are simulated.
128 devices in a mesh: blk: 32 (over z, y, x_hi), grp: 4 (over x_lo, core).
Axes of the slice: x: 4 (x_hi: 2, x_lo: 2; x = x_hi * 2 + x_lo), y: 4, z: 4, core: 2. Of those that a mesh axis runs over, the one named last changes fastest.
Arguments:
- queries: bfloat16 [65536, 2048], P('blk', 'grp'), may hold values from -64 to 64
- encoder: bfloat16 [4096, 2048], P('blk'), may hold values from -6 to 6
- key_weight: bfloat16 [2048, 2048], P(None, 'grp'), may hold values from -0.125 to 0.125
- value_weight: bfloat16 [2048, 2048], P(None, 'grp'), may hold values from -0.125 to 0.125
- out_grad: bfloat16 [65536, 2048], P('blk', 'grp'), may hold values from -6 to 6
- block_lists: int32 [512, 5], P('blk'), may hold values from 0 to 31, as said below
- list_counts: int32 [512], P('blk'), may hold values from 1 to 5, as said below
Outputs:
- attended: bfloat16 [65536, 2048], P('blk', 'grp')
- query_grad: bfloat16 [65536, 2048], P('blk', 'grp')
- encoder_grad: bfloat16 [4096, 2048], P('blk', 'grp')
- key_weight_grad: float32 [2048, 2048], P('blk', 'grp')
- value_weight_grad: float32 [2048, 2048], P('blk', 'grp')
Inputs may be any that keep to these rules, and one draw needn't show every extreme that they name: `block_lists`: query block b belongs to blk index b // 16. Each list holds 5 distinct encoder block ids, all within 4 of that index; every blk index has a query block whose list reaches exactly 4 blocks away, and entries past list_counts are valid but unused ids. `list_counts`: every blk index has a query block that uses all 5 entries.
All inputs are finite; a program needn't handle non-finite values.
Results may differ from a plain program's by a relative error of at most 0.015.
The roundings to bfloat16 on the way count: a program that leaves them out, or rounds other values in their place, can miss the bound.
Values may be sent and summed in bfloat16 or wider, within the bound.
No kernel may reach another device: no remote copies, remote signals or barrier semaphores. Data moves between devices by JAX's collectives and lax.ppermute only.
A program may use at most 128 MiB of HBM per device.

v0:
```python
import math

import jax
import jax.numpy as jnp
from jax import lax
from jax.sharding import PartitionSpec as P

HEAD_DIM = 64
REACH = 4
LISTED = 5


def passed_along(value, axis, by):
    size = lax.axis_size(axis)
    pairs = [(i, i + by) for i in range(size) if 0 <= i + by < size]
    return lax.ppermute(value, axis, pairs)


def on_device(queries, encoder, key_weight, value_weight, out_grad, block_lists, list_counts):
    factor = HEAD_DIM ** (-0.5)
    position = lax.axis_index("blk")
    head_cols = key_weight.shape[1]
    heads_here = head_cols // HEAD_DIM
    block_rows = encoder.shape[0]
    query_count = queries.shape[0] // block_rows
    arrived = []
    for offset in range(-REACH, REACH + 1):
        if offset == 0:
            arrived.append(encoder)
        else:
            arrived.append(passed_along(encoder, "blk", -offset))
    near_encoder = jnp.stack(arrived, 0)
    near_keys = jnp.einsum(
        "brd,dc->brc", near_encoder, key_weight, preferred_element_type=jnp.float32
    ).astype(jnp.bfloat16)
    near_values = jnp.einsum(
        "brd,dc->brc", near_encoder, value_weight, preferred_element_type=jnp.float32
    ).astype(jnp.bfloat16)
    stock = jnp.stack([near_keys, near_values], 1)
    lowest = position - REACH
    slot_ids = block_lists - lowest
    usable = jnp.arange(LISTED, dtype=jnp.int32)[None, :] < list_counts[:, None]
    batch_size = math.gcd(4, query_count)
    turns = query_count // batch_size
    query_steps = queries.reshape(turns, batch_size, block_rows, heads_here, HEAD_DIM)
    grad_steps = out_grad.reshape(turns, batch_size, block_rows, heads_here, HEAD_DIM)
    slot_steps = slot_ids.reshape(turns, batch_size, LISTED)
    usable_steps = usable.reshape(turns, batch_size, LISTED)

    def one_block(query, grad, slot_row, usable_row):
        picked = stock[slot_row]
        picked_keys = picked[:, 0].reshape(LISTED * block_rows, heads_here, HEAD_DIM)
        picked_values = picked[:, 1].reshape(LISTED * block_rows, heads_here, HEAD_DIM)
        keep_keys = jnp.repeat(usable_row, block_rows)
        scores = (
            jnp.einsum("qhd,khd->hqk", query, picked_keys, preferred_element_type=jnp.float32)
            * factor
        )
        scores = jnp.where(keep_keys[None, None, :], scores, -jnp.inf)
        peak = jnp.max(scores, axis=-1, keepdims=True)
        expo = jnp.exp(scores - peak)
        weights = (expo / jnp.sum(expo, axis=-1, keepdims=True)).astype(jnp.bfloat16)
        output = jnp.einsum(
            "hqk,khd->qhd", weights, picked_values, preferred_element_type=jnp.float32
        ).astype(jnp.bfloat16)
        dweights = jnp.einsum(
            "qhd,khd->hqk", grad, picked_values, preferred_element_type=jnp.float32
        )
        weights_full = weights.astype(jnp.float32)
        center = jnp.sum(weights_full * dweights, axis=-1, keepdims=True)
        dscores = (weights_full * (dweights - center) * factor).astype(jnp.bfloat16)
        dquery = jnp.einsum(
            "hqk,khd->qhd", dscores, picked_keys, preferred_element_type=jnp.float32
        ).astype(jnp.bfloat16)
        dkey = jnp.einsum("hqk,qhd->khd", dscores, query, preferred_element_type=jnp.float32)
        dvalue = jnp.einsum("hqk,qhd->khd", weights, grad, preferred_element_type=jnp.float32)
        terms = jnp.stack(
            [
                dkey.reshape(LISTED, block_rows, head_cols),
                dvalue.reshape(LISTED, block_rows, head_cols),
            ],
            1,
        )
        return (output.reshape(block_rows, head_cols), dquery.reshape(block_rows, head_cols), terms)

    def advance(running, item):
        query, grad, slot_row, usable_row = item
        output, dquery, terms = jax.vmap(one_block)(query, grad, slot_row, usable_row)
        running = running.at[slot_row.reshape(-1)].add(terms.reshape((-1,) + terms.shape[2:]))
        return (running, (output, dquery))

    start_sums = jnp.zeros(stock.shape, jnp.float32)
    running, (outputs, dqueries) = lax.scan(
        advance, start_sums, (query_steps, grad_steps, slot_steps, usable_steps)
    )
    attended = outputs.reshape(query_count * block_rows, head_cols)
    query_grad = dqueries.reshape(query_count * block_rows, head_cols)
    owned = running[REACH]
    for offset in range(-REACH, REACH + 1):
        if offset != 0:
            owned = owned + passed_along(running[REACH + offset], "blk", offset)
    rounded = owned.astype(jnp.bfloat16)
    contract_cols = (((1,), (1,)), ((), ()))
    encoder_terms = lax.dot_general(
        rounded[0], key_weight, contract_cols, preferred_element_type=jnp.float32
    ) + lax.dot_general(rounded[1], value_weight, contract_cols, preferred_element_type=jnp.float32)
    encoder_grad = lax.psum_scatter(encoder_terms, "grp", scatter_dimension=1, tiled=True).astype(
        jnp.bfloat16
    )
    both_grads = jnp.concatenate([rounded[0], rounded[1]], 1)
    weight_rows = lax.psum_scatter(
        lax.dot_general(
            encoder, both_grads, (((0,), (0,)), ((), ())), preferred_element_type=jnp.float32
        ),
        "blk",
        scatter_dimension=0,
        tiled=True,
    )
    return (
        attended,
        query_grad,
        encoder_grad,
        weight_rows[:, :head_cols],
        weight_rows[:, head_cols:],
    )


def solution(mesh):
    in_specs = (
        P("blk", "grp"),
        P("blk", None),
        P(None, "grp"),
        P(None, "grp"),
        P("blk", "grp"),
        P("blk", None),
        P("blk"),
    )
    out_specs = (
        P("blk", "grp"),
        P("blk", "grp"),
        P("blk", "grp"),
        P("blk", "grp"),
        P("blk", "grp"),
    )
    return jax.shard_map(
        on_device, mesh=mesh, in_specs=in_specs, out_specs=out_specs, check_vma=False
    )
```

profile of v0, /device:TPU:0, one launch (start us, length us, event | category | flops | bytes accessed | tf_op | source)
XLA Modules:
  0.0 1163.6 jit_solution(18235559099565779630)
XLA Ops:
  61.4 17.3 %collective-permute-done.5 = bf16[128,2048]{1,0:T(8,128)(2,1)S(1)} collective-permute-done((bf16[128,2048]{1,0:T(8,128)(2,1)S(1)}, bf16[128,2048]{1,0:T(8,128)(2,1)S(1)}, u32[]{:S(2)}, u32[]{:S(2)}) %collective-permute-start.5) | collective-permute-done | bytes 524320 | tf_op jit(solution)/shard_map/ppermute | solution.py:16
  88.7 736.4 %while.14 = (s32[]{:T(128)}, f32[9,2,128,512]{3,2,1,0:T(8,128)}, bf16[4,4,128,512]{3,2,1,0:T(8,128)(2,1)}, bf16[4,4,128,512]{3,2,1,0:T(8,128)(2,1)}, s32[4,4,5]{...) while((s32[]{:T(128)}, f32[9,2,128,512]{3,2,1,0:T(8,128)}, ...), condition=%wide.region_5.6_spmd, body=%wide.region_0.5_spmd.sunk | while | flops 2071473152 | bytes 280020544 | solution.py:93
  132.7 9.4 fusion.125
  163.3 7.5 fusion.126
  170.8 14.3 %fusion.128 = bf16[4,8,64,128]{3,2,1,0:T(8,128)(2,1)S(1)} fusion(bf16[4,640,8,64]{1,3,2,0:T(8,128)(2,1)} %squeeze.69, bf16[4,8,128,640]{3,2,1,0:T(8,128)(2,1)} %divide_convert_fusion.2, f32[4,8,128,640]{3,2,1,0:T(8,128)} %fusion.126), kind=kOutput, calls=%fused_computation.23.clone.1 | convolution fusion | flops 354161280 | bytes 18874368 | tf_op jit(solution)/shard_map/while/body/eval_jaxpr/vmap(hqk,khd->qhd)/dot_general | solution.py:72
  193.8 16.1 %fusion.127 = f32[4,640,8,64]{1,3,2,0:T(8,128)} fusion(bf16[4,8,128,640]{3,2,1,0:T(8,128)(2,1)} %divide_convert_fusion.2, f32[4,8,128,640]{3,2,1,0:T(8,128)} %fusion.126, bf16[4,4,128,8,64]{2,4,3,1,0:T(8,128)(2,1)} %get-tuple-element.247, s32[]{:T(128)} %get-tuple-element.232), kind=kOutput, calls=%fused_computation.21.clone.1 | convolution fusion | flops 353899136 | bytes 37224960 | tf_op jit(solution)/shard_map/while/body/eval_jaxpr/vmap(hqk,qhd->khd)/dot_general | solution.py:75
  210.0 8.2 copy.94
  218.1 7.4 stack.62
  234.9 7.4 stack.61
  242.3 9.9 pad_maximum_fusion.3
  252.3 11.8 %copy.95 = f32[20,2,128,512]{3,2,1,0:T(8,128)} copy(f32[20,2,128,512]{2,0,3,1:T(8,128)} %pad_maximum_fusion.3) | data formatting | bytes 20971520 | tf_op jit(solution)/shard_map/while/body/eval_jaxpr/vmap()/stack | solution.py:77
  264.2 22.5 %scatter_fusion = f32[9,2,128,512]{3,2,1,0:T(8,128)} fusion(f32[9,2,128,512]{3,2,1,0:T(8,128)} %get-tuple-element.233, s32[20]{0:T(128)S(1)} %fusion.123, f32[20,2,128,512]{3,2,1,0:T(8,128)} %copy.95), kind=kCustom, calls=%fused_computation.1.clone.1 | custom fusion | flops 2621440 | bytes 31457360 | tf_op jit(solution)/shard_map/while/body/eval_jaxpr/scatter-add | solution.py:89
  312.3 9.4 fusion.125
  342.9 7.5 fusion.126
  350.4 14.3 %fusion.128 = bf16[4,8,64,128]{3,2,1,0:T(8,128)(2,1)S(1)} fusion(bf16[4,640,8,64]{1,3,2,0:T(8,128)(2,1)} %squeeze.69, bf16[4,8,128,640]{3,2,1,0:T(8,128)(2,1)} %divide_convert_fusion.2, f32[4,8,128,640]{3,2,1,0:T(8,128)} %fusion.126), kind=kOutput, calls=%fused_computation.23.clone.1 | convolution fusion | flops 354161280 | bytes 18874368 | tf_op jit(solution)/shard_map/while/body/eval_jaxpr/vmap(hqk,khd->qhd)/dot_general | solution.py:72
  373.4 16.1 %fusion.127 = f32[4,640,8,64]{1,3,2,0:T(8,128)} fusion(bf16[4,8,128,640]{3,2,1,0:T(8,128)(2,1)} %divide_convert_fusion.2, f32[4,8,128,640]{3,2,1,0:T(8,128)} %fusion.126, bf16[4,4,128,8,64]{2,4,3,1,0:T(8,128)(2,1)} %get-tuple-element.247, s32[]{:T(128)} %get-tuple-element.232), kind=kOutput, calls=%fused_computation.21.clone.1 | convolution fusion | flops 353899136 | bytes 37224960 | tf_op jit(solution)/shard_map/while/body/eval_jaxpr/vmap(hqk,qhd->khd)/dot_general | solution.py:75
  389.6 8.2 copy.94
  397.7 7.4 stack.62
  414.5 7.4 stack.61
  421.9 9.9 pad_maximum_fusion.3
  431.9 11.8 %copy.95 = f32[20,2,128,512]{3,2,1,0:T(8,128)} copy(f32[20,2,128,512]{2,0,3,1:T(8,128)} %pad_maximum_fusion.3) | data formatting | bytes 20971520 | tf_op jit(solution)/shard_map/while/body/eval_jaxpr/vmap()/stack | solution.py:77
  443.8 22.7 %scatter_fusion = f32[9,2,128,512]{3,2,1,0:T(8,128)} fusion(f32[9,2,128,512]{3,2,1,0:T(8,128)} %get-tuple-element.233, s32[20]{0:T(128)S(1)} %fusion.123, f32[20,2,128,512]{3,2,1,0:T(8,128)} %copy.95), kind=kCustom, calls=%fused_computation.1.clone.1 | custom fusion | flops 2621440 | bytes 31457360 | tf_op jit(solution)/shard_map/while/body/eval_jaxpr/scatter-add | solution.py:89
  492.1 9.4 fusion.125
  522.7 7.5 fusion.126
  530.2 14.3 %fusion.128 = bf16[4,8,64,128]{3,2,1,0:T(8,128)(2,1)S(1)} fusion(bf16[4,640,8,64]{1,3,2,0:T(8,128)(2,1)} %squeeze.69, bf16[4,8,128,640]{3,2,1,0:T(8,128)(2,1)} %divide_convert_fusion.2, f32[4,8,128,640]{3,2,1,0:T(8,128)} %fusion.126), kind=kOutput, calls=%fused_computation.23.clone.1 | convolution fusion | flops 354161280 | bytes 18874368 | tf_op jit(solution)/shard_map/while/body/eval_jaxpr/vmap(hqk,khd->qhd)/dot_general | solution.py:72
  553.2 16.0 %fusion.127 = f32[4,640,8,64]{1,3,2,0:T(8,128)} fusion(bf16[4,8,128,640]{3,2,1,0:T(8,128)(2,1)} %divide_convert_fusion.2, f32[4,8,128,640]{3,2,1,0:T(8,128)} %fusion.126, bf16[4,4,128,8,64]{2,4,3,1,0:T(8,128)(2,1)} %get-tuple-element.247, s32[]{:T(128)} %get-tuple-element.232), kind=kOutput, calls=%fused_computation.21.clone.1 | convolution fusion | flops 353899136 | bytes 37224960 | tf_op jit(solution)/shard_map/while/body/eval_jaxpr/vmap(hqk,qhd->khd)/dot_general | solution.py:75
  569.3 8.2 copy.94
  594.2 7.4 stack.61
  601.6 9.9 pad_maximum_fusion.3
  611.6 11.8 %copy.95 = f32[20,2,128,512]{3,2,1,0:T(8,128)} copy(f32[20,2,128,512]{2,0,3,1:T(8,128)} %pad_maximum_fusion.3) | data formatting | bytes 20971520 | tf_op jit(solution)/shard_map/while/body/eval_jaxpr/vmap()/stack | solution.py:77
  623.5 22.5 %scatter_fusion = f32[9,2,128,512]{3,2,1,0:T(8,128)} fusion(f32[9,2,128,512]{3,2,1,0:T(8,128)} %get-tuple-element.233, s32[20]{0:T(128)S(1)} %fusion.123, f32[20,2,128,512]{3,2,1,0:T(8,128)} %copy.95), kind=kCustom, calls=%fused_computation.1.clone.1 | custom fusion | flops 2621440 | bytes 31457360 | tf_op jit(solution)/shard_map/while/body/eval_jaxpr/scatter-add | solution.py:89
  671.6 9.4 fusion.125
  702.2 7.5 fusion.126
  709.7 14.3 %fusion.128 = bf16[4,8,64,128]{3,2,1,0:T(8,128)(2,1)S(1)} fusion(bf16[4,640,8,64]{1,3,2,0:T(8,128)(2,1)} %squeeze.69, bf16[4,8,128,640]{3,2,1,0:T(8,128)(2,1)} %divide_convert_fusion.2, f32[4,8,128,640]{3,2,1,0:T(8,128)} %fusion.126), kind=kOutput, calls=%fused_computation.23.clone.1 | convolution fusion | flops 354161280 | bytes 18874368 | tf_op jit(solution)/shard_map/while/body/eval_jaxpr/vmap(hqk,khd->qhd)/dot_general | solution.py:72
  732.7 16.0 %fusion.127 = f32[4,640,8,64]{1,3,2,0:T(8,128)} fusion(bf16[4,8,128,640]{3,2,1,0:T(8,128)(2,1)} %divide_convert_fusion.2, f32[4,8,128,640]{3,2,1,0:T(8,128)} %fusion.126, bf16[4,4,128,8,64]{2,4,3,1,0:T(8,128)(2,1)} %get-tuple-element.247, s32[]{:T(128)} %get-tuple-element.232), kind=kOutput, calls=%fused_computation.21.clone.1 | convolution fusion | flops 353899136 | bytes 37224960 | tf_op jit(solution)/shard_map/while/body/eval_jaxpr/vmap(hqk,qhd->khd)/dot_general | solution.py:75
  748.8 8.2 copy.94
  773.7 7.4 stack.61
  781.2 9.9 pad_maximum_fusion.3
  791.1 11.8 %copy.95 = f32[20,2,128,512]{3,2,1,0:T(8,128)} copy(f32[20,2,128,512]{2,0,3,1:T(8,128)} %pad_maximum_fusion.3) | data formatting | bytes 20971520 | tf_op jit(solution)/shard_map/while/body/eval_jaxpr/vmap()/stack | solution.py:77
  803.0 22.1 %scatter_fusion = f32[9,2,128,512]{3,2,1,0:T(8,128)} fusion(f32[9,2,128,512]{3,2,1,0:T(8,128)} %get-tuple-element.233, s32[20]{0:T(128)S(1)} %fusion.123, f32[20,2,128,512]{3,2,1,0:T(8,128)} %copy.95), kind=kCustom, calls=%fused_computation.1.clone.1 | custom fusion | flops 2621440 | bytes 31457360 | tf_op jit(solution)/shard_map/while/body/eval_jaxpr/scatter-add | solution.py:89
  830.7 11.8 %collective-permute-start.12 = (f32[2,128,512]{2,1,0:T(8,128)S(1)}, f32[2,128,512]{2,1,0:T(8,128)S(1)}, u32[]{:S(2)}, u32[]{:S(2)}) collective-permute-start(f32[2,128,512]{2,1,0:T(8,128)S(1)} %get-tuple-element.143), channel_id=1, source_target_pairs={{0,4},{4,8},{8,12},{12,16},{16,20},{20,24},{24,28},{28,32},{32,36}... | collective-permute-start | bytes 1572872 | tf_op jit(solution)/shard_map/ppermute | solution.py:16
  842.5 12.1 %collective-permute-start.13 = (f32[2,128,512]{2,1,0:T(8,128)S(1)}, f32[2,128,512]{2,1,0:T(8,128)S(1)}, u32[]{:S(2)}, u32[]{:S(2)}) collective-permute-start(f32[2,128,512]{2,1,0:T(8,128)S(1)} %get-tuple-element.142), channel_id=1, source_target_pairs={{0,8},{4,12},{8,16},{12,20},{16,24},{20,28},{24,32},{28,36},{32,40... | collective-permute-start | bytes 1572872 | tf_op jit(solution)/shard_map/ppermute | solution.py:16
  858.9 8.1 collective-permute-start.15
  869.6 15.9 %collective-permute-done.13 = f32[2,128,512]{2,1,0:T(8,128)S(1)} collective-permute-done((f32[2,128,512]{2,1,0:T(8,128)S(1)}, f32[2,128,512]{2,1,0:T(8,128)S(1)}, u32[]{:S(2)}, u32[]{:S(2)}) %collective-permute-start.13) | collective-permute-done | bytes 524320 | tf_op jit(solution)/shard_map/ppermute | solution.py:16
  885.5 10.8 collective-permute-done.15
  896.3 15.4 %collective-permute-done.8 = f32[2,128,512]{2,1,0:T(8,128)S(1)} collective-permute-done((f32[2,128,512]{2,1,0:T(8,128)S(1)}, f32[2,128,512]{2,1,0:T(8,128)S(1)}, u32[]{:S(2)}, u32[]{:S(2)}) %collective-permute-start.8) | collective-permute-done | bytes 524320 | tf_op jit(solution)/shard_map/ppermute | solution.py:16
  920.5 9.3 copy.69
  938.5 216.2 %reduce-scatter.7.cloned.1.call-done = f32[64,1024]{1,0:T(8,128)} async-done(((f32[2048,1024]{1,0:T(8,128)}), f32[64,1024]{1,0:T(8,128)}) %reduce-scatter.7.cloned.1.call-update) | async-done | bytes 262160
  (158 shorter events, 370.4 us)
Async XLA Ops:
  7.2 71.7 %copy-start = (bf16[2048,512]{1,0:T(8,128)(2,1)S(1)}, bf16[2048,512]{1,0:T(8,128)(2,1)}, u32[]{:S(2)}) copy-start(bf16[2048,512]{1,0:T(8,128)(2,1)} %param.12) | copy-start | bytes 6291460
  7.2 929.7 %reduce-scatter.5.cloned.1.call-start = ((), (), s32[]{:S(2)}) async-start(), calls=%async_computation.2 | async-start | bytes 1310720 | tf_op jit(solution)/shard_map/reduce_scatter | solution.py:107
  7.2 44.3 %collective-permute-start = (bf16[128,2048]{1,0:T(8,128)(2,1)}, bf16[128,2048]{1,0:T(8,128)(2,1)}, u32[]{:S(2)}, u32[]{:S(2)}) collective-permute-start(bf16[128,2048]{1,0:T(8,128)(2,1)} %param.10), channel_id=1, source_target_pairs={{0,16},{4,20},{8,24},{12,28},{16,32},{20,36},{24,40},{28,44},{32,4... | collective-permute-start | bytes 1572872 | tf_op jit(solution)/shard_map/ppermute | solution.py:16
  13.4 40.6 %collective-permute-start.1 = (bf16[128,2048]{1,0:T(8,128)(2,1)}, bf16[128,2048]{1,0:T(8,128)(2,1)}, u32[]{:S(2)}, u32[]{:S(2)}) collective-permute-start(bf16[128,2048]{1,0:T(8,128)(2,1)} %param.10), channel_id=1, source_target_pairs={{0,12},{4,16},{8,20},{12,24},{16,28},{20,32},{24,36},{28,40},{32,4... | collective-permute-start | bytes 1572872 | tf_op jit(solution)/shard_map/ppermute | solution.py:16
  19.2 38.6 %collective-permute-start.2 = (bf16[128,2048]{1,0:T(8,128)(2,1)}, bf16[128,2048]{1,0:T(8,128)(2,1)}, u32[]{:S(2)}, u32[]{:S(2)}) collective-permute-start(bf16[128,2048]{1,0:T(8,128)(2,1)} %param.10), channel_id=1, source_target_pairs={{0,8},{4,12},{8,16},{12,20},{16,24},{20,28},{24,32},{28,36},{32,40... | collective-permute-start | bytes 1572872 | tf_op jit(solution)/shard_map/ppermute | solution.py:16
  22.1 38.1 %collective-permute-start.3 = (bf16[128,2048]{1,0:T(8,128)(2,1)}, bf16[128,2048]{1,0:T(8,128)(2,1)}, u32[]{:S(2)}, u32[]{:S(2)}) collective-permute-start(bf16[128,2048]{1,0:T(8,128)(2,1)} %param.10), channel_id=1, source_target_pairs={{0,4},{4,8},{8,12},{12,16},{16,20},{20,24},{24,28},{28,32},{32,36}... | collective-permute-start | bytes 1572872 | tf_op jit(solution)/shard_map/ppermute | solution.py:16
  26.2 35.1 %collective-permute-start.4 = (bf16[128,2048]{1,0:T(8,128)(2,1)}, bf16[128,2048]{1,0:T(8,128)(2,1)S(1)}, u32[]{:S(2)}, u32[]{:S(2)}) collective-permute-start(bf16[128,2048]{1,0:T(8,128)(2,1)} %param.10), channel_id=1, source_target_pairs={{4,0},{8,4},{12,8},{16,12},{20,16},{24,20},{28,24},{32,28},{36,32}... | collective-permute-start | bytes 1572872 | tf_op jit(solution)/shard_map/ppermute | solution.py:16
  46.3 5.2 copy-start.1
  51.5 27.1 %collective-permute-start.5 = (bf16[128,2048]{1,0:T(8,128)(2,1)S(1)}, bf16[128,2048]{1,0:T(8,128)(2,1)S(1)}, u32[]{:S(2)}, u32[]{:S(2)}) collective-permute-start(bf16[128,2048]{1,0:T(8,128)(2,1)S(1)} %copy-done.1), channel_id=1, source_target_pairs={{8,0},{12,4},{16,8},{20,12},{24,16},{28,20},{32,24},{36,28},{40,32... | collective-permute-start | bytes 1572872 | tf_op jit(solution)/shard_map/ppermute | solution.py:16
  53.9 24.8 %collective-permute-start.6 = (bf16[128,2048]{1,0:T(8,128)(2,1)S(1)}, bf16[128,2048]{1,0:T(8,128)(2,1)S(1)}, u32[]{:S(2)}, u32[]{:S(2)}) collective-permute-start(bf16[128,2048]{1,0:T(8,128)(2,1)S(1)} %copy-done.1), channel_id=1, source_target_pairs={{12,0},{16,4},{20,8},{24,12},{28,16},{32,20},{36,24},{40,28},{44,3... | collective-permute-start | bytes 1572872 | tf_op jit(solution)/shard_map/ppermute | solution.py:16
  57.8 21.0 %collective-permute-start.7 = (bf16[128,2048]{1,0:T(8,128)(2,1)S(1)}, bf16[128,2048]{1,0:T(8,128)(2,1)S(1)}, u32[]{:S(2)}, u32[]{:S(2)}) collective-permute-start(bf16[128,2048]{1,0:T(8,128)(2,1)S(1)} %copy-done.1), channel_id=1, source_target_pairs={{16,0},{20,4},{24,8},{28,12},{32,16},{36,20},{40,24},{44,28},{48,3... | collective-permute-start | bytes 1572872 | tf_op jit(solution)/shard_map/ppermute | solution.py:16
  78.9 2.6 copy-start.3
  828.0 86.1 %copy-start.4 = (bf16[2048,512]{1,0:T(8,128)(2,1)S(1)}, bf16[2048,512]{1,0:T(8,128)(2,1)}, u32[]{:S(2)}) copy-start(bf16[2048,512]{1,0:T(8,128)(2,1)} %param.11) | copy-start | bytes 6291460
  828.0 30.9 %collective-permute-start.10 = (f32[2,128,512]{2,1,0:T(8,128)S(1)}, f32[2,128,512]{2,1,0:T(8,128)S(1)}, u32[]{:S(2)}, u32[]{:S(2)}) collective-permute-start(f32[2,128,512]{2,1,0:T(8,128)S(1)} %get-tuple-element.145), channel_id=1, source_target_pairs={{8,0},{12,4},{16,8},{20,12},{24,16},{28,20},{32,24},{36,28},{40,32... | collective-permute-start | bytes 1572872 | tf_op jit(solution)/shard_map/ppermute | solution.py:16
  829.4 37.5 %collective-permute-start.11 = (f32[2,128,512]{2,1,0:T(8,128)S(1)}, f32[2,128,512]{2,1,0:T(8,128)S(1)}, u32[]{:S(2)}, u32[]{:S(2)}) collective-permute-start(f32[2,128,512]{2,1,0:T(8,128)S(1)} %get-tuple-element.144), channel_id=1, source_target_pairs={{4,0},{8,4},{12,8},{16,12},{20,16},{24,20},{28,24},{32,28},{36,32}... | collective-permute-start | bytes 1572872 | tf_op jit(solution)/shard_map/ppermute | solution.py:16
  830.7 37.5 %collective-permute-start.12 = (f32[2,128,512]{2,1,0:T(8,128)S(1)}, f32[2,128,512]{2,1,0:T(8,128)S(1)}, u32[]{:S(2)}, u32[]{:S(2)}) collective-permute-start(f32[2,128,512]{2,1,0:T(8,128)S(1)} %get-tuple-element.143), channel_id=1, source_target_pairs={{0,4},{4,8},{8,12},{12,16},{16,20},{20,24},{24,28},{28,32},{32,36}... | collective-permute-start | bytes 1572872 | tf_op jit(solution)/shard_map/ppermute | solution.py:16
  842.5 43.0 %collective-permute-start.13 = (f32[2,128,512]{2,1,0:T(8,128)S(1)}, f32[2,128,512]{2,1,0:T(8,128)S(1)}, u32[]{:S(2)}, u32[]{:S(2)}) collective-permute-start(f32[2,128,512]{2,1,0:T(8,128)S(1)} %get-tuple-element.142), channel_id=1, source_target_pairs={{0,8},{4,12},{8,16},{12,20},{16,24},{20,28},{24,32},{28,36},{32,40... | collective-permute-start | bytes 1572872 | tf_op jit(solution)/shard_map/ppermute | solution.py:16
  854.7 30.9 %collective-permute-start.14 = (f32[2,128,512]{2,1,0:T(8,128)S(1)}, f32[2,128,512]{2,1,0:T(8,128)S(1)}, u32[]{:S(2)}, u32[]{:S(2)}) collective-permute-start(f32[2,128,512]{2,1,0:T(8,128)S(1)} %get-tuple-element.141), channel_id=1, source_target_pairs={{0,12},{4,16},{8,20},{12,24},{16,28},{20,32},{24,36},{28,40},{32,4... | collective-permute-start | bytes 1572872 | tf_op jit(solution)/shard_map/ppermute | solution.py:16
  858.9 37.4 %collective-permute-start.15 = (f32[2,128,512]{2,1,0:T(8,128)S(1)}, f32[2,128,512]{2,1,0:T(8,128)S(1)}, u32[]{:S(2)}, u32[]{:S(2)}) collective-permute-start(f32[2,128,512]{2,1,0:T(8,128)S(1)} %get-tuple-element.140), channel_id=1, source_target_pairs={{0,16},{4,20},{8,24},{12,28},{16,32},{20,36},{24,40},{28,44},{32,4... | collective-permute-start | bytes 1572872 | tf_op jit(solution)/shard_map/ppermute | solution.py:16
  867.0 44.8 %collective-permute-start.8 = (f32[2,128,512]{2,1,0:T(8,128)S(1)}, f32[2,128,512]{2,1,0:T(8,128)S(1)}, u32[]{:S(2)}, u32[]{:S(2)}) collective-permute-start(f32[2,128,512]{2,1,0:T(8,128)S(1)} %get-tuple-element.139), channel_id=1, source_target_pairs={{16,0},{20,4},{24,8},{28,12},{32,16},{36,20},{40,24},{44,28},{48,3... | collective-permute-start | bytes 1572872 | tf_op jit(solution)/shard_map/ppermute | solution.py:16
  868.3 43.5 %collective-permute-start.9 = (f32[2,128,512]{2,1,0:T(8,128)S(1)}, f32[2,128,512]{2,1,0:T(8,128)S(1)}, u32[]{:S(2)}, u32[]{:S(2)}) collective-permute-start(f32[2,128,512]{2,1,0:T(8,128)S(1)} %get-tuple-element.146), channel_id=1, source_target_pairs={{12,0},{16,4},{20,8},{24,12},{28,16},{32,20},{36,24},{40,28},{44,3... | collective-permute-start | bytes 1572872 | tf_op jit(solution)/shard_map/ppermute | solution.py:16
  913.3 2.7 copy-start.2
  915.9 238.7 %reduce-scatter.7.cloned.1.call-start = ((), (), s32[]{:S(2)}) async-start(), calls=%async_computation.3 | async-start | bytes 8650752
Sparse Core Ops, SparseCore 0:
  916.1 20.7 reduce-scatter.4
  939.4 215.2 reduce-scatter.6
where the time goes:
time: 1180 us; the launch traced here: 1160 us
  local copies, waits for them, and re-layouts  381 us (32%)
  waiting for transfers between devices  284 us (24%)
  matrix products  237 us (20%)
  other arithmetic  162 us (14%)
  starting transfers between devices  65.6 us (6%)
  loops' own time  18.5 us (2%)
  between operations  14.8 us (1%)
    unnamed x3, waiting for transfers between devices  216 us
    another operation x12, local copies, waits for them, and re-layouts, one_block(): jnp.stack([dkey.reshape(LISTED, block_rows, head_cols), dvalue.reshape(LI...  107 us
    scatter-add x4, other arithmetic, advance(): running.at[slot_row.reshape(-1)].add(terms.reshape((-1,) + terms.shape[2:]))  89.8 us
    ppermute x16, starting transfers between devices, passed_along(): return lax.ppermute(value, axis, pairs)  65.6 us
    dot_general x4, matrix products, one_block(): jnp.einsum('hqk,qhd->khd', dscores, query, preferred_element_type=jnp.flo...  64.3 us
    ppermute x16, waiting for transfers between devices, passed_along(): return lax.ppermute(value, axis, pairs)  61 us
    dot_general x4, matrix products, one_block(): jnp.einsum('hqk,khd->qhd', dscores, picked_keys, preferred_element_type=j...  57.1 us
    while x16, local copies, waits for them, and re-layouts  57 us
  transfers between devices with their start and end apart: 18, of which 7 were waited for; matrix products, arithmetic and copies ran while one was open for 4% of the time, Pallas kernels for 0%

commit v1 on v0

v1 whole, which is shorter than its diff:
```python
import functools

import jax
import jax.numpy as jnp
from jax import lax
from jax.experimental import pallas as pl
from jax.experimental.pallas import tpu as pltpu
from jax.sharding import PartitionSpec as P

HEAD_DIM = 64
REACH = 4
LISTED = 5
LANES = 128


def passed_along(value, axis, by):
    size = lax.axis_size(axis)
    pairs = [(i, i + by) for i in range(size) if 0 <= i + by < size]
    return lax.ppermute(value, axis, pairs)


def attention_kernel(slots_ref, counts_ref, q_ref, g_ref, stock_ref, out_ref, dq_ref, acc_ref):
    factor = HEAD_DIM ** (-0.5)
    step = pl.program_id(0)

    @pl.when(step == 0)
    def _():
        acc_ref[...] = jnp.zeros_like(acc_ref)

    count = counts_ref[step]
    rows = q_ref.shape[0]
    lane = lax.broadcasted_iota(jnp.int32, (rows, LANES), 1)
    first = lane < HEAD_DIM
    slots = [slots_ref[step, j] for j in range(LISTED)]
    nt = (((1,), (1,)), ((), ()))
    tn = (((0,), (0,)), ((), ()))
    f32 = jnp.float32
    bf16 = jnp.bfloat16

    def pair(p, carry):
        off = pl.multiple_of(p * LANES, LANES)
        qp = q_ref[:, pl.ds(off, LANES)]
        gp = g_ref[:, pl.ds(off, LANES)]
        zq = jnp.zeros_like(qp)
        qh = [jnp.where(first, qp, zq), jnp.where(first, zq, qp)]
        gh = [jnp.where(first, gp, zq), jnp.where(first, zq, gp)]
        ks = [stock_ref[slots[j], 0, :, pl.ds(off, LANES)] for j in range(LISTED)]
        vs = [stock_ref[slots[j], 1, :, pl.ds(off, LANES)] for j in range(LISTED)]
        outs, dqs = [], []
        dks = [None] * LISTED
        dvs = [None] * LISTED
        for h in range(2):
            scores = []
            for j in range(LISTED):
                sc = lax.dot_general(qh[h], ks[j], nt, preferred_element_type=f32) * factor
                scores.append(jnp.where(j < count, sc, -jnp.inf))
            peak = jnp.max(scores[0], axis=1, keepdims=True)
            for j in range(1, LISTED):
                peak = jnp.maximum(peak, jnp.max(scores[j], axis=1, keepdims=True))
            expos = [jnp.exp(sc - peak) for sc in scores]
            total = jnp.sum(expos[0], axis=1, keepdims=True)
            for j in range(1, LISTED):
                total = total + jnp.sum(expos[j], axis=1, keepdims=True)
            ws = [(e / total).astype(bf16) for e in expos]
            out = jnp.dot(ws[0], vs[0], preferred_element_type=f32)
            for j in range(1, LISTED):
                out = out + jnp.dot(ws[j], vs[j], preferred_element_type=f32)
            dws = [lax.dot_general(gh[h], vs[j], nt, preferred_element_type=f32) for j in range(LISTED)]
            wf = [w.astype(f32) for w in ws]
            center = jnp.sum(wf[0] * dws[0], axis=1, keepdims=True)
            for j in range(1, LISTED):
                center = center + jnp.sum(wf[j] * dws[j], axis=1, keepdims=True)
            dss = [(wf[j] * (dws[j] - center) * factor).astype(bf16) for j in range(LISTED)]
            dq = jnp.dot(dss[0], ks[0], preferred_element_type=f32)
            for j in range(1, LISTED):
                dq = dq + jnp.dot(dss[j], ks[j], preferred_element_type=f32)
            for j in range(LISTED):
                dk = lax.dot_general(dss[j], qh[h], tn, preferred_element_type=f32)
                dv = lax.dot_general(ws[j], gh[h], tn, preferred_element_type=f32)
                dks[j] = dk if dks[j] is None else dks[j] + dk
                dvs[j] = dv if dvs[j] is None else dvs[j] + dv
            outs.append(out)
            dqs.append(dq)
        out_ref[:, pl.ds(off, LANES)] = jnp.where(first, outs[0], outs[1]).astype(out_ref.dtype)
        dq_ref[:, pl.ds(off, LANES)] = jnp.where(first, dqs[0], dqs[1]).astype(dq_ref.dtype)
        for j in range(LISTED):
            acc_ref[slots[j], 0, :, pl.ds(off, LANES)] += dks[j]
            acc_ref[slots[j], 1, :, pl.ds(off, LANES)] += dvs[j]
        return carry

    lax.fori_loop(0, q_ref.shape[1] // LANES, pair, 0)


def attention(queries, out_grad, stock, slot_ids, counts):
    rows, cols = stock.shape[2], stock.shape[3]
    blocks = queries.shape[0] // rows
    n_slots = stock.shape[0]
    flops = blocks * (cols // LANES) * 2 * LISTED * 6 * 2 * rows * LANES * LANES
    bytes_accessed = 4 * queries.size * 2 + stock.size * 2 + stock.size * 4
    grid_spec = pltpu.PrefetchScalarGridSpec(
        num_scalar_prefetch=2,
        grid=(blocks,),
        in_specs=[
            pl.BlockSpec((rows, cols), lambda i, s, c: (i, 0)),
            pl.BlockSpec((rows, cols), lambda i, s, c: (i, 0)),
            pl.BlockSpec((n_slots, 2, rows, cols), lambda i, s, c: (0, 0, 0, 0)),
        ],
        out_specs=[
            pl.BlockSpec((rows, cols), lambda i, s, c: (i, 0)),
            pl.BlockSpec((rows, cols), lambda i, s, c: (i, 0)),
            pl.BlockSpec((n_slots, 2, rows, cols), lambda i, s, c: (0, 0, 0, 0)),
        ],
    )
    return pl.pallas_call(
        attention_kernel,
        grid_spec=grid_spec,
        out_shape=[
            jax.ShapeDtypeStruct(queries.shape, jnp.bfloat16),
            jax.ShapeDtypeStruct(queries.shape, jnp.bfloat16),
            jax.ShapeDtypeStruct(stock.shape, jnp.float32),
        ],
        compiler_params=pltpu.CompilerParams(dimension_semantics=("arbitrary",)),
        cost_estimate=pl.CostEstimate(
            flops=flops, transcendentals=blocks * rows * LISTED * rows * (cols // HEAD_DIM),
            bytes_accessed=bytes_accessed,
        ),
    )(slot_ids, counts, queries, out_grad, stock)


def on_device(queries, encoder, key_weight, value_weight, out_grad, block_lists, list_counts):
    position = lax.axis_index("blk")
    head_cols = key_weight.shape[1]
    own_keys = jnp.dot(encoder, key_weight, preferred_element_type=jnp.float32).astype(jnp.bfloat16)
    own_values = jnp.dot(encoder, value_weight, preferred_element_type=jnp.float32).astype(
        jnp.bfloat16
    )
    own = jnp.stack([own_keys, own_values], 0)
    arrived = []
    for offset in range(-REACH, REACH + 1):
        if offset == 0:
            arrived.append(own)
        else:
            arrived.append(passed_along(own, "blk", -offset))
    stock = jnp.stack(arrived, 0)
    slot_ids = (block_lists - (position - REACH)).astype(jnp.int32)
    attended, query_grad, running = attention(
        queries, out_grad, stock, slot_ids, list_counts.astype(jnp.int32)
    )
    owned = running[REACH]
    for offset in range(-REACH, REACH + 1):
        if offset != 0:
            owned = owned + passed_along(running[REACH + offset], "blk", offset)
    rounded = owned.astype(jnp.bfloat16)
    contract_cols = (((1,), (1,)), ((), ()))
    encoder_terms = lax.dot_general(
        rounded[0], key_weight, contract_cols, preferred_element_type=jnp.float32
    ) + lax.dot_general(rounded[1], value_weight, contract_cols, preferred_element_type=jnp.float32)
    encoder_grad = lax.psum_scatter(encoder_terms, "grp", scatter_dimension=1, tiled=True).astype(
        jnp.bfloat16
    )
    both_grads = jnp.concatenate([rounded[0], rounded[1]], 1)
    weight_rows = lax.psum_scatter(
        lax.dot_general(
            encoder, both_grads, (((0,), (0,)), ((), ())), preferred_element_type=jnp.float32
        ),
        "blk",
        scatter_dimension=0,
        tiled=True,
    )
    return (
        attended,
        query_grad,
        encoder_grad,
        weight_rows[:, :head_cols],
        weight_rows[:, head_cols:],
    )


def solution(mesh):
    in_specs = (
        P("blk", "grp"),
        P("blk", None),
        P(None, "grp"),
        P(None, "grp"),
        P("blk", "grp"),
        P("blk", None),
        P("blk"),
    )
    out_specs = (
        P("blk", "grp"),
        P("blk", "grp"),
        P("blk", "grp"),
        P("blk", "grp"),
        P("blk", "grp"),
    )
    return jax.shard_map(
        on_device, mesh=mesh, in_specs=in_specs, out_specs=out_specs, check_vma=False
    )
```

time: 1180 us -> 534 us (0.45); the launches traced: 1160 us -> 533 us
  local copies, waits for them, and re-layouts: 381 us -> 24.4 us
  matrix products: 237 us -> 9.92 us
  other arithmetic: 162 us -> 4.46 us
  Pallas kernels: 0 us -> 138 us
  loops' own time: 18.5 us -> 0 us
    dot_general x22 -> x2, matrix products: 193 us -> 2.79 us  [the longest x1 2.35 us: on_device(): jnp.dot(encoder, key_weight, preferred_element_type=jnp.float32)]
    pallas_call x0 -> x1, Pallas kernels: none -> 138 us  [attention(): pl.pallas_call(attention_kernel, grid_spec=grid_spec, out_shape=[jax.Shap...]
    another operation x13 -> x1, local copies, waits for them, and re-layouts: 107 us -> 0.74 us  [on_device(): stock = jnp.stack(arrived, 0)]
    scatter-add x4 -> x0, other arithmetic: 89.8 us -> none  [advance(): running.at[slot_row.reshape(-1)].add(terms.reshape((-1,) + terms.shape[2:]))]
    while x20 -> x0, local copies, waits for them, and re-layouts: 68.9 us -> none
    squeeze x12 -> x0, local copies, waits for them, and re-layouts: 57.1 us -> none  [the longest x4 28.6 us: one_block(): picked[:, 1].reshape(LISTED * block_rows, heads_here, HEAD_DIM)]
    transpose x8 -> x0, local copies, waits for them, and re-layouts: 55.4 us -> none  [the longest x4 32.7 us: one_block(): jnp.einsum('hqk,qhd->khd', dscores, query, preferred_element_type=jnp.flo...]
    another operation x7 -> x1, other arithmetic: 40 us -> 0.03 us  [on_device(): own = jnp.stack([own_keys, own_values], 0)]
  transfers between devices with their start and end apart: 18 -> 18, of which waited for: 7 -> 9; matrix products, arithmetic and copies ran while one was open for 4% -> 5% of each run, Pallas kernels for 0% -> 0%
where the time goes in v1:
time: 534 us; the launch traced here: 533 us
  waiting for transfers between devices  285 us (53%)
  Pallas kernels  138 us (26%)
  starting transfers between devices  56.6 us (11%)
  local copies, waits for them, and re-layouts  24.4 us (5%)
  between operations  14.3 us (3%)
  matrix products  9.92 us (2%)
    unnamed x3, waiting for transfers between devices  217 us
    pallas_call x1, Pallas kernels, attention(): pl.pallas_call(attention_kernel, grid_spec=grid_spec, out_shape=[jax.Shap...  138 us
    ppermute x16, starting transfers between devices, passed_along(): return lax.ppermute(value, axis, pairs)  56.5 us
    ppermute x16, waiting for transfers between devices, passed_along(): return lax.ppermute(value, axis, pairs)  48.1 us
    reduce_scatter x1, waiting for transfers between devices, on_device(): lax.psum_scatter(encoder_terms, 'grp', scatter_dimension=1, tiled=True)  20.5 us
    unnamed x17, local copies, waits for them, and re-layouts  19.1 us
  transfers between devices with their start and end apart: 18, of which 9 were waited for; matrix products, arithmetic and copies ran while one was open for 5% of the time, Pallas kernels for 0%

profile of v1, /device:TPU:0, one launch (start us, length us, event | category | flops | bytes accessed | tf_op | source)
XLA Modules:
  0.0 532.8 jit_solution(16351281319498023874)
XLA Ops:
  7.2 2.3 fusion
  9.6 0.4 fusion.1
  10.1 5.9 %collective-permute-start = (bf16[2,128,512]{2,1,0:T(8,128)(2,1)S(1)}, bf16[2,128,512]{2,1,0:T(8,128)(2,1)}, u32[]{:S(2)}, u32[]{:S(2)}) collective-permute-start(bf16[2,128,512]{2,1,0:T(8,128)(2,1)S(1)} %pad_maximum_fusion), channel_id=1, source_target_pairs={{0,16},{4,20},{8,24},{12,28},{16,32},{20,36},{24,40},{28,44},{32,4... | collective-permute-start | bytes 786440 | tf_op jit(solution)/shard_map/ppermute | solution.py:19
  16.0 1.3 collective-permute-start.6
  17.3 1.3 collective-permute-start.5
  18.6 1.3 collective-permute-start.4
  19.9 8.9 %collective-permute-start.1 = (bf16[2,128,512]{2,1,0:T(8,128)(2,1)S(1)}, bf16[2,128,512]{2,1,0:T(8,128)(2,1)}, u32[]{:S(2)}, u32[]{:S(2)}) collective-permute-start(bf16[2,128,512]{2,1,0:T(8,128)(2,1)S(1)} %pad_maximum_fusion), channel_id=1, source_target_pairs={{0,12},{4,16},{8,20},{12,24},{16,28},{20,32},{24,36},{28,40},{32,4... | collective-permute-start | bytes 786440 | tf_op jit(solution)/shard_map/ppermute | solution.py:19
  28.8 0.1 copy.18
  28.9 0.6 broadcast_subtract_fusion.slots_ref
  29.5 6.4 %collective-permute-start.2 = (bf16[2,128,512]{2,1,0:T(8,128)(2,1)S(1)}, bf16[2,128,512]{2,1,0:T(8,128)(2,1)S(1)}, u32[]{:S(2)}, u32[]{:S(2)}) collective-permute-start(bf16[2,128,512]{2,1,0:T(8,128)(2,1)S(1)} %pad_maximum_fusion), channel_id=1, source_target_pairs={{0,8},{4,12},{8,16},{12,20},{16,24},{20,28},{24,32},{28,36},{32,40... | collective-permute-start | bytes 786440 | tf_op jit(solution)/shard_map/ppermute | solution.py:19
  35.9 1.7 bitcast_dynamic-update-slice_fusion.8
  37.6 3.2 collective-permute-start.3
  40.8 1.7 bitcast_dynamic-update-slice_fusion.7
  42.5 6.1 %collective-permute-done.2 = bf16[2,128,512]{2,1,0:T(8,128)(2,1)S(1)} collective-permute-done((bf16[2,128,512]{2,1,0:T(8,128)(2,1)S(1)}, bf16[2,128,512]{2,1,0:T(8,128)(2,1)S(1)}, u32[]{:S(2)}, u32[]{:S(2)}) %collective-permute-start.2) | collective-permute-done | bytes 262176 | tf_op jit(solution)/shard_map/ppermute | solution.py:19
  48.5 1.3 collective-permute-start.7
  49.8 0.7 bitcast_dynamic-update-slice_fusion.6
  50.5 0.7 bitcast_dynamic-update-slice_fusion.5
  51.3 0.7 bitcast_dynamic-update-slice_fusion.4
  52.0 1.7 bitcast_dynamic-update-slice_fusion.3
  53.6 1.7 bitcast_dynamic-update-slice_fusion.2
  55.3 0.7 bitcast_dynamic-update-slice_fusion.1
  56.0 4.4 collective-permute-done.7
  60.5 0.7 bitcast_dynamic-update-slice_fusion.stock_ref
  61.2 138.1 %shard_map.110 = (bf16[2048,512]{1,0:T(8,128)(2,1)}, bf16[2048,512]{1,0:T(8,128)(2,1)}, f32[9,2,128,512]{3,2,1,0:T(8,128)}) custom-call(s32[16,5]{1,0:T(8,128)} %broadcast_subtract_fusion.slots_ref, s32[16]{0:T(128)} %counts_ref.1, bf16[2048,512]{1,0:T(8,128)(2,1)} %q_ref.1, bf16[2048,512]{1,0:T(8,128)(2,1)} %g_ref.1, ...), custom_call_target="tpu_custom_call" | custom-call | flops 16106127360 | bytes 15466496 | tf_op jit(solution)/shard_map/pallas_call | solution.py:114
  199.3 2.9 slice_bitcast_fusion.7
  202.2 1.3 collective-permute-start.8
  203.5 6.1 %collective-permute-start.15 = (f32[2,128,512]{2,1,0:T(8,128)S(1)}, f32[2,128,512]{2,1,0:T(8,128)S(1)}, u32[]{:S(2)}, u32[]{:S(2)}) collective-permute-start(f32[2,128,512]{2,1,0:T(8,128)S(1)} %get-tuple-element.27), channel_id=1, source_target_pairs={{0,16},{4,20},{8,24},{12,28},{16,32},{20,36},{24,40},{28,44},{32,4... | collective-permute-start | bytes 1572872 | tf_op jit(solution)/shard_map/ppermute | solution.py:19
  209.6 1.6 collective-permute-start.14
  211.2 4.9 collective-permute-start.13
  216.1 9.2 %collective-permute-start.12 = (f32[2,128,512]{2,1,0:T(8,128)S(1)}, f32[2,128,512]{2,1,0:T(8,128)S(1)}, u32[]{:S(2)}, u32[]{:S(2)}) collective-permute-start(f32[2,128,512]{2,1,0:T(8,128)S(1)} %get-tuple-element.30), channel_id=1, source_target_pairs={{0,4},{4,8},{8,12},{12,16},{16,20},{20,24},{24,28},{28,32},{32,36}... | collective-permute-start | bytes 1572872 | tf_op jit(solution)/shard_map/ppermute | solution.py:19
  225.3 17.2 %collective-permute-done.8 = f32[2,128,512]{2,1,0:T(8,128)S(1)} collective-permute-done((f32[2,128,512]{2,1,0:T(8,128)S(1)}, f32[2,128,512]{2,1,0:T(8,128)S(1)}, u32[]{:S(2)}, u32[]{:S(2)}) %collective-permute-start.8) | collective-permute-done | bytes 524320 | tf_op jit(solution)/shard_map/ppermute | solution.py:19
  242.6 1.3 collective-permute-start.11
  243.8 0.6 collective-permute-done.15
  244.5 1.3 collective-permute-start.10
  245.8 1.3 collective-permute-start.9
  247.1 6.1 %collective-permute-done.13 = f32[2,128,512]{2,1,0:T(8,128)S(1)} collective-permute-done((f32[2,128,512]{2,1,0:T(8,128)S(1)}, f32[2,128,512]{2,1,0:T(8,128)S(1)}, u32[]{:S(2)}, u32[]{:S(2)}) %collective-permute-start.13) | collective-permute-done | bytes 524320 | tf_op jit(solution)/shard_map/ppermute | solution.py:19
  253.2 2.0 collective-permute-done.11
  255.1 11.6 %collective-permute-done.10 = f32[2,128,512]{2,1,0:T(8,128)S(1)} collective-permute-done((f32[2,128,512]{2,1,0:T(8,128)S(1)}, f32[2,128,512]{2,1,0:T(8,128)S(1)}, u32[]{:S(2)}, u32[]{:S(2)}) %collective-permute-start.10) | collective-permute-done | bytes 524320 | tf_op jit(solution)/shard_map/ppermute | solution.py:19
  266.8 1.5 fusion.9
  268.3 0.8 fusion.14
  269.1 0.8 copy-done.1
  269.9 1.8 convolution_add_fusion
  271.8 4.5 convolution_bitcast_fusion
  276.3 9.3 %copy.22 = f32[2048,1024]{1,0:T(8,128)} copy(f32[2048,1024]{0,1:T(8,128)} %convolution_bitcast_fusion) | data formatting | bytes 16777216
  285.6 20.5 %reduce-scatter.5.cloned.1.call-done = f32[128,512]{1,0:T(8,128)} async-done(((f32[128,2048]{1,0:T(8,128)}), f32[128,512]{1,0:T(8,128)}) %reduce-scatter.5.cloned.1.call-update) | async-done | bytes 262160 | tf_op jit(solution)/shard_map/reduce_scatter | solution.py:158
  306.2 1.6 convert_element_type.15
  307.8 216.5 %reduce-scatter.7.cloned.1.call-done = f32[64,1024]{1,0:T(8,128)} async-done(((f32[2048,1024]{1,0:T(8,128)}), f32[64,1024]{1,0:T(8,128)}) %reduce-scatter.7.cloned.1.call-update) | async-done | bytes 262160
  524.3 1.7 fusion.15
  (22 shorter events, 0.2 us)
Async XLA Ops:
  7.2 2.4 copy-start
  7.2 2.5 copy-start.2
  7.2 21.6 %copy-start.3 = (s32[16,5]{0,1:T(8,128)S(1)}, s32[16,5]{0,1:T(8,128)}, u32[]{:S(2)}) copy-start(s32[16,5]{0,1:T(8,128)} %param.12) | copy-start | bytes 964
  7.2 299.0 %reduce-scatter.5.cloned.1.call-start = ((), (), s32[]{:S(2)}) async-start(), calls=%async_computation.2 | async-start | bytes 1310720 | tf_op jit(solution)/shard_map/reduce_scatter | solution.py:158
  10.1 19.4 %collective-permute-start = (bf16[2,128,512]{2,1,0:T(8,128)(2,1)S(1)}, bf16[2,128,512]{2,1,0:T(8,128)(2,1)}, u32[]{:S(2)}, u32[]{:S(2)}) collective-permute-start(bf16[2,128,512]{2,1,0:T(8,128)(2,1)S(1)} %pad_maximum_fusion), channel_id=1, source_target_pairs={{0,16},{4,20},{8,24},{12,28},{16,32},{20,36},{24,40},{28,44},{32,4... | collective-permute-start | bytes 786440 | tf_op jit(solution)/shard_map/ppermute | solution.py:19
  16.0 39.3 %collective-permute-start.6 = (bf16[2,128,512]{2,1,0:T(8,128)(2,1)S(1)}, bf16[2,128,512]{2,1,0:T(8,128)(2,1)S(1)}, u32[]{:S(2)}, u32[]{:S(2)}) collective-permute-start(bf16[2,128,512]{2,1,0:T(8,128)(2,1)S(1)} %pad_maximum_fusion), channel_id=1, source_target_pairs={{12,0},{16,4},{20,8},{24,12},{28,16},{32,20},{36,24},{40,28},{44,3... | collective-permute-start | bytes 786440 | tf_op jit(solution)/shard_map/ppermute | solution.py:19
  17.3 36.3 %collective-permute-start.5 = (bf16[2,128,512]{2,1,0:T(8,128)(2,1)S(1)}, bf16[2,128,512]{2,1,0:T(8,128)(2,1)}, u32[]{:S(2)}, u32[]{:S(2)}) collective-permute-start(bf16[2,128,512]{2,1,0:T(8,128)(2,1)S(1)} %pad_maximum_fusion), channel_id=1, source_target_pairs={{8,0},{12,4},{16,8},{20,12},{24,16},{28,20},{32,24},{36,28},{40,32... | collective-permute-start | bytes 786440 | tf_op jit(solution)/shard_map/ppermute | solution.py:19
  18.6 33.4 %collective-permute-start.4 = (bf16[2,128,512]{2,1,0:T(8,128)(2,1)S(1)}, bf16[2,128,512]{2,1,0:T(8,128)(2,1)}, u32[]{:S(2)}, u32[]{:S(2)}) collective-permute-start(bf16[2,128,512]{2,1,0:T(8,128)(2,1)S(1)} %pad_maximum_fusion), channel_id=1, source_target_pairs={{4,0},{8,4},{12,8},{16,12},{20,16},{24,20},{28,24},{32,28},{36,32}... | collective-permute-start | bytes 786440 | tf_op jit(solution)/shard_map/ppermute | solution.py:19
  19.9 17.7 %collective-permute-start.1 = (bf16[2,128,512]{2,1,0:T(8,128)(2,1)S(1)}, bf16[2,128,512]{2,1,0:T(8,128)(2,1)}, u32[]{:S(2)}, u32[]{:S(2)}) collective-permute-start(bf16[2,128,512]{2,1,0:T(8,128)(2,1)S(1)} %pad_maximum_fusion), channel_id=1, source_target_pairs={{0,12},{4,16},{8,20},{12,24},{16,28},{20,32},{24,36},{28,40},{32,4... | collective-permute-start | bytes 786440 | tf_op jit(solution)/shard_map/ppermute | solution.py:19
  29.5 19.0 %collective-permute-start.2 = (bf16[2,128,512]{2,1,0:T(8,128)(2,1)S(1)}, bf16[2,128,512]{2,1,0:T(8,128)(2,1)S(1)}, u32[]{:S(2)}, u32[]{:S(2)}) collective-permute-start(bf16[2,128,512]{2,1,0:T(8,128)(2,1)S(1)} %pad_maximum_fusion), channel_id=1, source_target_pairs={{0,8},{4,12},{8,16},{12,20},{16,24},{20,28},{24,32},{28,36},{32,40... | collective-permute-start | bytes 786440 | tf_op jit(solution)/shard_map/ppermute | solution.py:19
  37.6 13.0 %collective-permute-start.3 = (bf16[2,128,512]{2,1,0:T(8,128)(2,1)S(1)}, bf16[2,128,512]{2,1,0:T(8,128)(2,1)S(1)}, u32[]{:S(2)}, u32[]{:S(2)}) collective-permute-start(bf16[2,128,512]{2,1,0:T(8,128)(2,1)S(1)} %pad_maximum_fusion), channel_id=1, source_target_pairs={{0,4},{4,8},{8,12},{12,16},{16,20},{20,24},{24,28},{28,32},{32,36}... | collective-permute-start | bytes 786440 | tf_op jit(solution)/shard_map/ppermute | solution.py:19
  48.5 12.0 %collective-permute-start.7 = (bf16[2,128,512]{2,1,0:T(8,128)(2,1)S(1)}, bf16[2,128,512]{2,1,0:T(8,128)(2,1)S(1)}, u32[]{:S(2)}, u32[]{:S(2)}) collective-permute-start(bf16[2,128,512]{2,1,0:T(8,128)(2,1)S(1)} %pad_maximum_fusion), channel_id=1, source_target_pairs={{16,0},{20,4},{24,8},{28,12},{32,16},{36,20},{40,24},{44,28},{48,3... | collective-permute-start | bytes 786440 | tf_op jit(solution)/shard_map/ppermute | solution.py:19
  202.2 40.4 %collective-permute-start.8 = (f32[2,128,512]{2,1,0:T(8,128)S(1)}, f32[2,128,512]{2,1,0:T(8,128)S(1)}, u32[]{:S(2)}, u32[]{:S(2)}) collective-permute-start(f32[2,128,512]{2,1,0:T(8,128)S(1)} %get-tuple-element.26), channel_id=1, source_target_pairs={{16,0},{20,4},{24,8},{28,12},{32,16},{36,20},{40,24},{44,28},{48,3... | collective-permute-start | bytes 1572872 | tf_op jit(solution)/shard_map/ppermute | solution.py:19
  203.5 41.0 %collective-permute-start.15 = (f32[2,128,512]{2,1,0:T(8,128)S(1)}, f32[2,128,512]{2,1,0:T(8,128)S(1)}, u32[]{:S(2)}, u32[]{:S(2)}) collective-permute-start(f32[2,128,512]{2,1,0:T(8,128)S(1)} %get-tuple-element.27), channel_id=1, source_target_pairs={{0,16},{4,20},{8,24},{12,28},{16,32},{20,36},{24,40},{28,44},{32,4... | collective-permute-start | bytes 1572872 | tf_op jit(solution)/shard_map/ppermute | solution.py:19
  209.6 36.2 %collective-permute-start.14 = (f32[2,128,512]{2,1,0:T(8,128)S(1)}, f32[2,128,512]{2,1,0:T(8,128)S(1)}, u32[]{:S(2)}, u32[]{:S(2)}) collective-permute-start(f32[2,128,512]{2,1,0:T(8,128)S(1)} %get-tuple-element.28), channel_id=1, source_target_pairs={{0,12},{4,16},{8,20},{12,24},{16,28},{20,32},{24,36},{28,40},{32,4... | collective-permute-start | bytes 1572872 | tf_op jit(solution)/shard_map/ppermute | solution.py:19
  211.2 42.0 %collective-permute-start.13 = (f32[2,128,512]{2,1,0:T(8,128)S(1)}, f32[2,128,512]{2,1,0:T(8,128)S(1)}, u32[]{:S(2)}, u32[]{:S(2)}) collective-permute-start(f32[2,128,512]{2,1,0:T(8,128)S(1)} %get-tuple-element.29), channel_id=1, source_target_pairs={{0,8},{4,12},{8,16},{12,20},{16,24},{20,28},{24,32},{28,36},{32,40... | collective-permute-start | bytes 1572872 | tf_op jit(solution)/shard_map/ppermute | solution.py:19
  216.1 37.0 %collective-permute-start.12 = (f32[2,128,512]{2,1,0:T(8,128)S(1)}, f32[2,128,512]{2,1,0:T(8,128)S(1)}, u32[]{:S(2)}, u32[]{:S(2)}) collective-permute-start(f32[2,128,512]{2,1,0:T(8,128)S(1)} %get-tuple-element.30), channel_id=1, source_target_pairs={{0,4},{4,8},{8,12},{12,16},{16,20},{20,24},{24,28},{28,32},{32,36}... | collective-permute-start | bytes 1572872 | tf_op jit(solution)/shard_map/ppermute | solution.py:19
  242.6 12.6 %collective-permute-start.11 = (f32[2,128,512]{2,1,0:T(8,128)S(1)}, f32[2,128,512]{2,1,0:T(8,128)S(1)}, u32[]{:S(2)}, u32[]{:S(2)}) collective-permute-start(f32[2,128,512]{2,1,0:T(8,128)S(1)} %get-tuple-element.31), channel_id=1, source_target_pairs={{4,0},{8,4},{12,8},{16,12},{20,16},{24,20},{28,24},{32,28},{36,32}... | collective-permute-start | bytes 1572872 | tf_op jit(solution)/shard_map/ppermute | solution.py:19
  244.5 22.3 %collective-permute-start.10 = (f32[2,128,512]{2,1,0:T(8,128)S(1)}, f32[2,128,512]{2,1,0:T(8,128)S(1)}, u32[]{:S(2)}, u32[]{:S(2)}) collective-permute-start(f32[2,128,512]{2,1,0:T(8,128)S(1)} %get-tuple-element.32), channel_id=1, source_target_pairs={{8,0},{12,4},{16,8},{20,12},{24,16},{28,20},{32,24},{36,28},{40,32... | collective-permute-start | bytes 1572872 | tf_op jit(solution)/shard_map/ppermute | solution.py:19
  245.8 21.0 %collective-permute-start.9 = (f32[2,128,512]{2,1,0:T(8,128)S(1)}, f32[2,128,512]{2,1,0:T(8,128)S(1)}, u32[]{:S(2)}, u32[]{:S(2)}) collective-permute-start(f32[2,128,512]{2,1,0:T(8,128)S(1)} %get-tuple-element.33), channel_id=1, source_target_pairs={{12,0},{16,4},{20,8},{24,12},{28,16},{32,20},{36,24},{40,28},{44,3... | collective-permute-start | bytes 1572872 | tf_op jit(solution)/shard_map/ppermute | solution.py:19
  268.3 1.6 copy-start.1
  271.7 252.6 %reduce-scatter.7.cloned.1.call-start = ((), (), s32[]{:S(2)}) async-start(), calls=%async_computation.3 | async-start | bytes 8650752
Sparse Core Ops, SparseCore 0:
  271.8 34.2 reduce-scatter.4
  308.7 215.5 reduce-scatter.6

commit v2 on v1

--- a/solution.py
+++ b/solution.py
@@ -13,8 +13,7 @@
 LANES = 128
 
 
-def passed_along(value, axis, by):
-    size = lax.axis_size(axis)
+def passed_along(value, axis, by, size):
     pairs = [(i, i + by) for i in range(size) if 0 <= i + by < size]
     return lax.ppermute(value, axis, pairs)
 
@@ -127,9 +126,14 @@
     )(slot_ids, counts, queries, out_grad, stock)
 
 
-def on_device(queries, encoder, key_weight, value_weight, out_grad, block_lists, list_counts):
-    position = lax.axis_index("blk")
+def on_device(
+    queries, encoder, key_weight, value_weight, out_grad, block_lists, list_counts, outer, inner
+):
+    blk = ("bz", "byx")
+    position = lax.axis_index(blk)
     head_cols = key_weight.shape[1]
+    model = encoder.shape[1]
+    near = lax.all_gather(encoder, "byx", axis=0, tiled=False)
     own_keys = jnp.dot(encoder, key_weight, preferred_element_type=jnp.float32).astype(jnp.bfloat16)
     own_values = jnp.dot(encoder, value_weight, preferred_element_type=jnp.float32).astype(
         jnp.bfloat16
@@ -140,7 +144,7 @@
         if offset == 0:
             arrived.append(own)
         else:
-            arrived.append(passed_along(own, "blk", -offset))
+            arrived.append(passed_along(own, blk, -offset, outer * inner))
     stock = jnp.stack(arrived, 0)
     slot_ids = (block_lists - (position - REACH)).astype(jnp.int32)
     attended, query_grad, running = attention(
@@ -149,7 +153,7 @@
     owned = running[REACH]
     for offset in range(-REACH, REACH + 1):
         if offset != 0:
-            owned = owned + passed_along(running[REACH + offset], "blk", offset)
+            owned = owned + passed_along(running[REACH + offset], blk, offset, outer * inner)
     rounded = owned.astype(jnp.bfloat16)
     contract_cols = (((1,), (1,)), ((), ()))
     encoder_terms = lax.dot_general(
@@ -159,14 +163,19 @@
         jnp.bfloat16
     )
     both_grads = jnp.concatenate([rounded[0], rounded[1]], 1)
-    weight_rows = lax.psum_scatter(
-        lax.dot_general(
-            encoder, both_grads, (((0,), (0,)), ((), ())), preferred_element_type=jnp.float32
-        ),
-        "blk",
-        scatter_dimension=0,
-        tiled=True,
-    )
+    group_grads = lax.all_gather(both_grads, "byx", axis=0, tiled=True)
+    rows = encoder.shape[0]
+    slice_rows = model // (outer * inner)
+    picked = lax.dynamic_slice_in_dim(
+        near.reshape(inner * rows, outer, inner, slice_rows),
+        lax.axis_index("byx"),
+        1,
+        axis=2,
+    ).reshape(inner * rows, outer * slice_rows)
+    partial = lax.dot_general(
+        picked, group_grads, (((0,), (0,)), ((), ())), preferred_element_type=jnp.float32
+    )
+    weight_rows = lax.psum_scatter(partial, "bz", scatter_dimension=0, tiled=True)
     return (
         attended,
         query_grad,
@@ -177,22 +186,33 @@
 
 
 def solution(mesh):
+    blk_size, grp_size = mesh.devices.shape
+    outer = 4 if blk_size % 4 == 0 else 1
+    inner = blk_size // outer
+    split = jax.sharding.Mesh(
+        mesh.devices.reshape(outer, inner, grp_size), ("bz", "byx", "grp")
+    )
+    blk = ("bz", "byx")
     in_specs = (
-        P("blk", "grp"),
-        P("blk", None),
+        P(blk, "grp"),
+        P(blk, None),
         P(None, "grp"),
         P(None, "grp"),
-        P("blk", "grp"),
-        P("blk", None),
-        P("blk"),
+        P(blk, "grp"),
+        P(blk, None),
+        P(blk),
     )
     out_specs = (
-        P("blk", "grp"),
-        P("blk", "grp"),
-        P("blk", "grp"),
-        P("blk", "grp"),
-        P("blk", "grp"),
+        P(blk, "grp"),
+        P(blk, "grp"),
+        P(blk, "grp"),
+        P(blk, "grp"),
+        P(blk, "grp"),
     )
     return jax.shard_map(
-        on_device, mesh=mesh, in_specs=in_specs, out_specs=out_specs, check_vma=False
-    )
+        functools.partial(on_device, outer=outer, inner=inner),
+        mesh=split,
+        in_specs=in_specs,
+        out_specs=out_specs,
+        check_vma=False,
+    )

time: 534 us -> 372 us (0.70)
  waiting for transfers between devices: 285 us -> 140 us
  starting transfers between devices: 56.6 us -> 47.8 us
  local copies, waits for them, and re-layouts: 24.4 us -> 16.5 us
    unnamed x3 -> x4, waiting for transfers between devices: 217 us -> 0.07 us
    all_gather x0 -> x2, waiting for transfers between devices: none -> 58.4 us  [the longest x1 58.4 us: on_device(): group_grads = lax.all_gather(both_grads, 'byx', axis=0, tiled=True)]
    reduce_scatter x1, waiting for transfers between devices: 20.5 us -> 0.03 us  [on_device(): lax.psum_scatter(encoder_terms, 'grp', scatter_dimension=1, tiled=True)]
    reduce_scatter x0 -> x1, waiting for transfers between devices: none -> 20.1 us  [on_device(): lax.psum_scatter(partial, 'bz', scatter_dimension=0, tiled=True)]
    ppermute x16, waiting for transfers between devices: 48.1 us -> 60.9 us  [passed_along(): return lax.ppermute(value, axis, pairs)]
    unnamed x17 -> x19, local copies, waits for them, and re-layouts: 19.1 us -> 10.2 us
    ppermute x16, starting transfers between devices: 56.5 us -> 47.6 us  [passed_along(): return lax.ppermute(value, axis, pairs)]
  transfers between devices with their start and end apart: 18 -> 20, of which waited for: 9 -> 11; matrix products, arithmetic and copies ran while one was open for 5% -> 7% of each run, Pallas kernels for 0% -> 37%
where the time goes in v2:
time: 372 us; the launch traced here: 371 us
  waiting for transfers between devices  140 us (38%)
  Pallas kernels  138 us (37%)
  starting transfers between devices  47.8 us (13%)
  local copies, waits for them, and re-layouts  16.5 us (4%)
  between operations  15.8 us (4%)
  matrix products  7.97 us (2%)
  other arithmetic  5.23 us (1%)
    pallas_call x1, Pallas kernels, attention(): pl.pallas_call(attention_kernel, grid_spec=grid_spec, out_shape=[jax.Shap...  138 us
    ppermute x16, waiting for transfers between devices, passed_along(): return lax.ppermute(value, axis, pairs)  60.9 us
    all_gather x1, waiting for transfers between devices, on_device(): group_grads = lax.all_gather(both_grads, 'byx', axis=0, tiled=True)  58.4 us
    ppermute x16, starting transfers between devices, passed_along(): return lax.ppermute(value, axis, pairs)  47.6 us
    reduce_scatter x1, waiting for transfers between devices, on_device(): lax.psum_scatter(partial, 'bz', scatter_dimension=0, tiled=True)  20.1 us
    unnamed x19, local copies, waits for them, and re-layouts  10.2 us
  transfers between devices with their start and end apart: 20, of which 11 were waited for; matrix products, arithmetic and copies ran while one was open for 7% of the time, Pallas kernels for 37%

profile of v2, /device:TPU:0, one launch (start us, length us, event | category | flops | bytes accessed | tf_op | source)
XLA Modules:
  0.0 371.0 jit_solution(10885214334494708550)
XLA Ops:
  8.1 2.2 copy.17
  10.4 1.6 fusion.1
  12.6 5.9 %collective-permute-start = (bf16[2,128,512]{2,1,0:T(8,128)(2,1)S(1)}, bf16[2,128,512]{2,1,0:T(8,128)(2,1)}, u32[]{:S(2)}, u32[]{:S(2)}) collective-permute-start(bf16[2,128,512]{2,1,0:T(8,128)(2,1)S(1)} %pad_maximum_fusion), channel_id=1, source_target_pairs={{0,16},{4,20},{8,24},{12,28},{16,32},{20,36},{24,40},{28,44},{32,4... | collective-permute-start | bytes 786440 | tf_op jit(solution)/shard_map/ppermute | solution.py:18
  18.5 5.7 %collective-permute-start.1 = (bf16[2,128,512]{2,1,0:T(8,128)(2,1)S(1)}, bf16[2,128,512]{2,1,0:T(8,128)(2,1)}, u32[]{:S(2)}, u32[]{:S(2)}) collective-permute-start(bf16[2,128,512]{2,1,0:T(8,128)(2,1)S(1)} %pad_maximum_fusion), channel_id=1, source_target_pairs={{0,12},{4,16},{8,20},{12,24},{16,28},{20,32},{24,36},{28,40},{32,4... | collective-permute-start | bytes 786440 | tf_op jit(solution)/shard_map/ppermute | solution.py:18
  24.3 2.2 collective-permute-start.2
  26.4 3.4 collective-permute-start.3
  29.8 1.3 collective-permute-start.4
  31.8 1.3 collective-permute-start.5
  33.1 1.7 bitcast_dynamic-update-slice_fusion.8
  34.8 0.8 collective-permute-done.1
  35.5 1.3 collective-permute-start.6
  36.8 1.7 bitcast_dynamic-update-slice_fusion.7
  38.5 4.6 %collective-permute-done.2 = bf16[2,128,512]{2,1,0:T(8,128)(2,1)S(1)} collective-permute-done((bf16[2,128,512]{2,1,0:T(8,128)(2,1)S(1)}, bf16[2,128,512]{2,1,0:T(8,128)(2,1)S(1)}, u32[]{:S(2)}, u32[]{:S(2)}) %collective-permute-start.2) | collective-permute-done | bytes 262176 | tf_op jit(solution)/shard_map/ppermute | solution.py:18
  43.2 1.3 collective-permute-start.7
  44.4 0.7 bitcast_dynamic-update-slice_fusion.6
  45.2 0.7 bitcast_dynamic-update-slice_fusion.5
  45.9 0.7 bitcast_dynamic-update-slice_fusion.4
  47.0 0.7 bitcast_dynamic-update-slice_fusion.3
  47.7 0.7 bitcast_dynamic-update-slice_fusion.2
  48.4 5.3 %collective-permute-done.6 = bf16[2,128,512]{2,1,0:T(8,128)(2,1)S(1)} collective-permute-done((bf16[2,128,512]{2,1,0:T(8,128)(2,1)S(1)}, bf16[2,128,512]{2,1,0:T(8,128)(2,1)S(1)}, u32[]{:S(2)}, u32[]{:S(2)}) %collective-permute-start.6) | collective-permute-done | bytes 262176 | tf_op jit(solution)/shard_map/ppermute | solution.py:18
  53.7 0.7 bitcast_dynamic-update-slice_fusion.1
  54.4 5.3 %collective-permute-done.7 = bf16[2,128,512]{2,1,0:T(8,128)(2,1)S(1)} collective-permute-done((bf16[2,128,512]{2,1,0:T(8,128)(2,1)S(1)}, bf16[2,128,512]{2,1,0:T(8,128)(2,1)S(1)}, u32[]{:S(2)}, u32[]{:S(2)}) %collective-permute-start.7) | collective-permute-done | bytes 262176 | tf_op jit(solution)/shard_map/ppermute | solution.py:18
  59.7 0.7 bitcast_dynamic-update-slice_fusion.stock_ref
  60.4 138.1 %shard_map.110 = (bf16[2048,512]{1,0:T(8,128)(2,1)}, bf16[2048,512]{1,0:T(8,128)(2,1)}, f32[9,2,128,512]{3,2,1,0:T(8,128)}) custom-call(s32[16,5]{1,0:T(8,128)} %broadcast_subtract_fusion.slots_ref, s32[16]{0:T(128)} %counts_ref.1, bf16[2048,512]{1,0:T(8,128)(2,1)} %q_ref.1, bf16[2048,512]{1,0:T(8,128)(2,1)} %g_ref.1, ...), custom_call_target="tpu_custom_call" | custom-call | flops 16106127360 | bytes 15466496 | tf_op jit(solution)/shard_map/pallas_call | solution.py:113
  198.6 2.9 slice_bitcast_fusion.7
  201.4 6.3 %collective-permute-start.15 = (f32[2,128,512]{2,1,0:T(8,128)S(1)}, f32[2,128,512]{2,1,0:T(8,128)S(1)}, u32[]{:S(2)}, u32[]{:S(2)}) collective-permute-start(f32[2,128,512]{2,1,0:T(8,128)S(1)} %get-tuple-element.12), channel_id=1, source_target_pairs={{0,16},{4,20},{8,24},{12,28},{16,32},{20,36},{24,40},{28,44},{32,4... | collective-permute-start | bytes 1572872 | tf_op jit(solution)/shard_map/ppermute | solution.py:18
  207.7 9.4 %collective-permute-start.14 = (f32[2,128,512]{2,1,0:T(8,128)S(1)}, f32[2,128,512]{2,1,0:T(8,128)S(1)}, u32[]{:S(2)}, u32[]{:S(2)}) collective-permute-start(f32[2,128,512]{2,1,0:T(8,128)S(1)} %get-tuple-element.13), channel_id=1, source_target_pairs={{0,12},{4,16},{8,20},{12,24},{16,28},{20,32},{24,36},{28,40},{32,4... | collective-permute-start | bytes 1572872 | tf_op jit(solution)/shard_map/ppermute | solution.py:18
  217.2 1.3 collective-permute-start.13
  218.5 3.1 collective-permute-start.12
  221.6 1.3 collective-permute-start.11
  222.9 22.3 %collective-permute-done.15 = f32[2,128,512]{2,1,0:T(8,128)S(1)} collective-permute-done((f32[2,128,512]{2,1,0:T(8,128)S(1)}, f32[2,128,512]{2,1,0:T(8,128)S(1)}, u32[]{:S(2)}, u32[]{:S(2)}) %collective-permute-start.15) | collective-permute-done | bytes 524320 | tf_op jit(solution)/shard_map/ppermute | solution.py:18
  245.3 1.3 collective-permute-start.10
  246.5 1.3 collective-permute-start.9
  247.8 7.5 %collective-permute-done.13 = f32[2,128,512]{2,1,0:T(8,128)S(1)} collective-permute-done((f32[2,128,512]{2,1,0:T(8,128)S(1)}, f32[2,128,512]{2,1,0:T(8,128)S(1)}, u32[]{:S(2)}, u32[]{:S(2)}) %collective-permute-start.13) | collective-permute-done | bytes 524320 | tf_op jit(solution)/shard_map/ppermute | solution.py:18
  255.3 1.3 collective-permute-start.8
  256.6 13.3 %collective-permute-done.10 = f32[2,128,512]{2,1,0:T(8,128)S(1)} collective-permute-done((f32[2,128,512]{2,1,0:T(8,128)S(1)}, f32[2,128,512]{2,1,0:T(8,128)S(1)}, u32[]{:S(2)}, u32[]{:S(2)}) %collective-permute-start.10) | collective-permute-done | bytes 524320 | tf_op jit(solution)/shard_map/ppermute | solution.py:18
  270.0 1.5 collective-permute-done.8
  271.5 1.5 fusion.9
  273.0 0.8 pad_maximum_fusion.1
  273.9 0.8 fusion.10
  274.7 0.8 copy-done.2
  275.4 1.8 convolution_add_fusion
  277.4 1.1 constant_dynamic-slice_fusion
  278.4 58.4 %all-gather.4.cloned.1.call-done = bf16[1024,1024]{1,0:T(8,128)(2,1)} async-done(((bf16[128,1024]{1,0:T(8,128)(2,1)}), bf16[1024,1024]{1,0:T(8,128)(2,1)}) %all-gather.4.cloned.1.call-update) | async-done | bytes 2097168 | tf_op jit(solution)/shard_map/all_gather | solution.py:166
  336.8 3.3 fusion.12
  340.2 1.6 convert_element_type.15
  341.8 20.1 %reduce-scatter.5.cloned.1.call-done = f32[64,1024]{1,0:T(8,128)} async-done(((f32[256,1024]{1,0:T(8,128)}), f32[64,1024]{1,0:T(8,128)}) %reduce-scatter.5.cloned.1.call-update) | async-done | bytes 262160 | tf_op jit(solution)/shard_map/reduce_scatter | solution.py:178
  361.9 1.7 fusion.11
  (32 shorter events, 1.9 us)
Async XLA Ops:
  8.0 2.4 copy-start
  8.0 4.0 %copy-start.3 = (bf16[128,2048]{1,0:T(8,128)(2,1)S(1)}, bf16[128,2048]{1,0:T(8,128)(2,1)}, u32[]{:S(2)}) copy-start(bf16[128,2048]{1,0:T(8,128)(2,1)} %param.8) | copy-start | bytes 1572868
  8.0 269.3 %all-gather.6.cloned.1.call-start = ((), (), s32[]{:S(2)}) async-start(), calls=%async_computation.5 | async-start | bytes 4718592 | tf_op jit(solution)/shard_map/all_gather | solution.py:136
  10.3 20.8 %copy-start.4 = (s32[16,5]{0,1:T(8,128)S(1)}, s32[16,5]{0,1:T(8,128)}, u32[]{:S(2)}) copy-start(s32[16,5]{0,1:T(8,128)} %param.12) | copy-start | bytes 964
  10.3 326.5 %all-gather.4.cloned.1.call-start = ((), (), s32[]{:S(2)}) async-start(), calls=%async_computation.3 | async-start | bytes 2359296 | tf_op jit(solution)/shard_map/all_gather | solution.py:166
  10.4 1.8 copy-start.1
  12.6 19.2 %collective-permute-start = (bf16[2,128,512]{2,1,0:T(8,128)(2,1)S(1)}, bf16[2,128,512]{2,1,0:T(8,128)(2,1)}, u32[]{:S(2)}, u32[]{:S(2)}) collective-permute-start(bf16[2,128,512]{2,1,0:T(8,128)(2,1)S(1)} %pad_maximum_fusion), channel_id=1, source_target_pairs={{0,16},{4,20},{8,24},{12,28},{16,32},{20,36},{24,40},{28,44},{32,4... | collective-permute-start | bytes 786440 | tf_op jit(solution)/shard_map/ppermute | solution.py:18
  18.5 17.0 %collective-permute-start.1 = (bf16[2,128,512]{2,1,0:T(8,128)(2,1)S(1)}, bf16[2,128,512]{2,1,0:T(8,128)(2,1)}, u32[]{:S(2)}, u32[]{:S(2)}) collective-permute-start(bf16[2,128,512]{2,1,0:T(8,128)(2,1)S(1)} %pad_maximum_fusion), channel_id=1, source_target_pairs={{0,12},{4,16},{8,20},{12,24},{16,28},{20,32},{24,36},{28,40},{32,4... | collective-permute-start | bytes 786440 | tf_op jit(solution)/shard_map/ppermute | solution.py:18
  24.3 18.9 %collective-permute-start.2 = (bf16[2,128,512]{2,1,0:T(8,128)(2,1)S(1)}, bf16[2,128,512]{2,1,0:T(8,128)(2,1)S(1)}, u32[]{:S(2)}, u32[]{:S(2)}) collective-permute-start(bf16[2,128,512]{2,1,0:T(8,128)(2,1)S(1)} %pad_maximum_fusion), channel_id=1, source_target_pairs={{0,8},{4,12},{8,16},{12,20},{16,24},{20,28},{24,32},{28,36},{32,40... | collective-permute-start | bytes 786440 | tf_op jit(solution)/shard_map/ppermute | solution.py:18
  26.4 18.7 %collective-permute-start.3 = (bf16[2,128,512]{2,1,0:T(8,128)(2,1)S(1)}, bf16[2,128,512]{2,1,0:T(8,128)(2,1)S(1)}, u32[]{:S(2)}, u32[]{:S(2)}) collective-permute-start(bf16[2,128,512]{2,1,0:T(8,128)(2,1)S(1)} %pad_maximum_fusion), channel_id=1, source_target_pairs={{0,4},{4,8},{8,12},{12,16},{16,20},{20,24},{24,28},{28,32},{32,36}... | collective-permute-start | bytes 786440 | tf_op jit(solution)/shard_map/ppermute | solution.py:18
  29.8 17.1 %collective-permute-start.4 = (bf16[2,128,512]{2,1,0:T(8,128)(2,1)S(1)}, bf16[2,128,512]{2,1,0:T(8,128)(2,1)S(1)}, u32[]{:S(2)}, u32[]{:S(2)}) collective-permute-start(bf16[2,128,512]{2,1,0:T(8,128)(2,1)S(1)} %pad_maximum_fusion), channel_id=1, source_target_pairs={{4,0},{8,4},{12,8},{16,12},{20,16},{24,20},{28,24},{32,28},{36,32}... | collective-permute-start | bytes 786440 | tf_op jit(solution)/shard_map/ppermute | solution.py:18
  31.8 15.9 %collective-permute-start.5 = (bf16[2,128,512]{2,1,0:T(8,128)(2,1)S(1)}, bf16[2,128,512]{2,1,0:T(8,128)(2,1)S(1)}, u32[]{:S(2)}, u32[]{:S(2)}) collective-permute-start(bf16[2,128,512]{2,1,0:T(8,128)(2,1)S(1)} %pad_maximum_fusion), channel_id=1, source_target_pairs={{8,0},{12,4},{16,8},{20,12},{24,16},{28,20},{32,24},{36,28},{40,32... | collective-permute-start | bytes 786440 | tf_op jit(solution)/shard_map/ppermute | solution.py:18
  35.5 18.1 %collective-permute-start.6 = (bf16[2,128,512]{2,1,0:T(8,128)(2,1)S(1)}, bf16[2,128,512]{2,1,0:T(8,128)(2,1)S(1)}, u32[]{:S(2)}, u32[]{:S(2)}) collective-permute-start(bf16[2,128,512]{2,1,0:T(8,128)(2,1)S(1)} %pad_maximum_fusion), channel_id=1, source_target_pairs={{12,0},{16,4},{20,8},{24,12},{28,16},{32,20},{36,24},{40,28},{44,3... | collective-permute-start | bytes 786440 | tf_op jit(solution)/shard_map/ppermute | solution.py:18
  43.2 16.6 %collective-permute-start.7 = (bf16[2,128,512]{2,1,0:T(8,128)(2,1)S(1)}, bf16[2,128,512]{2,1,0:T(8,128)(2,1)S(1)}, u32[]{:S(2)}, u32[]{:S(2)}) collective-permute-start(bf16[2,128,512]{2,1,0:T(8,128)(2,1)S(1)} %pad_maximum_fusion), channel_id=1, source_target_pairs={{16,0},{20,4},{24,8},{28,12},{32,16},{36,20},{40,24},{44,28},{48,3... | collective-permute-start | bytes 786440 | tf_op jit(solution)/shard_map/ppermute | solution.py:18
  201.4 43.8 %collective-permute-start.15 = (f32[2,128,512]{2,1,0:T(8,128)S(1)}, f32[2,128,512]{2,1,0:T(8,128)S(1)}, u32[]{:S(2)}, u32[]{:S(2)}) collective-permute-start(f32[2,128,512]{2,1,0:T(8,128)S(1)} %get-tuple-element.12), channel_id=1, source_target_pairs={{0,16},{4,20},{8,24},{12,28},{16,32},{20,36},{24,40},{28,44},{32,4... | collective-permute-start | bytes 1572872 | tf_op jit(solution)/shard_map/ppermute | solution.py:18
  207.7 38.8 %collective-permute-start.14 = (f32[2,128,512]{2,1,0:T(8,128)S(1)}, f32[2,128,512]{2,1,0:T(8,128)S(1)}, u32[]{:S(2)}, u32[]{:S(2)}) collective-permute-start(f32[2,128,512]{2,1,0:T(8,128)S(1)} %get-tuple-element.13), channel_id=1, source_target_pairs={{0,12},{4,16},{8,20},{12,24},{16,28},{20,32},{24,36},{28,40},{32,4... | collective-permute-start | bytes 1572872 | tf_op jit(solution)/shard_map/ppermute | solution.py:18
  217.2 38.2 %collective-permute-start.13 = (f32[2,128,512]{2,1,0:T(8,128)S(1)}, f32[2,128,512]{2,1,0:T(8,128)S(1)}, u32[]{:S(2)}, u32[]{:S(2)}) collective-permute-start(f32[2,128,512]{2,1,0:T(8,128)S(1)} %get-tuple-element.14), channel_id=1, source_target_pairs={{0,8},{4,12},{8,16},{12,20},{16,24},{20,28},{24,32},{28,36},{32,40... | collective-permute-start | bytes 1572872 | tf_op jit(solution)/shard_map/ppermute | solution.py:18
  218.5 38.1 %collective-permute-start.12 = (f32[2,128,512]{2,1,0:T(8,128)S(1)}, f32[2,128,512]{2,1,0:T(8,128)S(1)}, u32[]{:S(2)}, u32[]{:S(2)}) collective-permute-start(f32[2,128,512]{2,1,0:T(8,128)S(1)} %get-tuple-element.15), channel_id=1, source_target_pairs={{0,4},{4,8},{8,12},{12,16},{16,20},{20,24},{24,28},{28,32},{32,36}... | collective-permute-start | bytes 1572872 | tf_op jit(solution)/shard_map/ppermute | solution.py:18
  221.6 35.0 %collective-permute-start.11 = (f32[2,128,512]{2,1,0:T(8,128)S(1)}, f32[2,128,512]{2,1,0:T(8,128)S(1)}, u32[]{:S(2)}, u32[]{:S(2)}) collective-permute-start(f32[2,128,512]{2,1,0:T(8,128)S(1)} %get-tuple-element.16), channel_id=1, source_target_pairs={{4,0},{8,4},{12,8},{16,12},{20,16},{24,20},{28,24},{32,28},{36,32}... | collective-permute-start | bytes 1572872 | tf_op jit(solution)/shard_map/ppermute | solution.py:18
  245.3 24.7 %collective-permute-start.10 = (f32[2,128,512]{2,1,0:T(8,128)S(1)}, f32[2,128,512]{2,1,0:T(8,128)S(1)}, u32[]{:S(2)}, u32[]{:S(2)}) collective-permute-start(f32[2,128,512]{2,1,0:T(8,128)S(1)} %get-tuple-element.17), channel_id=1, source_target_pairs={{8,0},{12,4},{16,8},{20,12},{24,16},{28,20},{32,24},{36,28},{40,32... | collective-permute-start | bytes 1572872 | tf_op jit(solution)/shard_map/ppermute | solution.py:18
  246.5 23.4 %collective-permute-start.9 = (f32[2,128,512]{2,1,0:T(8,128)S(1)}, f32[2,128,512]{2,1,0:T(8,128)S(1)}, u32[]{:S(2)}, u32[]{:S(2)}) collective-permute-start(f32[2,128,512]{2,1,0:T(8,128)S(1)} %get-tuple-element.18), channel_id=1, source_target_pairs={{12,0},{16,4},{20,8},{24,12},{28,16},{32,20},{36,24},{40,28},{44,3... | collective-permute-start | bytes 1572872 | tf_op jit(solution)/shard_map/ppermute | solution.py:18
  255.3 16.2 %collective-permute-start.8 = (f32[2,128,512]{2,1,0:T(8,128)S(1)}, f32[2,128,512]{2,1,0:T(8,128)S(1)}, u32[]{:S(2)}, u32[]{:S(2)}) collective-permute-start(f32[2,128,512]{2,1,0:T(8,128)S(1)} %get-tuple-element.11), channel_id=1, source_target_pairs={{16,0},{20,4},{24,8},{28,12},{32,16},{36,20},{40,24},{44,28},{48,3... | collective-permute-start | bytes 1572872 | tf_op jit(solution)/shard_map/ppermute | solution.py:18
  273.8 66.4 %reduce-scatter.3.cloned.1.call-start = ((), (), s32[]{:S(2)}) async-start(), calls=%async_computation.2 | async-start | bytes 1310720 | tf_op jit(solution)/shard_map/reduce_scatter | solution.py:162
  273.8 1.6 copy-start.2
  277.3 84.6 %reduce-scatter.5.cloned.1.call-start = ((), (), s32[]{:S(2)}) async-start(), calls=%async_computation.4 | async-start | bytes 1310720 | tf_op jit(solution)/shard_map/reduce_scatter | solution.py:178
Sparse Core Ops, SparseCore 0:
  11.3 99.6 all-gather.5
  273.9 62.8 all-gather.3
Sparse Core Ops, SparseCore 1:
  277.4 30.6 reduce-scatter.2
  340.2 21.6 reduce-scatter.4

commit v3 on v2

--- a/solution.py
+++ b/solution.py
@@ -36,58 +36,70 @@
     f32 = jnp.float32
     bf16 = jnp.bfloat16
 
-    def pair(p, carry):
-        off = pl.multiple_of(p * LANES, LANES)
-        qp = q_ref[:, pl.ds(off, LANES)]
-        gp = g_ref[:, pl.ds(off, LANES)]
-        zq = jnp.zeros_like(qp)
-        qh = [jnp.where(first, qp, zq), jnp.where(first, zq, qp)]
-        gh = [jnp.where(first, gp, zq), jnp.where(first, zq, gp)]
-        ks = [stock_ref[slots[j], 0, :, pl.ds(off, LANES)] for j in range(LISTED)]
-        vs = [stock_ref[slots[j], 1, :, pl.ds(off, LANES)] for j in range(LISTED)]
-        outs, dqs = [], []
-        dks = [None] * LISTED
-        dvs = [None] * LISTED
-        for h in range(2):
-            scores = []
-            for j in range(LISTED):
-                sc = lax.dot_general(qh[h], ks[j], nt, preferred_element_type=f32) * factor
-                scores.append(jnp.where(j < count, sc, -jnp.inf))
-            peak = jnp.max(scores[0], axis=1, keepdims=True)
-            for j in range(1, LISTED):
-                peak = jnp.maximum(peak, jnp.max(scores[j], axis=1, keepdims=True))
-            expos = [jnp.exp(sc - peak) for sc in scores]
-            total = jnp.sum(expos[0], axis=1, keepdims=True)
-            for j in range(1, LISTED):
-                total = total + jnp.sum(expos[j], axis=1, keepdims=True)
-            ws = [(e / total).astype(bf16) for e in expos]
-            out = jnp.dot(ws[0], vs[0], preferred_element_type=f32)
-            for j in range(1, LISTED):
-                out = out + jnp.dot(ws[j], vs[j], preferred_element_type=f32)
-            dws = [lax.dot_general(gh[h], vs[j], nt, preferred_element_type=f32) for j in range(LISTED)]
-            wf = [w.astype(f32) for w in ws]
-            center = jnp.sum(wf[0] * dws[0], axis=1, keepdims=True)
-            for j in range(1, LISTED):
-                center = center + jnp.sum(wf[j] * dws[j], axis=1, keepdims=True)
-            dss = [(wf[j] * (dws[j] - center) * factor).astype(bf16) for j in range(LISTED)]
-            dq = jnp.dot(dss[0], ks[0], preferred_element_type=f32)
-            for j in range(1, LISTED):
-                dq = dq + jnp.dot(dss[j], ks[j], preferred_element_type=f32)
-            for j in range(LISTED):
-                dk = lax.dot_general(dss[j], qh[h], tn, preferred_element_type=f32)
-                dv = lax.dot_general(ws[j], gh[h], tn, preferred_element_type=f32)
-                dks[j] = dk if dks[j] is None else dks[j] + dk
-                dvs[j] = dv if dvs[j] is None else dvs[j] + dv
-            outs.append(out)
-            dqs.append(dq)
-        out_ref[:, pl.ds(off, LANES)] = jnp.where(first, outs[0], outs[1]).astype(out_ref.dtype)
-        dq_ref[:, pl.ds(off, LANES)] = jnp.where(first, dqs[0], dqs[1]).astype(dq_ref.dtype)
-        for j in range(LISTED):
-            acc_ref[slots[j], 0, :, pl.ds(off, LANES)] += dks[j]
-            acc_ref[slots[j], 1, :, pl.ds(off, LANES)] += dvs[j]
-        return carry
-
-    lax.fori_loop(0, q_ref.shape[1] // LANES, pair, 0)
+    def run(used):
+        def pair(p, carry):
+            off = pl.multiple_of(p * LANES, LANES)
+            qp = q_ref[:, pl.ds(off, LANES)]
+            gp = g_ref[:, pl.ds(off, LANES)]
+            qs = qp * jnp.asarray(factor, qp.dtype)
+            gs = gp * jnp.asarray(factor, gp.dtype)
+            zq = jnp.zeros_like(qp)
+            qh = [jnp.where(first, qp, zq), jnp.where(first, zq, qp)]
+            gh = [jnp.where(first, gp, zq), jnp.where(first, zq, gp)]
+            qsh = [jnp.where(first, qs, zq), jnp.where(first, zq, qs)]
+            gsh = [jnp.where(first, gs, zq), jnp.where(first, zq, gs)]
+            ks = [stock_ref[slots[j], 0, :, pl.ds(off, LANES)] for j in range(used)]
+            vs = [stock_ref[slots[j], 1, :, pl.ds(off, LANES)] for j in range(used)]
+            outs, dqs = [], []
+            dks = [None] * used
+            dvs = [None] * used
+            for h in range(2):
+                scores = [
+                    lax.dot_general(qsh[h], ks[j], nt, preferred_element_type=f32)
+                    for j in range(used)
+                ]
+                peak = jnp.max(scores[0], axis=1, keepdims=True)
+                for j in range(1, used):
+                    peak = jnp.maximum(peak, jnp.max(scores[j], axis=1, keepdims=True))
+                expos = [jnp.exp(sc - peak) for sc in scores]
+                total = jnp.sum(expos[0], axis=1, keepdims=True)
+                for j in range(1, used):
+                    total = total + jnp.sum(expos[j], axis=1, keepdims=True)
+                inverse = 1.0 / total
+                ws = [(e * inverse).astype(bf16) for e in expos]
+                out = jnp.dot(ws[0], vs[0], preferred_element_type=f32)
+                for j in range(1, used):
+                    out = out + jnp.dot(ws[j], vs[j], preferred_element_type=f32)
+                dws = [
+                    lax.dot_general(gsh[h], vs[j], nt, preferred_element_type=f32)
+                    for j in range(used)
+                ]
+                wf = [w.astype(f32) for w in ws]
+                center = jnp.sum(wf[0] * dws[0], axis=1, keepdims=True)
+                for j in range(1, used):
+                    center = center + jnp.sum(wf[j] * dws[j], axis=1, keepdims=True)
+                dss = [(wf[j] * (dws[j] - center)).astype(bf16) for j in range(used)]
+                dq = jnp.dot(dss[0], ks[0], preferred_element_type=f32)
+                for j in range(1, used):
+                    dq = dq + jnp.dot(dss[j], ks[j], preferred_element_type=f32)
+                for j in range(used):
+                    dk = lax.dot_general(dss[j], qh[h], tn, preferred_element_type=f32)
+                    dv = lax.dot_general(ws[j], gh[h], tn, preferred_element_type=f32)
+                    dks[j] = dk if dks[j] is None else dks[j] + dk
+                    dvs[j] = dv if dvs[j] is None else dvs[j] + dv
+                outs.append(out)
+                dqs.append(dq)
+            out_ref[:, pl.ds(off, LANES)] = jnp.where(first, outs[0], outs[1]).astype(out_ref.dtype)
+            dq_ref[:, pl.ds(off, LANES)] = jnp.where(first, dqs[0], dqs[1]).astype(dq_ref.dtype)
+            for j in range(used):
+                acc_ref[slots[j], 0, :, pl.ds(off, LANES)] += dks[j]
+                acc_ref[slots[j], 1, :, pl.ds(off, LANES)] += dvs[j]
+            return carry
+
+        lax.fori_loop(0, q_ref.shape[1] // LANES, pair, 0)
+
+    for used in range(1, LISTED + 1):
+        pl.when(count == used)(functools.partial(run, used))
 
 
 def attention(queries, out_grad, stock, slot_ids, counts):

time: 372 us -> 351 us (0.944)
  Pallas kernels: 138 us -> 109 us
  starting transfers between devices: 47.8 us -> 57.3 us
    pallas_call x1, Pallas kernels: 138 us -> 109 us  [attention(): pl.pallas_call(attention_kernel, grid_spec=grid_spec, out_shape=[jax.Shap...]
    ppermute x16, starting transfers between devices: 47.6 us -> 57.2 us  [passed_along(): return lax.ppermute(value, axis, pairs)]
    ppermute x16, waiting for transfers between devices: 60.9 us -> 52.5 us  [passed_along(): return lax.ppermute(value, axis, pairs)]
    all_gather x1, waiting for transfers between devices: 58.4 us -> 64.1 us  [on_device(): group_grads = lax.all_gather(both_grads, 'byx', axis=0, tiled=True)]
  transfers between devices with their start and end apart: 20 -> 20, of which waited for: 11 -> 10; matrix products, arithmetic and copies ran while one was open for 7% -> 7% of each run, Pallas kernels for 37% -> 31%
where the time goes in v3:
time: 351 us; the launch traced here: 348 us
  waiting for transfers between devices  137 us (39%)
  Pallas kernels  109 us (31%)
  starting transfers between devices  57.3 us (16%)
  local copies, waits for them, and re-layouts  16.5 us (5%)
  between operations  15.8 us (5%)
  matrix products  7.97 us (2%)
  other arithmetic  5.24 us (1%)
    pallas_call x1, Pallas kernels, attention(): pl.pallas_call(attention_kernel, grid_spec=grid_spec, out_shape=[jax.Shap...  109 us
    all_gather x1, waiting for transfers between devices, on_device(): group_grads = lax.all_gather(both_grads, 'byx', axis=0, tiled=True)  64.1 us
    ppermute x16, starting transfers between devices, passed_along(): return lax.ppermute(value, axis, pairs)  57.2 us
    ppermute x16, waiting for transfers between devices, passed_along(): return lax.ppermute(value, axis, pairs)  52.5 us
    reduce_scatter x1, waiting for transfers between devices, on_device(): lax.psum_scatter(partial, 'bz', scatter_dimension=0, tiled=True)  20.1 us
    unnamed x19, local copies, waits for them, and re-layouts  10.2 us
  transfers between devices with their start and end apart: 20, of which 10 were waited for; matrix products, arithmetic and copies ran while one was open for 7% of the time, Pallas kernels for 31%

profile of v3, /device:TPU:0, one launch (start us, length us, event | category | flops | bytes accessed | tf_op | source)
XLA Modules:
  0.0 348.2 jit_solution(475547885239178597)
XLA Ops:
  8.1 2.2 copy.17
  10.4 1.6 fusion.1
  12.6 5.9 %collective-permute-start = (bf16[2,128,512]{2,1,0:T(8,128)(2,1)S(1)}, bf16[2,128,512]{2,1,0:T(8,128)(2,1)}, u32[]{:S(2)}, u32[]{:S(2)}) collective-permute-start(bf16[2,128,512]{2,1,0:T(8,128)(2,1)S(1)} %pad_maximum_fusion), channel_id=1, source_target_pairs={{0,16},{4,20},{8,24},{12,28},{16,32},{20,36},{24,40},{28,44},{32,4... | collective-permute-start | bytes 786440 | tf_op jit(solution)/shard_map/ppermute | solution.py:18
  18.5 5.7 %collective-permute-start.1 = (bf16[2,128,512]{2,1,0:T(8,128)(2,1)S(1)}, bf16[2,128,512]{2,1,0:T(8,128)(2,1)}, u32[]{:S(2)}, u32[]{:S(2)}) collective-permute-start(bf16[2,128,512]{2,1,0:T(8,128)(2,1)S(1)} %pad_maximum_fusion), channel_id=1, source_target_pairs={{0,12},{4,16},{8,20},{12,24},{16,28},{20,32},{24,36},{28,40},{32,4... | collective-permute-start | bytes 786440 | tf_op jit(solution)/shard_map/ppermute | solution.py:18
  24.3 2.2 collective-permute-start.2
  26.4 3.4 collective-permute-start.3
  29.8 1.3 collective-permute-start.4
  31.2 0.6 broadcast_subtract_fusion.slots_ref
  31.8 1.3 collective-permute-start.5
  33.1 1.7 bitcast_dynamic-update-slice_fusion.8
  34.8 0.8 collective-permute-done.1
  35.5 1.3 collective-permute-start.6
  36.8 1.7 bitcast_dynamic-update-slice_fusion.7
  38.5 4.6 %collective-permute-done.2 = bf16[2,128,512]{2,1,0:T(8,128)(2,1)S(1)} collective-permute-done((bf16[2,128,512]{2,1,0:T(8,128)(2,1)S(1)}, bf16[2,128,512]{2,1,0:T(8,128)(2,1)S(1)}, u32[]{:S(2)}, u32[]{:S(2)}) %collective-permute-start.2) | collective-permute-done | bytes 262176 | tf_op jit(solution)/shard_map/ppermute | solution.py:18
  43.2 1.3 collective-permute-start.7
  44.4 0.7 bitcast_dynamic-update-slice_fusion.6
  45.2 0.7 bitcast_dynamic-update-slice_fusion.5
  45.9 0.7 bitcast_dynamic-update-slice_fusion.4
  47.0 0.7 bitcast_dynamic-update-slice_fusion.3
  47.7 0.7 bitcast_dynamic-update-slice_fusion.2
  48.4 5.3 %collective-permute-done.6 = bf16[2,128,512]{2,1,0:T(8,128)(2,1)S(1)} collective-permute-done((bf16[2,128,512]{2,1,0:T(8,128)(2,1)S(1)}, bf16[2,128,512]{2,1,0:T(8,128)(2,1)S(1)}, u32[]{:S(2)}, u32[]{:S(2)}) %collective-permute-start.6) | collective-permute-done | bytes 262176 | tf_op jit(solution)/shard_map/ppermute | solution.py:18
  53.7 0.7 bitcast_dynamic-update-slice_fusion.1
  54.4 5.3 %collective-permute-done.7 = bf16[2,128,512]{2,1,0:T(8,128)(2,1)S(1)} collective-permute-done((bf16[2,128,512]{2,1,0:T(8,128)(2,1)S(1)}, bf16[2,128,512]{2,1,0:T(8,128)(2,1)S(1)}, u32[]{:S(2)}, u32[]{:S(2)}) %collective-permute-start.7) | collective-permute-done | bytes 262176 | tf_op jit(solution)/shard_map/ppermute | solution.py:18
  59.7 0.7 bitcast_dynamic-update-slice_fusion.stock_ref
  60.4 108.6 %shard_map.110 = (bf16[2048,512]{1,0:T(8,128)(2,1)}, bf16[2048,512]{1,0:T(8,128)(2,1)}, f32[9,2,128,512]{3,2,1,0:T(8,128)}) custom-call(s32[16,5]{1,0:T(8,128)} %broadcast_subtract_fusion.slots_ref, s32[16]{0:T(128)} %counts_ref.1, bf16[2048,512]{1,0:T(8,128)(2,1)} %q_ref.1, bf16[2048,512]{1,0:T(8,128)(2,1)} %g_ref.1, ...), custom_call_target="tpu_custom_call" | custom-call | flops 16106127360 | bytes 15466496 | tf_op jit(solution)/shard_map/pallas_call | solution.py:125
  169.0 2.9 slice_bitcast_fusion.7
  171.8 7.2 %collective-permute-start.15 = (f32[2,128,512]{2,1,0:T(8,128)S(1)}, f32[2,128,512]{2,1,0:T(8,128)S(1)}, u32[]{:S(2)}, u32[]{:S(2)}) collective-permute-start(f32[2,128,512]{2,1,0:T(8,128)S(1)} %get-tuple-element.12), channel_id=1, source_target_pairs={{0,16},{4,20},{8,24},{12,28},{16,32},{20,36},{24,40},{28,44},{32,4... | collective-permute-start | bytes 1572872 | tf_op jit(solution)/shard_map/ppermute | solution.py:18
  179.1 14.3 %collective-permute-start.14 = (f32[2,128,512]{2,1,0:T(8,128)S(1)}, f32[2,128,512]{2,1,0:T(8,128)S(1)}, u32[]{:S(2)}, u32[]{:S(2)}) collective-permute-start(f32[2,128,512]{2,1,0:T(8,128)S(1)} %get-tuple-element.13), channel_id=1, source_target_pairs={{0,12},{4,16},{8,20},{12,24},{16,28},{20,32},{24,36},{28,40},{32,4... | collective-permute-start | bytes 1572872 | tf_op jit(solution)/shard_map/ppermute | solution.py:18
  193.4 1.3 collective-permute-start.13
  194.7 6.9 %collective-permute-start.12 = (f32[2,128,512]{2,1,0:T(8,128)S(1)}, f32[2,128,512]{2,1,0:T(8,128)S(1)}, u32[]{:S(2)}, u32[]{:S(2)}) collective-permute-start(f32[2,128,512]{2,1,0:T(8,128)S(1)} %get-tuple-element.15), channel_id=1, source_target_pairs={{0,4},{4,8},{8,12},{12,16},{16,20},{20,24},{24,28},{28,32},{32,36}... | collective-permute-start | bytes 1572872 | tf_op jit(solution)/shard_map/ppermute | solution.py:18
  201.6 1.3 collective-permute-start.11
  202.9 7.1 %collective-permute-done.15 = f32[2,128,512]{2,1,0:T(8,128)S(1)} collective-permute-done((f32[2,128,512]{2,1,0:T(8,128)S(1)}, f32[2,128,512]{2,1,0:T(8,128)S(1)}, u32[]{:S(2)}, u32[]{:S(2)}) %collective-permute-start.15) | collective-permute-done | bytes 524320 | tf_op jit(solution)/shard_map/ppermute | solution.py:18
  210.0 1.3 collective-permute-start.10
  211.3 1.3 collective-permute-start.9
  212.6 11.3 %collective-permute-done.13 = f32[2,128,512]{2,1,0:T(8,128)S(1)} collective-permute-done((f32[2,128,512]{2,1,0:T(8,128)S(1)}, f32[2,128,512]{2,1,0:T(8,128)S(1)}, u32[]{:S(2)}, u32[]{:S(2)}) %collective-permute-start.13) | collective-permute-done | bytes 524320 | tf_op jit(solution)/shard_map/ppermute | solution.py:18
  223.9 1.3 collective-permute-start.8
  225.3 17.7 %collective-permute-done.9 = f32[2,128,512]{2,1,0:T(8,128)S(1)} collective-permute-done((f32[2,128,512]{2,1,0:T(8,128)S(1)}, f32[2,128,512]{2,1,0:T(8,128)S(1)}, u32[]{:S(2)}, u32[]{:S(2)}) %collective-permute-start.9) | collective-permute-done | bytes 524320 | tf_op jit(solution)/shard_map/ppermute | solution.py:18
  243.0 1.5 fusion.9
  244.5 0.8 pad_maximum_fusion.1
  245.3 0.8 fusion.10
  246.2 0.8 copy-done.2
  246.9 1.8 convolution_add_fusion
  248.8 1.1 constant_dynamic-slice_fusion
  249.9 64.1 %all-gather.4.cloned.1.call-done = bf16[1024,1024]{1,0:T(8,128)(2,1)} async-done(((bf16[128,1024]{1,0:T(8,128)(2,1)}), bf16[1024,1024]{1,0:T(8,128)(2,1)}) %all-gather.4.cloned.1.call-update) | async-done | bytes 2097168 | tf_op jit(solution)/shard_map/all_gather | solution.py:178
  314.1 3.3 fusion.12
  317.4 1.6 convert_element_type.15
  319.0 20.1 %reduce-scatter.5.cloned.1.call-done = f32[64,1024]{1,0:T(8,128)} async-done(((f32[256,1024]{1,0:T(8,128)}), f32[64,1024]{1,0:T(8,128)}) %reduce-scatter.5.cloned.1.call-update) | async-done | bytes 262160 | tf_op jit(solution)/shard_map/reduce_scatter | solution.py:190
  339.1 1.7 fusion.11
  (32 shorter events, 1.3 us)
Async XLA Ops:
  8.0 2.4 copy-start
  8.0 4.0 %copy-start.3 = (bf16[128,2048]{1,0:T(8,128)(2,1)S(1)}, bf16[128,2048]{1,0:T(8,128)(2,1)}, u32[]{:S(2)}) copy-start(bf16[128,2048]{1,0:T(8,128)(2,1)} %param.8) | copy-start | bytes 1572868
  8.0 240.8 %all-gather.6.cloned.1.call-start = ((), (), s32[]{:S(2)}) async-start(), calls=%async_computation.5 | async-start | bytes 4718592 | tf_op jit(solution)/shard_map/all_gather | solution.py:148
  10.3 20.8 %copy-start.4 = (s32[16,5]{0,1:T(8,128)S(1)}, s32[16,5]{0,1:T(8,128)}, u32[]{:S(2)}) copy-start(s32[16,5]{0,1:T(8,128)} %param.12) | copy-start | bytes 964
  10.3 303.8 %all-gather.4.cloned.1.call-start = ((), (), s32[]{:S(2)}) async-start(), calls=%async_computation.3 | async-start | bytes 2359296 | tf_op jit(solution)/shard_map/all_gather | solution.py:178
  10.4 1.8 copy-start.1
  12.6 19.2 %collective-permute-start = (bf16[2,128,512]{2,1,0:T(8,128)(2,1)S(1)}, bf16[2,128,512]{2,1,0:T(8,128)(2,1)}, u32[]{:S(2)}, u32[]{:S(2)}) collective-permute-start(bf16[2,128,512]{2,1,0:T(8,128)(2,1)S(1)} %pad_maximum_fusion), channel_id=1, source_target_pairs={{0,16},{4,20},{8,24},{12,28},{16,32},{20,36},{24,40},{28,44},{32,4... | collective-permute-start | bytes 786440 | tf_op jit(solution)/shard_map/ppermute | solution.py:18
  18.5 17.0 %collective-permute-start.1 = (bf16[2,128,512]{2,1,0:T(8,128)(2,1)S(1)}, bf16[2,128,512]{2,1,0:T(8,128)(2,1)}, u32[]{:S(2)}, u32[]{:S(2)}) collective-permute-start(bf16[2,128,512]{2,1,0:T(8,128)(2,1)S(1)} %pad_maximum_fusion), channel_id=1, source_target_pairs={{0,12},{4,16},{8,20},{12,24},{16,28},{20,32},{24,36},{28,40},{32,4... | collective-permute-start | bytes 786440 | tf_op jit(solution)/shard_map/ppermute | solution.py:18
  24.3 18.9 %collective-permute-start.2 = (bf16[2,128,512]{2,1,0:T(8,128)(2,1)S(1)}, bf16[2,128,512]{2,1,0:T(8,128)(2,1)S(1)}, u32[]{:S(2)}, u32[]{:S(2)}) collective-permute-start(bf16[2,128,512]{2,1,0:T(8,128)(2,1)S(1)} %pad_maximum_fusion), channel_id=1, source_target_pairs={{0,8},{4,12},{8,16},{12,20},{16,24},{20,28},{24,32},{28,36},{32,40... | collective-permute-start | bytes 786440 | tf_op jit(solution)/shard_map/ppermute | solution.py:18
  26.4 18.7 %collective-permute-start.3 = (bf16[2,128,512]{2,1,0:T(8,128)(2,1)S(1)}, bf16[2,128,512]{2,1,0:T(8,128)(2,1)S(1)}, u32[]{:S(2)}, u32[]{:S(2)}) collective-permute-start(bf16[2,128,512]{2,1,0:T(8,128)(2,1)S(1)} %pad_maximum_fusion), channel_id=1, source_target_pairs={{0,4},{4,8},{8,12},{12,16},{16,20},{20,24},{24,28},{28,32},{32,36}... | collective-permute-start | bytes 786440 | tf_op jit(solution)/shard_map/ppermute | solution.py:18
  29.8 17.1 %collective-permute-start.4 = (bf16[2,128,512]{2,1,0:T(8,128)(2,1)S(1)}, bf16[2,128,512]{2,1,0:T(8,128)(2,1)S(1)}, u32[]{:S(2)}, u32[]{:S(2)}) collective-permute-start(bf16[2,128,512]{2,1,0:T(8,128)(2,1)S(1)} %pad_maximum_fusion), channel_id=1, source_target_pairs={{4,0},{8,4},{12,8},{16,12},{20,16},{24,20},{28,24},{32,28},{36,32}... | collective-permute-start | bytes 786440 | tf_op jit(solution)/shard_map/ppermute | solution.py:18
  31.8 15.9 %collective-permute-start.5 = (bf16[2,128,512]{2,1,0:T(8,128)(2,1)S(1)}, bf16[2,128,512]{2,1,0:T(8,128)(2,1)S(1)}, u32[]{:S(2)}, u32[]{:S(2)}) collective-permute-start(bf16[2,128,512]{2,1,0:T(8,128)(2,1)S(1)} %pad_maximum_fusion), channel_id=1, source_target_pairs={{8,0},{12,4},{16,8},{20,12},{24,16},{28,20},{32,24},{36,28},{40,32... | collective-permute-start | bytes 786440 | tf_op jit(solution)/shard_map/ppermute | solution.py:18
  35.5 18.1 %collective-permute-start.6 = (bf16[2,128,512]{2,1,0:T(8,128)(2,1)S(1)}, bf16[2,128,512]{2,1,0:T(8,128)(2,1)S(1)}, u32[]{:S(2)}, u32[]{:S(2)}) collective-permute-start(bf16[2,128,512]{2,1,0:T(8,128)(2,1)S(1)} %pad_maximum_fusion), channel_id=1, source_target_pairs={{12,0},{16,4},{20,8},{24,12},{28,16},{32,20},{36,24},{40,28},{44,3... | collective-permute-start | bytes 786440 | tf_op jit(solution)/shard_map/ppermute | solution.py:18
  43.2 16.6 %collective-permute-start.7 = (bf16[2,128,512]{2,1,0:T(8,128)(2,1)S(1)}, bf16[2,128,512]{2,1,0:T(8,128)(2,1)S(1)}, u32[]{:S(2)}, u32[]{:S(2)}) collective-permute-start(bf16[2,128,512]{2,1,0:T(8,128)(2,1)S(1)} %pad_maximum_fusion), channel_id=1, source_target_pairs={{16,0},{20,4},{24,8},{28,12},{32,16},{36,20},{40,24},{44,28},{48,3... | collective-permute-start | bytes 786440 | tf_op jit(solution)/shard_map/ppermute | solution.py:18
  171.8 38.1 %collective-permute-start.15 = (f32[2,128,512]{2,1,0:T(8,128)S(1)}, f32[2,128,512]{2,1,0:T(8,128)S(1)}, u32[]{:S(2)}, u32[]{:S(2)}) collective-permute-start(f32[2,128,512]{2,1,0:T(8,128)S(1)} %get-tuple-element.12), channel_id=1, source_target_pairs={{0,16},{4,20},{8,24},{12,28},{16,32},{20,36},{24,40},{28,44},{32,4... | collective-permute-start | bytes 1572872 | tf_op jit(solution)/shard_map/ppermute | solution.py:18
  179.1 32.2 %collective-permute-start.14 = (f32[2,128,512]{2,1,0:T(8,128)S(1)}, f32[2,128,512]{2,1,0:T(8,128)S(1)}, u32[]{:S(2)}, u32[]{:S(2)}) collective-permute-start(f32[2,128,512]{2,1,0:T(8,128)S(1)} %get-tuple-element.13), channel_id=1, source_target_pairs={{0,12},{4,16},{8,20},{12,24},{16,28},{20,32},{24,36},{28,40},{32,4... | collective-permute-start | bytes 1572872 | tf_op jit(solution)/shard_map/ppermute | solution.py:18
  193.4 30.6 %collective-permute-start.13 = (f32[2,128,512]{2,1,0:T(8,128)S(1)}, f32[2,128,512]{2,1,0:T(8,128)S(1)}, u32[]{:S(2)}, u32[]{:S(2)}) collective-permute-start(f32[2,128,512]{2,1,0:T(8,128)S(1)} %get-tuple-element.14), channel_id=1, source_target_pairs={{0,8},{4,12},{8,16},{12,20},{16,24},{20,28},{24,32},{28,36},{32,40... | collective-permute-start | bytes 1572872 | tf_op jit(solution)/shard_map/ppermute | solution.py:18
  194.7 30.5 %collective-permute-start.12 = (f32[2,128,512]{2,1,0:T(8,128)S(1)}, f32[2,128,512]{2,1,0:T(8,128)S(1)}, u32[]{:S(2)}, u32[]{:S(2)}) collective-permute-start(f32[2,128,512]{2,1,0:T(8,128)S(1)} %get-tuple-element.15), channel_id=1, source_target_pairs={{0,4},{4,8},{8,12},{12,16},{16,20},{20,24},{24,28},{28,32},{32,36}... | collective-permute-start | bytes 1572872 | tf_op jit(solution)/shard_map/ppermute | solution.py:18
  201.6 23.6 %collective-permute-start.11 = (f32[2,128,512]{2,1,0:T(8,128)S(1)}, f32[2,128,512]{2,1,0:T(8,128)S(1)}, u32[]{:S(2)}, u32[]{:S(2)}) collective-permute-start(f32[2,128,512]{2,1,0:T(8,128)S(1)} %get-tuple-element.16), channel_id=1, source_target_pairs={{4,0},{8,4},{12,8},{16,12},{20,16},{24,20},{28,24},{32,28},{36,32}... | collective-permute-start | bytes 1572872 | tf_op jit(solution)/shard_map/ppermute | solution.py:18
  210.0 15.3 %collective-permute-start.10 = (f32[2,128,512]{2,1,0:T(8,128)S(1)}, f32[2,128,512]{2,1,0:T(8,128)S(1)}, u32[]{:S(2)}, u32[]{:S(2)}) collective-permute-start(f32[2,128,512]{2,1,0:T(8,128)S(1)} %get-tuple-element.17), channel_id=1, source_target_pairs={{8,0},{12,4},{16,8},{20,12},{24,16},{28,20},{32,24},{36,28},{40,32... | collective-permute-start | bytes 1572872 | tf_op jit(solution)/shard_map/ppermute | solution.py:18
  211.3 31.7 %collective-permute-start.9 = (f32[2,128,512]{2,1,0:T(8,128)S(1)}, f32[2,128,512]{2,1,0:T(8,128)S(1)}, u32[]{:S(2)}, u32[]{:S(2)}) collective-permute-start(f32[2,128,512]{2,1,0:T(8,128)S(1)} %get-tuple-element.18), channel_id=1, source_target_pairs={{12,0},{16,4},{20,8},{24,12},{28,16},{32,20},{36,24},{40,28},{44,3... | collective-permute-start | bytes 1572872 | tf_op jit(solution)/shard_map/ppermute | solution.py:18
  223.9 19.0 %collective-permute-start.8 = (f32[2,128,512]{2,1,0:T(8,128)S(1)}, f32[2,128,512]{2,1,0:T(8,128)S(1)}, u32[]{:S(2)}, u32[]{:S(2)}) collective-permute-start(f32[2,128,512]{2,1,0:T(8,128)S(1)} %get-tuple-element.11), channel_id=1, source_target_pairs={{16,0},{20,4},{24,8},{28,12},{32,16},{36,20},{40,24},{44,28},{48,3... | collective-permute-start | bytes 1572872 | tf_op jit(solution)/shard_map/ppermute | solution.py:18
  245.3 72.1 %reduce-scatter.3.cloned.1.call-start = ((), (), s32[]{:S(2)}) async-start(), calls=%async_computation.2 | async-start | bytes 1310720 | tf_op jit(solution)/shard_map/reduce_scatter | solution.py:174
  245.3 1.6 copy-start.2
  248.8 90.4 %reduce-scatter.5.cloned.1.call-start = ((), (), s32[]{:S(2)}) async-start(), calls=%async_computation.4 | async-start | bytes 1310720 | tf_op jit(solution)/shard_map/reduce_scatter | solution.py:190
Sparse Core Ops, SparseCore 0:
  11.3 99.6 all-gather.5
  245.4 68.6 all-gather.3
Sparse Core Ops, SparseCore 1:
  248.9 36.3 reduce-scatter.2
  317.4 21.6 reduce-scatter.4

commit v4 on v3

--- a/solution.py
+++ b/solution.py
@@ -18,7 +18,9 @@
     return lax.ppermute(value, axis, pairs)
 
 
-def attention_kernel(slots_ref, counts_ref, q_ref, g_ref, stock_ref, out_ref, dq_ref, acc_ref):
+def attention_kernel(
+    slots_ref, counts_ref, q_ref, g_ref, stock_ref, flipped_ref, out_ref, dq_ref, acc_ref
+):
     factor = HEAD_DIM ** (-0.5)
     step = pl.program_id(0)
 
@@ -30,67 +32,67 @@
     rows = q_ref.shape[0]
     lane = lax.broadcasted_iota(jnp.int32, (rows, LANES), 1)
     first = lane < HEAD_DIM
+    row = lax.broadcasted_iota(jnp.int32, (LANES, rows), 0)
+    top = row < HEAD_DIM
     slots = [slots_ref[step, j] for j in range(LISTED)]
-    nt = (((1,), (1,)), ((), ()))
-    tn = (((0,), (0,)), ((), ()))
     f32 = jnp.float32
     bf16 = jnp.bfloat16
+
+    def dot(a, b):
+        return jnp.dot(a, b, preferred_element_type=f32)
 
     def run(used):
         def pair(p, carry):
             off = pl.multiple_of(p * LANES, LANES)
             qp = q_ref[:, pl.ds(off, LANES)]
             gp = g_ref[:, pl.ds(off, LANES)]
-            qs = qp * jnp.asarray(factor, qp.dtype)
-            gs = gp * jnp.asarray(factor, gp.dtype)
+            qt = qp.astype(f32).T * factor
+            gt = gp.astype(f32).T * factor
+            zf = jnp.zeros_like(qt)
+            qst = [jnp.where(top, qt, zf).astype(bf16), jnp.where(top, zf, qt).astype(bf16)]
+            gst = [jnp.where(top, gt, zf).astype(bf16), jnp.where(top, zf, gt).astype(bf16)]
             zq = jnp.zeros_like(qp)
             qh = [jnp.where(first, qp, zq), jnp.where(first, zq, qp)]
             gh = [jnp.where(first, gp, zq), jnp.where(first, zq, gp)]
-            qsh = [jnp.where(first, qs, zq), jnp.where(first, zq, qs)]
-            gsh = [jnp.where(first, gs, zq), jnp.where(first, zq, gs)]
             ks = [stock_ref[slots[j], 0, :, pl.ds(off, LANES)] for j in range(used)]
             vs = [stock_ref[slots[j], 1, :, pl.ds(off, LANES)] for j in range(used)]
+            kts = [flipped_ref[slots[j], 0, pl.ds(off, LANES), :] for j in range(used)]
+            vts = [flipped_ref[slots[j], 1, pl.ds(off, LANES), :] for j in range(used)]
             outs, dqs = [], []
             dks = [None] * used
             dvs = [None] * used
             for h in range(2):
-                scores = [
-                    lax.dot_general(qsh[h], ks[j], nt, preferred_element_type=f32)
-                    for j in range(used)
-                ]
-                peak = jnp.max(scores[0], axis=1, keepdims=True)
-                for j in range(1, used):
-                    peak = jnp.maximum(peak, jnp.max(scores[j], axis=1, keepdims=True))
+                scores = [dot(ks[j], qst[h]) for j in range(used)]
+                peak = jnp.max(scores[0], axis=0, keepdims=True)
+                for j in range(1, used):
+                    peak = jnp.maximum(peak, jnp.max(scores[j], axis=0, keepdims=True))
                 expos = [jnp.exp(sc - peak) for sc in scores]
-                total = jnp.sum(expos[0], axis=1, keepdims=True)
-                for j in range(1, used):
-                    total = total + jnp.sum(expos[j], axis=1, keepdims=True)
+                total = jnp.sum(expos[0], axis=0, keepdims=True)
+                for j in range(1, used):
+                    total = total + jnp.sum(expos[j], axis=0, keepdims=True)
                 inverse = 1.0 / total
                 ws = [(e * inverse).astype(bf16) for e in expos]
-                out = jnp.dot(ws[0], vs[0], preferred_element_type=f32)
-                for j in range(1, used):
-                    out = out + jnp.dot(ws[j], vs[j], preferred_element_type=f32)
-                dws = [
-                    lax.dot_general(gsh[h], vs[j], nt, preferred_element_type=f32)
-                    for j in range(used)
-                ]
+                out = dot(vts[0], ws[0])
+                for j in range(1, used):
+                    out = out + dot(vts[j], ws[j])
+                dws = [dot(vs[j], gst[h]) for j in range(used)]
                 wf = [w.astype(f32) for w in ws]
-                center = jnp.sum(wf[0] * dws[0], axis=1, keepdims=True)
-                for j in range(1, used):
-                    center = center + jnp.sum(wf[j] * dws[j], axis=1, keepdims=True)
+                center = jnp.sum(wf[0] * dws[0], axis=0, keepdims=True)
+                for j in range(1, used):
+                    center = center + jnp.sum(wf[j] * dws[j], axis=0, keepdims=True)
                 dss = [(wf[j] * (dws[j] - center)).astype(bf16) for j in range(used)]
-                dq = jnp.dot(dss[0], ks[0], preferred_element_type=f32)
-                for j in range(1, used):
-                    dq = dq + jnp.dot(dss[j], ks[j], preferred_element_type=f32)
+                dq = dot(kts[0], dss[0])
+                for j in range(1, used):
+                    dq = dq + dot(kts[j], dss[j])
                 for j in range(used):
-                    dk = lax.dot_general(dss[j], qh[h], tn, preferred_element_type=f32)
-                    dv = lax.dot_general(ws[j], gh[h], tn, preferred_element_type=f32)
+                    dk = dot(dss[j], qh[h])
+                    dv = dot(ws[j], gh[h])
                     dks[j] = dk if dks[j] is None else dks[j] + dk
                     dvs[j] = dv if dvs[j] is None else dvs[j] + dv
                 outs.append(out)
                 dqs.append(dq)
-            out_ref[:, pl.ds(off, LANES)] = jnp.where(first, outs[0], outs[1]).astype(out_ref.dtype)
-            dq_ref[:, pl.ds(off, LANES)] = jnp.where(first, dqs[0], dqs[1]).astype(dq_ref.dtype)
+            out_ref[:, pl.ds(off, LANES)] = jnp.where(top, outs[0], outs[1]).T.astype(out_ref.dtype)
+            dq_ref[:, pl.ds(off, LANES)] = jnp.where(top, dqs[0], dqs[1]).T.astype(dq_ref.dtype)
             for j in range(used):
                 acc_ref[slots[j], 0, :, pl.ds(off, LANES)] += dks[j]
                 acc_ref[slots[j], 1, :, pl.ds(off, LANES)] += dvs[j]
@@ -106,8 +108,9 @@
     rows, cols = stock.shape[2], stock.shape[3]
     blocks = queries.shape[0] // rows
     n_slots = stock.shape[0]
-    flops = blocks * (cols // LANES) * 2 * LISTED * 6 * 2 * rows * LANES * LANES
-    bytes_accessed = 4 * queries.size * 2 + stock.size * 2 + stock.size * 4
+    flipped = jnp.swapaxes(stock, 2, 3)
+    flops = blocks * (cols // LANES) * 2 * 3 * 6 * 2 * rows * LANES * LANES
+    bytes_accessed = 4 * queries.size * 2 + 2 * stock.size * 2 + stock.size * 4
     grid_spec = pltpu.PrefetchScalarGridSpec(
         num_scalar_prefetch=2,
         grid=(blocks,),
@@ -115,6 +118,7 @@
             pl.BlockSpec((rows, cols), lambda i, s, c: (i, 0)),
             pl.BlockSpec((rows, cols), lambda i, s, c: (i, 0)),
             pl.BlockSpec((n_slots, 2, rows, cols), lambda i, s, c: (0, 0, 0, 0)),
+            pl.BlockSpec((n_slots, 2, cols, rows), lambda i, s, c: (0, 0, 0, 0)),
         ],
         out_specs=[
             pl.BlockSpec((rows, cols), lambda i, s, c: (i, 0)),
@@ -132,10 +136,10 @@
         ],
         compiler_params=pltpu.CompilerParams(dimension_semantics=("arbitrary",)),
         cost_estimate=pl.CostEstimate(
-            flops=flops, transcendentals=blocks * rows * LISTED * rows * (cols // HEAD_DIM),
+            flops=flops, transcendentals=blocks * rows * 3 * rows * (cols // HEAD_DIM),
             bytes_accessed=bytes_accessed,
         ),
-    )(slot_ids, counts, queries, out_grad, stock)
+    )(slot_ids, counts, queries, out_grad, stock, flipped)
 
 
 def on_device(

time: 351 us -> 300 us (0.85)
  Pallas kernels: 109 us -> 65.4 us
  starting transfers between devices: 57.3 us -> 44.9 us
  local copies, waits for them, and re-layouts: 16.5 us -> 20.7 us
    pallas_call x1, Pallas kernels: 109 us -> 65.4 us  [attention(): pl.pallas_call(attention_kernel, grid_spec=grid_spec, out_shape=[jax.Shap...]
    ppermute x16, starting transfers between devices: 57.2 us -> 44.8 us  [passed_along(): return lax.ppermute(value, axis, pairs)]
    ppermute x16, waiting for transfers between devices: 52.5 us -> 61.6 us  [passed_along(): return lax.ppermute(value, axis, pairs)]
    all_gather x1, waiting for transfers between devices: 64.1 us -> 57 us  [on_device(): group_grads = lax.all_gather(both_grads, 'byx', axis=0, tiled=True)]
    another operation x1 -> x2, local copies, waits for them, and re-layouts: 0.72 us -> 4.99 us  [on_device(): stock = jnp.stack(arrived, 0)]
  transfers between devices with their start and end apart: 20 -> 20, of which waited for: 10 -> 10; matrix products, arithmetic and copies ran while one was open for 7% -> 10% of each run, Pallas kernels for 31% -> 22%
where the time goes in v4:
time: 300 us
  waiting for transfers between devices  139 us (46%)
  Pallas kernels  65.4 us (22%)
  starting transfers between devices  44.9 us (15%)
  local copies, waits for them, and re-layouts  20.7 us (7%)
  between operations  15.8 us (5%)
  matrix products  8.95 us (3%)
  other arithmetic  5.23 us (2%)
    pallas_call x1, Pallas kernels, attention(): pl.pallas_call(attention_kernel, grid_spec=grid_spec, out_shape=[jax.Shap...  65.4 us
    ppermute x16, waiting for transfers between devices, passed_along(): return lax.ppermute(value, axis, pairs)  61.6 us
    all_gather x1, waiting for transfers between devices, on_device(): group_grads = lax.all_gather(both_grads, 'byx', axis=0, tiled=True)  57 us
    ppermute x16, starting transfers between devices, passed_along(): return lax.ppermute(value, axis, pairs)  44.8 us
    reduce_scatter x1, waiting for transfers between devices, on_device(): lax.psum_scatter(partial, 'bz', scatter_dimension=0, tiled=True)  20.1 us
    unnamed x19, local copies, waits for them, and re-layouts  10.1 us
  transfers between devices with their start and end apart: 20, of which 10 were waited for; matrix products, arithmetic and copies ran while one was open for 10% of the time, Pallas kernels for 22%

profile of v4, /device:TPU:0, one launch (start us, length us, event | category | flops | bytes accessed | tf_op | source)
XLA Modules:
  0.0 299.8 jit_solution(10069133740730851025)
XLA Ops:
  8.1 2.2 copy.26
  10.4 2.1 fusion.1
  12.5 1.0 fusion
  13.5 5.9 %collective-permute-start = (bf16[2,128,512]{1,2,0:T(8,128)(2,1)S(1)}, bf16[2,128,512]{1,2,0:T(8,128)(2,1)}, u32[]{:S(2)}, u32[]{:S(2)}) collective-permute-start(bf16[2,128,512]{1,2,0:T(8,128)(2,1)S(1)} %pad_maximum_fusion), channel_id=1, source_target_pairs={{0,16},{4,20},{8,24},{12,28},{16,32},{20,36},{24,40},{28,44},{32,4... | collective-permute-start | bytes 786440 | tf_op jit(solution)/shard_map/ppermute | solution.py:18
  19.4 5.7 %collective-permute-start.1 = (bf16[2,128,512]{1,2,0:T(8,128)(2,1)S(1)}, bf16[2,128,512]{1,2,0:T(8,128)(2,1)}, u32[]{:S(2)}, u32[]{:S(2)}) collective-permute-start(bf16[2,128,512]{1,2,0:T(8,128)(2,1)S(1)} %pad_maximum_fusion), channel_id=1, source_target_pairs={{0,12},{4,16},{8,20},{12,24},{16,28},{20,32},{24,36},{28,40},{32,4... | collective-permute-start | bytes 786440 | tf_op jit(solution)/shard_map/ppermute | solution.py:18
  25.1 2.2 collective-permute-start.2
  27.3 3.4 %collective-permute-start.3 = (bf16[2,128,512]{1,2,0:T(8,128)(2,1)S(1)}, bf16[2,128,512]{1,2,0:T(8,128)(2,1)S(1)}, u32[]{:S(2)}, u32[]{:S(2)}) collective-permute-start(bf16[2,128,512]{1,2,0:T(8,128)(2,1)S(1)} %pad_maximum_fusion), channel_id=1, source_target_pairs={{0,4},{4,8},{8,12},{12,16},{16,20},{20,24},{24,28},{28,32},{32,36}... | collective-permute-start | bytes 786440 | tf_op jit(solution)/shard_map/ppermute | solution.py:18
  30.7 1.3 collective-permute-start.4
  32.7 1.3 collective-permute-start.5
  34.0 1.7 bitcast_dynamic-update-slice_fusion.8
  35.8 1.3 collective-permute-start.6
  37.1 1.7 bitcast_dynamic-update-slice_fusion.7
  38.8 7.5 %collective-permute-done.2 = bf16[2,128,512]{1,2,0:T(8,128)(2,1)S(1)} collective-permute-done((bf16[2,128,512]{1,2,0:T(8,128)(2,1)S(1)}, bf16[2,128,512]{1,2,0:T(8,128)(2,1)S(1)}, u32[]{:S(2)}, u32[]{:S(2)}) %collective-permute-start.2) | collective-permute-done | bytes 262176 | tf_op jit(solution)/shard_map/ppermute | solution.py:18
  46.3 1.3 collective-permute-start.7
  47.6 0.7 bitcast_dynamic-update-slice_fusion.6
  48.4 0.7 bitcast_dynamic-update-slice_fusion.5
  49.1 0.7 bitcast_dynamic-update-slice_fusion.4
  49.8 0.7 bitcast_dynamic-update-slice_fusion.3
  50.6 0.7 bitcast_dynamic-update-slice_fusion.2
  51.3 3.3 %collective-permute-done.6 = bf16[2,128,512]{1,2,0:T(8,128)(2,1)S(1)} collective-permute-done((bf16[2,128,512]{1,2,0:T(8,128)(2,1)S(1)}, bf16[2,128,512]{1,2,0:T(8,128)(2,1)S(1)}, u32[]{:S(2)}, u32[]{:S(2)}) %collective-permute-start.6) | collective-permute-done | bytes 262176 | tf_op jit(solution)/shard_map/ppermute | solution.py:18
  55.3 5.3 %collective-permute-done.7 = bf16[2,128,512]{1,2,0:T(8,128)(2,1)S(1)} collective-permute-done((bf16[2,128,512]{1,2,0:T(8,128)(2,1)S(1)}, bf16[2,128,512]{1,2,0:T(8,128)(2,1)S(1)}, u32[]{:S(2)}, u32[]{:S(2)}) %collective-permute-start.7) | collective-permute-done | bytes 262176 | tf_op jit(solution)/shard_map/ppermute | solution.py:18
  60.6 0.7 bitcast_dynamic-update-slice_fusion
  61.3 4.3 %copy.25.stock_ref = bf16[9,2,128,512]{3,2,1,0:T(8,128)(2,1)} copy(bf16[9,2,128,512]{2,3,1,0:T(8,128)(2,1)} %bitcast_dynamic-update-slice_fusion) | data formatting | bytes 4718592 | tf_op jit(solution)/shard_map/stack | solution.py:164
  65.6 65.4 %shard_map.110 = (bf16[2048,512]{1,0:T(8,128)(2,1)}, bf16[2048,512]{1,0:T(8,128)(2,1)}, f32[9,2,128,512]{3,2,1,0:T(8,128)}) custom-call(s32[16,5]{1,0:T(8,128)} %broadcast_subtract_fusion.slots_ref, s32[16]{0:T(128)} %counts_ref.1, bf16[2048,512]{1,0:T(8,128)(2,1)} %q_ref.1, bf16[2048,512]{1,0:T(8,128)(2,1)} %g_ref.1, ...), custom_call_target="tpu_custom_call" | custom-call | flops 9663676416 | bytes 17825792 | tf_op jit(solution)/shard_map/pallas_call | solution.py:129
  131.0 2.9 slice_bitcast_fusion.7
  133.9 3.8 %collective-permute-start.15 = (f32[2,128,512]{2,1,0:T(8,128)S(1)}, f32[2,128,512]{2,1,0:T(8,128)S(1)}, u32[]{:S(2)}, u32[]{:S(2)}) collective-permute-start(f32[2,128,512]{2,1,0:T(8,128)S(1)} %get-tuple-element.12), channel_id=1, source_target_pairs={{0,16},{4,20},{8,24},{12,28},{16,32},{20,36},{24,40},{28,44},{32,4... | collective-permute-start | bytes 1572872 | tf_op jit(solution)/shard_map/ppermute | solution.py:18
  137.7 8.7 %collective-permute-start.14 = (f32[2,128,512]{2,1,0:T(8,128)S(1)}, f32[2,128,512]{2,1,0:T(8,128)S(1)}, u32[]{:S(2)}, u32[]{:S(2)}) collective-permute-start(f32[2,128,512]{2,1,0:T(8,128)S(1)} %get-tuple-element.13), channel_id=1, source_target_pairs={{0,12},{4,16},{8,20},{12,24},{16,28},{20,32},{24,36},{28,40},{32,4... | collective-permute-start | bytes 1572872 | tf_op jit(solution)/shard_map/ppermute | solution.py:18
  146.4 1.3 collective-permute-start.13
  147.7 3.5 %collective-permute-start.12 = (f32[2,128,512]{2,1,0:T(8,128)S(1)}, f32[2,128,512]{2,1,0:T(8,128)S(1)}, u32[]{:S(2)}, u32[]{:S(2)}) collective-permute-start(f32[2,128,512]{2,1,0:T(8,128)S(1)} %get-tuple-element.15), channel_id=1, source_target_pairs={{0,4},{4,8},{8,12},{12,16},{16,20},{20,24},{24,28},{28,32},{32,36}... | collective-permute-start | bytes 1572872 | tf_op jit(solution)/shard_map/ppermute | solution.py:18
  151.2 1.3 collective-permute-start.11
  152.5 23.4 %collective-permute-done.15 = f32[2,128,512]{2,1,0:T(8,128)S(1)} collective-permute-done((f32[2,128,512]{2,1,0:T(8,128)S(1)}, f32[2,128,512]{2,1,0:T(8,128)S(1)}, u32[]{:S(2)}, u32[]{:S(2)}) %collective-permute-start.15) | collective-permute-done | bytes 524320 | tf_op jit(solution)/shard_map/ppermute | solution.py:18
  175.9 1.3 collective-permute-start.10
  177.2 1.3 collective-permute-start.9
  178.5 7.3 %collective-permute-done.13 = f32[2,128,512]{2,1,0:T(8,128)S(1)} collective-permute-done((f32[2,128,512]{2,1,0:T(8,128)S(1)}, f32[2,128,512]{2,1,0:T(8,128)S(1)}, u32[]{:S(2)}, u32[]{:S(2)}) %collective-permute-start.13) | collective-permute-done | bytes 524320 | tf_op jit(solution)/shard_map/ppermute | solution.py:18
  185.8 1.3 collective-permute-start.8
  187.1 13.2 %collective-permute-done.10 = f32[2,128,512]{2,1,0:T(8,128)S(1)} collective-permute-done((f32[2,128,512]{2,1,0:T(8,128)S(1)}, f32[2,128,512]{2,1,0:T(8,128)S(1)}, u32[]{:S(2)}, u32[]{:S(2)}) %collective-permute-start.10) | collective-permute-done | bytes 524320 | tf_op jit(solution)/shard_map/ppermute | solution.py:18
  200.2 1.5 collective-permute-done.8
  201.7 1.5 fusion.9
  203.3 0.8 pad_maximum_fusion.1
  204.1 0.8 fusion.10
  204.9 0.8 copy-done.2
  205.7 1.8 convolution_add_fusion
  207.6 1.1 constant_dynamic-slice_fusion
  208.7 57.0 %all-gather.4.cloned.1.call-done = bf16[1024,1024]{1,0:T(8,128)(2,1)} async-done(((bf16[128,1024]{1,0:T(8,128)(2,1)}), bf16[1024,1024]{1,0:T(8,128)(2,1)}) %all-gather.4.cloned.1.call-update) | async-done | bytes 2097168 | tf_op jit(solution)/shard_map/all_gather | solution.py:182
  265.7 3.3 %fusion.12 = f32[256,1024]{1,0:T(8,128)} fusion(bf16[1024,256]{0,1:T(8,128)(2,1)S(1)} %bitcast.73, bf16[1024,1024]{1,0:T(8,128)(2,1)} %all-gather.4.cloned.1.call-done), kind=kOutput, calls=%fused_computation.39 | convolution fusion | flops 536870912 | bytes 3670016 | tf_op jit(solution)/shard_map/dot_general | solution.py:191
  269.0 1.6 convert_element_type.15
  270.6 20.1 %reduce-scatter.5.cloned.1.call-done = f32[64,1024]{1,0:T(8,128)} async-done(((f32[256,1024]{1,0:T(8,128)}), f32[64,1024]{1,0:T(8,128)}) %reduce-scatter.5.cloned.1.call-update) | async-done | bytes 262160 | tf_op jit(solution)/shard_map/reduce_scatter | solution.py:194
  290.7 1.7 fusion.11
  (33 shorter events, 1.9 us)
Async XLA Ops:
  8.0 2.4 copy-start
  8.0 4.5 %copy-start.3 = (bf16[128,2048]{1,0:T(8,128)(2,1)S(1)}, bf16[128,2048]{1,0:T(8,128)(2,1)}, u32[]{:S(2)}) copy-start(bf16[128,2048]{1,0:T(8,128)(2,1)} %param.8) | copy-start | bytes 1572868
  8.0 199.6 %all-gather.6.cloned.1.call-start = ((), (), s32[]{:S(2)}) async-start(), calls=%async_computation.5 | async-start | bytes 4718592 | tf_op jit(solution)/shard_map/all_gather | solution.py:152
  10.3 21.7 %copy-start.4 = (s32[16,5]{0,1:T(8,128)S(1)}, s32[16,5]{0,1:T(8,128)}, u32[]{:S(2)}) copy-start(s32[16,5]{0,1:T(8,128)} %param.12) | copy-start | bytes 964
  10.3 255.4 %all-gather.4.cloned.1.call-start = ((), (), s32[]{:S(2)}) async-start(), calls=%async_computation.3 | async-start | bytes 2359296 | tf_op jit(solution)/shard_map/all_gather | solution.py:182
  10.4 2.1 copy-start.1
  13.5 19.2 %collective-permute-start = (bf16[2,128,512]{1,2,0:T(8,128)(2,1)S(1)}, bf16[2,128,512]{1,2,0:T(8,128)(2,1)}, u32[]{:S(2)}, u32[]{:S(2)}) collective-permute-start(bf16[2,128,512]{1,2,0:T(8,128)(2,1)S(1)} %pad_maximum_fusion), channel_id=1, source_target_pairs={{0,16},{4,20},{8,24},{12,28},{16,32},{20,36},{24,40},{28,44},{32,4... | collective-permute-start | bytes 786440 | tf_op jit(solution)/shard_map/ppermute | solution.py:18
  19.4 16.4 %collective-permute-start.1 = (bf16[2,128,512]{1,2,0:T(8,128)(2,1)S(1)}, bf16[2,128,512]{1,2,0:T(8,128)(2,1)}, u32[]{:S(2)}, u32[]{:S(2)}) collective-permute-start(bf16[2,128,512]{1,2,0:T(8,128)(2,1)S(1)} %pad_maximum_fusion), channel_id=1, source_target_pairs={{0,12},{4,16},{8,20},{12,24},{16,28},{20,32},{24,36},{28,40},{32,4... | collective-permute-start | bytes 786440 | tf_op jit(solution)/shard_map/ppermute | solution.py:18
  25.1 21.2 %collective-permute-start.2 = (bf16[2,128,512]{1,2,0:T(8,128)(2,1)S(1)}, bf16[2,128,512]{1,2,0:T(8,128)(2,1)S(1)}, u32[]{:S(2)}, u32[]{:S(2)}) collective-permute-start(bf16[2,128,512]{1,2,0:T(8,128)(2,1)S(1)} %pad_maximum_fusion), channel_id=1, source_target_pairs={{0,8},{4,12},{8,16},{12,20},{16,24},{20,28},{24,32},{28,36},{32,40... | collective-permute-start | bytes 786440 | tf_op jit(solution)/shard_map/ppermute | solution.py:18
  27.3 21.0 %collective-permute-start.3 = (bf16[2,128,512]{1,2,0:T(8,128)(2,1)S(1)}, bf16[2,128,512]{1,2,0:T(8,128)(2,1)S(1)}, u32[]{:S(2)}, u32[]{:S(2)}) collective-permute-start(bf16[2,128,512]{1,2,0:T(8,128)(2,1)S(1)} %pad_maximum_fusion), channel_id=1, source_target_pairs={{0,4},{4,8},{8,12},{12,16},{16,20},{20,24},{24,28},{28,32},{32,36}... | collective-permute-start | bytes 786440 | tf_op jit(solution)/shard_map/ppermute | solution.py:18
  30.7 19.1 %collective-permute-start.4 = (bf16[2,128,512]{1,2,0:T(8,128)(2,1)S(1)}, bf16[2,128,512]{1,2,0:T(8,128)(2,1)S(1)}, u32[]{:S(2)}, u32[]{:S(2)}) collective-permute-start(bf16[2,128,512]{1,2,0:T(8,128)(2,1)S(1)} %pad_maximum_fusion), channel_id=1, source_target_pairs={{4,0},{8,4},{12,8},{16,12},{20,16},{24,20},{28,24},{32,28},{36,32}... | collective-permute-start | bytes 786440 | tf_op jit(solution)/shard_map/ppermute | solution.py:18
  32.7 17.9 %collective-permute-start.5 = (bf16[2,128,512]{1,2,0:T(8,128)(2,1)S(1)}, bf16[2,128,512]{1,2,0:T(8,128)(2,1)S(1)}, u32[]{:S(2)}, u32[]{:S(2)}) collective-permute-start(bf16[2,128,512]{1,2,0:T(8,128)(2,1)S(1)} %pad_maximum_fusion), channel_id=1, source_target_pairs={{8,0},{12,4},{16,8},{20,12},{24,16},{28,20},{32,24},{36,28},{40,32... | collective-permute-start | bytes 786440 | tf_op jit(solution)/shard_map/ppermute | solution.py:18
  35.8 18.8 %collective-permute-start.6 = (bf16[2,128,512]{1,2,0:T(8,128)(2,1)S(1)}, bf16[2,128,512]{1,2,0:T(8,128)(2,1)S(1)}, u32[]{:S(2)}, u32[]{:S(2)}) collective-permute-start(bf16[2,128,512]{1,2,0:T(8,128)(2,1)S(1)} %pad_maximum_fusion), channel_id=1, source_target_pairs={{12,0},{16,4},{20,8},{24,12},{28,16},{32,20},{36,24},{40,28},{44,3... | collective-permute-start | bytes 786440 | tf_op jit(solution)/shard_map/ppermute | solution.py:18
  46.3 14.3 %collective-permute-start.7 = (bf16[2,128,512]{1,2,0:T(8,128)(2,1)S(1)}, bf16[2,128,512]{1,2,0:T(8,128)(2,1)S(1)}, u32[]{:S(2)}, u32[]{:S(2)}) collective-permute-start(bf16[2,128,512]{1,2,0:T(8,128)(2,1)S(1)} %pad_maximum_fusion), channel_id=1, source_target_pairs={{16,0},{20,4},{24,8},{28,12},{32,16},{36,20},{40,24},{44,28},{48,3... | collective-permute-start | bytes 786440 | tf_op jit(solution)/shard_map/ppermute | solution.py:18
  133.9 42.0 %collective-permute-start.15 = (f32[2,128,512]{2,1,0:T(8,128)S(1)}, f32[2,128,512]{2,1,0:T(8,128)S(1)}, u32[]{:S(2)}, u32[]{:S(2)}) collective-permute-start(f32[2,128,512]{2,1,0:T(8,128)S(1)} %get-tuple-element.12), channel_id=1, source_target_pairs={{0,16},{4,20},{8,24},{12,28},{16,32},{20,36},{24,40},{28,44},{32,4... | collective-permute-start | bytes 1572872 | tf_op jit(solution)/shard_map/ppermute | solution.py:18
  137.7 39.5 %collective-permute-start.14 = (f32[2,128,512]{2,1,0:T(8,128)S(1)}, f32[2,128,512]{2,1,0:T(8,128)S(1)}, u32[]{:S(2)}, u32[]{:S(2)}) collective-permute-start(f32[2,128,512]{2,1,0:T(8,128)S(1)} %get-tuple-element.13), channel_id=1, source_target_pairs={{0,12},{4,16},{8,20},{12,24},{16,28},{20,32},{24,36},{28,40},{32,4... | collective-permute-start | bytes 1572872 | tf_op jit(solution)/shard_map/ppermute | solution.py:18
  146.4 39.4 %collective-permute-start.13 = (f32[2,128,512]{2,1,0:T(8,128)S(1)}, f32[2,128,512]{2,1,0:T(8,128)S(1)}, u32[]{:S(2)}, u32[]{:S(2)}) collective-permute-start(f32[2,128,512]{2,1,0:T(8,128)S(1)} %get-tuple-element.14), channel_id=1, source_target_pairs={{0,8},{4,12},{8,16},{12,20},{16,24},{20,28},{24,32},{28,36},{32,40... | collective-permute-start | bytes 1572872 | tf_op jit(solution)/shard_map/ppermute | solution.py:18
  147.7 39.3 %collective-permute-start.12 = (f32[2,128,512]{2,1,0:T(8,128)S(1)}, f32[2,128,512]{2,1,0:T(8,128)S(1)}, u32[]{:S(2)}, u32[]{:S(2)}) collective-permute-start(f32[2,128,512]{2,1,0:T(8,128)S(1)} %get-tuple-element.15), channel_id=1, source_target_pairs={{0,4},{4,8},{8,12},{12,16},{16,20},{20,24},{24,28},{28,32},{32,36}... | collective-permute-start | bytes 1572872 | tf_op jit(solution)/shard_map/ppermute | solution.py:18
  151.2 35.9 %collective-permute-start.11 = (f32[2,128,512]{2,1,0:T(8,128)S(1)}, f32[2,128,512]{2,1,0:T(8,128)S(1)}, u32[]{:S(2)}, u32[]{:S(2)}) collective-permute-start(f32[2,128,512]{2,1,0:T(8,128)S(1)} %get-tuple-element.16), channel_id=1, source_target_pairs={{4,0},{8,4},{12,8},{16,12},{20,16},{24,20},{28,24},{32,28},{36,32}... | collective-permute-start | bytes 1572872 | tf_op jit(solution)/shard_map/ppermute | solution.py:18
  175.9 24.4 %collective-permute-start.10 = (f32[2,128,512]{2,1,0:T(8,128)S(1)}, f32[2,128,512]{2,1,0:T(8,128)S(1)}, u32[]{:S(2)}, u32[]{:S(2)}) collective-permute-start(f32[2,128,512]{2,1,0:T(8,128)S(1)} %get-tuple-element.17), channel_id=1, source_target_pairs={{8,0},{12,4},{16,8},{20,12},{24,16},{28,20},{32,24},{36,28},{40,32... | collective-permute-start | bytes 1572872 | tf_op jit(solution)/shard_map/ppermute | solution.py:18
  177.2 23.1 %collective-permute-start.9 = (f32[2,128,512]{2,1,0:T(8,128)S(1)}, f32[2,128,512]{2,1,0:T(8,128)S(1)}, u32[]{:S(2)}, u32[]{:S(2)}) collective-permute-start(f32[2,128,512]{2,1,0:T(8,128)S(1)} %get-tuple-element.18), channel_id=1, source_target_pairs={{12,0},{16,4},{20,8},{24,12},{28,16},{32,20},{36,24},{40,28},{44,3... | collective-permute-start | bytes 1572872 | tf_op jit(solution)/shard_map/ppermute | solution.py:18
  185.8 16.0 %collective-permute-start.8 = (f32[2,128,512]{2,1,0:T(8,128)S(1)}, f32[2,128,512]{2,1,0:T(8,128)S(1)}, u32[]{:S(2)}, u32[]{:S(2)}) collective-permute-start(f32[2,128,512]{2,1,0:T(8,128)S(1)} %get-tuple-element.11), channel_id=1, source_target_pairs={{16,0},{20,4},{24,8},{28,12},{32,16},{36,20},{40,24},{44,28},{48,3... | collective-permute-start | bytes 1572872 | tf_op jit(solution)/shard_map/ppermute | solution.py:18
  204.0 64.9 %reduce-scatter.3.cloned.1.call-start = ((), (), s32[]{:S(2)}) async-start(), calls=%async_computation.2 | async-start | bytes 1310720 | tf_op jit(solution)/shard_map/reduce_scatter | solution.py:178
  204.1 1.6 copy-start.2
  207.5 83.2 %reduce-scatter.5.cloned.1.call-start = ((), (), s32[]{:S(2)}) async-start(), calls=%async_computation.4 | async-start | bytes 1310720 | tf_op jit(solution)/shard_map/reduce_scatter | solution.py:194
Sparse Core Ops, SparseCore 0:
  11.3 100.5 all-gather.5
  204.2 61.4 all-gather.3
Sparse Core Ops, SparseCore 1:
  207.6 29.2 reduce-scatter.2
  269.1 21.6 reduce-scatter.4

commit v5 on v4

--- a/solution.py
+++ b/solution.py
@@ -169,7 +169,8 @@
     owned = running[REACH]
     for offset in range(-REACH, REACH + 1):
         if offset != 0:
-            owned = owned + passed_along(running[REACH + offset], blk, offset, outer * inner)
+            sent = running[REACH + offset].astype(jnp.bfloat16)
+            owned = owned + passed_along(sent, blk, offset, outer * inner).astype(jnp.float32)
     rounded = owned.astype(jnp.bfloat16)
     contract_cols = (((1,), (1,)), ((), ()))
     encoder_terms = lax.dot_general(

time: 300 us -> 274 us (0.913)
  waiting for transfers between devices: 139 us -> 97.4 us
  starting transfers between devices: 44.9 us -> 58.9 us
    ppermute x16, waiting for transfers between devices: 61.6 us -> 25.6 us  [passed_along(): return lax.ppermute(value, axis, pairs)]
    ppermute x16, starting transfers between devices: 44.8 us -> 58.8 us  [passed_along(): return lax.ppermute(value, axis, pairs)]
    all_gather x1, waiting for transfers between devices: 57 us -> 51.5 us  [on_device(): group_grads = lax.all_gather(both_grads, 'byx', axis=0, tiled=True)]
  transfers between devices with their start and end apart: 20 -> 20, of which waited for: 10 -> 9; matrix products, arithmetic and copies ran while one was open for 10% -> 11% of each run, Pallas kernels for 22% -> 24%
where the time goes in v5:
time: 274 us
  waiting for transfers between devices  97.4 us (36%)
  Pallas kernels  66.9 us (24%)
  starting transfers between devices  58.9 us (21%)
  local copies, waits for them, and re-layouts  18 us (7%)
  between operations  15.8 us (6%)
  matrix products  8.95 us (3%)
  other arithmetic  7.76 us (3%)
    pallas_call x1, Pallas kernels, attention(): pl.pallas_call(attention_kernel, grid_spec=grid_spec, out_shape=[jax.Shap...  66.9 us
    ppermute x16, starting transfers between devices, passed_along(): return lax.ppermute(value, axis, pairs)  58.8 us
    all_gather x1, waiting for transfers between devices, on_device(): group_grads = lax.all_gather(both_grads, 'byx', axis=0, tiled=True)  51.5 us
    ppermute x16, waiting for transfers between devices, passed_along(): return lax.ppermute(value, axis, pairs)  25.6 us
    reduce_scatter x1, waiting for transfers between devices, on_device(): lax.psum_scatter(partial, 'bz', scatter_dimension=0, tiled=True)  20.1 us
    unnamed x19, local copies, waits for them, and re-layouts  10.1 us
  transfers between devices with their start and end apart: 20, of which 9 were waited for; matrix products, arithmetic and copies ran while one was open for 11% of the time, Pallas kernels for 24%

profile of v5, /device:TPU:0, one launch (start us, length us, event | category | flops | bytes accessed | tf_op | source)
XLA Modules:
  0.0 273.7 jit_solution(1060106070375887380)
XLA Ops:
  8.1 2.2 copy.26
  10.4 2.1 fusion
  12.5 1.0 fusion.1
  13.5 5.9 %collective-permute-start = (bf16[2,128,512]{1,2,0:T(8,128)(2,1)S(1)}, bf16[2,128,512]{1,2,0:T(8,128)(2,1)}, u32[]{:S(2)}, u32[]{:S(2)}) collective-permute-start(bf16[2,128,512]{1,2,0:T(8,128)(2,1)S(1)} %pad_maximum_fusion), channel_id=1, source_target_pairs={{0,16},{4,20},{8,24},{12,28},{16,32},{20,36},{24,40},{28,44},{32,4... | collective-permute-start | bytes 786440 | tf_op jit(solution)/shard_map/ppermute | solution.py:18
  19.4 5.7 %collective-permute-start.1 = (bf16[2,128,512]{1,2,0:T(8,128)(2,1)S(1)}, bf16[2,128,512]{1,2,0:T(8,128)(2,1)}, u32[]{:S(2)}, u32[]{:S(2)}) collective-permute-start(bf16[2,128,512]{1,2,0:T(8,128)(2,1)S(1)} %pad_maximum_fusion), channel_id=1, source_target_pairs={{0,12},{4,16},{8,20},{12,24},{16,28},{20,32},{24,36},{28,40},{32,4... | collective-permute-start | bytes 786440 | tf_op jit(solution)/shard_map/ppermute | solution.py:18
  25.1 2.2 collective-permute-start.2
  27.3 3.4 %collective-permute-start.3 = (bf16[2,128,512]{1,2,0:T(8,128)(2,1)S(1)}, bf16[2,128,512]{1,2,0:T(8,128)(2,1)S(1)}, u32[]{:S(2)}, u32[]{:S(2)}) collective-permute-start(bf16[2,128,512]{1,2,0:T(8,128)(2,1)S(1)} %pad_maximum_fusion), channel_id=1, source_target_pairs={{0,4},{4,8},{8,12},{12,16},{16,20},{20,24},{24,28},{28,32},{32,36}... | collective-permute-start | bytes 786440 | tf_op jit(solution)/shard_map/ppermute | solution.py:18
  30.7 1.3 collective-permute-start.4
  32.1 0.6 broadcast_subtract_fusion.slots_ref
  32.7 1.3 collective-permute-start.5
  34.0 1.7 bitcast_dynamic-update-slice_fusion.8
  35.8 1.3 collective-permute-start.6
  37.1 1.7 bitcast_dynamic-update-slice_fusion.7
  38.8 7.5 %collective-permute-done.2 = bf16[2,128,512]{1,2,0:T(8,128)(2,1)S(1)} collective-permute-done((bf16[2,128,512]{1,2,0:T(8,128)(2,1)S(1)}, bf16[2,128,512]{1,2,0:T(8,128)(2,1)S(1)}, u32[]{:S(2)}, u32[]{:S(2)}) %collective-permute-start.2) | collective-permute-done | bytes 262176 | tf_op jit(solution)/shard_map/ppermute | solution.py:18
  46.3 1.3 collective-permute-start.7
  47.6 0.7 bitcast_dynamic-update-slice_fusion.6
  48.4 0.7 bitcast_dynamic-update-slice_fusion.5
  49.1 0.7 bitcast_dynamic-update-slice_fusion.4
  49.8 0.7 bitcast_dynamic-update-slice_fusion.3
  50.6 0.7 bitcast_dynamic-update-slice_fusion.2
  51.3 3.3 %collective-permute-done.6 = bf16[2,128,512]{1,2,0:T(8,128)(2,1)S(1)} collective-permute-done((bf16[2,128,512]{1,2,0:T(8,128)(2,1)S(1)}, bf16[2,128,512]{1,2,0:T(8,128)(2,1)S(1)}, u32[]{:S(2)}, u32[]{:S(2)}) %collective-permute-start.6) | collective-permute-done | bytes 262176 | tf_op jit(solution)/shard_map/ppermute | solution.py:18
  54.6 0.7 bitcast_dynamic-update-slice_fusion.1
  55.3 5.3 %collective-permute-done.7 = bf16[2,128,512]{1,2,0:T(8,128)(2,1)S(1)} collective-permute-done((bf16[2,128,512]{1,2,0:T(8,128)(2,1)S(1)}, bf16[2,128,512]{1,2,0:T(8,128)(2,1)S(1)}, u32[]{:S(2)}, u32[]{:S(2)}) %collective-permute-start.7) | collective-permute-done | bytes 262176 | tf_op jit(solution)/shard_map/ppermute | solution.py:18
  60.6 0.7 bitcast_dynamic-update-slice_fusion
  61.3 4.3 %copy.25.stock_ref = bf16[9,2,128,512]{3,2,1,0:T(8,128)(2,1)} copy(bf16[9,2,128,512]{2,3,1,0:T(8,128)(2,1)} %bitcast_dynamic-update-slice_fusion) | data formatting | bytes 4718592 | tf_op jit(solution)/shard_map/stack | solution.py:164
  65.6 66.9 %shard_map.110 = (bf16[2048,512]{1,0:T(8,128)(2,1)}, bf16[2048,512]{1,0:T(8,128)(2,1)}, f32[9,2,128,512]{3,2,1,0:T(8,128)}) custom-call(s32[16,5]{1,0:T(8,128)} %broadcast_subtract_fusion.slots_ref, s32[16]{0:T(128)} %counts_ref.1, bf16[2048,512]{1,0:T(8,128)(2,1)} %q_ref.1, bf16[2048,512]{1,0:T(8,128)(2,1)} %g_ref.1, ...), custom_call_target="tpu_custom_call" | custom-call | flops 9663676416 | bytes 17825792 | tf_op jit(solution)/shard_map/pallas_call | solution.py:129
  132.5 2.7 convert.10
  135.3 1.3 collective-permute-start.10
  136.6 1.3 collective-permute-start.11
  137.9 6.1 %collective-permute-start.12 = (bf16[2,128,512]{2,1,0:T(8,128)(2,1)S(1)}, bf16[2,128,512]{2,1,0:T(8,128)(2,1)S(1)}, u32[]{:S(2)}, u32[]{:S(2)}) collective-permute-start(bf16[2,128,512]{2,1,0:T(8,128)(2,1)S(1)} %get-tuple-element.15), channel_id=1, source_target_pairs={{0,4},{4,8},{8,12},{12,16},{16,20},{20,24},{24,28},{28,32},{32,36}... | collective-permute-start | bytes 786440 | tf_op jit(solution)/shard_map/ppermute | solution.py:18
  144.0 5.8 %collective-permute-start.13 = (bf16[2,128,512]{2,1,0:T(8,128)(2,1)S(1)}, bf16[2,128,512]{2,1,0:T(8,128)(2,1)S(1)}, u32[]{:S(2)}, u32[]{:S(2)}) collective-permute-start(bf16[2,128,512]{2,1,0:T(8,128)(2,1)S(1)} %get-tuple-element.14), channel_id=1, source_target_pairs={{0,8},{4,12},{8,16},{12,20},{16,24},{20,28},{24,32},{28,36},{32,40... | collective-permute-start | bytes 786440 | tf_op jit(solution)/shard_map/ppermute | solution.py:18
  149.8 3.9 %collective-permute-start.14 = (bf16[2,128,512]{2,1,0:T(8,128)(2,1)S(1)}, bf16[2,128,512]{2,1,0:T(8,128)(2,1)S(1)}, u32[]{:S(2)}, u32[]{:S(2)}) collective-permute-start(bf16[2,128,512]{2,1,0:T(8,128)(2,1)S(1)} %get-tuple-element.13), channel_id=1, source_target_pairs={{0,12},{4,16},{8,20},{12,24},{16,28},{20,32},{24,36},{28,40},{32,4... | collective-permute-start | bytes 786440 | tf_op jit(solution)/shard_map/ppermute | solution.py:18
  153.7 15.5 %collective-permute-start.15 = (bf16[2,128,512]{2,1,0:T(8,128)(2,1)S(1)}, bf16[2,128,512]{2,1,0:T(8,128)(2,1)S(1)}, u32[]{:S(2)}, u32[]{:S(2)}) collective-permute-start(bf16[2,128,512]{2,1,0:T(8,128)(2,1)S(1)} %get-tuple-element.12), channel_id=1, source_target_pairs={{0,16},{4,20},{8,24},{12,28},{16,32},{20,36},{24,40},{28,44},{32,4... | collective-permute-start | bytes 786440 | tf_op jit(solution)/shard_map/ppermute | solution.py:18
  169.2 1.3 collective-permute-start.8
  170.6 1.3 collective-permute-start.9
  171.9 1.2 collective-permute-done.15
  173.1 8.0 %collective-permute-done.8 = bf16[2,128,512]{2,1,0:T(8,128)(2,1)S(1)} collective-permute-done((bf16[2,128,512]{2,1,0:T(8,128)(2,1)S(1)}, bf16[2,128,512]{2,1,0:T(8,128)(2,1)S(1)}, u32[]{:S(2)}, u32[]{:S(2)}) %collective-permute-start.8) | collective-permute-done | bytes 262176 | tf_op jit(solution)/shard_map/ppermute | solution.py:18
  181.2 1.4 fusion.9
  182.6 0.8 pad_maximum_fusion.1
  183.4 0.8 fusion.10
  184.3 0.8 copy-done.2
  185.0 1.8 convolution_add_fusion
  186.9 1.1 constant_dynamic-slice_fusion
  188.0 51.5 %all-gather.4.cloned.1.call-done = bf16[1024,1024]{1,0:T(8,128)(2,1)} async-done(((bf16[128,1024]{1,0:T(8,128)(2,1)}), bf16[1024,1024]{1,0:T(8,128)(2,1)}) %all-gather.4.cloned.1.call-update) | async-done | bytes 2097168 | tf_op jit(solution)/shard_map/all_gather | solution.py:183
  239.6 3.3 %fusion.12 = f32[256,1024]{1,0:T(8,128)} fusion(bf16[1024,256]{0,1:T(8,128)(2,1)S(1)} %bitcast.73, bf16[1024,1024]{1,0:T(8,128)(2,1)} %all-gather.4.cloned.1.call-done), kind=kOutput, calls=%fused_computation.39 | convolution fusion | flops 536870912 | bytes 3670016 | tf_op jit(solution)/shard_map/dot_general | solution.py:192
  242.9 1.6 convert_element_type.87
  244.5 20.1 %reduce-scatter.5.cloned.1.call-done = f32[64,1024]{1,0:T(8,128)} async-done(((f32[256,1024]{1,0:T(8,128)}), f32[64,1024]{1,0:T(8,128)}) %reduce-scatter.5.cloned.1.call-update) | async-done | bytes 262160 | tf_op jit(solution)/shard_map/reduce_scatter | solution.py:195
  264.6 1.7 fusion.11
  (34 shorter events, 0.9 us)
Async XLA Ops:
  8.0 2.4 copy-start
  8.0 4.5 %copy-start.3 = (bf16[128,2048]{1,0:T(8,128)(2,1)S(1)}, bf16[128,2048]{1,0:T(8,128)(2,1)}, u32[]{:S(2)}) copy-start(bf16[128,2048]{1,0:T(8,128)(2,1)} %param.8) | copy-start | bytes 1572868
  8.0 178.9 %all-gather.6.cloned.1.call-start = ((), (), s32[]{:S(2)}) async-start(), calls=%async_computation.5 | async-start | bytes 4718592 | tf_op jit(solution)/shard_map/all_gather | solution.py:152
  10.3 21.7 %copy-start.4 = (s32[16,5]{0,1:T(8,128)S(1)}, s32[16,5]{0,1:T(8,128)}, u32[]{:S(2)}) copy-start(s32[16,5]{0,1:T(8,128)} %param.12) | copy-start | bytes 964
  10.3 229.3 %all-gather.4.cloned.1.call-start = ((), (), s32[]{:S(2)}) async-start(), calls=%async_computation.3 | async-start | bytes 2359296 | tf_op jit(solution)/shard_map/all_gather | solution.py:183
  10.4 2.1 copy-start.1
  13.5 19.2 %collective-permute-start = (bf16[2,128,512]{1,2,0:T(8,128)(2,1)S(1)}, bf16[2,128,512]{1,2,0:T(8,128)(2,1)}, u32[]{:S(2)}, u32[]{:S(2)}) collective-permute-start(bf16[2,128,512]{1,2,0:T(8,128)(2,1)S(1)} %pad_maximum_fusion), channel_id=1, source_target_pairs={{0,16},{4,20},{8,24},{12,28},{16,32},{20,36},{24,40},{28,44},{32,4... | collective-permute-start | bytes 786440 | tf_op jit(solution)/shard_map/ppermute | solution.py:18
  19.4 16.4 %collective-permute-start.1 = (bf16[2,128,512]{1,2,0:T(8,128)(2,1)S(1)}, bf16[2,128,512]{1,2,0:T(8,128)(2,1)}, u32[]{:S(2)}, u32[]{:S(2)}) collective-permute-start(bf16[2,128,512]{1,2,0:T(8,128)(2,1)S(1)} %pad_maximum_fusion), channel_id=1, source_target_pairs={{0,12},{4,16},{8,20},{12,24},{16,28},{20,32},{24,36},{28,40},{32,4... | collective-permute-start | bytes 786440 | tf_op jit(solution)/shard_map/ppermute | solution.py:18
  25.1 21.2 %collective-permute-start.2 = (bf16[2,128,512]{1,2,0:T(8,128)(2,1)S(1)}, bf16[2,128,512]{1,2,0:T(8,128)(2,1)S(1)}, u32[]{:S(2)}, u32[]{:S(2)}) collective-permute-start(bf16[2,128,512]{1,2,0:T(8,128)(2,1)S(1)} %pad_maximum_fusion), channel_id=1, source_target_pairs={{0,8},{4,12},{8,16},{12,20},{16,24},{20,28},{24,32},{28,36},{32,40... | collective-permute-start | bytes 786440 | tf_op jit(solution)/shard_map/ppermute | solution.py:18
  27.3 21.0 %collective-permute-start.3 = (bf16[2,128,512]{1,2,0:T(8,128)(2,1)S(1)}, bf16[2,128,512]{1,2,0:T(8,128)(2,1)S(1)}, u32[]{:S(2)}, u32[]{:S(2)}) collective-permute-start(bf16[2,128,512]{1,2,0:T(8,128)(2,1)S(1)} %pad_maximum_fusion), channel_id=1, source_target_pairs={{0,4},{4,8},{8,12},{12,16},{16,20},{20,24},{24,28},{28,32},{32,36}... | collective-permute-start | bytes 786440 | tf_op jit(solution)/shard_map/ppermute | solution.py:18
  30.7 19.1 %collective-permute-start.4 = (bf16[2,128,512]{1,2,0:T(8,128)(2,1)S(1)}, bf16[2,128,512]{1,2,0:T(8,128)(2,1)S(1)}, u32[]{:S(2)}, u32[]{:S(2)}) collective-permute-start(bf16[2,128,512]{1,2,0:T(8,128)(2,1)S(1)} %pad_maximum_fusion), channel_id=1, source_target_pairs={{4,0},{8,4},{12,8},{16,12},{20,16},{24,20},{28,24},{32,28},{36,32}... | collective-permute-start | bytes 786440 | tf_op jit(solution)/shard_map/ppermute | solution.py:18
  32.7 17.9 %collective-permute-start.5 = (bf16[2,128,512]{1,2,0:T(8,128)(2,1)S(1)}, bf16[2,128,512]{1,2,0:T(8,128)(2,1)S(1)}, u32[]{:S(2)}, u32[]{:S(2)}) collective-permute-start(bf16[2,128,512]{1,2,0:T(8,128)(2,1)S(1)} %pad_maximum_fusion), channel_id=1, source_target_pairs={{8,0},{12,4},{16,8},{20,12},{24,16},{28,20},{32,24},{36,28},{40,32... | collective-permute-start | bytes 786440 | tf_op jit(solution)/shard_map/ppermute | solution.py:18
  35.8 18.8 %collective-permute-start.6 = (bf16[2,128,512]{1,2,0:T(8,128)(2,1)S(1)}, bf16[2,128,512]{1,2,0:T(8,128)(2,1)S(1)}, u32[]{:S(2)}, u32[]{:S(2)}) collective-permute-start(bf16[2,128,512]{1,2,0:T(8,128)(2,1)S(1)} %pad_maximum_fusion), channel_id=1, source_target_pairs={{12,0},{16,4},{20,8},{24,12},{28,16},{32,20},{36,24},{40,28},{44,3... | collective-permute-start | bytes 786440 | tf_op jit(solution)/shard_map/ppermute | solution.py:18
  46.3 14.3 %collective-permute-start.7 = (bf16[2,128,512]{1,2,0:T(8,128)(2,1)S(1)}, bf16[2,128,512]{1,2,0:T(8,128)(2,1)S(1)}, u32[]{:S(2)}, u32[]{:S(2)}) collective-permute-start(bf16[2,128,512]{1,2,0:T(8,128)(2,1)S(1)} %pad_maximum_fusion), channel_id=1, source_target_pairs={{16,0},{20,4},{24,8},{28,12},{32,16},{36,20},{40,24},{44,28},{48,3... | collective-permute-start | bytes 786440 | tf_op jit(solution)/shard_map/ppermute | solution.py:18
  135.3 18.4 %collective-permute-start.10 = (bf16[2,128,512]{2,1,0:T(8,128)(2,1)S(1)}, bf16[2,128,512]{2,1,0:T(8,128)(2,1)S(1)}, u32[]{:S(2)}, u32[]{:S(2)}) collective-permute-start(bf16[2,128,512]{2,1,0:T(8,128)(2,1)S(1)} %get-tuple-element.17), channel_id=1, source_target_pairs={{8,0},{12,4},{16,8},{20,12},{24,16},{28,20},{32,24},{36,28},{40,32... | collective-permute-start | bytes 786440 | tf_op jit(solution)/shard_map/ppermute | solution.py:18
  136.6 32.6 %collective-permute-start.11 = (bf16[2,128,512]{2,1,0:T(8,128)(2,1)S(1)}, bf16[2,128,512]{2,1,0:T(8,128)(2,1)S(1)}, u32[]{:S(2)}, u32[]{:S(2)}) collective-permute-start(bf16[2,128,512]{2,1,0:T(8,128)(2,1)S(1)} %get-tuple-element.16), channel_id=1, source_target_pairs={{4,0},{8,4},{12,8},{16,12},{20,16},{24,20},{28,24},{32,28},{36,32}... | collective-permute-start | bytes 786440 | tf_op jit(solution)/shard_map/ppermute | solution.py:18
  137.9 32.6 %collective-permute-start.12 = (bf16[2,128,512]{2,1,0:T(8,128)(2,1)S(1)}, bf16[2,128,512]{2,1,0:T(8,128)(2,1)S(1)}, u32[]{:S(2)}, u32[]{:S(2)}) collective-permute-start(bf16[2,128,512]{2,1,0:T(8,128)(2,1)S(1)} %get-tuple-element.15), channel_id=1, source_target_pairs={{0,4},{4,8},{8,12},{12,16},{16,20},{20,24},{24,28},{28,32},{32,36}... | collective-permute-start | bytes 786440 | tf_op jit(solution)/shard_map/ppermute | solution.py:18
  144.0 27.9 %collective-permute-start.13 = (bf16[2,128,512]{2,1,0:T(8,128)(2,1)S(1)}, bf16[2,128,512]{2,1,0:T(8,128)(2,1)S(1)}, u32[]{:S(2)}, u32[]{:S(2)}) collective-permute-start(bf16[2,128,512]{2,1,0:T(8,128)(2,1)S(1)} %get-tuple-element.14), channel_id=1, source_target_pairs={{0,8},{4,12},{8,16},{12,20},{16,24},{20,28},{24,32},{28,36},{32,40... | collective-permute-start | bytes 786440 | tf_op jit(solution)/shard_map/ppermute | solution.py:18
  149.8 22.1 %collective-permute-start.14 = (bf16[2,128,512]{2,1,0:T(8,128)(2,1)S(1)}, bf16[2,128,512]{2,1,0:T(8,128)(2,1)S(1)}, u32[]{:S(2)}, u32[]{:S(2)}) collective-permute-start(bf16[2,128,512]{2,1,0:T(8,128)(2,1)S(1)} %get-tuple-element.13), channel_id=1, source_target_pairs={{0,12},{4,16},{8,20},{12,24},{16,28},{20,32},{24,36},{28,40},{32,4... | collective-permute-start | bytes 786440 | tf_op jit(solution)/shard_map/ppermute | solution.py:18
  153.7 19.4 %collective-permute-start.15 = (bf16[2,128,512]{2,1,0:T(8,128)(2,1)S(1)}, bf16[2,128,512]{2,1,0:T(8,128)(2,1)S(1)}, u32[]{:S(2)}, u32[]{:S(2)}) collective-permute-start(bf16[2,128,512]{2,1,0:T(8,128)(2,1)S(1)} %get-tuple-element.12), channel_id=1, source_target_pairs={{0,16},{4,20},{8,24},{12,28},{16,32},{20,36},{24,40},{28,44},{32,4... | collective-permute-start | bytes 786440 | tf_op jit(solution)/shard_map/ppermute | solution.py:18
  169.2 11.9 %collective-permute-start.8 = (bf16[2,128,512]{2,1,0:T(8,128)(2,1)S(1)}, bf16[2,128,512]{2,1,0:T(8,128)(2,1)S(1)}, u32[]{:S(2)}, u32[]{:S(2)}) collective-permute-start(bf16[2,128,512]{2,1,0:T(8,128)(2,1)S(1)} %get-tuple-element.11), channel_id=1, source_target_pairs={{16,0},{20,4},{24,8},{28,12},{32,16},{36,20},{40,24},{44,28},{48,3... | collective-permute-start | bytes 786440 | tf_op jit(solution)/shard_map/ppermute | solution.py:18
  170.6 10.7 %collective-permute-start.9 = (bf16[2,128,512]{2,1,0:T(8,128)(2,1)S(1)}, bf16[2,128,512]{2,1,0:T(8,128)(2,1)S(1)}, u32[]{:S(2)}, u32[]{:S(2)}) collective-permute-start(bf16[2,128,512]{2,1,0:T(8,128)(2,1)S(1)} %get-tuple-element.18), channel_id=1, source_target_pairs={{12,0},{16,4},{20,8},{24,12},{28,16},{32,20},{36,24},{40,28},{44,3... | collective-permute-start | bytes 786440 | tf_op jit(solution)/shard_map/ppermute | solution.py:18
  183.4 59.5 %reduce-scatter.3.cloned.1.call-start = ((), (), s32[]{:S(2)}) async-start(), calls=%async_computation.2 | async-start | bytes 1310720 | tf_op jit(solution)/shard_map/reduce_scatter | solution.py:179
  183.4 1.6 copy-start.2
  186.9 77.8 %reduce-scatter.5.cloned.1.call-start = ((), (), s32[]{:S(2)}) async-start(), calls=%async_computation.4 | async-start | bytes 1310720 | tf_op jit(solution)/shard_map/reduce_scatter | solution.py:195
Sparse Core Ops, SparseCore 0:
  11.3 100.5 all-gather.5
  183.5 56.0 all-gather.3
Sparse Core Ops, SparseCore 1:
  186.9 23.6 reduce-scatter.2
  242.9 21.6 reduce-scatter.4

commit v6 on v5

--- a/solution.py
+++ b/solution.py
@@ -142,14 +142,12 @@
     )(slot_ids, counts, queries, out_grad, stock, flipped)
 
 
-def on_device(
-    queries, encoder, key_weight, value_weight, out_grad, block_lists, list_counts, outer, inner
-):
-    blk = ("bz", "byx")
+def on_device(queries, encoder, key_weight, value_weight, out_grad, block_lists, list_counts, size):
+    blk = ("bz", "by", "bx")
     position = lax.axis_index(blk)
     head_cols = key_weight.shape[1]
-    model = encoder.shape[1]
-    near = lax.all_gather(encoder, "byx", axis=0, tiled=False)
+    rows, model = encoder.shape
+    column = lax.all_gather(encoder, "bz", axis=0, tiled=True)
     own_keys = jnp.dot(encoder, key_weight, preferred_element_type=jnp.float32).astype(jnp.bfloat16)
     own_values = jnp.dot(encoder, value_weight, preferred_element_type=jnp.float32).astype(
         jnp.bfloat16
@@ -160,7 +158,7 @@
         if offset == 0:
             arrived.append(own)
         else:
-            arrived.append(passed_along(own, blk, -offset, outer * inner))
+            arrived.append(passed_along(own, blk, -offset, size))
     stock = jnp.stack(arrived, 0)
     slot_ids = (block_lists - (position - REACH)).astype(jnp.int32)
     attended, query_grad, running = attention(
@@ -170,7 +168,7 @@
     for offset in range(-REACH, REACH + 1):
         if offset != 0:
             sent = running[REACH + offset].astype(jnp.bfloat16)
-            owned = owned + passed_along(sent, blk, offset, outer * inner).astype(jnp.float32)
+            owned = owned + passed_along(sent, blk, offset, size).astype(jnp.float32)
     rounded = owned.astype(jnp.bfloat16)
     contract_cols = (((1,), (1,)), ((), ()))
     encoder_terms = lax.dot_general(
@@ -180,19 +178,14 @@
         jnp.bfloat16
     )
     both_grads = jnp.concatenate([rounded[0], rounded[1]], 1)
-    group_grads = lax.all_gather(both_grads, "byx", axis=0, tiled=True)
-    rows = encoder.shape[0]
-    slice_rows = model // (outer * inner)
-    picked = lax.dynamic_slice_in_dim(
-        near.reshape(inner * rows, outer, inner, slice_rows),
-        lax.axis_index("byx"),
-        1,
-        axis=2,
-    ).reshape(inner * rows, outer * slice_rows)
+    column_grads = lax.all_gather(both_grads, "bz", axis=0, tiled=True)
+    span = model // (column.shape[0] // rows)
+    picked = lax.dynamic_slice_in_dim(column, lax.axis_index("bz") * span, span, axis=1)
     partial = lax.dot_general(
-        picked, group_grads, (((0,), (0,)), ((), ())), preferred_element_type=jnp.float32
-    )
-    weight_rows = lax.psum_scatter(partial, "bz", scatter_dimension=0, tiled=True)
+        picked, column_grads, (((0,), (0,)), ((), ())), preferred_element_type=jnp.float32
+    )
+    partial = lax.psum_scatter(partial, "by", scatter_dimension=0, tiled=True)
+    weight_rows = lax.psum_scatter(partial, "bx", scatter_dimension=0, tiled=True)
     return (
         attended,
         query_grad,
@@ -204,12 +197,10 @@
 
 def solution(mesh):
     blk_size, grp_size = mesh.devices.shape
-    outer = 4 if blk_size % 4 == 0 else 1
-    inner = blk_size // outer
     split = jax.sharding.Mesh(
-        mesh.devices.reshape(outer, inner, grp_size), ("bz", "byx", "grp")
-    )
-    blk = ("bz", "byx")
+        mesh.devices.reshape(4, blk_size // 8, 2, grp_size), ("bz", "by", "bx", "grp")
+    )
+    blk = ("bz", "by", "bx")
     in_specs = (
         P(blk, "grp"),
         P(blk, None),
@@ -227,7 +218,7 @@
         P(blk, "grp"),
     )
     return jax.shard_map(
-        functools.partial(on_device, outer=outer, inner=inner),
+        functools.partial(on_device, size=blk_size),
         mesh=split,
         in_specs=in_specs,
         out_specs=out_specs,

time: 274 us -> 325 us (1.19)
  waiting for transfers between devices: 97.4 us -> 157 us
  Pallas kernels: 66.9 us -> 61.4 us
    reduce_scatter x1 -> x2, waiting for transfers between devices: 20.1 us -> 46.6 us  [the longest x1 26.2 us: on_device(): partial = lax.psum_scatter(partial, 'by', scatter_dimension=0, tiled=True)]
    reduce_scatter x1, waiting for transfers between devices: 0.03 us -> 22.2 us  [on_device(): lax.psum_scatter(encoder_terms, 'grp', scatter_dimension=1, tiled=True)]
    all_gather x2, waiting for transfers between devices: 51.6 us -> 66 us  [the longest x1 33.2 us: on_device(): column = lax.all_gather(encoder, 'bz', axis=0, tiled=True)]
    pallas_call x1, Pallas kernels: 66.9 us -> 61.4 us  [attention(): pl.pallas_call(attention_kernel, grid_spec=grid_spec, out_shape=[jax.Shap...]
    ppermute x16, waiting for transfers between devices: 25.6 us -> 21.3 us  [passed_along(): return lax.ppermute(value, axis, pairs)]
    unnamed x19 -> x18, local copies, waits for them, and re-layouts: 10.1 us -> 9.4 us
  transfers between devices with their start and end apart: 20 -> 21, of which waited for: 9 -> 10; matrix products, arithmetic and copies ran while one was open for 11% -> 4% of each run, Pallas kernels for 24% -> 0%
where the time goes in v6:
time: 325 us; the launch traced here: 324 us
  waiting for transfers between devices  157 us (48%)
  Pallas kernels  61.4 us (19%)
  starting transfers between devices  59 us (18%)
  local copies, waits for them, and re-layouts  16.2 us (5%)
  between operations  14.1 us (4%)
  matrix products  9.16 us (3%)
  other arithmetic  7.73 us (2%)
    pallas_call x1, Pallas kernels, attention(): pl.pallas_call(attention_kernel, grid_spec=grid_spec, out_shape=[jax.Shap...  61.4 us
    ppermute x16, starting transfers between devices, passed_along(): return lax.ppermute(value, axis, pairs)  58.8 us
    all_gather x1, waiting for transfers between devices, on_device(): column = lax.all_gather(encoder, 'bz', axis=0, tiled=True)  33.2 us
    all_gather x1, waiting for transfers between devices, on_device(): column_grads = lax.all_gather(both_grads, 'bz', axis=0, tiled=True)  32.8 us
    reduce_scatter x1, waiting for transfers between devices, on_device(): partial = lax.psum_scatter(partial, 'by', scatter_dimension=0, tiled=True)  26.2 us
    reduce_scatter x1, waiting for transfers between devices, on_device(): lax.psum_scatter(encoder_terms, 'grp', scatter_dimension=1, tiled=True)  22.2 us
    ppermute x16, waiting for transfers between devices, passed_along(): return lax.ppermute(value, axis, pairs)  21.3 us
    reduce_scatter x1, waiting for transfers between devices, on_device(): lax.psum_scatter(partial, 'bx', scatter_dimension=0, tiled=True)  20.4 us
  transfers between devices with their start and end apart: 21, of which 10 were waited for; matrix products, arithmetic and copies ran while one was open for 4% of the time, Pallas kernels for 0%

profile of v6, /device:TPU:0, one launch (start us, length us, event | category | flops | bytes accessed | tf_op | source)
XLA Modules:
  0.0 324.4 jit_solution(8088097157353118967)
XLA Ops:
  7.2 1.5 copy-done
  8.8 2.1 fusion
  10.9 1.0 fusion.1
  11.9 5.9 %collective-permute-start = (bf16[2,128,512]{1,2,0:T(8,128)(2,1)S(1)}, bf16[2,128,512]{1,2,0:T(8,128)(2,1)}, u32[]{:S(2)}, u32[]{:S(2)}) collective-permute-start(bf16[2,128,512]{1,2,0:T(8,128)(2,1)S(1)} %pad_maximum_fusion), channel_id=1, source_target_pairs={{0,16},{4,20},{8,24},{12,28},{16,32},{20,36},{24,40},{28,44},{32,4... | collective-permute-start | bytes 786440 | tf_op jit(solution)/shard_map/ppermute | solution.py:18
  17.8 5.7 %collective-permute-start.1 = (bf16[2,128,512]{1,2,0:T(8,128)(2,1)S(1)}, bf16[2,128,512]{1,2,0:T(8,128)(2,1)}, u32[]{:S(2)}, u32[]{:S(2)}) collective-permute-start(bf16[2,128,512]{1,2,0:T(8,128)(2,1)S(1)} %pad_maximum_fusion), channel_id=1, source_target_pairs={{0,12},{4,16},{8,20},{12,24},{16,28},{20,32},{24,36},{28,40},{32,4... | collective-permute-start | bytes 786440 | tf_op jit(solution)/shard_map/ppermute | solution.py:18
  23.5 2.2 collective-permute-start.2
  25.7 3.4 %collective-permute-start.3 = (bf16[2,128,512]{1,2,0:T(8,128)(2,1)S(1)}, bf16[2,128,512]{1,2,0:T(8,128)(2,1)S(1)}, u32[]{:S(2)}, u32[]{:S(2)}) collective-permute-start(bf16[2,128,512]{1,2,0:T(8,128)(2,1)S(1)} %pad_maximum_fusion), channel_id=1, source_target_pairs={{0,4},{4,8},{8,12},{12,16},{16,20},{20,24},{24,28},{28,32},{32,36}... | collective-permute-start | bytes 786440 | tf_op jit(solution)/shard_map/ppermute | solution.py:18
  29.1 1.3 collective-permute-start.4
  31.1 1.3 collective-permute-start.5
  32.4 1.7 bitcast_dynamic-update-slice_fusion.8
  34.1 1.3 collective-permute-start.6
  35.4 1.7 bitcast_dynamic-update-slice_fusion.7
  37.1 2.5 collective-permute-done.2
  39.6 1.3 collective-permute-start.7
  40.9 0.7 bitcast_dynamic-update-slice_fusion.6
  41.6 0.7 bitcast_dynamic-update-slice_fusion.5
  42.4 0.7 bitcast_dynamic-update-slice_fusion.4
  43.1 0.7 bitcast_dynamic-update-slice_fusion.3
  43.8 0.7 bitcast_dynamic-update-slice_fusion.2
  44.5 5.6 %collective-permute-done.6 = bf16[2,128,512]{1,2,0:T(8,128)(2,1)S(1)} collective-permute-done((bf16[2,128,512]{1,2,0:T(8,128)(2,1)S(1)}, bf16[2,128,512]{1,2,0:T(8,128)(2,1)S(1)}, u32[]{:S(2)}, u32[]{:S(2)}) %collective-permute-start.6) | collective-permute-done | bytes 262176 | tf_op jit(solution)/shard_map/ppermute | solution.py:18
  50.2 0.7 bitcast_dynamic-update-slice_fusion.1
  50.9 1.5 collective-permute-done.7
  53.1 4.3 %copy.20.stock_ref = bf16[9,2,128,512]{3,2,1,0:T(8,128)(2,1)} copy(bf16[9,2,128,512]{2,3,1,0:T(8,128)(2,1)} %bitcast_dynamic-update-slice_fusion) | data formatting | bytes 4718592 | tf_op jit(solution)/shard_map/stack | solution.py:162
  57.4 61.4 %shard_map.110 = (bf16[2048,512]{1,0:T(8,128)(2,1)}, bf16[2048,512]{1,0:T(8,128)(2,1)}, f32[9,2,128,512]{3,2,1,0:T(8,128)}) custom-call(s32[16,5]{1,0:T(8,128)} %broadcast_subtract_fusion.slots_ref, s32[16]{0:T(128)} %counts_ref.1, bf16[2048,512]{1,0:T(8,128)(2,1)} %q_ref.1, bf16[2048,512]{1,0:T(8,128)(2,1)} %g_ref.1, ...), custom_call_target="tpu_custom_call" | custom-call | flops 9663676416 | bytes 17825792 | tf_op jit(solution)/shard_map/pallas_call | solution.py:129
  118.8 2.7 convert.10
  121.6 1.3 collective-permute-start.10
  122.9 1.3 collective-permute-start.11
  124.2 6.1 %collective-permute-start.12 = (bf16[2,128,512]{2,1,0:T(8,128)(2,1)S(1)}, bf16[2,128,512]{2,1,0:T(8,128)(2,1)S(1)}, u32[]{:S(2)}, u32[]{:S(2)}) collective-permute-start(bf16[2,128,512]{2,1,0:T(8,128)(2,1)S(1)} %get-tuple-element.15), channel_id=1, source_target_pairs={{0,4},{4,8},{8,12},{12,16},{16,20},{20,24},{24,28},{28,32},{32,36}... | collective-permute-start | bytes 786440 | tf_op jit(solution)/shard_map/ppermute | solution.py:18
  130.3 7.7 %collective-permute-start.13 = (bf16[2,128,512]{2,1,0:T(8,128)(2,1)S(1)}, bf16[2,128,512]{2,1,0:T(8,128)(2,1)S(1)}, u32[]{:S(2)}, u32[]{:S(2)}) collective-permute-start(bf16[2,128,512]{2,1,0:T(8,128)(2,1)S(1)} %get-tuple-element.14), channel_id=1, source_target_pairs={{0,8},{4,12},{8,16},{12,20},{16,24},{20,28},{24,32},{28,36},{32,40... | collective-permute-start | bytes 786440 | tf_op jit(solution)/shard_map/ppermute | solution.py:18
  138.0 8.2 %collective-permute-start.14 = (bf16[2,128,512]{2,1,0:T(8,128)(2,1)S(1)}, bf16[2,128,512]{2,1,0:T(8,128)(2,1)S(1)}, u32[]{:S(2)}, u32[]{:S(2)}) collective-permute-start(bf16[2,128,512]{2,1,0:T(8,128)(2,1)S(1)} %get-tuple-element.13), channel_id=1, source_target_pairs={{0,12},{4,16},{8,20},{12,24},{16,28},{20,32},{24,36},{28,40},{32,4... | collective-permute-start | bytes 786440 | tf_op jit(solution)/shard_map/ppermute | solution.py:18
  146.2 9.4 %collective-permute-start.15 = (bf16[2,128,512]{2,1,0:T(8,128)(2,1)S(1)}, bf16[2,128,512]{2,1,0:T(8,128)(2,1)S(1)}, u32[]{:S(2)}, u32[]{:S(2)}) collective-permute-start(bf16[2,128,512]{2,1,0:T(8,128)(2,1)S(1)} %get-tuple-element.12), channel_id=1, source_target_pairs={{0,16},{4,20},{8,24},{12,28},{16,32},{20,36},{24,40},{28,44},{32,4... | collective-permute-start | bytes 786440 | tf_op jit(solution)/shard_map/ppermute | solution.py:18
  155.6 1.3 collective-permute-start.8
  157.0 1.3 collective-permute-start.9
  158.3 1.3 collective-permute-done.15
  159.5 10.3 %collective-permute-done.8 = bf16[2,128,512]{2,1,0:T(8,128)(2,1)S(1)} collective-permute-done((bf16[2,128,512]{2,1,0:T(8,128)(2,1)S(1)}, bf16[2,128,512]{2,1,0:T(8,128)(2,1)S(1)}, u32[]{:S(2)}, u32[]{:S(2)}) %collective-permute-start.8) | collective-permute-done | bytes 262176 | tf_op jit(solution)/shard_map/ppermute | solution.py:18
  169.8 1.4 fusion.9
  171.2 0.7 pad_maximum_fusion.1
  172.8 32.8 %all-gather.5.cloned.1.call-done = bf16[512,1024]{1,0:T(8,128)(2,1)} async-done(((bf16[128,1024]{1,0:T(8,128)(2,1)}), bf16[512,1024]{1,0:T(8,128)(2,1)}) %all-gather.5.cloned.1.call-update) | async-done | bytes 1048592 | tf_op jit(solution)/shard_map/all_gather | solution.py:181
  205.6 33.2 %all-gather.3.cloned.1.call-done = bf16[512,2048]{1,0:T(8,128)(2,1)} async-done(((bf16[128,2048]{1,0:T(8,128)(2,1)}), bf16[512,2048]{1,0:T(8,128)(2,1)}) %all-gather.3.cloned.1.call-update) | async-done | bytes 2097168 | tf_op jit(solution)/shard_map/all_gather | solution.py:150
  238.7 3.5 %fusion.10 = f32[512,1024]{1,0:T(8,128)} fusion(bf16[512,1024]{1,0:T(8,128)(2,1)} %all-gather.5.cloned.1.call-done, bf16[512,2048]{1,0:T(8,128)(2,1)} %all-gather.3.cloned.1.call-done, s32[]{:T(128)S(6)} %select_n.3), kind=kOutput, calls=%fused_computation.14 | convolution fusion | flops 536870912 | bytes 3670020 | tf_op jit(solution)/shard_map/dot_general | solution.py:184
  242.3 0.8 fusion.13
  243.1 0.8 copy-done.2
  243.9 1.8 convolution_add_fusion
  245.8 26.2 %reduce-scatter.6.cloned.1.call-done = f32[128,1024]{1,0:T(8,128)} async-done(((f32[512,1024]{1,0:T(8,128)}), f32[128,1024]{1,0:T(8,128)}) %reduce-scatter.6.cloned.1.call-update) | async-done | bytes 524304 | tf_op jit(solution)/shard_map/reduce_scatter | solution.py:187
  272.0 22.2 %reduce-scatter.4.cloned.1.call-done = f32[128,512]{1,0:T(8,128)} async-done(((f32[128,2048]{1,0:T(8,128)}), f32[128,512]{1,0:T(8,128)}) %reduce-scatter.4.cloned.1.call-update) | async-done | bytes 262160 | tf_op jit(solution)/shard_map/reduce_scatter | solution.py:177
  294.1 1.6 convert_element_type.87
  295.8 20.4 %reduce-scatter.8.cloned.1.call-done = f32[64,1024]{1,0:T(8,128)} async-done(((f32[128,1024]{1,0:T(8,128)}), f32[64,1024]{1,0:T(8,128)}) %reduce-scatter.8.cloned.1.call-update) | async-done | bytes 262160 | tf_op jit(solution)/shard_map/reduce_scatter | solution.py:188
  316.2 1.7 fusion.14
  (35 shorter events, 2.6 us)
Async XLA Ops:
  7.2 1.6 copy-start
  7.2 3.7 %copy-start.3 = (bf16[128,2048]{1,0:T(8,128)(2,1)S(1)}, bf16[128,2048]{1,0:T(8,128)(2,1)}, u32[]{:S(2)}) copy-start(bf16[128,2048]{1,0:T(8,128)(2,1)} %param.8) | copy-start | bytes 1572868
  7.2 23.2 %copy-start.4 = (s32[16,5]{0,1:T(8,128)S(1)}, s32[16,5]{0,1:T(8,128)}, u32[]{:S(2)}) copy-start(s32[16,5]{0,1:T(8,128)} %param.12) | copy-start | bytes 964
  7.2 198.4 %all-gather.5.cloned.1.call-start = ((), (), s32[]{:S(2)}) async-start(), calls=%async_computation.5 | async-start | bytes 1310720 | tf_op jit(solution)/shard_map/all_gather | solution.py:181
  8.8 2.1 copy-start.1
  11.9 19.2 %collective-permute-start = (bf16[2,128,512]{1,2,0:T(8,128)(2,1)S(1)}, bf16[2,128,512]{1,2,0:T(8,128)(2,1)}, u32[]{:S(2)}, u32[]{:S(2)}) collective-permute-start(bf16[2,128,512]{1,2,0:T(8,128)(2,1)S(1)} %pad_maximum_fusion), channel_id=1, source_target_pairs={{0,16},{4,20},{8,24},{12,28},{16,32},{20,36},{24,40},{28,44},{32,4... | collective-permute-start | bytes 786440 | tf_op jit(solution)/shard_map/ppermute | solution.py:18
  17.8 16.3 %collective-permute-start.1 = (bf16[2,128,512]{1,2,0:T(8,128)(2,1)S(1)}, bf16[2,128,512]{1,2,0:T(8,128)(2,1)}, u32[]{:S(2)}, u32[]{:S(2)}) collective-permute-start(bf16[2,128,512]{1,2,0:T(8,128)(2,1)S(1)} %pad_maximum_fusion), channel_id=1, source_target_pairs={{0,12},{4,16},{8,20},{12,24},{16,28},{20,32},{24,36},{28,40},{32,4... | collective-permute-start | bytes 786440 | tf_op jit(solution)/shard_map/ppermute | solution.py:18
  23.5 16.1 %collective-permute-start.2 = (bf16[2,128,512]{1,2,0:T(8,128)(2,1)S(1)}, bf16[2,128,512]{1,2,0:T(8,128)(2,1)S(1)}, u32[]{:S(2)}, u32[]{:S(2)}) collective-permute-start(bf16[2,128,512]{1,2,0:T(8,128)(2,1)S(1)} %pad_maximum_fusion), channel_id=1, source_target_pairs={{0,8},{4,12},{8,16},{12,20},{16,24},{20,28},{24,32},{28,36},{32,40... | collective-permute-start | bytes 786440 | tf_op jit(solution)/shard_map/ppermute | solution.py:18
  25.7 15.9 %collective-permute-start.3 = (bf16[2,128,512]{1,2,0:T(8,128)(2,1)S(1)}, bf16[2,128,512]{1,2,0:T(8,128)(2,1)S(1)}, u32[]{:S(2)}, u32[]{:S(2)}) collective-permute-start(bf16[2,128,512]{1,2,0:T(8,128)(2,1)S(1)} %pad_maximum_fusion), channel_id=1, source_target_pairs={{0,4},{4,8},{8,12},{12,16},{16,20},{20,24},{24,28},{28,32},{32,36}... | collective-permute-start | bytes 786440 | tf_op jit(solution)/shard_map/ppermute | solution.py:18
  29.1 14.0 %collective-permute-start.4 = (bf16[2,128,512]{1,2,0:T(8,128)(2,1)S(1)}, bf16[2,128,512]{1,2,0:T(8,128)(2,1)S(1)}, u32[]{:S(2)}, u32[]{:S(2)}) collective-permute-start(bf16[2,128,512]{1,2,0:T(8,128)(2,1)S(1)} %pad_maximum_fusion), channel_id=1, source_target_pairs={{4,0},{8,4},{12,8},{16,12},{20,16},{24,20},{28,24},{32,28},{36,32}... | collective-permute-start | bytes 786440 | tf_op jit(solution)/shard_map/ppermute | solution.py:18
  31.1 12.7 %collective-permute-start.5 = (bf16[2,128,512]{1,2,0:T(8,128)(2,1)S(1)}, bf16[2,128,512]{1,2,0:T(8,128)(2,1)S(1)}, u32[]{:S(2)}, u32[]{:S(2)}) collective-permute-start(bf16[2,128,512]{1,2,0:T(8,128)(2,1)S(1)} %pad_maximum_fusion), channel_id=1, source_target_pairs={{8,0},{12,4},{16,8},{20,12},{24,16},{28,20},{32,24},{36,28},{40,32... | collective-permute-start | bytes 786440 | tf_op jit(solution)/shard_map/ppermute | solution.py:18
  34.1 16.1 %collective-permute-start.6 = (bf16[2,128,512]{1,2,0:T(8,128)(2,1)S(1)}, bf16[2,128,512]{1,2,0:T(8,128)(2,1)S(1)}, u32[]{:S(2)}, u32[]{:S(2)}) collective-permute-start(bf16[2,128,512]{1,2,0:T(8,128)(2,1)S(1)} %pad_maximum_fusion), channel_id=1, source_target_pairs={{12,0},{16,4},{20,8},{24,12},{28,16},{32,20},{36,24},{40,28},{44,3... | collective-permute-start | bytes 786440 | tf_op jit(solution)/shard_map/ppermute | solution.py:18
  39.6 12.8 %collective-permute-start.7 = (bf16[2,128,512]{1,2,0:T(8,128)(2,1)S(1)}, bf16[2,128,512]{1,2,0:T(8,128)(2,1)S(1)}, u32[]{:S(2)}, u32[]{:S(2)}) collective-permute-start(bf16[2,128,512]{1,2,0:T(8,128)(2,1)S(1)} %pad_maximum_fusion), channel_id=1, source_target_pairs={{16,0},{20,4},{24,8},{28,12},{32,16},{36,20},{40,24},{44,28},{48,3... | collective-permute-start | bytes 786440 | tf_op jit(solution)/shard_map/ppermute | solution.py:18
  121.6 24.6 %collective-permute-start.10 = (bf16[2,128,512]{2,1,0:T(8,128)(2,1)S(1)}, bf16[2,128,512]{2,1,0:T(8,128)(2,1)S(1)}, u32[]{:S(2)}, u32[]{:S(2)}) collective-permute-start(bf16[2,128,512]{2,1,0:T(8,128)(2,1)S(1)} %get-tuple-element.17), channel_id=1, source_target_pairs={{8,0},{12,4},{16,8},{20,12},{24,16},{28,20},{32,24},{36,28},{40,32... | collective-permute-start | bytes 786440 | tf_op jit(solution)/shard_map/ppermute | solution.py:18
  122.9 32.7 %collective-permute-start.11 = (bf16[2,128,512]{2,1,0:T(8,128)(2,1)S(1)}, bf16[2,128,512]{2,1,0:T(8,128)(2,1)S(1)}, u32[]{:S(2)}, u32[]{:S(2)}) collective-permute-start(bf16[2,128,512]{2,1,0:T(8,128)(2,1)S(1)} %get-tuple-element.16), channel_id=1, source_target_pairs={{4,0},{8,4},{12,8},{16,12},{20,16},{24,20},{28,24},{32,28},{36,32}... | collective-permute-start | bytes 786440 | tf_op jit(solution)/shard_map/ppermute | solution.py:18
  124.2 32.7 %collective-permute-start.12 = (bf16[2,128,512]{2,1,0:T(8,128)(2,1)S(1)}, bf16[2,128,512]{2,1,0:T(8,128)(2,1)S(1)}, u32[]{:S(2)}, u32[]{:S(2)}) collective-permute-start(bf16[2,128,512]{2,1,0:T(8,128)(2,1)S(1)} %get-tuple-element.15), channel_id=1, source_target_pairs={{0,4},{4,8},{8,12},{12,16},{16,20},{20,24},{24,28},{28,32},{32,36}... | collective-permute-start | bytes 786440 | tf_op jit(solution)/shard_map/ppermute | solution.py:18
  130.3 28.0 %collective-permute-start.13 = (bf16[2,128,512]{2,1,0:T(8,128)(2,1)S(1)}, bf16[2,128,512]{2,1,0:T(8,128)(2,1)S(1)}, u32[]{:S(2)}, u32[]{:S(2)}) collective-permute-start(bf16[2,128,512]{2,1,0:T(8,128)(2,1)S(1)} %get-tuple-element.14), channel_id=1, source_target_pairs={{0,8},{4,12},{8,16},{12,20},{16,24},{20,28},{24,32},{28,36},{32,40... | collective-permute-start | bytes 786440 | tf_op jit(solution)/shard_map/ppermute | solution.py:18
  138.0 20.3 %collective-permute-start.14 = (bf16[2,128,512]{2,1,0:T(8,128)(2,1)S(1)}, bf16[2,128,512]{2,1,0:T(8,128)(2,1)S(1)}, u32[]{:S(2)}, u32[]{:S(2)}) collective-permute-start(bf16[2,128,512]{2,1,0:T(8,128)(2,1)S(1)} %get-tuple-element.13), channel_id=1, source_target_pairs={{0,12},{4,16},{8,20},{12,24},{16,28},{20,32},{24,36},{28,40},{32,4... | collective-permute-start | bytes 786440 | tf_op jit(solution)/shard_map/ppermute | solution.py:18
  146.2 13.3 %collective-permute-start.15 = (bf16[2,128,512]{2,1,0:T(8,128)(2,1)S(1)}, bf16[2,128,512]{2,1,0:T(8,128)(2,1)S(1)}, u32[]{:S(2)}, u32[]{:S(2)}) collective-permute-start(bf16[2,128,512]{2,1,0:T(8,128)(2,1)S(1)} %get-tuple-element.12), channel_id=1, source_target_pairs={{0,16},{4,20},{8,24},{12,28},{16,32},{20,36},{24,40},{28,44},{32,4... | collective-permute-start | bytes 786440 | tf_op jit(solution)/shard_map/ppermute | solution.py:18
  155.6 14.2 %collective-permute-start.8 = (bf16[2,128,512]{2,1,0:T(8,128)(2,1)S(1)}, bf16[2,128,512]{2,1,0:T(8,128)(2,1)S(1)}, u32[]{:S(2)}, u32[]{:S(2)}) collective-permute-start(bf16[2,128,512]{2,1,0:T(8,128)(2,1)S(1)} %get-tuple-element.11), channel_id=1, source_target_pairs={{16,0},{20,4},{24,8},{28,12},{32,16},{36,20},{40,24},{44,28},{48,3... | collective-permute-start | bytes 786440 | tf_op jit(solution)/shard_map/ppermute | solution.py:18
  157.0 12.9 %collective-permute-start.9 = (bf16[2,128,512]{2,1,0:T(8,128)(2,1)S(1)}, bf16[2,128,512]{2,1,0:T(8,128)(2,1)S(1)}, u32[]{:S(2)}, u32[]{:S(2)}) collective-permute-start(bf16[2,128,512]{2,1,0:T(8,128)(2,1)S(1)} %get-tuple-element.18), channel_id=1, source_target_pairs={{12,0},{16,4},{20,8},{24,12},{28,16},{32,20},{36,24},{40,28},{44,3... | collective-permute-start | bytes 786440 | tf_op jit(solution)/shard_map/ppermute | solution.py:18
  172.0 66.8 %all-gather.3.cloned.1.call-start = ((), (), s32[]{:S(2)}) async-start(), calls=%async_computation.4 | async-start | bytes 2621440 | tf_op jit(solution)/shard_map/all_gather | solution.py:150
  172.7 99.2 %reduce-scatter.6.cloned.1.call-start = ((), (), s32[]{:S(2)}) async-start(), calls=%async_computation.6 | async-start | bytes 2621440 | tf_op jit(solution)/shard_map/reduce_scatter | solution.py:187
  242.2 51.9 %reduce-scatter.4.cloned.1.call-start = ((), (), s32[]{:S(2)}) async-start(), calls=%async_computation.3 | async-start | bytes 1310720 | tf_op jit(solution)/shard_map/reduce_scatter | solution.py:177
  242.3 1.6 copy-start.2
  245.7 70.5 %reduce-scatter.8.cloned.1.call-start = ((), (), s32[]{:S(2)}) async-start(), calls=%async_computation.7 | async-start | bytes 786432 | tf_op jit(solution)/shard_map/reduce_scatter | solution.py:188
Sparse Core Ops, SparseCore 0:
  172.1 33.4 all-gather.4
  207.3 31.4 all-gather.2
  242.4 29.5 reduce-scatter.5
  274.3 19.7 reduce-scatter.3
  296.3 19.8 reduce-scatter.7

commit v7 on v5

--- a/solution.py
+++ b/solution.py
@@ -58,41 +58,40 @@
             vs = [stock_ref[slots[j], 1, :, pl.ds(off, LANES)] for j in range(used)]
             kts = [flipped_ref[slots[j], 0, pl.ds(off, LANES), :] for j in range(used)]
             vts = [flipped_ref[slots[j], 1, pl.ds(off, LANES), :] for j in range(used)]
-            outs, dqs = [], []
-            dks = [None] * used
-            dvs = [None] * used
-            for h in range(2):
-                scores = [dot(ks[j], qst[h]) for j in range(used)]
-                peak = jnp.max(scores[0], axis=0, keepdims=True)
-                for j in range(1, used):
-                    peak = jnp.maximum(peak, jnp.max(scores[j], axis=0, keepdims=True))
-                expos = [jnp.exp(sc - peak) for sc in scores]
-                total = jnp.sum(expos[0], axis=0, keepdims=True)
-                for j in range(1, used):
-                    total = total + jnp.sum(expos[j], axis=0, keepdims=True)
-                inverse = 1.0 / total
-                ws = [(e * inverse).astype(bf16) for e in expos]
-                out = dot(vts[0], ws[0])
-                for j in range(1, used):
-                    out = out + dot(vts[j], ws[j])
-                dws = [dot(vs[j], gst[h]) for j in range(used)]
-                wf = [w.astype(f32) for w in ws]
-                center = jnp.sum(wf[0] * dws[0], axis=0, keepdims=True)
-                for j in range(1, used):
-                    center = center + jnp.sum(wf[j] * dws[j], axis=0, keepdims=True)
-                dss = [(wf[j] * (dws[j] - center)).astype(bf16) for j in range(used)]
-                dq = dot(kts[0], dss[0])
-                for j in range(1, used):
-                    dq = dq + dot(kts[j], dss[j])
-                for j in range(used):
-                    dk = dot(dss[j], qh[h])
-                    dv = dot(ws[j], gh[h])
-                    dks[j] = dk if dks[j] is None else dks[j] + dk
-                    dvs[j] = dv if dvs[j] is None else dvs[j] + dv
-                outs.append(out)
-                dqs.append(dq)
-            out_ref[:, pl.ds(off, LANES)] = jnp.where(top, outs[0], outs[1]).T.astype(out_ref.dtype)
-            dq_ref[:, pl.ds(off, LANES)] = jnp.where(top, dqs[0], dqs[1]).T.astype(dq_ref.dtype)
+            qs2 = jnp.concatenate(qst, axis=1)
+            gs2 = jnp.concatenate(gst, axis=1)
+            q2 = jnp.concatenate(qh, axis=0)
+            g2 = jnp.concatenate(gh, axis=0)
+            scores = [dot(ks[j], qs2) for j in range(used)]
+            peak = jnp.max(scores[0], axis=0, keepdims=True)
+            for j in range(1, used):
+                peak = jnp.maximum(peak, jnp.max(scores[j], axis=0, keepdims=True))
+            expos = [jnp.exp(sc - peak) for sc in scores]
+            total = jnp.sum(expos[0], axis=0, keepdims=True)
+            for j in range(1, used):
+                total = total + jnp.sum(expos[j], axis=0, keepdims=True)
+            inverse = 1.0 / total
+            ws = [(e * inverse).astype(bf16) for e in expos]
+            out = dot(vts[0], ws[0])
+            for j in range(1, used):
+                out = out + dot(vts[j], ws[j])
+            dws = [dot(vs[j], gs2) for j in range(used)]
+            wf = [w.astype(f32) for w in ws]
+            center = jnp.sum(wf[0] * dws[0], axis=0, keepdims=True)
+            for j in range(1, used):
+                center = center + jnp.sum(wf[j] * dws[j], axis=0, keepdims=True)
+            dss = [(wf[j] * (dws[j] - center)).astype(bf16) for j in range(used)]
+            dq = dot(kts[0], dss[0])
+            for j in range(1, used):
+                dq = dq + dot(kts[j], dss[j])
+            dks = [dot(dss[j], q2) for j in range(used)]
+            dvs = [dot(ws[j], g2) for j in range(used)]
+            out_ref[:, pl.ds(off, LANES)] = jnp.where(
+                top, out[:, :rows], out[:, rows:]
+            ).T.astype(out_ref.dtype)
+            dq_ref[:, pl.ds(off, LANES)] = jnp.where(
+                top, dq[:, :rows], dq[:, rows:]
+            ).T.astype(dq_ref.dtype)
             for j in range(used):
                 acc_ref[slots[j], 0, :, pl.ds(off, LANES)] += dks[j]
                 acc_ref[slots[j], 1, :, pl.ds(off, LANES)] += dvs[j]

time: 274 us -> 275 us (level)
  starting transfers between devices: 58.9 us -> 52.7 us
  waiting for transfers between devices: 97.4 us -> 101 us
    ppermute x16, starting transfers between devices: 58.8 us -> 52.6 us  [passed_along(): return lax.ppermute(value, axis, pairs)]
  transfers between devices with their start and end apart: 20 -> 20, of which waited for: 9 -> 8; matrix products, arithmetic and copies ran while one was open for 11% -> 11% of each run, Pallas kernels for 24% -> 25%
where the time goes in v7:
time: 275 us; the launch traced here: 272 us
  waiting for transfers between devices  101 us (37%)
  Pallas kernels  68.2 us (25%)
  starting transfers between devices  52.7 us (19%)
  local copies, waits for them, and re-layouts  18 us (7%)
  between operations  15.8 us (6%)
  matrix products  8.95 us (3%)
  other arithmetic  7.76 us (3%)
    pallas_call x1, Pallas kernels, attention(): pl.pallas_call(attention_kernel, grid_spec=grid_spec, out_shape=[jax.Shap...  68.2 us
    all_gather x1, waiting for transfers between devices, on_device(): group_grads = lax.all_gather(both_grads, 'byx', axis=0, tiled=True)  52.8 us
    ppermute x16, starting transfers between devices, passed_along(): return lax.ppermute(value, axis, pairs)  52.6 us
    ppermute x16, waiting for transfers between devices, passed_along(): return lax.ppermute(value, axis, pairs)  27.9 us
    reduce_scatter x1, waiting for transfers between devices, on_device(): lax.psum_scatter(partial, 'bz', scatter_dimension=0, tiled=True)  20.1 us
    unnamed x19, local copies, waits for them, and re-layouts  10.1 us
  transfers between devices with their start and end apart: 20, of which 8 were waited for; matrix products, arithmetic and copies ran while one was open for 11% of the time, Pallas kernels for 25%

profile of v7, /device:TPU:0, one launch (start us, length us, event | category | flops | bytes accessed | tf_op | source)
XLA Modules:
  0.0 272.3 jit_solution(3312597788235616764)
XLA Ops:
  8.1 2.2 copy.26
  10.4 2.1 fusion
  12.5 1.0 fusion.1
  13.5 5.9 %collective-permute-start = (bf16[2,128,512]{1,2,0:T(8,128)(2,1)S(1)}, bf16[2,128,512]{1,2,0:T(8,128)(2,1)}, u32[]{:S(2)}, u32[]{:S(2)}) collective-permute-start(bf16[2,128,512]{1,2,0:T(8,128)(2,1)S(1)} %pad_maximum_fusion), channel_id=1, source_target_pairs={{0,16},{4,20},{8,24},{12,28},{16,32},{20,36},{24,40},{28,44},{32,4... | collective-permute-start | bytes 786440 | tf_op jit(solution)/shard_map/ppermute | solution.py:18
  19.4 5.7 %collective-permute-start.1 = (bf16[2,128,512]{1,2,0:T(8,128)(2,1)S(1)}, bf16[2,128,512]{1,2,0:T(8,128)(2,1)}, u32[]{:S(2)}, u32[]{:S(2)}) collective-permute-start(bf16[2,128,512]{1,2,0:T(8,128)(2,1)S(1)} %pad_maximum_fusion), channel_id=1, source_target_pairs={{0,12},{4,16},{8,20},{12,24},{16,28},{20,32},{24,36},{28,40},{32,4... | collective-permute-start | bytes 786440 | tf_op jit(solution)/shard_map/ppermute | solution.py:18
  25.1 2.2 collective-permute-start.2
  27.3 3.4 %collective-permute-start.3 = (bf16[2,128,512]{1,2,0:T(8,128)(2,1)S(1)}, bf16[2,128,512]{1,2,0:T(8,128)(2,1)S(1)}, u32[]{:S(2)}, u32[]{:S(2)}) collective-permute-start(bf16[2,128,512]{1,2,0:T(8,128)(2,1)S(1)} %pad_maximum_fusion), channel_id=1, source_target_pairs={{0,4},{4,8},{8,12},{12,16},{16,20},{20,24},{24,28},{28,32},{32,36}... | collective-permute-start | bytes 786440 | tf_op jit(solution)/shard_map/ppermute | solution.py:18
  30.7 1.3 collective-permute-start.4
  32.1 0.6 broadcast_subtract_fusion.slots_ref
  32.7 1.3 collective-permute-start.5
  34.0 1.7 bitcast_dynamic-update-slice_fusion.8
  35.8 1.3 collective-permute-start.6
  37.1 1.7 bitcast_dynamic-update-slice_fusion.7
  38.8 7.5 %collective-permute-done.2 = bf16[2,128,512]{1,2,0:T(8,128)(2,1)S(1)} collective-permute-done((bf16[2,128,512]{1,2,0:T(8,128)(2,1)S(1)}, bf16[2,128,512]{1,2,0:T(8,128)(2,1)S(1)}, u32[]{:S(2)}, u32[]{:S(2)}) %collective-permute-start.2) | collective-permute-done | bytes 262176 | tf_op jit(solution)/shard_map/ppermute | solution.py:18
  46.3 1.3 collective-permute-start.7
  47.6 0.7 bitcast_dynamic-update-slice_fusion.6
  48.4 0.7 bitcast_dynamic-update-slice_fusion.5
  49.1 0.7 bitcast_dynamic-update-slice_fusion.4
  49.8 0.7 bitcast_dynamic-update-slice_fusion.3
  50.6 0.7 bitcast_dynamic-update-slice_fusion.2
  51.3 3.3 %collective-permute-done.6 = bf16[2,128,512]{1,2,0:T(8,128)(2,1)S(1)} collective-permute-done((bf16[2,128,512]{1,2,0:T(8,128)(2,1)S(1)}, bf16[2,128,512]{1,2,0:T(8,128)(2,1)S(1)}, u32[]{:S(2)}, u32[]{:S(2)}) %collective-permute-start.6) | collective-permute-done | bytes 262176 | tf_op jit(solution)/shard_map/ppermute | solution.py:18
  54.6 0.7 bitcast_dynamic-update-slice_fusion.1
  55.3 5.3 %collective-permute-done.7 = bf16[2,128,512]{1,2,0:T(8,128)(2,1)S(1)} collective-permute-done((bf16[2,128,512]{1,2,0:T(8,128)(2,1)S(1)}, bf16[2,128,512]{1,2,0:T(8,128)(2,1)S(1)}, u32[]{:S(2)}, u32[]{:S(2)}) %collective-permute-start.7) | collective-permute-done | bytes 262176 | tf_op jit(solution)/shard_map/ppermute | solution.py:18
  60.6 0.7 bitcast_dynamic-update-slice_fusion
  61.3 4.3 %copy.25.stock_ref = bf16[9,2,128,512]{3,2,1,0:T(8,128)(2,1)} copy(bf16[9,2,128,512]{2,3,1,0:T(8,128)(2,1)} %bitcast_dynamic-update-slice_fusion) | data formatting | bytes 4718592 | tf_op jit(solution)/shard_map/stack | solution.py:163
  65.6 68.2 %shard_map.110 = (bf16[2048,512]{1,0:T(8,128)(2,1)}, bf16[2048,512]{1,0:T(8,128)(2,1)}, f32[9,2,128,512]{3,2,1,0:T(8,128)}) custom-call(s32[16,5]{1,0:T(8,128)} %broadcast_subtract_fusion.slots_ref, s32[16]{0:T(128)} %counts_ref.1, bf16[2048,512]{1,0:T(8,128)(2,1)} %q_ref.1, bf16[2048,512]{1,0:T(8,128)(2,1)} %g_ref.1, ...), custom_call_target="tpu_custom_call" | custom-call | flops 9663676416 | bytes 17825792 | tf_op jit(solution)/shard_map/pallas_call | solution.py:128
  133.8 2.7 convert.10
  136.6 1.3 collective-permute-start.10
  137.9 1.3 collective-permute-start.11
  139.2 6.1 %collective-permute-start.12 = (bf16[2,128,512]{2,1,0:T(8,128)(2,1)S(1)}, bf16[2,128,512]{2,1,0:T(8,128)(2,1)S(1)}, u32[]{:S(2)}, u32[]{:S(2)}) collective-permute-start(bf16[2,128,512]{2,1,0:T(8,128)(2,1)S(1)} %get-tuple-element.15), channel_id=1, source_target_pairs={{0,4},{4,8},{8,12},{12,16},{16,20},{20,24},{24,28},{28,32},{32,36}... | collective-permute-start | bytes 786440 | tf_op jit(solution)/shard_map/ppermute | solution.py:18
  145.3 4.6 %collective-permute-start.13 = (bf16[2,128,512]{2,1,0:T(8,128)(2,1)S(1)}, bf16[2,128,512]{2,1,0:T(8,128)(2,1)S(1)}, u32[]{:S(2)}, u32[]{:S(2)}) collective-permute-start(bf16[2,128,512]{2,1,0:T(8,128)(2,1)S(1)} %get-tuple-element.14), channel_id=1, source_target_pairs={{0,8},{4,12},{8,16},{12,20},{16,24},{20,28},{24,32},{28,36},{32,40... | collective-permute-start | bytes 786440 | tf_op jit(solution)/shard_map/ppermute | solution.py:18
  149.8 6.0 %collective-permute-start.14 = (bf16[2,128,512]{2,1,0:T(8,128)(2,1)S(1)}, bf16[2,128,512]{2,1,0:T(8,128)(2,1)S(1)}, u32[]{:S(2)}, u32[]{:S(2)}) collective-permute-start(bf16[2,128,512]{2,1,0:T(8,128)(2,1)S(1)} %get-tuple-element.13), channel_id=1, source_target_pairs={{0,12},{4,16},{8,20},{12,24},{16,28},{20,32},{24,36},{28,40},{32,4... | collective-permute-start | bytes 786440 | tf_op jit(solution)/shard_map/ppermute | solution.py:18
  155.9 8.5 %collective-permute-start.15 = (bf16[2,128,512]{2,1,0:T(8,128)(2,1)S(1)}, bf16[2,128,512]{2,1,0:T(8,128)(2,1)S(1)}, u32[]{:S(2)}, u32[]{:S(2)}) collective-permute-start(bf16[2,128,512]{2,1,0:T(8,128)(2,1)S(1)} %get-tuple-element.12), channel_id=1, source_target_pairs={{0,16},{4,20},{8,24},{12,28},{16,32},{20,36},{24,40},{28,44},{32,4... | collective-permute-start | bytes 786440 | tf_op jit(solution)/shard_map/ppermute | solution.py:18
  164.3 1.3 collective-permute-start.8
  165.7 1.3 collective-permute-start.9
  167.0 3.3 %collective-permute-done.15 = bf16[2,128,512]{2,1,0:T(8,128)(2,1)S(1)} collective-permute-done((bf16[2,128,512]{2,1,0:T(8,128)(2,1)S(1)}, bf16[2,128,512]{2,1,0:T(8,128)(2,1)S(1)}, u32[]{:S(2)}, u32[]{:S(2)}) %collective-permute-start.15) | collective-permute-done | bytes 262176 | tf_op jit(solution)/shard_map/ppermute | solution.py:18
  170.2 8.3 %collective-permute-done.8 = bf16[2,128,512]{2,1,0:T(8,128)(2,1)S(1)} collective-permute-done((bf16[2,128,512]{2,1,0:T(8,128)(2,1)S(1)}, bf16[2,128,512]{2,1,0:T(8,128)(2,1)S(1)}, u32[]{:S(2)}, u32[]{:S(2)}) %collective-permute-start.8) | collective-permute-done | bytes 262176 | tf_op jit(solution)/shard_map/ppermute | solution.py:18
  178.5 1.4 fusion.9
  179.9 0.8 pad_maximum_fusion.1
  180.8 0.8 fusion.10
  181.6 0.8 copy-done.2
  182.3 1.8 convolution_add_fusion
  184.3 1.1 constant_dynamic-slice_fusion
  185.3 52.8 %all-gather.4.cloned.1.call-done = bf16[1024,1024]{1,0:T(8,128)(2,1)} async-done(((bf16[128,1024]{1,0:T(8,128)(2,1)}), bf16[1024,1024]{1,0:T(8,128)(2,1)}) %all-gather.4.cloned.1.call-update) | async-done | bytes 2097168 | tf_op jit(solution)/shard_map/all_gather | solution.py:182
  238.1 3.3 %fusion.12 = f32[256,1024]{1,0:T(8,128)} fusion(bf16[1024,256]{0,1:T(8,128)(2,1)S(1)} %bitcast.73, bf16[1024,1024]{1,0:T(8,128)(2,1)} %all-gather.4.cloned.1.call-done), kind=kOutput, calls=%fused_computation.39 | convolution fusion | flops 536870912 | bytes 3670016 | tf_op jit(solution)/shard_map/dot_general | solution.py:191
  241.5 1.6 convert_element_type.87
  243.1 20.1 %reduce-scatter.5.cloned.1.call-done = f32[64,1024]{1,0:T(8,128)} async-done(((f32[256,1024]{1,0:T(8,128)}), f32[64,1024]{1,0:T(8,128)}) %reduce-scatter.5.cloned.1.call-update) | async-done | bytes 262160 | tf_op jit(solution)/shard_map/reduce_scatter | solution.py:194
  263.2 1.7 fusion.11
  (34 shorter events, 0.8 us)
Async XLA Ops:
  8.0 2.4 copy-start
  8.0 4.5 %copy-start.3 = (bf16[128,2048]{1,0:T(8,128)(2,1)S(1)}, bf16[128,2048]{1,0:T(8,128)(2,1)}, u32[]{:S(2)}) copy-start(bf16[128,2048]{1,0:T(8,128)(2,1)} %param.8) | copy-start | bytes 1572868
  8.0 176.2 %all-gather.6.cloned.1.call-start = ((), (), s32[]{:S(2)}) async-start(), calls=%async_computation.5 | async-start | bytes 4718592 | tf_op jit(solution)/shard_map/all_gather | solution.py:151
  10.3 21.7 %copy-start.4 = (s32[16,5]{0,1:T(8,128)S(1)}, s32[16,5]{0,1:T(8,128)}, u32[]{:S(2)}) copy-start(s32[16,5]{0,1:T(8,128)} %param.12) | copy-start | bytes 964
  10.3 227.8 %all-gather.4.cloned.1.call-start = ((), (), s32[]{:S(2)}) async-start(), calls=%async_computation.3 | async-start | bytes 2359296 | tf_op jit(solution)/shard_map/all_gather | solution.py:182
  10.4 2.1 copy-start.1
  13.5 19.2 %collective-permute-start = (bf16[2,128,512]{1,2,0:T(8,128)(2,1)S(1)}, bf16[2,128,512]{1,2,0:T(8,128)(2,1)}, u32[]{:S(2)}, u32[]{:S(2)}) collective-permute-start(bf16[2,128,512]{1,2,0:T(8,128)(2,1)S(1)} %pad_maximum_fusion), channel_id=1, source_target_pairs={{0,16},{4,20},{8,24},{12,28},{16,32},{20,36},{24,40},{28,44},{32,4... | collective-permute-start | bytes 786440 | tf_op jit(solution)/shard_map/ppermute | solution.py:18
  19.4 16.4 %collective-permute-start.1 = (bf16[2,128,512]{1,2,0:T(8,128)(2,1)S(1)}, bf16[2,128,512]{1,2,0:T(8,128)(2,1)}, u32[]{:S(2)}, u32[]{:S(2)}) collective-permute-start(bf16[2,128,512]{1,2,0:T(8,128)(2,1)S(1)} %pad_maximum_fusion), channel_id=1, source_target_pairs={{0,12},{4,16},{8,20},{12,24},{16,28},{20,32},{24,36},{28,40},{32,4... | collective-permute-start | bytes 786440 | tf_op jit(solution)/shard_map/ppermute | solution.py:18
  25.1 21.2 %collective-permute-start.2 = (bf16[2,128,512]{1,2,0:T(8,128)(2,1)S(1)}, bf16[2,128,512]{1,2,0:T(8,128)(2,1)S(1)}, u32[]{:S(2)}, u32[]{:S(2)}) collective-permute-start(bf16[2,128,512]{1,2,0:T(8,128)(2,1)S(1)} %pad_maximum_fusion), channel_id=1, source_target_pairs={{0,8},{4,12},{8,16},{12,20},{16,24},{20,28},{24,32},{28,36},{32,40... | collective-permute-start | bytes 786440 | tf_op jit(solution)/shard_map/ppermute | solution.py:18
  27.3 21.0 %collective-permute-start.3 = (bf16[2,128,512]{1,2,0:T(8,128)(2,1)S(1)}, bf16[2,128,512]{1,2,0:T(8,128)(2,1)S(1)}, u32[]{:S(2)}, u32[]{:S(2)}) collective-permute-start(bf16[2,128,512]{1,2,0:T(8,128)(2,1)S(1)} %pad_maximum_fusion), channel_id=1, source_target_pairs={{0,4},{4,8},{8,12},{12,16},{16,20},{20,24},{24,28},{28,32},{32,36}... | collective-permute-start | bytes 786440 | tf_op jit(solution)/shard_map/ppermute | solution.py:18
  30.7 19.1 %collective-permute-start.4 = (bf16[2,128,512]{1,2,0:T(8,128)(2,1)S(1)}, bf16[2,128,512]{1,2,0:T(8,128)(2,1)S(1)}, u32[]{:S(2)}, u32[]{:S(2)}) collective-permute-start(bf16[2,128,512]{1,2,0:T(8,128)(2,1)S(1)} %pad_maximum_fusion), channel_id=1, source_target_pairs={{4,0},{8,4},{12,8},{16,12},{20,16},{24,20},{28,24},{32,28},{36,32}... | collective-permute-start | bytes 786440 | tf_op jit(solution)/shard_map/ppermute | solution.py:18
  32.7 17.9 %collective-permute-start.5 = (bf16[2,128,512]{1,2,0:T(8,128)(2,1)S(1)}, bf16[2,128,512]{1,2,0:T(8,128)(2,1)S(1)}, u32[]{:S(2)}, u32[]{:S(2)}) collective-permute-start(bf16[2,128,512]{1,2,0:T(8,128)(2,1)S(1)} %pad_maximum_fusion), channel_id=1, source_target_pairs={{8,0},{12,4},{16,8},{20,12},{24,16},{28,20},{32,24},{36,28},{40,32... | collective-permute-start | bytes 786440 | tf_op jit(solution)/shard_map/ppermute | solution.py:18
  35.8 18.8 %collective-permute-start.6 = (bf16[2,128,512]{1,2,0:T(8,128)(2,1)S(1)}, bf16[2,128,512]{1,2,0:T(8,128)(2,1)S(1)}, u32[]{:S(2)}, u32[]{:S(2)}) collective-permute-start(bf16[2,128,512]{1,2,0:T(8,128)(2,1)S(1)} %pad_maximum_fusion), channel_id=1, source_target_pairs={{12,0},{16,4},{20,8},{24,12},{28,16},{32,20},{36,24},{40,28},{44,3... | collective-permute-start | bytes 786440 | tf_op jit(solution)/shard_map/ppermute | solution.py:18
  46.3 14.3 %collective-permute-start.7 = (bf16[2,128,512]{1,2,0:T(8,128)(2,1)S(1)}, bf16[2,128,512]{1,2,0:T(8,128)(2,1)S(1)}, u32[]{:S(2)}, u32[]{:S(2)}) collective-permute-start(bf16[2,128,512]{1,2,0:T(8,128)(2,1)S(1)} %pad_maximum_fusion), channel_id=1, source_target_pairs={{16,0},{20,4},{24,8},{28,12},{32,16},{36,20},{40,24},{44,28},{48,3... | collective-permute-start | bytes 786440 | tf_op jit(solution)/shard_map/ppermute | solution.py:18
  136.6 19.3 %collective-permute-start.10 = (bf16[2,128,512]{2,1,0:T(8,128)(2,1)S(1)}, bf16[2,128,512]{2,1,0:T(8,128)(2,1)S(1)}, u32[]{:S(2)}, u32[]{:S(2)}) collective-permute-start(bf16[2,128,512]{2,1,0:T(8,128)(2,1)S(1)} %get-tuple-element.17), channel_id=1, source_target_pairs={{8,0},{12,4},{16,8},{20,12},{24,16},{28,20},{32,24},{36,28},{40,32... | collective-permute-start | bytes 786440 | tf_op jit(solution)/shard_map/ppermute | solution.py:18
  137.9 26.4 %collective-permute-start.11 = (bf16[2,128,512]{2,1,0:T(8,128)(2,1)S(1)}, bf16[2,128,512]{2,1,0:T(8,128)(2,1)S(1)}, u32[]{:S(2)}, u32[]{:S(2)}) collective-permute-start(bf16[2,128,512]{2,1,0:T(8,128)(2,1)S(1)} %get-tuple-element.16), channel_id=1, source_target_pairs={{4,0},{8,4},{12,8},{16,12},{20,16},{24,20},{28,24},{32,28},{36,32}... | collective-permute-start | bytes 786440 | tf_op jit(solution)/shard_map/ppermute | solution.py:18
  139.2 26.4 %collective-permute-start.12 = (bf16[2,128,512]{2,1,0:T(8,128)(2,1)S(1)}, bf16[2,128,512]{2,1,0:T(8,128)(2,1)S(1)}, u32[]{:S(2)}, u32[]{:S(2)}) collective-permute-start(bf16[2,128,512]{2,1,0:T(8,128)(2,1)S(1)} %get-tuple-element.15), channel_id=1, source_target_pairs={{0,4},{4,8},{8,12},{12,16},{16,20},{20,24},{24,28},{28,32},{32,36}... | collective-permute-start | bytes 786440 | tf_op jit(solution)/shard_map/ppermute | solution.py:18
  145.3 21.7 %collective-permute-start.13 = (bf16[2,128,512]{2,1,0:T(8,128)(2,1)S(1)}, bf16[2,128,512]{2,1,0:T(8,128)(2,1)S(1)}, u32[]{:S(2)}, u32[]{:S(2)}) collective-permute-start(bf16[2,128,512]{2,1,0:T(8,128)(2,1)S(1)} %get-tuple-element.14), channel_id=1, source_target_pairs={{0,8},{4,12},{8,16},{12,20},{16,24},{20,28},{24,32},{28,36},{32,40... | collective-permute-start | bytes 786440 | tf_op jit(solution)/shard_map/ppermute | solution.py:18
  149.8 17.1 %collective-permute-start.14 = (bf16[2,128,512]{2,1,0:T(8,128)(2,1)S(1)}, bf16[2,128,512]{2,1,0:T(8,128)(2,1)S(1)}, u32[]{:S(2)}, u32[]{:S(2)}) collective-permute-start(bf16[2,128,512]{2,1,0:T(8,128)(2,1)S(1)} %get-tuple-element.13), channel_id=1, source_target_pairs={{0,12},{4,16},{8,20},{12,24},{16,28},{20,32},{24,36},{28,40},{32,4... | collective-permute-start | bytes 786440 | tf_op jit(solution)/shard_map/ppermute | solution.py:18
  155.9 14.4 %collective-permute-start.15 = (bf16[2,128,512]{2,1,0:T(8,128)(2,1)S(1)}, bf16[2,128,512]{2,1,0:T(8,128)(2,1)S(1)}, u32[]{:S(2)}, u32[]{:S(2)}) collective-permute-start(bf16[2,128,512]{2,1,0:T(8,128)(2,1)S(1)} %get-tuple-element.12), channel_id=1, source_target_pairs={{0,16},{4,20},{8,24},{12,28},{16,32},{20,36},{24,40},{28,44},{32,4... | collective-permute-start | bytes 786440 | tf_op jit(solution)/shard_map/ppermute | solution.py:18
  164.3 14.2 %collective-permute-start.8 = (bf16[2,128,512]{2,1,0:T(8,128)(2,1)S(1)}, bf16[2,128,512]{2,1,0:T(8,128)(2,1)S(1)}, u32[]{:S(2)}, u32[]{:S(2)}) collective-permute-start(bf16[2,128,512]{2,1,0:T(8,128)(2,1)S(1)} %get-tuple-element.11), channel_id=1, source_target_pairs={{16,0},{20,4},{24,8},{28,12},{32,16},{36,20},{40,24},{44,28},{48,3... | collective-permute-start | bytes 786440 | tf_op jit(solution)/shard_map/ppermute | solution.py:18
  165.7 12.9 %collective-permute-start.9 = (bf16[2,128,512]{2,1,0:T(8,128)(2,1)S(1)}, bf16[2,128,512]{2,1,0:T(8,128)(2,1)S(1)}, u32[]{:S(2)}, u32[]{:S(2)}) collective-permute-start(bf16[2,128,512]{2,1,0:T(8,128)(2,1)S(1)} %get-tuple-element.18), channel_id=1, source_target_pairs={{12,0},{16,4},{20,8},{24,12},{28,16},{32,20},{36,24},{40,28},{44,3... | collective-permute-start | bytes 786440 | tf_op jit(solution)/shard_map/ppermute | solution.py:18
  180.7 60.8 %reduce-scatter.3.cloned.1.call-start = ((), (), s32[]{:S(2)}) async-start(), calls=%async_computation.2 | async-start | bytes 1310720 | tf_op jit(solution)/shard_map/reduce_scatter | solution.py:178
  180.7 1.6 copy-start.2
  184.2 79.0 %reduce-scatter.5.cloned.1.call-start = ((), (), s32[]{:S(2)}) async-start(), calls=%async_computation.4 | async-start | bytes 1310720 | tf_op jit(solution)/shard_map/reduce_scatter | solution.py:194
Sparse Core Ops, SparseCore 0:
  11.3 100.5 all-gather.5
  180.8 57.2 all-gather.3
Sparse Core Ops, SparseCore 1:
  184.3 25.0 reduce-scatter.2
  241.5 21.6 reduce-scatter.4

commit v8 on v5

--- a/solution.py
+++ b/solution.py
@@ -98,7 +98,7 @@
                 acc_ref[slots[j], 1, :, pl.ds(off, LANES)] += dvs[j]
             return carry
 
-        lax.fori_loop(0, q_ref.shape[1] // LANES, pair, 0)
+        lax.fori_loop(0, q_ref.shape[1] // LANES, pair, 0, unroll=True)
 
     for used in range(1, LISTED + 1):
         pl.when(count == used)(functools.partial(run, used))

time: 274 us -> 262 us (0.956)
  Pallas kernels: 66.9 us -> 51.4 us
  waiting for transfers between devices: 97.4 us -> 102 us
    pallas_call x1, Pallas kernels: 66.9 us -> 51.4 us  [attention(): pl.pallas_call(attention_kernel, grid_spec=grid_spec, out_shape=[jax.Shap...]
    ppermute x16, waiting for transfers between devices: 25.6 us -> 30 us  [passed_along(): return lax.ppermute(value, axis, pairs)]
  transfers between devices with their start and end apart: 20 -> 20, of which waited for: 9 -> 8; matrix products, arithmetic and copies ran while one was open for 11% -> 11% of each run, Pallas kernels for 24% -> 20%
where the time goes in v8:
time: 262 us; the launch traced here: 261 us
  waiting for transfers between devices  102 us (39%)
  starting transfers between devices  57.8 us (22%)
  Pallas kernels  51.4 us (20%)
  local copies, waits for them, and re-layouts  18 us (7%)
  between operations  15.8 us (6%)
  matrix products  8.95 us (3%)
  other arithmetic  7.76 us (3%)
    ppermute x16, starting transfers between devices, passed_along(): return lax.ppermute(value, axis, pairs)  57.6 us
    pallas_call x1, Pallas kernels, attention(): pl.pallas_call(attention_kernel, grid_spec=grid_spec, out_shape=[jax.Shap...  51.4 us
    all_gather x1, waiting for transfers between devices, on_device(): group_grads = lax.all_gather(both_grads, 'byx', axis=0, tiled=True)  51.4 us
    ppermute x16, waiting for transfers between devices, passed_along(): return lax.ppermute(value, axis, pairs)  30 us
    reduce_scatter x1, waiting for transfers between devices, on_device(): lax.psum_scatter(partial, 'bz', scatter_dimension=0, tiled=True)  20.1 us
    unnamed x19, local copies, waits for them, and re-layouts  10.1 us
  transfers between devices with their start and end apart: 20, of which 8 were waited for; matrix products, arithmetic and copies ran while one was open for 11% of the time, Pallas kernels for 20%

profile of v8, /device:TPU:0, one launch (start us, length us, event | category | flops | bytes accessed | tf_op | source)
XLA Modules:
  0.0 261.3 jit_solution(13698582544186987227)
XLA Ops:
  8.1 2.2 copy.26
  10.4 2.1 fusion
  12.5 1.0 fusion.1
  13.5 5.9 %collective-permute-start = (bf16[2,128,512]{1,2,0:T(8,128)(2,1)S(1)}, bf16[2,128,512]{1,2,0:T(8,128)(2,1)}, u32[]{:S(2)}, u32[]{:S(2)}) collective-permute-start(bf16[2,128,512]{1,2,0:T(8,128)(2,1)S(1)} %pad_maximum_fusion), channel_id=1, source_target_pairs={{0,16},{4,20},{8,24},{12,28},{16,32},{20,36},{24,40},{28,44},{32,4... | collective-permute-start | bytes 786440 | tf_op jit(solution)/shard_map/ppermute | solution.py:18
  19.4 5.7 %collective-permute-start.1 = (bf16[2,128,512]{1,2,0:T(8,128)(2,1)S(1)}, bf16[2,128,512]{1,2,0:T(8,128)(2,1)}, u32[]{:S(2)}, u32[]{:S(2)}) collective-permute-start(bf16[2,128,512]{1,2,0:T(8,128)(2,1)S(1)} %pad_maximum_fusion), channel_id=1, source_target_pairs={{0,12},{4,16},{8,20},{12,24},{16,28},{20,32},{24,36},{28,40},{32,4... | collective-permute-start | bytes 786440 | tf_op jit(solution)/shard_map/ppermute | solution.py:18
  25.1 2.2 collective-permute-start.2
  27.3 3.4 %collective-permute-start.3 = (bf16[2,128,512]{1,2,0:T(8,128)(2,1)S(1)}, bf16[2,128,512]{1,2,0:T(8,128)(2,1)S(1)}, u32[]{:S(2)}, u32[]{:S(2)}) collective-permute-start(bf16[2,128,512]{1,2,0:T(8,128)(2,1)S(1)} %pad_maximum_fusion), channel_id=1, source_target_pairs={{0,4},{4,8},{8,12},{12,16},{16,20},{20,24},{24,28},{28,32},{32,36}... | collective-permute-start | bytes 786440 | tf_op jit(solution)/shard_map/ppermute | solution.py:18
  30.7 1.3 collective-permute-start.4
  32.1 0.6 broadcast_subtract_fusion.slots_ref
  32.7 1.3 collective-permute-start.5
  34.0 1.7 bitcast_dynamic-update-slice_fusion.8
  35.8 1.3 collective-permute-start.6
  37.1 1.7 bitcast_dynamic-update-slice_fusion.7
  38.8 7.5 %collective-permute-done.2 = bf16[2,128,512]{1,2,0:T(8,128)(2,1)S(1)} collective-permute-done((bf16[2,128,512]{1,2,0:T(8,128)(2,1)S(1)}, bf16[2,128,512]{1,2,0:T(8,128)(2,1)S(1)}, u32[]{:S(2)}, u32[]{:S(2)}) %collective-permute-start.2) | collective-permute-done | bytes 262176 | tf_op jit(solution)/shard_map/ppermute | solution.py:18
  46.3 1.3 collective-permute-start.7
  47.6 0.7 bitcast_dynamic-update-slice_fusion.6
  48.4 0.7 bitcast_dynamic-update-slice_fusion.5
  49.1 0.7 bitcast_dynamic-update-slice_fusion.4
  49.8 0.7 bitcast_dynamic-update-slice_fusion.3
  50.6 0.7 bitcast_dynamic-update-slice_fusion.2
  51.3 3.3 %collective-permute-done.6 = bf16[2,128,512]{1,2,0:T(8,128)(2,1)S(1)} collective-permute-done((bf16[2,128,512]{1,2,0:T(8,128)(2,1)S(1)}, bf16[2,128,512]{1,2,0:T(8,128)(2,1)S(1)}, u32[]{:S(2)}, u32[]{:S(2)}) %collective-permute-start.6) | collective-permute-done | bytes 262176 | tf_op jit(solution)/shard_map/ppermute | solution.py:18
  54.6 0.7 bitcast_dynamic-update-slice_fusion.1
  55.3 5.3 %collective-permute-done.7 = bf16[2,128,512]{1,2,0:T(8,128)(2,1)S(1)} collective-permute-done((bf16[2,128,512]{1,2,0:T(8,128)(2,1)S(1)}, bf16[2,128,512]{1,2,0:T(8,128)(2,1)S(1)}, u32[]{:S(2)}, u32[]{:S(2)}) %collective-permute-start.7) | collective-permute-done | bytes 262176 | tf_op jit(solution)/shard_map/ppermute | solution.py:18
  60.6 0.7 bitcast_dynamic-update-slice_fusion
  61.3 4.3 %copy.25.stock_ref = bf16[9,2,128,512]{3,2,1,0:T(8,128)(2,1)} copy(bf16[9,2,128,512]{2,3,1,0:T(8,128)(2,1)} %bitcast_dynamic-update-slice_fusion) | data formatting | bytes 4718592 | tf_op jit(solution)/shard_map/stack | solution.py:164
  65.6 51.4 %shard_map.110 = (bf16[2048,512]{1,0:T(8,128)(2,1)}, bf16[2048,512]{1,0:T(8,128)(2,1)}, f32[9,2,128,512]{3,2,1,0:T(8,128)}) custom-call(s32[16,5]{1,0:T(8,128)} %broadcast_subtract_fusion.slots_ref, s32[16]{0:T(128)} %counts_ref.1, bf16[2048,512]{1,0:T(8,128)(2,1)} %q_ref.1, bf16[2048,512]{1,0:T(8,128)(2,1)} %g_ref.1, ...), custom_call_target="tpu_custom_call" | custom-call | flops 9663676416 | bytes 17825792 | tf_op jit(solution)/shard_map/pallas_call | solution.py:129
  117.0 2.7 %convert.10 = bf16[9,2,128,512]{3,2,1,0:T(8,128)(2,1)S(1)} convert(f32[9,2,128,512]{3,2,1,0:T(8,128)} %get-tuple-element.10) | non-fusion elementwise | flops 1179648 | bytes 7077888 | tf_op jit(solution)/shard_map/convert.7
  119.8 1.3 collective-permute-start.10
  121.1 1.3 collective-permute-start.11
  122.4 6.1 %collective-permute-start.12 = (bf16[2,128,512]{2,1,0:T(8,128)(2,1)S(1)}, bf16[2,128,512]{2,1,0:T(8,128)(2,1)S(1)}, u32[]{:S(2)}, u32[]{:S(2)}) collective-permute-start(bf16[2,128,512]{2,1,0:T(8,128)(2,1)S(1)} %get-tuple-element.15), channel_id=1, source_target_pairs={{0,4},{4,8},{8,12},{12,16},{16,20},{20,24},{24,28},{28,32},{32,36}... | collective-permute-start | bytes 786440 | tf_op jit(solution)/shard_map/ppermute | solution.py:18
  128.5 4.6 %collective-permute-start.13 = (bf16[2,128,512]{2,1,0:T(8,128)(2,1)S(1)}, bf16[2,128,512]{2,1,0:T(8,128)(2,1)S(1)}, u32[]{:S(2)}, u32[]{:S(2)}) collective-permute-start(bf16[2,128,512]{2,1,0:T(8,128)(2,1)S(1)} %get-tuple-element.14), channel_id=1, source_target_pairs={{0,8},{4,12},{8,16},{12,20},{16,24},{20,28},{24,32},{28,36},{32,40... | collective-permute-start | bytes 786440 | tf_op jit(solution)/shard_map/ppermute | solution.py:18
  133.1 10.8 %collective-permute-start.14 = (bf16[2,128,512]{2,1,0:T(8,128)(2,1)S(1)}, bf16[2,128,512]{2,1,0:T(8,128)(2,1)S(1)}, u32[]{:S(2)}, u32[]{:S(2)}) collective-permute-start(bf16[2,128,512]{2,1,0:T(8,128)(2,1)S(1)} %get-tuple-element.13), channel_id=1, source_target_pairs={{0,12},{4,16},{8,20},{12,24},{16,28},{20,32},{24,36},{28,40},{32,4... | collective-permute-start | bytes 786440 | tf_op jit(solution)/shard_map/ppermute | solution.py:18
  143.9 8.7 %collective-permute-start.15 = (bf16[2,128,512]{2,1,0:T(8,128)(2,1)S(1)}, bf16[2,128,512]{2,1,0:T(8,128)(2,1)S(1)}, u32[]{:S(2)}, u32[]{:S(2)}) collective-permute-start(bf16[2,128,512]{2,1,0:T(8,128)(2,1)S(1)} %get-tuple-element.12), channel_id=1, source_target_pairs={{0,16},{4,20},{8,24},{12,28},{16,32},{20,36},{24,40},{28,44},{32,4... | collective-permute-start | bytes 786440 | tf_op jit(solution)/shard_map/ppermute | solution.py:18
  152.6 1.3 collective-permute-start.8
  153.9 1.3 collective-permute-start.9
  155.2 2.8 %collective-permute-done.15 = bf16[2,128,512]{2,1,0:T(8,128)(2,1)S(1)} collective-permute-done((bf16[2,128,512]{2,1,0:T(8,128)(2,1)S(1)}, bf16[2,128,512]{2,1,0:T(8,128)(2,1)S(1)}, u32[]{:S(2)}, u32[]{:S(2)}) %collective-permute-start.15) | collective-permute-done | bytes 262176 | tf_op jit(solution)/shard_map/ppermute | solution.py:18
  158.0 10.9 %collective-permute-done.8 = bf16[2,128,512]{2,1,0:T(8,128)(2,1)S(1)} collective-permute-done((bf16[2,128,512]{2,1,0:T(8,128)(2,1)S(1)}, bf16[2,128,512]{2,1,0:T(8,128)(2,1)S(1)}, u32[]{:S(2)}, u32[]{:S(2)}) %collective-permute-start.8) | collective-permute-done | bytes 262176 | tf_op jit(solution)/shard_map/ppermute | solution.py:18
  168.9 1.4 fusion.9
  170.3 0.8 pad_maximum_fusion.1
  171.1 0.8 fusion.10
  171.9 0.8 copy-done.2
  172.7 1.8 convolution_add_fusion
  174.6 1.1 constant_dynamic-slice_fusion
  175.7 51.4 %all-gather.4.cloned.1.call-done = bf16[1024,1024]{1,0:T(8,128)(2,1)} async-done(((bf16[128,1024]{1,0:T(8,128)(2,1)}), bf16[1024,1024]{1,0:T(8,128)(2,1)}) %all-gather.4.cloned.1.call-update) | async-done | bytes 2097168 | tf_op jit(solution)/shard_map/all_gather | solution.py:183
  227.1 3.3 %fusion.12 = f32[256,1024]{1,0:T(8,128)} fusion(bf16[1024,256]{0,1:T(8,128)(2,1)S(1)} %bitcast.73, bf16[1024,1024]{1,0:T(8,128)(2,1)} %all-gather.4.cloned.1.call-done), kind=kOutput, calls=%fused_computation.39 | convolution fusion | flops 536870912 | bytes 3670016 | tf_op jit(solution)/shard_map/dot_general | solution.py:192
  230.4 1.6 convert_element_type.87
  232.1 20.1 %reduce-scatter.5.cloned.1.call-done = f32[64,1024]{1,0:T(8,128)} async-done(((f32[256,1024]{1,0:T(8,128)}), f32[64,1024]{1,0:T(8,128)}) %reduce-scatter.5.cloned.1.call-update) | async-done | bytes 262160 | tf_op jit(solution)/shard_map/reduce_scatter | solution.py:195
  252.2 1.7 fusion.11
  (34 shorter events, 0.8 us)
Async XLA Ops:
  8.0 2.4 copy-start
  8.0 4.5 %copy-start.3 = (bf16[128,2048]{1,0:T(8,128)(2,1)S(1)}, bf16[128,2048]{1,0:T(8,128)(2,1)}, u32[]{:S(2)}) copy-start(bf16[128,2048]{1,0:T(8,128)(2,1)} %param.8) | copy-start | bytes 1572868
  8.0 166.6 %all-gather.6.cloned.1.call-start = ((), (), s32[]{:S(2)}) async-start(), calls=%async_computation.5 | async-start | bytes 4718592 | tf_op jit(solution)/shard_map/all_gather | solution.py:152
  10.3 21.7 %copy-start.4 = (s32[16,5]{0,1:T(8,128)S(1)}, s32[16,5]{0,1:T(8,128)}, u32[]{:S(2)}) copy-start(s32[16,5]{0,1:T(8,128)} %param.12) | copy-start | bytes 964
  10.3 216.8 %all-gather.4.cloned.1.call-start = ((), (), s32[]{:S(2)}) async-start(), calls=%async_computation.3 | async-start | bytes 2359296 | tf_op jit(solution)/shard_map/all_gather | solution.py:183
  10.4 2.1 copy-start.1
  13.5 19.2 %collective-permute-start = (bf16[2,128,512]{1,2,0:T(8,128)(2,1)S(1)}, bf16[2,128,512]{1,2,0:T(8,128)(2,1)}, u32[]{:S(2)}, u32[]{:S(2)}) collective-permute-start(bf16[2,128,512]{1,2,0:T(8,128)(2,1)S(1)} %pad_maximum_fusion), channel_id=1, source_target_pairs={{0,16},{4,20},{8,24},{12,28},{16,32},{20,36},{24,40},{28,44},{32,4... | collective-permute-start | bytes 786440 | tf_op jit(solution)/shard_map/ppermute | solution.py:18
  19.4 16.4 %collective-permute-start.1 = (bf16[2,128,512]{1,2,0:T(8,128)(2,1)S(1)}, bf16[2,128,512]{1,2,0:T(8,128)(2,1)}, u32[]{:S(2)}, u32[]{:S(2)}) collective-permute-start(bf16[2,128,512]{1,2,0:T(8,128)(2,1)S(1)} %pad_maximum_fusion), channel_id=1, source_target_pairs={{0,12},{4,16},{8,20},{12,24},{16,28},{20,32},{24,36},{28,40},{32,4... | collective-permute-start | bytes 786440 | tf_op jit(solution)/shard_map/ppermute | solution.py:18
  25.1 21.2 %collective-permute-start.2 = (bf16[2,128,512]{1,2,0:T(8,128)(2,1)S(1)}, bf16[2,128,512]{1,2,0:T(8,128)(2,1)S(1)}, u32[]{:S(2)}, u32[]{:S(2)}) collective-permute-start(bf16[2,128,512]{1,2,0:T(8,128)(2,1)S(1)} %pad_maximum_fusion), channel_id=1, source_target_pairs={{0,8},{4,12},{8,16},{12,20},{16,24},{20,28},{24,32},{28,36},{32,40... | collective-permute-start | bytes 786440 | tf_op jit(solution)/shard_map/ppermute | solution.py:18
  27.3 21.0 %collective-permute-start.3 = (bf16[2,128,512]{1,2,0:T(8,128)(2,1)S(1)}, bf16[2,128,512]{1,2,0:T(8,128)(2,1)S(1)}, u32[]{:S(2)}, u32[]{:S(2)}) collective-permute-start(bf16[2,128,512]{1,2,0:T(8,128)(2,1)S(1)} %pad_maximum_fusion), channel_id=1, source_target_pairs={{0,4},{4,8},{8,12},{12,16},{16,20},{20,24},{24,28},{28,32},{32,36}... | collective-permute-start | bytes 786440 | tf_op jit(solution)/shard_map/ppermute | solution.py:18
  30.7 19.1 %collective-permute-start.4 = (bf16[2,128,512]{1,2,0:T(8,128)(2,1)S(1)}, bf16[2,128,512]{1,2,0:T(8,128)(2,1)S(1)}, u32[]{:S(2)}, u32[]{:S(2)}) collective-permute-start(bf16[2,128,512]{1,2,0:T(8,128)(2,1)S(1)} %pad_maximum_fusion), channel_id=1, source_target_pairs={{4,0},{8,4},{12,8},{16,12},{20,16},{24,20},{28,24},{32,28},{36,32}... | collective-permute-start | bytes 786440 | tf_op jit(solution)/shard_map/ppermute | solution.py:18
  32.7 17.9 %collective-permute-start.5 = (bf16[2,128,512]{1,2,0:T(8,128)(2,1)S(1)}, bf16[2,128,512]{1,2,0:T(8,128)(2,1)S(1)}, u32[]{:S(2)}, u32[]{:S(2)}) collective-permute-start(bf16[2,128,512]{1,2,0:T(8,128)(2,1)S(1)} %pad_maximum_fusion), channel_id=1, source_target_pairs={{8,0},{12,4},{16,8},{20,12},{24,16},{28,20},{32,24},{36,28},{40,32... | collective-permute-start | bytes 786440 | tf_op jit(solution)/shard_map/ppermute | solution.py:18
  35.8 18.8 %collective-permute-start.6 = (bf16[2,128,512]{1,2,0:T(8,128)(2,1)S(1)}, bf16[2,128,512]{1,2,0:T(8,128)(2,1)S(1)}, u32[]{:S(2)}, u32[]{:S(2)}) collective-permute-start(bf16[2,128,512]{1,2,0:T(8,128)(2,1)S(1)} %pad_maximum_fusion), channel_id=1, source_target_pairs={{12,0},{16,4},{20,8},{24,12},{28,16},{32,20},{36,24},{40,28},{44,3... | collective-permute-start | bytes 786440 | tf_op jit(solution)/shard_map/ppermute | solution.py:18
  46.3 14.3 %collective-permute-start.7 = (bf16[2,128,512]{1,2,0:T(8,128)(2,1)S(1)}, bf16[2,128,512]{1,2,0:T(8,128)(2,1)S(1)}, u32[]{:S(2)}, u32[]{:S(2)}) collective-permute-start(bf16[2,128,512]{1,2,0:T(8,128)(2,1)S(1)} %pad_maximum_fusion), channel_id=1, source_target_pairs={{16,0},{20,4},{24,8},{28,12},{32,16},{36,20},{40,24},{44,28},{48,3... | collective-permute-start | bytes 786440 | tf_op jit(solution)/shard_map/ppermute | solution.py:18
  119.8 24.1 %collective-permute-start.10 = (bf16[2,128,512]{2,1,0:T(8,128)(2,1)S(1)}, bf16[2,128,512]{2,1,0:T(8,128)(2,1)S(1)}, u32[]{:S(2)}, u32[]{:S(2)}) collective-permute-start(bf16[2,128,512]{2,1,0:T(8,128)(2,1)S(1)} %get-tuple-element.17), channel_id=1, source_target_pairs={{8,0},{12,4},{16,8},{20,12},{24,16},{28,20},{32,24},{36,28},{40,32... | collective-permute-start | bytes 786440 | tf_op jit(solution)/shard_map/ppermute | solution.py:18
  121.1 31.4 %collective-permute-start.11 = (bf16[2,128,512]{2,1,0:T(8,128)(2,1)S(1)}, bf16[2,128,512]{2,1,0:T(8,128)(2,1)S(1)}, u32[]{:S(2)}, u32[]{:S(2)}) collective-permute-start(bf16[2,128,512]{2,1,0:T(8,128)(2,1)S(1)} %get-tuple-element.16), channel_id=1, source_target_pairs={{4,0},{8,4},{12,8},{16,12},{20,16},{24,20},{28,24},{32,28},{36,32}... | collective-permute-start | bytes 786440 | tf_op jit(solution)/shard_map/ppermute | solution.py:18
  122.4 31.5 %collective-permute-start.12 = (bf16[2,128,512]{2,1,0:T(8,128)(2,1)S(1)}, bf16[2,128,512]{2,1,0:T(8,128)(2,1)S(1)}, u32[]{:S(2)}, u32[]{:S(2)}) collective-permute-start(bf16[2,128,512]{2,1,0:T(8,128)(2,1)S(1)} %get-tuple-element.15), channel_id=1, source_target_pairs={{0,4},{4,8},{8,12},{12,16},{16,20},{20,24},{24,28},{28,32},{32,36}... | collective-permute-start | bytes 786440 | tf_op jit(solution)/shard_map/ppermute | solution.py:18
  128.5 26.7 %collective-permute-start.13 = (bf16[2,128,512]{2,1,0:T(8,128)(2,1)S(1)}, bf16[2,128,512]{2,1,0:T(8,128)(2,1)S(1)}, u32[]{:S(2)}, u32[]{:S(2)}) collective-permute-start(bf16[2,128,512]{2,1,0:T(8,128)(2,1)S(1)} %get-tuple-element.14), channel_id=1, source_target_pairs={{0,8},{4,12},{8,16},{12,20},{16,24},{20,28},{24,32},{28,36},{32,40... | collective-permute-start | bytes 786440 | tf_op jit(solution)/shard_map/ppermute | solution.py:18
  133.1 22.1 %collective-permute-start.14 = (bf16[2,128,512]{2,1,0:T(8,128)(2,1)S(1)}, bf16[2,128,512]{2,1,0:T(8,128)(2,1)S(1)}, u32[]{:S(2)}, u32[]{:S(2)}) collective-permute-start(bf16[2,128,512]{2,1,0:T(8,128)(2,1)S(1)} %get-tuple-element.13), channel_id=1, source_target_pairs={{0,12},{4,16},{8,20},{12,24},{16,28},{20,32},{24,36},{28,40},{32,4... | collective-permute-start | bytes 786440 | tf_op jit(solution)/shard_map/ppermute | solution.py:18
  143.9 14.1 %collective-permute-start.15 = (bf16[2,128,512]{2,1,0:T(8,128)(2,1)S(1)}, bf16[2,128,512]{2,1,0:T(8,128)(2,1)S(1)}, u32[]{:S(2)}, u32[]{:S(2)}) collective-permute-start(bf16[2,128,512]{2,1,0:T(8,128)(2,1)S(1)} %get-tuple-element.12), channel_id=1, source_target_pairs={{0,16},{4,20},{8,24},{12,28},{16,32},{20,36},{24,40},{28,44},{32,4... | collective-permute-start | bytes 786440 | tf_op jit(solution)/shard_map/ppermute | solution.py:18
  152.6 16.3 %collective-permute-start.8 = (bf16[2,128,512]{2,1,0:T(8,128)(2,1)S(1)}, bf16[2,128,512]{2,1,0:T(8,128)(2,1)S(1)}, u32[]{:S(2)}, u32[]{:S(2)}) collective-permute-start(bf16[2,128,512]{2,1,0:T(8,128)(2,1)S(1)} %get-tuple-element.11), channel_id=1, source_target_pairs={{16,0},{20,4},{24,8},{28,12},{32,16},{36,20},{40,24},{44,28},{48,3... | collective-permute-start | bytes 786440 | tf_op jit(solution)/shard_map/ppermute | solution.py:18
  153.9 15.0 %collective-permute-start.9 = (bf16[2,128,512]{2,1,0:T(8,128)(2,1)S(1)}, bf16[2,128,512]{2,1,0:T(8,128)(2,1)S(1)}, u32[]{:S(2)}, u32[]{:S(2)}) collective-permute-start(bf16[2,128,512]{2,1,0:T(8,128)(2,1)S(1)} %get-tuple-element.18), channel_id=1, source_target_pairs={{12,0},{16,4},{20,8},{24,12},{28,16},{32,20},{36,24},{40,28},{44,3... | collective-permute-start | bytes 786440 | tf_op jit(solution)/shard_map/ppermute | solution.py:18
  171.1 59.4 %reduce-scatter.3.cloned.1.call-start = ((), (), s32[]{:S(2)}) async-start(), calls=%async_computation.2 | async-start | bytes 1310720 | tf_op jit(solution)/shard_map/reduce_scatter | solution.py:179
  171.1 1.6 copy-start.2
  174.6 77.6 %reduce-scatter.5.cloned.1.call-start = ((), (), s32[]{:S(2)}) async-start(), calls=%async_computation.4 | async-start | bytes 1310720 | tf_op jit(solution)/shard_map/reduce_scatter | solution.py:195
Sparse Core Ops, SparseCore 0:
  11.3 100.5 all-gather.5
  171.2 55.8 all-gather.3
Sparse Core Ops, SparseCore 1:
  174.6 23.6 reduce-scatter.2
  230.5 21.6 reduce-scatter.4

commit v9 on v8

--- a/solution.py
+++ b/solution.py
@@ -19,7 +19,8 @@
 
 
 def attention_kernel(
-    slots_ref, counts_ref, q_ref, g_ref, stock_ref, flipped_ref, out_ref, dq_ref, acc_ref
+    slots_ref, counts_ref, q_ref, g_ref, stock_ref, flipped_ref, out_ref, dq_ref, own_ref,
+    sent_ref, acc_ref,
 ):
     factor = HEAD_DIM ** (-0.5)
     step = pl.program_id(0)
@@ -103,6 +104,11 @@
     for used in range(1, LISTED + 1):
         pl.when(count == used)(functools.partial(run, used))
 
+    @pl.when(step == pl.num_programs(0) - 1)
+    def _():
+        own_ref[...] = acc_ref[REACH]
+        sent_ref[...] = acc_ref[...].astype(sent_ref.dtype)
+
 
 def attention(queries, out_grad, stock, slot_ids, counts):
     rows, cols = stock.shape[2], stock.shape[3]
@@ -123,8 +129,10 @@
         out_specs=[
             pl.BlockSpec((rows, cols), lambda i, s, c: (i, 0)),
             pl.BlockSpec((rows, cols), lambda i, s, c: (i, 0)),
+            pl.BlockSpec((2, rows, cols), lambda i, s, c: (0, 0, 0)),
             pl.BlockSpec((n_slots, 2, rows, cols), lambda i, s, c: (0, 0, 0, 0)),
         ],
+        scratch_shapes=[pltpu.VMEM(stock.shape, jnp.float32)],
     )
     return pl.pallas_call(
         attention_kernel,
@@ -132,7 +140,8 @@
         out_shape=[
             jax.ShapeDtypeStruct(queries.shape, jnp.bfloat16),
             jax.ShapeDtypeStruct(queries.shape, jnp.bfloat16),
-            jax.ShapeDtypeStruct(stock.shape, jnp.float32),
+            jax.ShapeDtypeStruct(stock.shape[1:], jnp.float32),
+            jax.ShapeDtypeStruct(stock.shape, jnp.bfloat16),
         ],
         compiler_params=pltpu.CompilerParams(dimension_semantics=("arbitrary",)),
         cost_estimate=pl.CostEstimate(
@@ -163,13 +172,12 @@
             arrived.append(passed_along(own, blk, -offset, outer * inner))
     stock = jnp.stack(arrived, 0)
     slot_ids = (block_lists - (position - REACH)).astype(jnp.int32)
-    attended, query_grad, running = attention(
+    attended, query_grad, owned, sending = attention(
         queries, out_grad, stock, slot_ids, list_counts.astype(jnp.int32)
     )
-    owned = running[REACH]
     for offset in range(-REACH, REACH + 1):
         if offset != 0:
-            sent = running[REACH + offset].astype(jnp.bfloat16)
+            sent = sending[REACH + offset]
             owned = owned + passed_along(sent, blk, offset, outer * inner).astype(jnp.float32)
     rounded = owned.astype(jnp.bfloat16)
     contract_cols = (((1,), (1,)), ((), ()))

time: 262 us -> 262 us (level)
  starting transfers between devices: 57.8 us -> 52.8 us
  waiting for transfers between devices: 102 us -> 106 us
  other arithmetic: 7.76 us -> 4.1 us
    ppermute x16, starting transfers between devices: 57.6 us -> 52.7 us  [passed_along(): return lax.ppermute(value, axis, pairs)]
    all_gather x1, waiting for transfers between devices: 51.4 us -> 55 us  [on_device(): group_grads = lax.all_gather(both_grads, 'byx', axis=0, tiled=True)]
    another operation x1 -> x0, other arithmetic: 2.67 us -> none
    unnamed x19 -> x21, local copies, waits for them, and re-layouts: 10.1 us -> 10.1 us
  transfers between devices with their start and end apart: 20 -> 20, of which waited for: 8 -> 8; matrix products, arithmetic and copies ran while one was open for 11% -> 11% of each run, Pallas kernels for 20% -> 21%
where the time goes in v9:
time: 262 us; the launch traced here: 261 us
  waiting for transfers between devices  106 us (40%)
  Pallas kernels  53.9 us (21%)
  starting transfers between devices  52.8 us (20%)
  local copies, waits for them, and re-layouts  19.7 us (8%)
  between operations  15.8 us (6%)
  matrix products  8.94 us (3%)
  other arithmetic  4.1 us (2%)
    all_gather x1, waiting for transfers between devices, on_device(): group_grads = lax.all_gather(both_grads, 'byx', axis=0, tiled=True)  55 us
    pallas_call x1, Pallas kernels, attention(): pl.pallas_call(attention_kernel, grid_spec=grid_spec, out_shape=[jax.Shap...  53.9 us
    ppermute x16, starting transfers between devices, passed_along(): return lax.ppermute(value, axis, pairs)  52.7 us
    ppermute x16, waiting for transfers between devices, passed_along(): return lax.ppermute(value, axis, pairs)  30.9 us
    reduce_scatter x1, waiting for transfers between devices, on_device(): lax.psum_scatter(partial, 'bz', scatter_dimension=0, tiled=True)  20.1 us
    unnamed x21, local copies, waits for them, and re-layouts  10.1 us
  transfers between devices with their start and end apart: 20, of which 8 were waited for; matrix products, arithmetic and copies ran while one was open for 11% of the time, Pallas kernels for 21%

profile of v9, /device:TPU:0, one launch (start us, length us, event | category | flops | bytes accessed | tf_op | source)
XLA Modules:
  0.0 261.4 jit_solution(10749170601154481106)
XLA Ops:
  8.1 2.2 copy.26
  10.4 2.1 fusion
  12.5 1.0 fusion.1
  13.5 5.9 %collective-permute-start = (bf16[2,128,512]{1,2,0:T(8,128)(2,1)S(1)}, bf16[2,128,512]{1,2,0:T(8,128)(2,1)}, u32[]{:S(2)}, u32[]{:S(2)}) collective-permute-start(bf16[2,128,512]{1,2,0:T(8,128)(2,1)S(1)} %pad_maximum_fusion), channel_id=1, source_target_pairs={{0,16},{4,20},{8,24},{12,28},{16,32},{20,36},{24,40},{28,44},{32,4... | collective-permute-start | bytes 786440 | tf_op jit(solution)/shard_map/ppermute | solution.py:18
  19.4 5.8 %collective-permute-start.1 = (bf16[2,128,512]{1,2,0:T(8,128)(2,1)S(1)}, bf16[2,128,512]{1,2,0:T(8,128)(2,1)}, u32[]{:S(2)}, u32[]{:S(2)}) collective-permute-start(bf16[2,128,512]{1,2,0:T(8,128)(2,1)S(1)} %pad_maximum_fusion), channel_id=1, source_target_pairs={{0,12},{4,16},{8,20},{12,24},{16,28},{20,32},{24,36},{28,40},{32,4... | collective-permute-start | bytes 786440 | tf_op jit(solution)/shard_map/ppermute | solution.py:18
  25.2 2.2 collective-permute-start.2
  27.4 3.3 %collective-permute-start.3 = (bf16[2,128,512]{1,2,0:T(8,128)(2,1)S(1)}, bf16[2,128,512]{1,2,0:T(8,128)(2,1)S(1)}, u32[]{:S(2)}, u32[]{:S(2)}) collective-permute-start(bf16[2,128,512]{1,2,0:T(8,128)(2,1)S(1)} %pad_maximum_fusion), channel_id=1, source_target_pairs={{0,4},{4,8},{8,12},{12,16},{16,20},{20,24},{24,28},{28,32},{32,36}... | collective-permute-start | bytes 786440 | tf_op jit(solution)/shard_map/ppermute | solution.py:18
  30.7 1.3 collective-permute-start.4
  32.1 0.6 broadcast_subtract_fusion.slots_ref
  32.7 1.3 collective-permute-start.5
  34.0 1.7 bitcast_dynamic-update-slice_fusion.8
  35.8 1.3 collective-permute-start.6
  37.1 1.7 bitcast_dynamic-update-slice_fusion.7
  38.8 7.6 %collective-permute-done.2 = bf16[2,128,512]{1,2,0:T(8,128)(2,1)S(1)} collective-permute-done((bf16[2,128,512]{1,2,0:T(8,128)(2,1)S(1)}, bf16[2,128,512]{1,2,0:T(8,128)(2,1)S(1)}, u32[]{:S(2)}, u32[]{:S(2)}) %collective-permute-start.2) | collective-permute-done | bytes 262176 | tf_op jit(solution)/shard_map/ppermute | solution.py:18
  46.4 1.3 collective-permute-start.7
  47.6 0.7 bitcast_dynamic-update-slice_fusion.6
  48.4 0.7 bitcast_dynamic-update-slice_fusion.5
  49.1 0.7 bitcast_dynamic-update-slice_fusion.4
  49.9 0.7 bitcast_dynamic-update-slice_fusion.3
  50.6 0.7 bitcast_dynamic-update-slice_fusion.2
  51.4 3.2 %collective-permute-done.6 = bf16[2,128,512]{1,2,0:T(8,128)(2,1)S(1)} collective-permute-done((bf16[2,128,512]{1,2,0:T(8,128)(2,1)S(1)}, bf16[2,128,512]{1,2,0:T(8,128)(2,1)S(1)}, u32[]{:S(2)}, u32[]{:S(2)}) %collective-permute-start.6) | collective-permute-done | bytes 262176 | tf_op jit(solution)/shard_map/ppermute | solution.py:18
  54.6 0.7 bitcast_dynamic-update-slice_fusion.1
  55.3 5.3 %collective-permute-done.7 = bf16[2,128,512]{1,2,0:T(8,128)(2,1)S(1)} collective-permute-done((bf16[2,128,512]{1,2,0:T(8,128)(2,1)S(1)}, bf16[2,128,512]{1,2,0:T(8,128)(2,1)S(1)}, u32[]{:S(2)}, u32[]{:S(2)}) %collective-permute-start.7) | collective-permute-done | bytes 262176 | tf_op jit(solution)/shard_map/ppermute | solution.py:18
  60.6 0.7 bitcast_dynamic-update-slice_fusion
  61.4 4.4 %copy.25.stock_ref = bf16[9,2,128,512]{3,2,1,0:T(8,128)(2,1)} copy(bf16[9,2,128,512]{2,3,1,0:T(8,128)(2,1)} %bitcast_dynamic-update-slice_fusion) | data formatting | bytes 4718592 | tf_op jit(solution)/shard_map/stack | solution.py:173
  65.7 53.9 %shard_map.110 = (bf16[2048,512]{1,0:T(8,128)(2,1)}, bf16[2048,512]{1,0:T(8,128)(2,1)}, f32[2,128,512]{2,1,0:T(8,128)}, bf16[9,2,128,512]{3,2,1,0:T(8,128)(2,1)}) custom-call(s32[16,5]{1,0:T(8,128)} %broadcast_subtract_fusion.slots_ref, s32[16]{0:T(128)} %counts_ref.1, bf16[2048,512]{1,0:T(8,128)(2,1)} %q_ref.1, bf16[2048,512]{1,0:T(8,128)(2,1)} %g_ref.1, ...), custom_call_target="tpu_custom_call" | custom-call | flops 9663676416 | bytes 17825792 | tf_op jit(solution)/shard_map/pallas_call | solution.py:137
  119.7 1.7 slice_bitcast_fusion.7
  121.4 1.3 collective-permute-start.10
  122.7 1.3 collective-permute-start.11
  124.0 6.1 %collective-permute-start.12 = (bf16[2,128,512]{2,1,0:T(8,128)(2,1)S(1)}, bf16[2,128,512]{2,1,0:T(8,128)(2,1)S(1)}, u32[]{:S(2)}, u32[]{:S(2)}) collective-permute-start(bf16[2,128,512]{2,1,0:T(8,128)(2,1)S(1)} %get-tuple-element.17), channel_id=1, source_target_pairs={{0,4},{4,8},{8,12},{12,16},{16,20},{20,24},{24,28},{28,32},{32,36}... | collective-permute-start | bytes 786440 | tf_op jit(solution)/shard_map/ppermute | solution.py:18
  130.0 4.6 %collective-permute-start.13 = (bf16[2,128,512]{2,1,0:T(8,128)(2,1)S(1)}, bf16[2,128,512]{2,1,0:T(8,128)(2,1)S(1)}, u32[]{:S(2)}, u32[]{:S(2)}) collective-permute-start(bf16[2,128,512]{2,1,0:T(8,128)(2,1)S(1)} %get-tuple-element.16), channel_id=1, source_target_pairs={{0,8},{4,12},{8,16},{12,20},{16,24},{20,28},{24,32},{28,36},{32,40... | collective-permute-start | bytes 786440 | tf_op jit(solution)/shard_map/ppermute | solution.py:18
  134.6 5.9 %collective-permute-start.14 = (bf16[2,128,512]{2,1,0:T(8,128)(2,1)S(1)}, bf16[2,128,512]{2,1,0:T(8,128)(2,1)S(1)}, u32[]{:S(2)}, u32[]{:S(2)}) collective-permute-start(bf16[2,128,512]{2,1,0:T(8,128)(2,1)S(1)} %get-tuple-element.15), channel_id=1, source_target_pairs={{0,12},{4,16},{8,20},{12,24},{16,28},{20,32},{24,36},{28,40},{32,4... | collective-permute-start | bytes 786440 | tf_op jit(solution)/shard_map/ppermute | solution.py:18
  140.5 8.7 %collective-permute-start.15 = (bf16[2,128,512]{2,1,0:T(8,128)(2,1)S(1)}, bf16[2,128,512]{2,1,0:T(8,128)(2,1)S(1)}, u32[]{:S(2)}, u32[]{:S(2)}) collective-permute-start(bf16[2,128,512]{2,1,0:T(8,128)(2,1)S(1)} %get-tuple-element.14), channel_id=1, source_target_pairs={{0,16},{4,20},{8,24},{12,28},{16,32},{20,36},{24,40},{28,44},{32,4... | collective-permute-start | bytes 786440 | tf_op jit(solution)/shard_map/ppermute | solution.py:18
  149.2 1.3 collective-permute-start.8
  150.5 1.3 collective-permute-start.9
  151.8 3.1 %collective-permute-done.15 = bf16[2,128,512]{2,1,0:T(8,128)(2,1)S(1)} collective-permute-done((bf16[2,128,512]{2,1,0:T(8,128)(2,1)S(1)}, bf16[2,128,512]{2,1,0:T(8,128)(2,1)S(1)}, u32[]{:S(2)}, u32[]{:S(2)}) %collective-permute-start.15) | collective-permute-done | bytes 262176 | tf_op jit(solution)/shard_map/ppermute | solution.py:18
  154.9 11.6 %collective-permute-done.8 = bf16[2,128,512]{2,1,0:T(8,128)(2,1)S(1)} collective-permute-done((bf16[2,128,512]{2,1,0:T(8,128)(2,1)S(1)}, bf16[2,128,512]{2,1,0:T(8,128)(2,1)S(1)}, u32[]{:S(2)}, u32[]{:S(2)}) %collective-permute-start.8) | collective-permute-done | bytes 262176 | tf_op jit(solution)/shard_map/ppermute | solution.py:18
  166.5 0.3 add_convert_fusion
  166.9 0.8 pad_maximum_fusion.1
  167.7 0.8 fusion.2
  168.5 0.8 copy-done.2
  169.3 1.8 convolution_add_fusion
  171.2 1.1 constant_dynamic-slice_fusion
  172.3 55.0 %all-gather.4.cloned.1.call-done = bf16[1024,1024]{1,0:T(8,128)(2,1)} async-done(((bf16[128,1024]{1,0:T(8,128)(2,1)}), bf16[1024,1024]{1,0:T(8,128)(2,1)}) %all-gather.4.cloned.1.call-update) | async-done | bytes 2097168 | tf_op jit(solution)/shard_map/all_gather | solution.py:191
  227.2 3.3 %fusion.4 = f32[256,1024]{1,0:T(8,128)} fusion(bf16[1024,256]{0,1:T(8,128)(2,1)S(1)} %bitcast.55, bf16[1024,1024]{1,0:T(8,128)(2,1)} %all-gather.4.cloned.1.call-done), kind=kOutput, calls=%fused_computation.31 | convolution fusion | flops 536870912 | bytes 3670016 | tf_op jit(solution)/shard_map/dot_general | solution.py:200
  230.6 1.6 convert_element_type.47
  232.2 20.1 %reduce-scatter.5.cloned.1.call-done = f32[64,1024]{1,0:T(8,128)} async-done(((f32[256,1024]{1,0:T(8,128)}), f32[64,1024]{1,0:T(8,128)}) %reduce-scatter.5.cloned.1.call-update) | async-done | bytes 262160 | tf_op jit(solution)/shard_map/reduce_scatter | solution.py:203
  252.3 1.7 fusion.3
  (35 shorter events, 0.6 us)
Async XLA Ops:
  8.0 2.4 copy-start
  8.0 4.5 %copy-start.3 = (bf16[128,2048]{1,0:T(8,128)(2,1)S(1)}, bf16[128,2048]{1,0:T(8,128)(2,1)}, u32[]{:S(2)}) copy-start(bf16[128,2048]{1,0:T(8,128)(2,1)} %param.8) | copy-start | bytes 1572868
  8.0 163.1 %all-gather.6.cloned.1.call-start = ((), (), s32[]{:S(2)}) async-start(), calls=%async_computation.5 | async-start | bytes 4718592 | tf_op jit(solution)/shard_map/all_gather | solution.py:161
  10.3 21.7 %copy-start.5 = (s32[16,5]{0,1:T(8,128)S(1)}, s32[16,5]{0,1:T(8,128)}, u32[]{:S(2)}) copy-start(s32[16,5]{0,1:T(8,128)} %param.12) | copy-start | bytes 964
  10.3 216.9 %all-gather.4.cloned.1.call-start = ((), (), s32[]{:S(2)}) async-start(), calls=%async_computation.3 | async-start | bytes 2359296 | tf_op jit(solution)/shard_map/all_gather | solution.py:191
  10.4 2.1 copy-start.1
  13.5 19.2 %collective-permute-start = (bf16[2,128,512]{1,2,0:T(8,128)(2,1)S(1)}, bf16[2,128,512]{1,2,0:T(8,128)(2,1)}, u32[]{:S(2)}, u32[]{:S(2)}) collective-permute-start(bf16[2,128,512]{1,2,0:T(8,128)(2,1)S(1)} %pad_maximum_fusion), channel_id=1, source_target_pairs={{0,16},{4,20},{8,24},{12,28},{16,32},{20,36},{24,40},{28,44},{32,4... | collective-permute-start | bytes 786440 | tf_op jit(solution)/shard_map/ppermute | solution.py:18
  19.4 16.4 %collective-permute-start.1 = (bf16[2,128,512]{1,2,0:T(8,128)(2,1)S(1)}, bf16[2,128,512]{1,2,0:T(8,128)(2,1)}, u32[]{:S(2)}, u32[]{:S(2)}) collective-permute-start(bf16[2,128,512]{1,2,0:T(8,128)(2,1)S(1)} %pad_maximum_fusion), channel_id=1, source_target_pairs={{0,12},{4,16},{8,20},{12,24},{16,28},{20,32},{24,36},{28,40},{32,4... | collective-permute-start | bytes 786440 | tf_op jit(solution)/shard_map/ppermute | solution.py:18
  25.2 21.2 %collective-permute-start.2 = (bf16[2,128,512]{1,2,0:T(8,128)(2,1)S(1)}, bf16[2,128,512]{1,2,0:T(8,128)(2,1)S(1)}, u32[]{:S(2)}, u32[]{:S(2)}) collective-permute-start(bf16[2,128,512]{1,2,0:T(8,128)(2,1)S(1)} %pad_maximum_fusion), channel_id=1, source_target_pairs={{0,8},{4,12},{8,16},{12,20},{16,24},{20,28},{24,32},{28,36},{32,40... | collective-permute-start | bytes 786440 | tf_op jit(solution)/shard_map/ppermute | solution.py:18
  27.4 21.0 %collective-permute-start.3 = (bf16[2,128,512]{1,2,0:T(8,128)(2,1)S(1)}, bf16[2,128,512]{1,2,0:T(8,128)(2,1)S(1)}, u32[]{:S(2)}, u32[]{:S(2)}) collective-permute-start(bf16[2,128,512]{1,2,0:T(8,128)(2,1)S(1)} %pad_maximum_fusion), channel_id=1, source_target_pairs={{0,4},{4,8},{8,12},{12,16},{16,20},{20,24},{24,28},{28,32},{32,36}... | collective-permute-start | bytes 786440 | tf_op jit(solution)/shard_map/ppermute | solution.py:18
  30.7 19.2 %collective-permute-start.4 = (bf16[2,128,512]{1,2,0:T(8,128)(2,1)S(1)}, bf16[2,128,512]{1,2,0:T(8,128)(2,1)S(1)}, u32[]{:S(2)}, u32[]{:S(2)}) collective-permute-start(bf16[2,128,512]{1,2,0:T(8,128)(2,1)S(1)} %pad_maximum_fusion), channel_id=1, source_target_pairs={{4,0},{8,4},{12,8},{16,12},{20,16},{24,20},{28,24},{32,28},{36,32}... | collective-permute-start | bytes 786440 | tf_op jit(solution)/shard_map/ppermute | solution.py:18
  32.7 17.9 %collective-permute-start.5 = (bf16[2,128,512]{1,2,0:T(8,128)(2,1)S(1)}, bf16[2,128,512]{1,2,0:T(8,128)(2,1)S(1)}, u32[]{:S(2)}, u32[]{:S(2)}) collective-permute-start(bf16[2,128,512]{1,2,0:T(8,128)(2,1)S(1)} %pad_maximum_fusion), channel_id=1, source_target_pairs={{8,0},{12,4},{16,8},{20,12},{24,16},{28,20},{32,24},{36,28},{40,32... | collective-permute-start | bytes 786440 | tf_op jit(solution)/shard_map/ppermute | solution.py:18
  35.8 18.8 %collective-permute-start.6 = (bf16[2,128,512]{1,2,0:T(8,128)(2,1)S(1)}, bf16[2,128,512]{1,2,0:T(8,128)(2,1)S(1)}, u32[]{:S(2)}, u32[]{:S(2)}) collective-permute-start(bf16[2,128,512]{1,2,0:T(8,128)(2,1)S(1)} %pad_maximum_fusion), channel_id=1, source_target_pairs={{12,0},{16,4},{20,8},{24,12},{28,16},{32,20},{36,24},{40,28},{44,3... | collective-permute-start | bytes 786440 | tf_op jit(solution)/shard_map/ppermute | solution.py:18
  46.4 14.3 %collective-permute-start.7 = (bf16[2,128,512]{1,2,0:T(8,128)(2,1)S(1)}, bf16[2,128,512]{1,2,0:T(8,128)(2,1)S(1)}, u32[]{:S(2)}, u32[]{:S(2)}) collective-permute-start(bf16[2,128,512]{1,2,0:T(8,128)(2,1)S(1)} %pad_maximum_fusion), channel_id=1, source_target_pairs={{16,0},{20,4},{24,8},{28,12},{32,16},{36,20},{40,24},{44,28},{48,3... | collective-permute-start | bytes 786440 | tf_op jit(solution)/shard_map/ppermute | solution.py:18
  119.6 46.8 %copy-start.4 = (f32[2,128,512]{2,1,0:T(8,128)S(1)}, f32[2,128,512]{2,1,0:T(8,128)}, u32[]{:S(2)}) copy-start(f32[2,128,512]{2,1,0:T(8,128)} %get-tuple-element.11) | copy-start | bytes 1572868
  121.4 19.1 %collective-permute-start.10 = (bf16[2,128,512]{2,1,0:T(8,128)(2,1)S(1)}, bf16[2,128,512]{2,1,0:T(8,128)(2,1)S(1)}, u32[]{:S(2)}, u32[]{:S(2)}) collective-permute-start(bf16[2,128,512]{2,1,0:T(8,128)(2,1)S(1)} %get-tuple-element.19), channel_id=1, source_target_pairs={{8,0},{12,4},{16,8},{20,12},{24,16},{28,20},{32,24},{36,28},{40,32... | collective-permute-start | bytes 786440 | tf_op jit(solution)/shard_map/ppermute | solution.py:18
  122.7 26.5 %collective-permute-start.11 = (bf16[2,128,512]{2,1,0:T(8,128)(2,1)S(1)}, bf16[2,128,512]{2,1,0:T(8,128)(2,1)S(1)}, u32[]{:S(2)}, u32[]{:S(2)}) collective-permute-start(bf16[2,128,512]{2,1,0:T(8,128)(2,1)S(1)} %get-tuple-element.18), channel_id=1, source_target_pairs={{4,0},{8,4},{12,8},{16,12},{20,16},{24,20},{28,24},{32,28},{36,32}... | collective-permute-start | bytes 786440 | tf_op jit(solution)/shard_map/ppermute | solution.py:18
  124.0 26.5 %collective-permute-start.12 = (bf16[2,128,512]{2,1,0:T(8,128)(2,1)S(1)}, bf16[2,128,512]{2,1,0:T(8,128)(2,1)S(1)}, u32[]{:S(2)}, u32[]{:S(2)}) collective-permute-start(bf16[2,128,512]{2,1,0:T(8,128)(2,1)S(1)} %get-tuple-element.17), channel_id=1, source_target_pairs={{0,4},{4,8},{8,12},{12,16},{16,20},{20,24},{24,28},{28,32},{32,36}... | collective-permute-start | bytes 786440 | tf_op jit(solution)/shard_map/ppermute | solution.py:18
  130.0 21.8 %collective-permute-start.13 = (bf16[2,128,512]{2,1,0:T(8,128)(2,1)S(1)}, bf16[2,128,512]{2,1,0:T(8,128)(2,1)S(1)}, u32[]{:S(2)}, u32[]{:S(2)}) collective-permute-start(bf16[2,128,512]{2,1,0:T(8,128)(2,1)S(1)} %get-tuple-element.16), channel_id=1, source_target_pairs={{0,8},{4,12},{8,16},{12,20},{16,24},{20,28},{24,32},{28,36},{32,40... | collective-permute-start | bytes 786440 | tf_op jit(solution)/shard_map/ppermute | solution.py:18
  134.6 17.2 %collective-permute-start.14 = (bf16[2,128,512]{2,1,0:T(8,128)(2,1)S(1)}, bf16[2,128,512]{2,1,0:T(8,128)(2,1)S(1)}, u32[]{:S(2)}, u32[]{:S(2)}) collective-permute-start(bf16[2,128,512]{2,1,0:T(8,128)(2,1)S(1)} %get-tuple-element.15), channel_id=1, source_target_pairs={{0,12},{4,16},{8,20},{12,24},{16,28},{20,32},{24,36},{28,40},{32,4... | collective-permute-start | bytes 786440 | tf_op jit(solution)/shard_map/ppermute | solution.py:18
  140.5 14.4 %collective-permute-start.15 = (bf16[2,128,512]{2,1,0:T(8,128)(2,1)S(1)}, bf16[2,128,512]{2,1,0:T(8,128)(2,1)S(1)}, u32[]{:S(2)}, u32[]{:S(2)}) collective-permute-start(bf16[2,128,512]{2,1,0:T(8,128)(2,1)S(1)} %get-tuple-element.14), channel_id=1, source_target_pairs={{0,16},{4,20},{8,24},{12,28},{16,32},{20,36},{24,40},{28,44},{32,4... | collective-permute-start | bytes 786440 | tf_op jit(solution)/shard_map/ppermute | solution.py:18
  149.2 17.3 %collective-permute-start.8 = (bf16[2,128,512]{2,1,0:T(8,128)(2,1)S(1)}, bf16[2,128,512]{2,1,0:T(8,128)(2,1)S(1)}, u32[]{:S(2)}, u32[]{:S(2)}) collective-permute-start(bf16[2,128,512]{2,1,0:T(8,128)(2,1)S(1)} %get-tuple-element.13), channel_id=1, source_target_pairs={{16,0},{20,4},{24,8},{28,12},{32,16},{36,20},{40,24},{44,28},{48,3... | collective-permute-start | bytes 786440 | tf_op jit(solution)/shard_map/ppermute | solution.py:18
  150.5 16.0 %collective-permute-start.9 = (bf16[2,128,512]{2,1,0:T(8,128)(2,1)S(1)}, bf16[2,128,512]{2,1,0:T(8,128)(2,1)S(1)}, u32[]{:S(2)}, u32[]{:S(2)}) collective-permute-start(bf16[2,128,512]{2,1,0:T(8,128)(2,1)S(1)} %get-tuple-element.20), channel_id=1, source_target_pairs={{12,0},{16,4},{20,8},{24,12},{28,16},{32,20},{36,24},{40,28},{44,3... | collective-permute-start | bytes 786440 | tf_op jit(solution)/shard_map/ppermute | solution.py:18
  167.6 62.9 %reduce-scatter.3.cloned.1.call-start = ((), (), s32[]{:S(2)}) async-start(), calls=%async_computation.2 | async-start | bytes 1310720 | tf_op jit(solution)/shard_map/reduce_scatter | solution.py:187
  167.7 1.6 copy-start.2
  171.1 81.2 %reduce-scatter.5.cloned.1.call-start = ((), (), s32[]{:S(2)}) async-start(), calls=%async_computation.4 | async-start | bytes 1310720 | tf_op jit(solution)/shard_map/reduce_scatter | solution.py:203
Sparse Core Ops, SparseCore 0:
  11.3 100.5 all-gather.5
  167.8 59.4 all-gather.3
Sparse Core Ops, SparseCore 1:
  171.2 27.1 reduce-scatter.2
  230.6 21.6 reduce-scatter.4

commit v10 on v9

--- a/solution.py
+++ b/solution.py
@@ -187,8 +187,8 @@
     encoder_grad = lax.psum_scatter(encoder_terms, "grp", scatter_dimension=1, tiled=True).astype(
         jnp.bfloat16
     )
-    both_grads = jnp.concatenate([rounded[0], rounded[1]], 1)
-    group_grads = lax.all_gather(both_grads, "byx", axis=0, tiled=True)
+    group_keys = lax.all_gather(rounded[0], "byx", axis=0, tiled=True)
+    group_values = lax.all_gather(rounded[1], "byx", axis=0, tiled=True)
     rows = encoder.shape[0]
     slice_rows = model // (outer * inner)
     picked = lax.dynamic_slice_in_dim(
@@ -197,8 +197,13 @@
         1,
         axis=2,
     ).reshape(inner * rows, outer * slice_rows)
-    partial = lax.dot_general(
-        picked, group_grads, (((0,), (0,)), ((), ())), preferred_element_type=jnp.float32
+    contract_rows = (((0,), (0,)), ((), ()))
+    partial = jnp.concatenate(
+        [
+            lax.dot_general(picked, group_keys, contract_rows, preferred_element_type=jnp.float32),
+            lax.dot_general(picked, group_values, contract_rows, preferred_element_type=jnp.float32),
+        ],
+        1,
     )
     weight_rows = lax.psum_scatter(partial, "bz", scatter_dimension=0, tiled=True)
     return (

time: 262 us -> 300 us (1.15)
  waiting for transfers between devices: 106 us -> 138 us
  starting transfers between devices: 52.8 us -> 58.6 us
    all_gather x1 -> x2, waiting for transfers between devices: 55 us -> 90.4 us  [the longest x1 46.7 us: on_device(): group_keys = lax.all_gather(rounded[0], 'byx', axis=0, tiled=True)]
    ppermute x16, starting transfers between devices: 52.7 us -> 58.3 us  [passed_along(): return lax.ppermute(value, axis, pairs)]
    ppermute x16, waiting for transfers between devices: 30.9 us -> 26.1 us  [passed_along(): return lax.ppermute(value, axis, pairs)]
  transfers between devices with their start and end apart: 20 -> 21, of which waited for: 8 -> 9; matrix products, arithmetic and copies ran while one was open for 11% -> 10% of each run, Pallas kernels for 21% -> 18%
where the time goes in v10:
time: 300 us; the launch traced here: 299 us
  waiting for transfers between devices  138 us (46%)
  starting transfers between devices  58.6 us (20%)
  Pallas kernels  52.9 us (18%)
  local copies, waits for them, and re-layouts  20.3 us (7%)
  between operations  15.5 us (5%)
  matrix products  9.03 us (3%)
  other arithmetic  4.4 us (1%)
    ppermute x16, starting transfers between devices, passed_along(): return lax.ppermute(value, axis, pairs)  58.3 us
    pallas_call x1, Pallas kernels, attention(): pl.pallas_call(attention_kernel, grid_spec=grid_spec, out_shape=[jax.Shap...  52.9 us
    all_gather x1, waiting for transfers between devices, on_device(): group_keys = lax.all_gather(rounded[0], 'byx', axis=0, tiled=True)  46.7 us
    all_gather x1, waiting for transfers between devices, on_device(): group_values = lax.all_gather(rounded[1], 'byx', axis=0, tiled=True)  43.7 us
    ppermute x16, waiting for transfers between devices, passed_along(): return lax.ppermute(value, axis, pairs)  26.1 us
    reduce_scatter x1, waiting for transfers between devices, on_device(): lax.psum_scatter(partial, 'bz', scatter_dimension=0, tiled=True)  21 us
    unnamed x21, local copies, waits for them, and re-layouts  10.1 us
  transfers between devices with their start and end apart: 21, of which 9 were waited for; matrix products, arithmetic and copies ran while one was open for 10% of the time, Pallas kernels for 18%

profile of v10, /device:TPU:0, one launch (start us, length us, event | category | flops | bytes accessed | tf_op | source)
XLA Modules:
  0.0 299.0 jit_solution(9959127148701265359)
XLA Ops:
  8.1 2.2 copy.26
  10.4 2.1 fusion
  12.5 1.0 fusion.1
  13.5 5.9 %collective-permute-start = (bf16[2,128,512]{1,2,0:T(8,128)(2,1)S(1)}, bf16[2,128,512]{1,2,0:T(8,128)(2,1)}, u32[]{:S(2)}, u32[]{:S(2)}) collective-permute-start(bf16[2,128,512]{1,2,0:T(8,128)(2,1)S(1)} %pad_maximum_fusion.1), channel_id=1, source_target_pairs={{0,16},{4,20},{8,24},{12,28},{16,32},{20,36},{24,40},{28,44},{32,4... | collective-permute-start | bytes 786440 | tf_op jit(solution)/shard_map/ppermute | solution.py:18
  19.4 5.8 %collective-permute-start.1 = (bf16[2,128,512]{1,2,0:T(8,128)(2,1)S(1)}, bf16[2,128,512]{1,2,0:T(8,128)(2,1)}, u32[]{:S(2)}, u32[]{:S(2)}) collective-permute-start(bf16[2,128,512]{1,2,0:T(8,128)(2,1)S(1)} %pad_maximum_fusion.1), channel_id=1, source_target_pairs={{0,12},{4,16},{8,20},{12,24},{16,28},{20,32},{24,36},{28,40},{32,4... | collective-permute-start | bytes 786440 | tf_op jit(solution)/shard_map/ppermute | solution.py:18
  25.2 2.2 collective-permute-start.2
  27.4 3.3 %collective-permute-start.3 = (bf16[2,128,512]{1,2,0:T(8,128)(2,1)S(1)}, bf16[2,128,512]{1,2,0:T(8,128)(2,1)S(1)}, u32[]{:S(2)}, u32[]{:S(2)}) collective-permute-start(bf16[2,128,512]{1,2,0:T(8,128)(2,1)S(1)} %pad_maximum_fusion.1), channel_id=1, source_target_pairs={{0,4},{4,8},{8,12},{12,16},{16,20},{20,24},{24,28},{28,32},{32,36}... | collective-permute-start | bytes 786440 | tf_op jit(solution)/shard_map/ppermute | solution.py:18
  30.7 1.3 collective-permute-start.4
  32.7 1.3 collective-permute-start.5
  34.0 1.7 bitcast_dynamic-update-slice_fusion.8
  35.8 1.3 collective-permute-start.6
  37.1 1.7 bitcast_dynamic-update-slice_fusion.7
  38.8 7.5 %collective-permute-done.2 = bf16[2,128,512]{1,2,0:T(8,128)(2,1)S(1)} collective-permute-done((bf16[2,128,512]{1,2,0:T(8,128)(2,1)S(1)}, bf16[2,128,512]{1,2,0:T(8,128)(2,1)S(1)}, u32[]{:S(2)}, u32[]{:S(2)}) %collective-permute-start.2) | collective-permute-done | bytes 262176 | tf_op jit(solution)/shard_map/ppermute | solution.py:18
  46.3 1.3 collective-permute-start.7
  48.3 0.7 bitcast_dynamic-update-slice_fusion.5
  49.1 0.7 bitcast_dynamic-update-slice_fusion.4
  49.8 0.7 bitcast_dynamic-update-slice_fusion.3
  50.5 0.7 bitcast_dynamic-update-slice_fusion.2
  51.3 3.3 %collective-permute-done.6 = bf16[2,128,512]{1,2,0:T(8,128)(2,1)S(1)} collective-permute-done((bf16[2,128,512]{1,2,0:T(8,128)(2,1)S(1)}, bf16[2,128,512]{1,2,0:T(8,128)(2,1)S(1)}, u32[]{:S(2)}, u32[]{:S(2)}) %collective-permute-start.6) | collective-permute-done | bytes 262176 | tf_op jit(solution)/shard_map/ppermute | solution.py:18
  54.6 0.7 bitcast_dynamic-update-slice_fusion.1
  55.3 5.3 %collective-permute-done.7 = bf16[2,128,512]{1,2,0:T(8,128)(2,1)S(1)} collective-permute-done((bf16[2,128,512]{1,2,0:T(8,128)(2,1)S(1)}, bf16[2,128,512]{1,2,0:T(8,128)(2,1)S(1)}, u32[]{:S(2)}, u32[]{:S(2)}) %collective-permute-start.7) | collective-permute-done | bytes 262176 | tf_op jit(solution)/shard_map/ppermute | solution.py:18
  60.6 0.7 bitcast_dynamic-update-slice_fusion
  61.3 4.4 %copy.25.stock_ref = bf16[9,2,128,512]{3,2,1,0:T(8,128)(2,1)} copy(bf16[9,2,128,512]{2,3,1,0:T(8,128)(2,1)} %bitcast_dynamic-update-slice_fusion) | data formatting | bytes 4718592 | tf_op jit(solution)/shard_map/stack | solution.py:173
  65.7 52.9 %shard_map.110 = (bf16[2048,512]{1,0:T(8,128)(2,1)}, bf16[2048,512]{1,0:T(8,128)(2,1)}, f32[2,128,512]{2,1,0:T(8,128)}, bf16[9,2,128,512]{3,2,1,0:T(8,128)(2,1)}) custom-call(s32[16,5]{1,0:T(8,128)} %broadcast_subtract_fusion.slots_ref, s32[16]{0:T(128)} %counts_ref.1, bf16[2048,512]{1,0:T(8,128)(2,1)} %q_ref.1, bf16[2048,512]{1,0:T(8,128)(2,1)} %g_ref.1, ...), custom_call_target="tpu_custom_call" | custom-call | flops 9663676416 | bytes 17825792 | tf_op jit(solution)/shard_map/pallas_call | solution.py:137
  118.6 1.7 slice_bitcast_fusion.7
  120.3 1.3 collective-permute-start.10
  121.6 1.3 collective-permute-start.11
  122.9 6.1 %collective-permute-start.12 = (bf16[2,128,512]{2,1,0:T(8,128)(2,1)S(1)}, bf16[2,128,512]{2,1,0:T(8,128)(2,1)S(1)}, u32[]{:S(2)}, u32[]{:S(2)}) collective-permute-start(bf16[2,128,512]{2,1,0:T(8,128)(2,1)S(1)} %get-tuple-element.17), channel_id=1, source_target_pairs={{0,4},{4,8},{8,12},{12,16},{16,20},{20,24},{24,28},{28,32},{32,36}... | collective-permute-start | bytes 786440 | tf_op jit(solution)/shard_map/ppermute | solution.py:18
  129.0 6.4 %collective-permute-start.13 = (bf16[2,128,512]{2,1,0:T(8,128)(2,1)S(1)}, bf16[2,128,512]{2,1,0:T(8,128)(2,1)S(1)}, u32[]{:S(2)}, u32[]{:S(2)}) collective-permute-start(bf16[2,128,512]{2,1,0:T(8,128)(2,1)S(1)} %get-tuple-element.16), channel_id=1, source_target_pairs={{0,8},{4,12},{8,16},{12,20},{16,24},{20,28},{24,32},{28,36},{32,40... | collective-permute-start | bytes 786440 | tf_op jit(solution)/shard_map/ppermute | solution.py:18
  135.4 7.3 %collective-permute-start.14 = (bf16[2,128,512]{2,1,0:T(8,128)(2,1)S(1)}, bf16[2,128,512]{2,1,0:T(8,128)(2,1)S(1)}, u32[]{:S(2)}, u32[]{:S(2)}) collective-permute-start(bf16[2,128,512]{2,1,0:T(8,128)(2,1)S(1)} %get-tuple-element.15), channel_id=1, source_target_pairs={{0,12},{4,16},{8,20},{12,24},{16,28},{20,32},{24,36},{28,40},{32,4... | collective-permute-start | bytes 786440 | tf_op jit(solution)/shard_map/ppermute | solution.py:18
  142.7 11.1 %collective-permute-start.15 = (bf16[2,128,512]{2,1,0:T(8,128)(2,1)S(1)}, bf16[2,128,512]{2,1,0:T(8,128)(2,1)S(1)}, u32[]{:S(2)}, u32[]{:S(2)}) collective-permute-start(bf16[2,128,512]{2,1,0:T(8,128)(2,1)S(1)} %get-tuple-element.14), channel_id=1, source_target_pairs={{0,16},{4,20},{8,24},{12,28},{16,32},{20,36},{24,40},{28,44},{32,4... | collective-permute-start | bytes 786440 | tf_op jit(solution)/shard_map/ppermute | solution.py:18
  153.9 1.3 collective-permute-start.8
  155.2 1.3 collective-permute-start.9
  156.5 1.2 collective-permute-done.15
  157.7 8.6 %collective-permute-done.8 = bf16[2,128,512]{2,1,0:T(8,128)(2,1)S(1)} collective-permute-done((bf16[2,128,512]{2,1,0:T(8,128)(2,1)S(1)}, bf16[2,128,512]{2,1,0:T(8,128)(2,1)S(1)}, u32[]{:S(2)}, u32[]{:S(2)}) %collective-permute-start.8) | collective-permute-done | bytes 262176 | tf_op jit(solution)/shard_map/ppermute | solution.py:18
  166.6 0.7 fusion.12
  168.2 0.8 fusion.7
  169.0 0.8 copy-done.2
  169.8 1.8 convolution_add_fusion
  171.7 1.1 constant_dynamic-slice_fusion
  172.8 43.7 %all-gather.11.cloned.1.call-done = bf16[1,1024,512]{2,1,0:T(8,128)(2,1)} async-done(((bf16[1,128,512]{2,1,0:T(8,128)(2,1)}), bf16[1,1024,512]{2,1,0:T(8,128)(2,1)}) %all-gather.11.cloned.1.call-update) | async-done | bytes 1048592 | tf_op jit(solution)/shard_map/all_gather | solution.py:191
  216.5 1.7 fusion.2
  218.2 46.7 %all-gather.9.cloned.1.call-done = bf16[1,1024,512]{2,1,0:T(8,128)(2,1)} async-done(((bf16[1,128,512]{2,1,0:T(8,128)(2,1)}), bf16[1,1024,512]{2,1,0:T(8,128)(2,1)}) %all-gather.9.cloned.1.call-update) | async-done | bytes 1048592 | tf_op jit(solution)/shard_map/all_gather | solution.py:190
  264.9 1.7 fusion.4
  266.5 1.1 pad_maximum_fusion
  267.6 1.6 convert_element_type.47
  269.3 21.0 %reduce-scatter.5.cloned.1.call-done = f32[64,1024]{1,0:T(8,128)} async-done(((f32[256,1024]{1,0:T(8,128)}), f32[64,1024]{1,0:T(8,128)}) %reduce-scatter.5.cloned.1.call-update) | async-done | bytes 262160 | tf_op jit(solution)/shard_map/reduce_scatter | solution.py:208
  290.2 1.7 fusion.11
  (39 shorter events, 3.0 us)
Async XLA Ops:
  8.0 2.4 copy-start
  8.0 4.5 %copy-start.3 = (bf16[128,2048]{1,0:T(8,128)(2,1)S(1)}, bf16[128,2048]{1,0:T(8,128)(2,1)}, u32[]{:S(2)}) copy-start(bf16[128,2048]{1,0:T(8,128)(2,1)} %param.8) | copy-start | bytes 1572868
  8.0 163.7 %all-gather.7.cloned.1.call-start = ((), (), s32[]{:S(2)}) async-start(), calls=%async_computation.4 | async-start | bytes 4718592 | tf_op jit(solution)/shard_map/all_gather | solution.py:161
  10.3 21.7 %copy-start.5 = (s32[16,5]{0,1:T(8,128)S(1)}, s32[16,5]{0,1:T(8,128)}, u32[]{:S(2)}) copy-start(s32[16,5]{0,1:T(8,128)} %param.12) | copy-start | bytes 964
  10.3 206.2 %all-gather.11.cloned.1.call-start = ((), (), s32[]{:S(2)}) async-start(), calls=%async_computation.6 | async-start | bytes 1179648 | tf_op jit(solution)/shard_map/all_gather | solution.py:191
  10.4 2.1 copy-start.1
  13.5 19.2 %collective-permute-start = (bf16[2,128,512]{1,2,0:T(8,128)(2,1)S(1)}, bf16[2,128,512]{1,2,0:T(8,128)(2,1)}, u32[]{:S(2)}, u32[]{:S(2)}) collective-permute-start(bf16[2,128,512]{1,2,0:T(8,128)(2,1)S(1)} %pad_maximum_fusion.1), channel_id=1, source_target_pairs={{0,16},{4,20},{8,24},{12,28},{16,32},{20,36},{24,40},{28,44},{32,4... | collective-permute-start | bytes 786440 | tf_op jit(solution)/shard_map/ppermute | solution.py:18
  19.4 16.4 %collective-permute-start.1 = (bf16[2,128,512]{1,2,0:T(8,128)(2,1)S(1)}, bf16[2,128,512]{1,2,0:T(8,128)(2,1)}, u32[]{:S(2)}, u32[]{:S(2)}) collective-permute-start(bf16[2,128,512]{1,2,0:T(8,128)(2,1)S(1)} %pad_maximum_fusion.1), channel_id=1, source_target_pairs={{0,12},{4,16},{8,20},{12,24},{16,28},{20,32},{24,36},{28,40},{32,4... | collective-permute-start | bytes 786440 | tf_op jit(solution)/shard_map/ppermute | solution.py:18
  25.2 21.2 %collective-permute-start.2 = (bf16[2,128,512]{1,2,0:T(8,128)(2,1)S(1)}, bf16[2,128,512]{1,2,0:T(8,128)(2,1)S(1)}, u32[]{:S(2)}, u32[]{:S(2)}) collective-permute-start(bf16[2,128,512]{1,2,0:T(8,128)(2,1)S(1)} %pad_maximum_fusion.1), channel_id=1, source_target_pairs={{0,8},{4,12},{8,16},{12,20},{16,24},{20,28},{24,32},{28,36},{32,40... | collective-permute-start | bytes 786440 | tf_op jit(solution)/shard_map/ppermute | solution.py:18
  27.4 21.0 %collective-permute-start.3 = (bf16[2,128,512]{1,2,0:T(8,128)(2,1)S(1)}, bf16[2,128,512]{1,2,0:T(8,128)(2,1)S(1)}, u32[]{:S(2)}, u32[]{:S(2)}) collective-permute-start(bf16[2,128,512]{1,2,0:T(8,128)(2,1)S(1)} %pad_maximum_fusion.1), channel_id=1, source_target_pairs={{0,4},{4,8},{8,12},{12,16},{16,20},{20,24},{24,28},{28,32},{32,36}... | collective-permute-start | bytes 786440 | tf_op jit(solution)/shard_map/ppermute | solution.py:18
  30.7 19.1 %collective-permute-start.4 = (bf16[2,128,512]{1,2,0:T(8,128)(2,1)S(1)}, bf16[2,128,512]{1,2,0:T(8,128)(2,1)S(1)}, u32[]{:S(2)}, u32[]{:S(2)}) collective-permute-start(bf16[2,128,512]{1,2,0:T(8,128)(2,1)S(1)} %pad_maximum_fusion.1), channel_id=1, source_target_pairs={{4,0},{8,4},{12,8},{16,12},{20,16},{24,20},{28,24},{32,28},{36,32}... | collective-permute-start | bytes 786440 | tf_op jit(solution)/shard_map/ppermute | solution.py:18
  32.7 17.8 %collective-permute-start.5 = (bf16[2,128,512]{1,2,0:T(8,128)(2,1)S(1)}, bf16[2,128,512]{1,2,0:T(8,128)(2,1)S(1)}, u32[]{:S(2)}, u32[]{:S(2)}) collective-permute-start(bf16[2,128,512]{1,2,0:T(8,128)(2,1)S(1)} %pad_maximum_fusion.1), channel_id=1, source_target_pairs={{8,0},{12,4},{16,8},{20,12},{24,16},{28,20},{32,24},{36,28},{40,32... | collective-permute-start | bytes 786440 | tf_op jit(solution)/shard_map/ppermute | solution.py:18
  35.8 18.8 %collective-permute-start.6 = (bf16[2,128,512]{1,2,0:T(8,128)(2,1)S(1)}, bf16[2,128,512]{1,2,0:T(8,128)(2,1)S(1)}, u32[]{:S(2)}, u32[]{:S(2)}) collective-permute-start(bf16[2,128,512]{1,2,0:T(8,128)(2,1)S(1)} %pad_maximum_fusion.1), channel_id=1, source_target_pairs={{12,0},{16,4},{20,8},{24,12},{28,16},{32,20},{36,24},{40,28},{44,3... | collective-permute-start | bytes 786440 | tf_op jit(solution)/shard_map/ppermute | solution.py:18
  46.3 14.3 %collective-permute-start.7 = (bf16[2,128,512]{1,2,0:T(8,128)(2,1)S(1)}, bf16[2,128,512]{1,2,0:T(8,128)(2,1)S(1)}, u32[]{:S(2)}, u32[]{:S(2)}) collective-permute-start(bf16[2,128,512]{1,2,0:T(8,128)(2,1)S(1)} %pad_maximum_fusion.1), channel_id=1, source_target_pairs={{16,0},{20,4},{24,8},{28,12},{32,16},{36,20},{40,24},{44,28},{48,3... | collective-permute-start | bytes 786440 | tf_op jit(solution)/shard_map/ppermute | solution.py:18
  118.6 47.6 %copy-start.4 = (f32[2,128,512]{2,1,0:T(8,128)S(1)}, f32[2,128,512]{2,1,0:T(8,128)}, u32[]{:S(2)}) copy-start(f32[2,128,512]{2,1,0:T(8,128)} %get-tuple-element.11) | copy-start | bytes 1572868
  120.3 22.4 %collective-permute-start.10 = (bf16[2,128,512]{2,1,0:T(8,128)(2,1)S(1)}, bf16[2,128,512]{2,1,0:T(8,128)(2,1)S(1)}, u32[]{:S(2)}, u32[]{:S(2)}) collective-permute-start(bf16[2,128,512]{2,1,0:T(8,128)(2,1)S(1)} %get-tuple-element.19), channel_id=1, source_target_pairs={{8,0},{12,4},{16,8},{20,12},{24,16},{28,20},{32,24},{36,28},{40,32... | collective-permute-start | bytes 786440 | tf_op jit(solution)/shard_map/ppermute | solution.py:18
  121.6 32.2 %collective-permute-start.11 = (bf16[2,128,512]{2,1,0:T(8,128)(2,1)S(1)}, bf16[2,128,512]{2,1,0:T(8,128)(2,1)S(1)}, u32[]{:S(2)}, u32[]{:S(2)}) collective-permute-start(bf16[2,128,512]{2,1,0:T(8,128)(2,1)S(1)} %get-tuple-element.18), channel_id=1, source_target_pairs={{4,0},{8,4},{12,8},{16,12},{20,16},{24,20},{28,24},{32,28},{36,32}... | collective-permute-start | bytes 786440 | tf_op jit(solution)/shard_map/ppermute | solution.py:18
  122.9 32.2 %collective-permute-start.12 = (bf16[2,128,512]{2,1,0:T(8,128)(2,1)S(1)}, bf16[2,128,512]{2,1,0:T(8,128)(2,1)S(1)}, u32[]{:S(2)}, u32[]{:S(2)}) collective-permute-start(bf16[2,128,512]{2,1,0:T(8,128)(2,1)S(1)} %get-tuple-element.17), channel_id=1, source_target_pairs={{0,4},{4,8},{8,12},{12,16},{16,20},{20,24},{24,28},{28,32},{32,36}... | collective-permute-start | bytes 786440 | tf_op jit(solution)/shard_map/ppermute | solution.py:18
  129.0 27.4 %collective-permute-start.13 = (bf16[2,128,512]{2,1,0:T(8,128)(2,1)S(1)}, bf16[2,128,512]{2,1,0:T(8,128)(2,1)S(1)}, u32[]{:S(2)}, u32[]{:S(2)}) collective-permute-start(bf16[2,128,512]{2,1,0:T(8,128)(2,1)S(1)} %get-tuple-element.16), channel_id=1, source_target_pairs={{0,8},{4,12},{8,16},{12,20},{16,24},{20,28},{24,32},{28,36},{32,40... | collective-permute-start | bytes 786440 | tf_op jit(solution)/shard_map/ppermute | solution.py:18
  135.4 21.1 %collective-permute-start.14 = (bf16[2,128,512]{2,1,0:T(8,128)(2,1)S(1)}, bf16[2,128,512]{2,1,0:T(8,128)(2,1)S(1)}, u32[]{:S(2)}, u32[]{:S(2)}) collective-permute-start(bf16[2,128,512]{2,1,0:T(8,128)(2,1)S(1)} %get-tuple-element.15), channel_id=1, source_target_pairs={{0,12},{4,16},{8,20},{12,24},{16,28},{20,32},{24,36},{28,40},{32,4... | collective-permute-start | bytes 786440 | tf_op jit(solution)/shard_map/ppermute | solution.py:18
  142.7 15.0 %collective-permute-start.15 = (bf16[2,128,512]{2,1,0:T(8,128)(2,1)S(1)}, bf16[2,128,512]{2,1,0:T(8,128)(2,1)S(1)}, u32[]{:S(2)}, u32[]{:S(2)}) collective-permute-start(bf16[2,128,512]{2,1,0:T(8,128)(2,1)S(1)} %get-tuple-element.14), channel_id=1, source_target_pairs={{0,16},{4,20},{8,24},{12,28},{16,32},{20,36},{24,40},{28,44},{32,4... | collective-permute-start | bytes 786440 | tf_op jit(solution)/shard_map/ppermute | solution.py:18
  153.9 12.4 %collective-permute-start.8 = (bf16[2,128,512]{2,1,0:T(8,128)(2,1)S(1)}, bf16[2,128,512]{2,1,0:T(8,128)(2,1)S(1)}, u32[]{:S(2)}, u32[]{:S(2)}) collective-permute-start(bf16[2,128,512]{2,1,0:T(8,128)(2,1)S(1)} %get-tuple-element.13), channel_id=1, source_target_pairs={{16,0},{20,4},{24,8},{28,12},{32,16},{36,20},{40,24},{44,28},{48,3... | collective-permute-start | bytes 786440 | tf_op jit(solution)/shard_map/ppermute | solution.py:18
  155.2 11.1 %collective-permute-start.9 = (bf16[2,128,512]{2,1,0:T(8,128)(2,1)S(1)}, bf16[2,128,512]{2,1,0:T(8,128)(2,1)S(1)}, u32[]{:S(2)}, u32[]{:S(2)}) collective-permute-start(bf16[2,128,512]{2,1,0:T(8,128)(2,1)S(1)} %get-tuple-element.20), channel_id=1, source_target_pairs={{12,0},{16,4},{20,8},{24,12},{28,16},{32,20},{36,24},{40,28},{44,3... | collective-permute-start | bytes 786440 | tf_op jit(solution)/shard_map/ppermute | solution.py:18
  167.4 97.5 %all-gather.9.cloned.1.call-start = ((), (), s32[]{:S(2)}) async-start(), calls=%async_computation.5 | async-start | bytes 1179648 | tf_op jit(solution)/shard_map/all_gather | solution.py:190
  168.1 99.5 %reduce-scatter.3.cloned.1.call-start = ((), (), s32[]{:S(2)}) async-start(), calls=%async_computation.2 | async-start | bytes 1310720 | tf_op jit(solution)/shard_map/reduce_scatter | solution.py:187
  168.2 1.6 copy-start.2
  171.6 118.6 %reduce-scatter.5.cloned.1.call-start = ((), (), s32[]{:S(2)}) async-start(), calls=%async_computation.3 | async-start | bytes 1310720 | tf_op jit(solution)/shard_map/reduce_scatter | solution.py:208
Sparse Core Ops, SparseCore 0:
  11.3 100.5 all-gather.6
  167.5 48.9 all-gather.10
  219.7 45.0 all-gather.8
Sparse Core Ops, SparseCore 1:
  171.7 22.8 reduce-scatter.2
  267.7 22.5 reduce-scatter.4

commit v11 on v9

--- a/solution.py
+++ b/solution.py
@@ -19,8 +19,8 @@
 
 
 def attention_kernel(
-    slots_ref, counts_ref, q_ref, g_ref, stock_ref, flipped_ref, out_ref, dq_ref, own_ref,
-    sent_ref, acc_ref,
+    slots_ref, counts_ref, q_ref, g_ref, stock_ref, out_ref, dq_ref, own_ref,
+    sent_ref, acc_ref, flipped_ref,
 ):
     factor = HEAD_DIM ** (-0.5)
     step = pl.program_id(0)
@@ -28,6 +28,17 @@
     @pl.when(step == 0)
     def _():
         acc_ref[...] = jnp.zeros_like(acc_ref)
+
+        def flip(s, carry):
+            for kind in range(2):
+                for p in range(stock_ref.shape[3] // LANES):
+                    piece = stock_ref[s, kind, :, pl.ds(p * LANES, LANES)]
+                    flipped_ref[s, kind, pl.ds(p * LANES, LANES), :] = (
+                        piece.astype(jnp.float32).T.astype(flipped_ref.dtype)
+                    )
+            return carry
+
+        lax.fori_loop(0, stock_ref.shape[0], flip, 0)
 
     count = counts_ref[step]
     rows = q_ref.shape[0]
@@ -114,9 +125,8 @@
     rows, cols = stock.shape[2], stock.shape[3]
     blocks = queries.shape[0] // rows
     n_slots = stock.shape[0]
-    flipped = jnp.swapaxes(stock, 2, 3)
     flops = blocks * (cols // LANES) * 2 * 3 * 6 * 2 * rows * LANES * LANES
-    bytes_accessed = 4 * queries.size * 2 + 2 * stock.size * 2 + stock.size * 4
+    bytes_accessed = 4 * queries.size * 2 + stock.size * 2 + stock.size * 4
     grid_spec = pltpu.PrefetchScalarGridSpec(
         num_scalar_prefetch=2,
         grid=(blocks,),
@@ -124,7 +134,6 @@
             pl.BlockSpec((rows, cols), lambda i, s, c: (i, 0)),
             pl.BlockSpec((rows, cols), lambda i, s, c: (i, 0)),
             pl.BlockSpec((n_slots, 2, rows, cols), lambda i, s, c: (0, 0, 0, 0)),
-            pl.BlockSpec((n_slots, 2, cols, rows), lambda i, s, c: (0, 0, 0, 0)),
         ],
         out_specs=[
             pl.BlockSpec((rows, cols), lambda i, s, c: (i, 0)),
@@ -132,7 +141,10 @@
             pl.BlockSpec((2, rows, cols), lambda i, s, c: (0, 0, 0)),
             pl.BlockSpec((n_slots, 2, rows, cols), lambda i, s, c: (0, 0, 0, 0)),
         ],
-        scratch_shapes=[pltpu.VMEM(stock.shape, jnp.float32)],
+        scratch_shapes=[
+            pltpu.VMEM(stock.shape, jnp.float32),
+            pltpu.VMEM((n_slots, 2, cols, rows), stock.dtype),
+        ],
     )
     return pl.pallas_call(
         attention_kernel,
@@ -148,7 +160,7 @@
             flops=flops, transcendentals=blocks * rows * 3 * rows * (cols // HEAD_DIM),
             bytes_accessed=bytes_accessed,
         ),
-    )(slot_ids, counts, queries, out_grad, stock, flipped)
+    )(slot_ids, counts, queries, out_grad, stock)
 
 
 def on_device(

time: 262 us -> 253 us (0.966)
  Pallas kernels: 53.9 us -> 49.4 us
  local copies, waits for them, and re-layouts: 19.7 us -> 15.3 us
    pallas_call x1, Pallas kernels: 53.9 us -> 49.4 us  [attention(): pl.pallas_call(attention_kernel, grid_spec=grid_spec, out_shape=[jax.Shap...]
    another operation x2 -> x1, local copies, waits for them, and re-layouts: 5.11 us -> 0.73 us  [on_device(): stock = jnp.stack(arrived, 0)]
    unnamed x21 -> x19, local copies, waits for them, and re-layouts: 10.1 us -> 10.1 us
  transfers between devices with their start and end apart: 20 -> 20, of which waited for: 8 -> 10; matrix products, arithmetic and copies ran while one was open for 11% -> 9% of each run, Pallas kernels for 21% -> 20%
where the time goes in v11:
time: 253 us; the launch traced here: 251 us
  waiting for transfers between devices  107 us (42%)
  starting transfers between devices  51.2 us (20%)
  Pallas kernels  49.4 us (20%)
  between operations  15.8 us (6%)
  local copies, waits for them, and re-layouts  15.3 us (6%)
  matrix products  8.54 us (3%)
  other arithmetic  4.07 us (2%)
    all_gather x1, waiting for transfers between devices, on_device(): group_grads = lax.all_gather(both_grads, 'byx', axis=0, tiled=True)  55.6 us
    ppermute x16, starting transfers between devices, passed_along(): return lax.ppermute(value, axis, pairs)  51.1 us
    pallas_call x1, Pallas kernels, attention(): pl.pallas_call(attention_kernel, grid_spec=grid_spec, out_shape=[jax.Shap...  49.4 us
    ppermute x16, waiting for transfers between devices, passed_along(): return lax.ppermute(value, axis, pairs)  31.4 us
    reduce_scatter x1, waiting for transfers between devices, on_device(): lax.psum_scatter(partial, 'bz', scatter_dimension=0, tiled=True)  20.1 us
    unnamed x19, local copies, waits for them, and re-layouts  10.1 us
  transfers between devices with their start and end apart: 20, of which 10 were waited for; matrix products, arithmetic and copies ran while one was open for 9% of the time, Pallas kernels for 20%

profile of v11, /device:TPU:0, one launch (start us, length us, event | category | flops | bytes accessed | tf_op | source)
XLA Modules:
  0.0 251.5 jit_solution(8438997877384286456)
XLA Ops:
  8.1 2.2 copy.17
  10.3 2.2 fusion.1
  12.6 0.5 fusion
  13.1 5.9 %collective-permute-start = (bf16[2,128,512]{2,1,0:T(8,128)(2,1)S(1)}, bf16[2,128,512]{2,1,0:T(8,128)(2,1)}, u32[]{:S(2)}, u32[]{:S(2)}) collective-permute-start(bf16[2,128,512]{2,1,0:T(8,128)(2,1)S(1)} %pad_maximum_fusion), channel_id=1, source_target_pairs={{0,16},{4,20},{8,24},{12,28},{16,32},{20,36},{24,40},{28,44},{32,4... | collective-permute-start | bytes 786440 | tf_op jit(solution)/shard_map/ppermute | solution.py:18
  19.0 5.8 %collective-permute-start.1 = (bf16[2,128,512]{2,1,0:T(8,128)(2,1)S(1)}, bf16[2,128,512]{2,1,0:T(8,128)(2,1)}, u32[]{:S(2)}, u32[]{:S(2)}) collective-permute-start(bf16[2,128,512]{2,1,0:T(8,128)(2,1)S(1)} %pad_maximum_fusion), channel_id=1, source_target_pairs={{0,12},{4,16},{8,20},{12,24},{16,28},{20,32},{24,36},{28,40},{32,4... | collective-permute-start | bytes 786440 | tf_op jit(solution)/shard_map/ppermute | solution.py:18
  24.7 2.2 collective-permute-start.2
  26.9 3.3 %collective-permute-start.3 = (bf16[2,128,512]{2,1,0:T(8,128)(2,1)S(1)}, bf16[2,128,512]{2,1,0:T(8,128)(2,1)S(1)}, u32[]{:S(2)}, u32[]{:S(2)}) collective-permute-start(bf16[2,128,512]{2,1,0:T(8,128)(2,1)S(1)} %pad_maximum_fusion), channel_id=1, source_target_pairs={{0,4},{4,8},{8,12},{12,16},{16,20},{20,24},{24,28},{28,32},{32,36}... | collective-permute-start | bytes 786440 | tf_op jit(solution)/shard_map/ppermute | solution.py:18
  30.3 1.3 collective-permute-start.4
  31.7 0.6 broadcast_subtract_fusion.slots_ref
  32.3 1.3 collective-permute-start.5
  33.6 1.7 bitcast_dynamic-update-slice_fusion.8
  35.3 0.4 collective-permute-done.1
  35.6 1.3 collective-permute-start.6
  36.9 1.7 bitcast_dynamic-update-slice_fusion.7
  38.6 5.0 %collective-permute-done.2 = bf16[2,128,512]{2,1,0:T(8,128)(2,1)S(1)} collective-permute-done((bf16[2,128,512]{2,1,0:T(8,128)(2,1)S(1)}, bf16[2,128,512]{2,1,0:T(8,128)(2,1)S(1)}, u32[]{:S(2)}, u32[]{:S(2)}) %collective-permute-start.2) | collective-permute-done | bytes 262176 | tf_op jit(solution)/shard_map/ppermute | solution.py:18
  43.6 1.3 collective-permute-start.7
  44.9 0.7 bitcast_dynamic-update-slice_fusion.6
  45.6 0.7 bitcast_dynamic-update-slice_fusion.5
  46.4 0.7 bitcast_dynamic-update-slice_fusion.4
  47.4 0.7 bitcast_dynamic-update-slice_fusion.3
  48.2 0.7 bitcast_dynamic-update-slice_fusion.2
  48.9 5.3 %collective-permute-done.6 = bf16[2,128,512]{2,1,0:T(8,128)(2,1)S(1)} collective-permute-done((bf16[2,128,512]{2,1,0:T(8,128)(2,1)S(1)}, bf16[2,128,512]{2,1,0:T(8,128)(2,1)S(1)}, u32[]{:S(2)}, u32[]{:S(2)}) %collective-permute-start.6) | collective-permute-done | bytes 262176 | tf_op jit(solution)/shard_map/ppermute | solution.py:18
  54.2 0.7 bitcast_dynamic-update-slice_fusion.1
  54.9 5.3 %collective-permute-done.7 = bf16[2,128,512]{2,1,0:T(8,128)(2,1)S(1)} collective-permute-done((bf16[2,128,512]{2,1,0:T(8,128)(2,1)S(1)}, bf16[2,128,512]{2,1,0:T(8,128)(2,1)S(1)}, u32[]{:S(2)}, u32[]{:S(2)}) %collective-permute-start.7) | collective-permute-done | bytes 262176 | tf_op jit(solution)/shard_map/ppermute | solution.py:18
  60.2 0.7 bitcast_dynamic-update-slice_fusion.stock_ref
  60.9 49.4 %shard_map.110 = (bf16[2048,512]{1,0:T(8,128)(2,1)}, bf16[2048,512]{1,0:T(8,128)(2,1)}, f32[2,128,512]{2,1,0:T(8,128)}, bf16[9,2,128,512]{3,2,1,0:T(8,128)(2,1)}) custom-call(s32[16,5]{1,0:T(8,128)} %broadcast_subtract_fusion.slots_ref, s32[16]{0:T(128)} %counts_ref.1, bf16[2048,512]{1,0:T(8,128)(2,1)} %q_ref.1, bf16[2048,512]{1,0:T(8,128)(2,1)} %g_ref.1, ...), custom_call_target="tpu_custom_call" | custom-call | flops 9663676416 | bytes 15466496 | tf_op jit(solution)/shard_map/pallas_call | solution.py:149
  110.3 1.7 slice_bitcast_fusion.7
  112.0 6.0 %collective-permute-start.15 = (bf16[2,128,512]{2,1,0:T(8,128)(2,1)S(1)}, bf16[2,128,512]{2,1,0:T(8,128)(2,1)S(1)}, u32[]{:S(2)}, u32[]{:S(2)}) collective-permute-start(bf16[2,128,512]{2,1,0:T(8,128)(2,1)S(1)} %get-tuple-element.14), channel_id=1, source_target_pairs={{0,16},{4,20},{8,24},{12,28},{16,32},{20,36},{24,40},{28,44},{32,4... | collective-permute-start | bytes 786440 | tf_op jit(solution)/shard_map/ppermute | solution.py:18
  118.0 6.1 %collective-permute-start.14 = (bf16[2,128,512]{2,1,0:T(8,128)(2,1)S(1)}, bf16[2,128,512]{2,1,0:T(8,128)(2,1)S(1)}, u32[]{:S(2)}, u32[]{:S(2)}) collective-permute-start(bf16[2,128,512]{2,1,0:T(8,128)(2,1)S(1)} %get-tuple-element.15), channel_id=1, source_target_pairs={{0,12},{4,16},{8,20},{12,24},{16,28},{20,32},{24,36},{28,40},{32,4... | collective-permute-start | bytes 786440 | tf_op jit(solution)/shard_map/ppermute | solution.py:18
  124.1 1.3 collective-permute-start.13
  125.4 10.2 %collective-permute-start.12 = (bf16[2,128,512]{2,1,0:T(8,128)(2,1)S(1)}, bf16[2,128,512]{2,1,0:T(8,128)(2,1)S(1)}, u32[]{:S(2)}, u32[]{:S(2)}) collective-permute-start(bf16[2,128,512]{2,1,0:T(8,128)(2,1)S(1)} %get-tuple-element.17), channel_id=1, source_target_pairs={{0,4},{4,8},{8,12},{12,16},{16,20},{20,24},{24,28},{28,32},{32,36}... | collective-permute-start | bytes 786440 | tf_op jit(solution)/shard_map/ppermute | solution.py:18
  135.6 1.3 collective-permute-start.11
  136.9 1.3 collective-permute-start.10
  138.2 1.3 collective-permute-start.9
  139.5 1.3 collective-permute-start.8
  140.9 8.2 %collective-permute-done.11 = bf16[2,128,512]{2,1,0:T(8,128)(2,1)S(1)} collective-permute-done((bf16[2,128,512]{2,1,0:T(8,128)(2,1)S(1)}, bf16[2,128,512]{2,1,0:T(8,128)(2,1)S(1)}, u32[]{:S(2)}, u32[]{:S(2)}) %collective-permute-start.11) | collective-permute-done | bytes 262176 | tf_op jit(solution)/shard_map/ppermute | solution.py:18
  149.0 5.9 %collective-permute-done.10 = bf16[2,128,512]{2,1,0:T(8,128)(2,1)S(1)} collective-permute-done((bf16[2,128,512]{2,1,0:T(8,128)(2,1)S(1)}, bf16[2,128,512]{2,1,0:T(8,128)(2,1)S(1)}, u32[]{:S(2)}, u32[]{:S(2)}) %collective-permute-start.10) | collective-permute-done | bytes 262176 | tf_op jit(solution)/shard_map/ppermute | solution.py:18
  154.9 1.1 collective-permute-done.8
  156.3 0.7 pad_maximum_fusion.1
  157.2 0.8 fusion.2
  158.0 0.8 copy-done.1
  158.7 1.8 convolution_add_fusion
  160.6 1.1 constant_dynamic-slice_fusion
  161.7 55.6 %all-gather.4.cloned.1.call-done = bf16[1024,1024]{1,0:T(8,128)(2,1)} async-done(((bf16[128,1024]{1,0:T(8,128)(2,1)}), bf16[1024,1024]{1,0:T(8,128)(2,1)}) %all-gather.4.cloned.1.call-update) | async-done | bytes 2097168 | tf_op jit(solution)/shard_map/all_gather | solution.py:203
  217.3 3.3 %fusion.4 = f32[256,1024]{1,0:T(8,128)} fusion(bf16[1024,256]{0,1:T(8,128)(2,1)S(1)} %bitcast.54, bf16[1024,1024]{1,0:T(8,128)(2,1)} %all-gather.4.cloned.1.call-done), kind=kOutput, calls=%fused_computation.31 | convolution fusion | flops 536870912 | bytes 3670016 | tf_op jit(solution)/shard_map/dot_general | solution.py:212
  220.6 1.6 convert_element_type.47
  222.3 20.1 %reduce-scatter.5.cloned.1.call-done = f32[64,1024]{1,0:T(8,128)} async-done(((f32[256,1024]{1,0:T(8,128)}), f32[64,1024]{1,0:T(8,128)}) %reduce-scatter.5.cloned.1.call-update) | async-done | bytes 262160 | tf_op jit(solution)/shard_map/reduce_scatter | solution.py:215
  242.4 1.7 fusion.3
  (32 shorter events, 1.2 us)
Async XLA Ops:
  8.0 4.6 %copy-start = (bf16[2048,512]{1,0:T(8,128)(2,1)S(1)}, bf16[2048,512]{1,0:T(8,128)(2,1)}, u32[]{:S(2)}) copy-start(bf16[2048,512]{1,0:T(8,128)(2,1)} %param.9) | copy-start | bytes 6291460
  8.0 4.6 %copy-start.2 = (bf16[128,2048]{1,0:T(8,128)(2,1)S(1)}, bf16[128,2048]{1,0:T(8,128)(2,1)}, u32[]{:S(2)}) copy-start(bf16[128,2048]{1,0:T(8,128)(2,1)} %param.8) | copy-start | bytes 1572868
  8.0 152.6 %all-gather.6.cloned.1.call-start = ((), (), s32[]{:S(2)}) async-start(), calls=%async_computation.5 | async-start | bytes 4718592 | tf_op jit(solution)/shard_map/all_gather | solution.py:173
  10.3 21.3 %copy-start.4 = (s32[16,5]{0,1:T(8,128)S(1)}, s32[16,5]{0,1:T(8,128)}, u32[]{:S(2)}) copy-start(s32[16,5]{0,1:T(8,128)} %param.12) | copy-start | bytes 964
  10.3 207.0 %all-gather.4.cloned.1.call-start = ((), (), s32[]{:S(2)}) async-start(), calls=%async_computation.3 | async-start | bytes 2359296 | tf_op jit(solution)/shard_map/all_gather | solution.py:203
  13.1 19.2 %collective-permute-start = (bf16[2,128,512]{2,1,0:T(8,128)(2,1)S(1)}, bf16[2,128,512]{2,1,0:T(8,128)(2,1)}, u32[]{:S(2)}, u32[]{:S(2)}) collective-permute-start(bf16[2,128,512]{2,1,0:T(8,128)(2,1)S(1)} %pad_maximum_fusion), channel_id=1, source_target_pairs={{0,16},{4,20},{8,24},{12,28},{16,32},{20,36},{24,40},{28,44},{32,4... | collective-permute-start | bytes 786440 | tf_op jit(solution)/shard_map/ppermute | solution.py:18
  19.0 16.7 %collective-permute-start.1 = (bf16[2,128,512]{2,1,0:T(8,128)(2,1)S(1)}, bf16[2,128,512]{2,1,0:T(8,128)(2,1)}, u32[]{:S(2)}, u32[]{:S(2)}) collective-permute-start(bf16[2,128,512]{2,1,0:T(8,128)(2,1)S(1)} %pad_maximum_fusion), channel_id=1, source_target_pairs={{0,12},{4,16},{8,20},{12,24},{16,28},{20,32},{24,36},{28,40},{32,4... | collective-permute-start | bytes 786440 | tf_op jit(solution)/shard_map/ppermute | solution.py:18
  24.7 18.9 %collective-permute-start.2 = (bf16[2,128,512]{2,1,0:T(8,128)(2,1)S(1)}, bf16[2,128,512]{2,1,0:T(8,128)(2,1)S(1)}, u32[]{:S(2)}, u32[]{:S(2)}) collective-permute-start(bf16[2,128,512]{2,1,0:T(8,128)(2,1)S(1)} %pad_maximum_fusion), channel_id=1, source_target_pairs={{0,8},{4,12},{8,16},{12,20},{16,24},{20,28},{24,32},{28,36},{32,40... | collective-permute-start | bytes 786440 | tf_op jit(solution)/shard_map/ppermute | solution.py:18
  26.9 18.7 %collective-permute-start.3 = (bf16[2,128,512]{2,1,0:T(8,128)(2,1)S(1)}, bf16[2,128,512]{2,1,0:T(8,128)(2,1)S(1)}, u32[]{:S(2)}, u32[]{:S(2)}) collective-permute-start(bf16[2,128,512]{2,1,0:T(8,128)(2,1)S(1)} %pad_maximum_fusion), channel_id=1, source_target_pairs={{0,4},{4,8},{8,12},{12,16},{16,20},{20,24},{24,28},{28,32},{32,36}... | collective-permute-start | bytes 786440 | tf_op jit(solution)/shard_map/ppermute | solution.py:18
  30.3 17.1 %collective-permute-start.4 = (bf16[2,128,512]{2,1,0:T(8,128)(2,1)S(1)}, bf16[2,128,512]{2,1,0:T(8,128)(2,1)S(1)}, u32[]{:S(2)}, u32[]{:S(2)}) collective-permute-start(bf16[2,128,512]{2,1,0:T(8,128)(2,1)S(1)} %pad_maximum_fusion), channel_id=1, source_target_pairs={{4,0},{8,4},{12,8},{16,12},{20,16},{24,20},{28,24},{32,28},{36,32}... | collective-permute-start | bytes 786440 | tf_op jit(solution)/shard_map/ppermute | solution.py:18
  32.3 15.9 %collective-permute-start.5 = (bf16[2,128,512]{2,1,0:T(8,128)(2,1)S(1)}, bf16[2,128,512]{2,1,0:T(8,128)(2,1)S(1)}, u32[]{:S(2)}, u32[]{:S(2)}) collective-permute-start(bf16[2,128,512]{2,1,0:T(8,128)(2,1)S(1)} %pad_maximum_fusion), channel_id=1, source_target_pairs={{8,0},{12,4},{16,8},{20,12},{24,16},{28,20},{32,24},{36,28},{40,32... | collective-permute-start | bytes 786440 | tf_op jit(solution)/shard_map/ppermute | solution.py:18
  35.6 18.5 %collective-permute-start.6 = (bf16[2,128,512]{2,1,0:T(8,128)(2,1)S(1)}, bf16[2,128,512]{2,1,0:T(8,128)(2,1)S(1)}, u32[]{:S(2)}, u32[]{:S(2)}) collective-permute-start(bf16[2,128,512]{2,1,0:T(8,128)(2,1)S(1)} %pad_maximum_fusion), channel_id=1, source_target_pairs={{12,0},{16,4},{20,8},{24,12},{28,16},{32,20},{36,24},{40,28},{44,3... | collective-permute-start | bytes 786440 | tf_op jit(solution)/shard_map/ppermute | solution.py:18
  43.6 16.6 %collective-permute-start.7 = (bf16[2,128,512]{2,1,0:T(8,128)(2,1)S(1)}, bf16[2,128,512]{2,1,0:T(8,128)(2,1)S(1)}, u32[]{:S(2)}, u32[]{:S(2)}) collective-permute-start(bf16[2,128,512]{2,1,0:T(8,128)(2,1)S(1)} %pad_maximum_fusion), channel_id=1, source_target_pairs={{16,0},{20,4},{24,8},{28,12},{32,16},{36,20},{40,24},{44,28},{48,3... | collective-permute-start | bytes 786440 | tf_op jit(solution)/shard_map/ppermute | solution.py:18
  110.3 45.7 %copy-start.3 = (f32[2,128,512]{2,1,0:T(8,128)S(1)}, f32[2,128,512]{2,1,0:T(8,128)}, u32[]{:S(2)}) copy-start(f32[2,128,512]{2,1,0:T(8,128)} %get-tuple-element.11) | copy-start | bytes 1572868
  112.0 24.9 %collective-permute-start.15 = (bf16[2,128,512]{2,1,0:T(8,128)(2,1)S(1)}, bf16[2,128,512]{2,1,0:T(8,128)(2,1)S(1)}, u32[]{:S(2)}, u32[]{:S(2)}) collective-permute-start(bf16[2,128,512]{2,1,0:T(8,128)(2,1)S(1)} %get-tuple-element.14), channel_id=1, source_target_pairs={{0,16},{4,20},{8,24},{12,28},{16,32},{20,36},{24,40},{28,44},{32,4... | collective-permute-start | bytes 786440 | tf_op jit(solution)/shard_map/ppermute | solution.py:18
  118.0 20.3 %collective-permute-start.14 = (bf16[2,128,512]{2,1,0:T(8,128)(2,1)S(1)}, bf16[2,128,512]{2,1,0:T(8,128)(2,1)S(1)}, u32[]{:S(2)}, u32[]{:S(2)}) collective-permute-start(bf16[2,128,512]{2,1,0:T(8,128)(2,1)S(1)} %get-tuple-element.15), channel_id=1, source_target_pairs={{0,12},{4,16},{8,20},{12,24},{16,28},{20,32},{24,36},{28,40},{32,4... | collective-permute-start | bytes 786440 | tf_op jit(solution)/shard_map/ppermute | solution.py:18
  124.1 15.4 %collective-permute-start.13 = (bf16[2,128,512]{2,1,0:T(8,128)(2,1)S(1)}, bf16[2,128,512]{2,1,0:T(8,128)(2,1)S(1)}, u32[]{:S(2)}, u32[]{:S(2)}) collective-permute-start(bf16[2,128,512]{2,1,0:T(8,128)(2,1)S(1)} %get-tuple-element.16), channel_id=1, source_target_pairs={{0,8},{4,12},{8,16},{12,20},{16,24},{20,28},{24,32},{28,36},{32,40... | collective-permute-start | bytes 786440 | tf_op jit(solution)/shard_map/ppermute | solution.py:18
  125.4 15.4 %collective-permute-start.12 = (bf16[2,128,512]{2,1,0:T(8,128)(2,1)S(1)}, bf16[2,128,512]{2,1,0:T(8,128)(2,1)S(1)}, u32[]{:S(2)}, u32[]{:S(2)}) collective-permute-start(bf16[2,128,512]{2,1,0:T(8,128)(2,1)S(1)} %get-tuple-element.17), channel_id=1, source_target_pairs={{0,4},{4,8},{8,12},{12,16},{16,20},{20,24},{24,28},{28,32},{32,36}... | collective-permute-start | bytes 786440 | tf_op jit(solution)/shard_map/ppermute | solution.py:18
  135.6 13.4 %collective-permute-start.11 = (bf16[2,128,512]{2,1,0:T(8,128)(2,1)S(1)}, bf16[2,128,512]{2,1,0:T(8,128)(2,1)S(1)}, u32[]{:S(2)}, u32[]{:S(2)}) collective-permute-start(bf16[2,128,512]{2,1,0:T(8,128)(2,1)S(1)} %get-tuple-element.18), channel_id=1, source_target_pairs={{4,0},{8,4},{12,8},{16,12},{20,16},{24,20},{28,24},{32,28},{36,32}... | collective-permute-start | bytes 786440 | tf_op jit(solution)/shard_map/ppermute | solution.py:18
  136.9 18.0 %collective-permute-start.10 = (bf16[2,128,512]{2,1,0:T(8,128)(2,1)S(1)}, bf16[2,128,512]{2,1,0:T(8,128)(2,1)S(1)}, u32[]{:S(2)}, u32[]{:S(2)}) collective-permute-start(bf16[2,128,512]{2,1,0:T(8,128)(2,1)S(1)} %get-tuple-element.19), channel_id=1, source_target_pairs={{8,0},{12,4},{16,8},{20,12},{24,16},{28,20},{32,24},{36,28},{40,32... | collective-permute-start | bytes 786440 | tf_op jit(solution)/shard_map/ppermute | solution.py:18
  138.2 16.7 %collective-permute-start.9 = (bf16[2,128,512]{2,1,0:T(8,128)(2,1)S(1)}, bf16[2,128,512]{2,1,0:T(8,128)(2,1)S(1)}, u32[]{:S(2)}, u32[]{:S(2)}) collective-permute-start(bf16[2,128,512]{2,1,0:T(8,128)(2,1)S(1)} %get-tuple-element.20), channel_id=1, source_target_pairs={{12,0},{16,4},{20,8},{24,12},{28,16},{32,20},{36,24},{40,28},{44,3... | collective-permute-start | bytes 786440 | tf_op jit(solution)/shard_map/ppermute | solution.py:18
  139.5 16.4 %collective-permute-start.8 = (bf16[2,128,512]{2,1,0:T(8,128)(2,1)S(1)}, bf16[2,128,512]{2,1,0:T(8,128)(2,1)S(1)}, u32[]{:S(2)}, u32[]{:S(2)}) collective-permute-start(bf16[2,128,512]{2,1,0:T(8,128)(2,1)S(1)} %get-tuple-element.13), channel_id=1, source_target_pairs={{16,0},{20,4},{24,8},{28,12},{32,16},{36,20},{40,24},{44,28},{48,3... | collective-permute-start | bytes 786440 | tf_op jit(solution)/shard_map/ppermute | solution.py:18
  157.1 63.5 %reduce-scatter.3.cloned.1.call-start = ((), (), s32[]{:S(2)}) async-start(), calls=%async_computation.2 | async-start | bytes 1310720 | tf_op jit(solution)/shard_map/reduce_scatter | solution.py:199
  157.1 1.6 copy-start.1
  160.6 81.8 %reduce-scatter.5.cloned.1.call-start = ((), (), s32[]{:S(2)}) async-start(), calls=%async_computation.4 | async-start | bytes 1310720 | tf_op jit(solution)/shard_map/reduce_scatter | solution.py:215
Sparse Core Ops, SparseCore 0:
  11.3 100.1 all-gather.5
  157.2 60.0 all-gather.3
Sparse Core Ops, SparseCore 1:
  160.6 27.8 reduce-scatter.2
  220.7 21.6 reduce-scatter.4

commit v12 on v11

--- a/solution.py
+++ b/solution.py
@@ -170,7 +170,12 @@
     position = lax.axis_index(blk)
     head_cols = key_weight.shape[1]
     model = encoder.shape[1]
-    near = lax.all_gather(encoder, "byx", axis=0, tiled=False)
+    rows = encoder.shape[0]
+    slice_rows = model // (outer * inner)
+    pieces = encoder.reshape(rows, outer, inner, slice_rows).transpose(2, 0, 1, 3)
+    picked = lax.all_to_all(
+        pieces.reshape(inner, rows, outer * slice_rows), "byx", 0, 0, tiled=False
+    ).reshape(inner * rows, outer * slice_rows)
     own_keys = jnp.dot(encoder, key_weight, preferred_element_type=jnp.float32).astype(jnp.bfloat16)
     own_values = jnp.dot(encoder, value_weight, preferred_element_type=jnp.float32).astype(
         jnp.bfloat16
@@ -201,14 +206,6 @@
     )
     both_grads = jnp.concatenate([rounded[0], rounded[1]], 1)
     group_grads = lax.all_gather(both_grads, "byx", axis=0, tiled=True)
-    rows = encoder.shape[0]
-    slice_rows = model // (outer * inner)
-    picked = lax.dynamic_slice_in_dim(
-        near.reshape(inner * rows, outer, inner, slice_rows),
-        lax.axis_index("byx"),
-        1,
-        axis=2,
-    ).reshape(inner * rows, outer * slice_rows)
     partial = lax.dot_general(
         picked, group_grads, (((0,), (0,)), ((), ())), preferred_element_type=jnp.float32
     )

time: 253 us -> 257 us (1.016)
  waiting for transfers between devices: 107 us -> 79.1 us
  blocking collectives: 0 us -> 25 us
  starting transfers between devices: 51.2 us -> 54.7 us
  local copies, waits for them, and re-layouts: 15.3 us -> 18.6 us
  Pallas kernels: 49.4 us -> 52 us
    all_to_all x0 -> x1, blocking collectives: none -> 25 us  [on_device(): lax.all_to_all(pieces.reshape(inner, rows, outer * slice_rows), 'byx', 0,...]
    reduce_scatter x1 -> x0, waiting for transfers between devices: 20.1 us -> none  [on_device(): lax.psum_scatter(partial, 'bz', scatter_dimension=0, tiled=True)]
    unnamed x4, waiting for transfers between devices: 0.07 us -> 20.2 us
    all_gather x1, waiting for transfers between devices: 55.6 us -> 35.8 us  [on_device(): group_grads = lax.all_gather(both_grads, 'byx', axis=0, tiled=True)]
    ppermute x16, waiting for transfers between devices: 31.4 us -> 23.1 us  [passed_along(): return lax.ppermute(value, axis, pairs)]
    unnamed x19 -> x22, local copies, waits for them, and re-layouts: 10.1 us -> 14.2 us
    ppermute x16, starting transfers between devices: 51.1 us -> 54.6 us  [passed_along(): return lax.ppermute(value, axis, pairs)]
    pallas_call x1, Pallas kernels: 49.4 us -> 52 us  [attention(): pl.pallas_call(attention_kernel, grid_spec=grid_spec, out_shape=[jax.Shap...]
  transfers between devices with their start and end apart: 20 -> 19, of which waited for: 10 -> 8; matrix products, arithmetic and copies ran while one was open for 9% -> 8% of each run, Pallas kernels for 20% -> 0%
where the time goes in v12:
time: 257 us
  waiting for transfers between devices  79.1 us (31%)
  starting transfers between devices  54.7 us (21%)
  Pallas kernels  52 us (20%)
  blocking collectives  25 us (10%)
  local copies, waits for them, and re-layouts  18.6 us (7%)
  between operations  15.8 us (6%)
  matrix products  7.97 us (3%)
  other arithmetic  4.04 us (2%)
    ppermute x16, starting transfers between devices, passed_along(): return lax.ppermute(value, axis, pairs)  54.6 us
    pallas_call x1, Pallas kernels, attention(): pl.pallas_call(attention_kernel, grid_spec=grid_spec, out_shape=[jax.Shap...  52 us
    all_gather x1, waiting for transfers between devices, on_device(): group_grads = lax.all_gather(both_grads, 'byx', axis=0, tiled=True)  35.8 us
    all_to_all x1, blocking collectives, on_device(): lax.all_to_all(pieces.reshape(inner, rows, outer * slice_rows), 'byx', 0,...  25 us
    ppermute x16, waiting for transfers between devices, passed_along(): return lax.ppermute(value, axis, pairs)  23.1 us
    unnamed x4, waiting for transfers between devices  20.2 us
    unnamed x22, local copies, waits for them, and re-layouts  14.2 us
  transfers between devices with their start and end apart: 19, of which 8 were waited for; matrix products, arithmetic and copies ran while one was open for 8% of the time, Pallas kernels for 0%

profile of v12, /device:TPU:0, one launch (start us, length us, event | category | flops | bytes accessed | tf_op | source)
XLA Modules:
  0.0 257.1 jit_solution(1288319281015747903)
XLA Ops:
  8.1 1.5 copy-done
  9.6 1.6 fusion
  11.3 0.4 fusion.1
  11.8 5.9 %collective-permute-start = (bf16[2,128,512]{2,1,0:T(8,128)(2,1)S(1)}, bf16[2,128,512]{2,1,0:T(8,128)(2,1)}, u32[]{:S(2)}, u32[]{:S(2)}) collective-permute-start(bf16[2,128,512]{2,1,0:T(8,128)(2,1)S(1)} %pad_maximum_fusion), channel_id=1, source_target_pairs={{0,16},{4,20},{8,24},{12,28},{16,32},{20,36},{24,40},{28,44},{32,4... | collective-permute-start | bytes 786440 | tf_op jit(solution)/shard_map/ppermute | solution.py:18
  17.7 5.7 %collective-permute-start.1 = (bf16[2,128,512]{2,1,0:T(8,128)(2,1)S(1)}, bf16[2,128,512]{2,1,0:T(8,128)(2,1)}, u32[]{:S(2)}, u32[]{:S(2)}) collective-permute-start(bf16[2,128,512]{2,1,0:T(8,128)(2,1)S(1)} %pad_maximum_fusion), channel_id=1, source_target_pairs={{0,12},{4,16},{8,20},{12,24},{16,28},{20,32},{24,36},{28,40},{32,4... | collective-permute-start | bytes 786440 | tf_op jit(solution)/shard_map/ppermute | solution.py:18
  23.5 2.9 %collective-permute-start.2 = (bf16[2,128,512]{2,1,0:T(8,128)(2,1)S(1)}, bf16[2,128,512]{2,1,0:T(8,128)(2,1)}, u32[]{:S(2)}, u32[]{:S(2)}) collective-permute-start(bf16[2,128,512]{2,1,0:T(8,128)(2,1)S(1)} %pad_maximum_fusion), channel_id=1, source_target_pairs={{0,8},{4,12},{8,16},{12,20},{16,24},{20,28},{24,32},{28,36},{32,40... | collective-permute-start | bytes 786440 | tf_op jit(solution)/shard_map/ppermute | solution.py:18
  26.4 4.0 %collective-permute-start.3 = (bf16[2,128,512]{2,1,0:T(8,128)(2,1)S(1)}, bf16[2,128,512]{2,1,0:T(8,128)(2,1)}, u32[]{:S(2)}, u32[]{:S(2)}) collective-permute-start(bf16[2,128,512]{2,1,0:T(8,128)(2,1)S(1)} %pad_maximum_fusion), channel_id=1, source_target_pairs={{0,4},{4,8},{8,12},{12,16},{16,20},{20,24},{24,28},{28,32},{32,36}... | collective-permute-start | bytes 786440 | tf_op jit(solution)/shard_map/ppermute | solution.py:18
  30.4 1.3 collective-permute-start.4
  31.8 0.6 broadcast_subtract_fusion.slots_ref
  32.4 1.3 collective-permute-start.5
  33.7 1.7 bitcast_dynamic-update-slice_fusion.8
  35.4 1.3 collective-permute-start.6
  36.7 1.7 bitcast_dynamic-update-slice_fusion.7
  38.3 1.2 collective-permute-done.2
  39.5 1.3 collective-permute-start.7
  40.8 1.7 bitcast_dynamic-update-slice_fusion.6
  42.5 1.7 bitcast_dynamic-update-slice_fusion.5
  44.2 0.7 bitcast_dynamic-update-slice_fusion.4
  44.9 0.7 bitcast_dynamic-update-slice_fusion.3
  45.6 0.7 bitcast_dynamic-update-slice_fusion.2
  46.4 3.7 %collective-permute-done.6 = bf16[2,128,512]{2,1,0:T(8,128)(2,1)S(1)} collective-permute-done((bf16[2,128,512]{2,1,0:T(8,128)(2,1)S(1)}, bf16[2,128,512]{2,1,0:T(8,128)(2,1)S(1)}, u32[]{:S(2)}, u32[]{:S(2)}) %collective-permute-start.6) | collective-permute-done | bytes 262176 | tf_op jit(solution)/shard_map/ppermute | solution.py:18
  50.1 0.7 bitcast_dynamic-update-slice_fusion.1
  50.8 1.8 collective-permute-done.7
  52.6 0.7 bitcast_dynamic-update-slice_fusion.stock_ref
  53.3 52.0 %shard_map.110 = (bf16[2048,512]{1,0:T(8,128)(2,1)}, bf16[2048,512]{1,0:T(8,128)(2,1)}, f32[2,128,512]{2,1,0:T(8,128)}, bf16[9,2,128,512]{3,2,1,0:T(8,128)(2,1)}) custom-call(s32[16,5]{1,0:T(8,128)} %broadcast_subtract_fusion.slots_ref, s32[16]{0:T(128)} %counts_ref.1, bf16[2048,512]{1,0:T(8,128)(2,1)} %q_ref.1, bf16[2048,512]{1,0:T(8,128)(2,1)} %g_ref.1, ...), custom_call_target="tpu_custom_call" | custom-call | flops 9663676416 | bytes 15466496 | tf_op jit(solution)/shard_map/pallas_call | solution.py:149
  105.3 1.7 slice_bitcast_fusion.7
  107.0 1.3 collective-permute-start.10
  108.3 1.3 collective-permute-start.11
  109.6 6.1 %collective-permute-start.12 = (bf16[2,128,512]{2,1,0:T(8,128)(2,1)S(1)}, bf16[2,128,512]{2,1,0:T(8,128)(2,1)S(1)}, u32[]{:S(2)}, u32[]{:S(2)}) collective-permute-start(bf16[2,128,512]{2,1,0:T(8,128)(2,1)S(1)} %get-tuple-element.42), channel_id=1, source_target_pairs={{0,4},{4,8},{8,12},{12,16},{16,20},{20,24},{24,28},{28,32},{32,36}... | collective-permute-start | bytes 786440 | tf_op jit(solution)/shard_map/ppermute | solution.py:18
  115.7 8.5 %collective-permute-start.13 = (bf16[2,128,512]{2,1,0:T(8,128)(2,1)S(1)}, bf16[2,128,512]{2,1,0:T(8,128)(2,1)S(1)}, u32[]{:S(2)}, u32[]{:S(2)}) collective-permute-start(bf16[2,128,512]{2,1,0:T(8,128)(2,1)S(1)} %get-tuple-element.41), channel_id=1, source_target_pairs={{0,8},{4,12},{8,16},{12,20},{16,24},{20,28},{24,32},{28,36},{32,40... | collective-permute-start | bytes 786440 | tf_op jit(solution)/shard_map/ppermute | solution.py:18
  124.2 4.3 %collective-permute-start.14 = (bf16[2,128,512]{2,1,0:T(8,128)(2,1)S(1)}, bf16[2,128,512]{2,1,0:T(8,128)(2,1)S(1)}, u32[]{:S(2)}, u32[]{:S(2)}) collective-permute-start(bf16[2,128,512]{2,1,0:T(8,128)(2,1)S(1)} %get-tuple-element.40), channel_id=1, source_target_pairs={{0,12},{4,16},{8,20},{12,24},{16,28},{20,32},{24,36},{28,40},{32,4... | collective-permute-start | bytes 786440 | tf_op jit(solution)/shard_map/ppermute | solution.py:18
  128.6 6.8 %collective-permute-start.15 = (bf16[2,128,512]{2,1,0:T(8,128)(2,1)S(1)}, bf16[2,128,512]{2,1,0:T(8,128)(2,1)S(1)}, u32[]{:S(2)}, u32[]{:S(2)}) collective-permute-start(bf16[2,128,512]{2,1,0:T(8,128)(2,1)S(1)} %get-tuple-element.39), channel_id=1, source_target_pairs={{0,16},{4,20},{8,24},{12,28},{16,32},{20,36},{24,40},{28,44},{32,4... | collective-permute-start | bytes 786440 | tf_op jit(solution)/shard_map/ppermute | solution.py:18
  135.3 1.3 collective-permute-start.8
  136.6 1.3 collective-permute-start.9
  138.2 5.6 %collective-permute-done.15 = bf16[2,128,512]{2,1,0:T(8,128)(2,1)S(1)} collective-permute-done((bf16[2,128,512]{2,1,0:T(8,128)(2,1)S(1)}, bf16[2,128,512]{2,1,0:T(8,128)(2,1)S(1)}, u32[]{:S(2)}, u32[]{:S(2)}) %collective-permute-start.15) | collective-permute-done | bytes 262176 | tf_op jit(solution)/shard_map/ppermute | solution.py:18
  143.8 10.6 %collective-permute-done.8 = bf16[2,128,512]{2,1,0:T(8,128)(2,1)S(1)} collective-permute-done((bf16[2,128,512]{2,1,0:T(8,128)(2,1)S(1)}, bf16[2,128,512]{2,1,0:T(8,128)(2,1)S(1)}, u32[]{:S(2)}, u32[]{:S(2)}) %collective-permute-start.8) | collective-permute-done | bytes 262176 | tf_op jit(solution)/shard_map/ppermute | solution.py:18
  154.3 0.3 add_convert_fusion
  154.7 0.7 pad_maximum_fusion.1
  155.5 0.8 fusion.2
  156.3 0.8 copy-done.2
  157.1 1.8 convolution_add_fusion
  159.3 25.0 %all_to_all.5 = bf16[8,128,256]{1,2,0:T(8,128)(2,1)S(1)} all-to-all(bf16[8,128,256]{1,2,0:T(8,128)(2,1)S(1)} %bitcast.60), channel_id=1, replica_groups=mesh['bz'=4,'byx'=8,'grp'=4] {'byx'}, dimensions={0} | all-to-all | bytes 1048576 | tf_op jit(solution)/shard_map/all_to_all | solution.py:176
  184.6 35.8 %all-gather.2.cloned.1.call-done = bf16[1024,1024]{1,0:T(8,128)(2,1)} async-done(((bf16[128,1024]{1,0:T(8,128)(2,1)}), bf16[1024,1024]{1,0:T(8,128)(2,1)}) %all-gather.2.cloned.1.call-update) | async-done | bytes 2097168 | tf_op jit(solution)/shard_map/all_gather | solution.py:208
  220.4 3.3 %convolution_bitcast_fusion = f32[256,1024]{0,1:T(8,128)} fusion(bf16[1024,1024]{1,0:T(8,128)(2,1)} %all-gather.2.cloned.1.call-done, bf16[1024,256]{1,0:T(8,128)(2,1)S(1)} %bitcast.62), kind=kOutput, calls=%fused_computation.1 | convolution fusion | flops 536870912 | bytes 3670016 | tf_op jit(solution)/shard_map/dot_general | solution.py:209
  223.7 2.6 copy.39
  226.3 1.6 convert_element_type.47
  227.9 20.1 %reduce-scatter.7.cloned.1.call-done = f32[64,1024]{1,0:T(8,128)} async-done(((f32[256,1024]{1,0:T(8,128)}), f32[64,1024]{1,0:T(8,128)}) %reduce-scatter.7.cloned.1.call-update) | async-done | bytes 262160
  248.0 1.7 fusion.3
  (34 shorter events, 1.3 us)
Async XLA Ops:
  8.0 1.6 copy-start
  8.0 3.2 %copy-start.3 = (bf16[128,2048]{1,0:T(8,128)(2,1)S(1)}, bf16[128,2048]{1,0:T(8,128)(2,1)}, u32[]{:S(2)}) copy-start(bf16[128,2048]{1,0:T(8,128)(2,1)} %param.8) | copy-start | bytes 1572868
  8.0 23.7 %copy-start.5 = (s32[16,5]{0,1:T(8,128)S(1)}, s32[16,5]{0,1:T(8,128)}, u32[]{:S(2)}) copy-start(s32[16,5]{0,1:T(8,128)} %param.12) | copy-start | bytes 964
  8.0 212.4 %all-gather.2.cloned.1.call-start = ((), (), s32[]{:S(2)}) async-start(), calls=%async_computation.4 | async-start | bytes 2359296 | tf_op jit(solution)/shard_map/all_gather | solution.py:208
  9.6 1.7 copy-start.1
  11.8 20.6 %collective-permute-start = (bf16[2,128,512]{2,1,0:T(8,128)(2,1)S(1)}, bf16[2,128,512]{2,1,0:T(8,128)(2,1)}, u32[]{:S(2)}, u32[]{:S(2)}) collective-permute-start(bf16[2,128,512]{2,1,0:T(8,128)(2,1)S(1)} %pad_maximum_fusion), channel_id=1, source_target_pairs={{0,16},{4,20},{8,24},{12,28},{16,32},{20,36},{24,40},{28,44},{32,4... | collective-permute-start | bytes 786440 | tf_op jit(solution)/shard_map/ppermute | solution.py:18
  17.7 17.6 %collective-permute-start.1 = (bf16[2,128,512]{2,1,0:T(8,128)(2,1)S(1)}, bf16[2,128,512]{2,1,0:T(8,128)(2,1)}, u32[]{:S(2)}, u32[]{:S(2)}) collective-permute-start(bf16[2,128,512]{2,1,0:T(8,128)(2,1)S(1)} %pad_maximum_fusion), channel_id=1, source_target_pairs={{0,12},{4,16},{8,20},{12,24},{16,28},{20,32},{24,36},{28,40},{32,4... | collective-permute-start | bytes 786440 | tf_op jit(solution)/shard_map/ppermute | solution.py:18
  23.5 16.1 %collective-permute-start.2 = (bf16[2,128,512]{2,1,0:T(8,128)(2,1)S(1)}, bf16[2,128,512]{2,1,0:T(8,128)(2,1)}, u32[]{:S(2)}, u32[]{:S(2)}) collective-permute-start(bf16[2,128,512]{2,1,0:T(8,128)(2,1)S(1)} %pad_maximum_fusion), channel_id=1, source_target_pairs={{0,8},{4,12},{8,16},{12,20},{16,24},{20,28},{24,32},{28,36},{32,40... | collective-permute-start | bytes 786440 | tf_op jit(solution)/shard_map/ppermute | solution.py:18
  26.4 16.1 %collective-permute-start.3 = (bf16[2,128,512]{2,1,0:T(8,128)(2,1)S(1)}, bf16[2,128,512]{2,1,0:T(8,128)(2,1)}, u32[]{:S(2)}, u32[]{:S(2)}) collective-permute-start(bf16[2,128,512]{2,1,0:T(8,128)(2,1)S(1)} %pad_maximum_fusion), channel_id=1, source_target_pairs={{0,4},{4,8},{8,12},{12,16},{16,20},{20,24},{24,28},{28,32},{32,36}... | collective-permute-start | bytes 786440 | tf_op jit(solution)/shard_map/ppermute | solution.py:18
  30.4 14.5 %collective-permute-start.4 = (bf16[2,128,512]{2,1,0:T(8,128)(2,1)S(1)}, bf16[2,128,512]{2,1,0:T(8,128)(2,1)S(1)}, u32[]{:S(2)}, u32[]{:S(2)}) collective-permute-start(bf16[2,128,512]{2,1,0:T(8,128)(2,1)S(1)} %pad_maximum_fusion), channel_id=1, source_target_pairs={{4,0},{8,4},{12,8},{16,12},{20,16},{24,20},{28,24},{32,28},{36,32}... | collective-permute-start | bytes 786440 | tf_op jit(solution)/shard_map/ppermute | solution.py:18
  32.4 13.2 %collective-permute-start.5 = (bf16[2,128,512]{2,1,0:T(8,128)(2,1)S(1)}, bf16[2,128,512]{2,1,0:T(8,128)(2,1)S(1)}, u32[]{:S(2)}, u32[]{:S(2)}) collective-permute-start(bf16[2,128,512]{2,1,0:T(8,128)(2,1)S(1)} %pad_maximum_fusion), channel_id=1, source_target_pairs={{8,0},{12,4},{16,8},{20,12},{24,16},{28,20},{32,24},{36,28},{40,32... | collective-permute-start | bytes 786440 | tf_op jit(solution)/shard_map/ppermute | solution.py:18
  35.4 14.7 %collective-permute-start.6 = (bf16[2,128,512]{2,1,0:T(8,128)(2,1)S(1)}, bf16[2,128,512]{2,1,0:T(8,128)(2,1)S(1)}, u32[]{:S(2)}, u32[]{:S(2)}) collective-permute-start(bf16[2,128,512]{2,1,0:T(8,128)(2,1)S(1)} %pad_maximum_fusion), channel_id=1, source_target_pairs={{12,0},{16,4},{20,8},{24,12},{28,16},{32,20},{36,24},{40,28},{44,3... | collective-permute-start | bytes 786440 | tf_op jit(solution)/shard_map/ppermute | solution.py:18
  39.5 13.0 %collective-permute-start.7 = (bf16[2,128,512]{2,1,0:T(8,128)(2,1)S(1)}, bf16[2,128,512]{2,1,0:T(8,128)(2,1)S(1)}, u32[]{:S(2)}, u32[]{:S(2)}) collective-permute-start(bf16[2,128,512]{2,1,0:T(8,128)(2,1)S(1)} %pad_maximum_fusion), channel_id=1, source_target_pairs={{16,0},{20,4},{24,8},{28,12},{32,16},{36,20},{40,24},{44,28},{48,3... | collective-permute-start | bytes 786440 | tf_op jit(solution)/shard_map/ppermute | solution.py:18
  105.3 49.1 %copy-start.4 = (f32[2,128,512]{2,1,0:T(8,128)S(1)}, f32[2,128,512]{2,1,0:T(8,128)}, u32[]{:S(2)}) copy-start(f32[2,128,512]{2,1,0:T(8,128)} %get-tuple-element.11) | copy-start | bytes 1572868
  107.0 21.6 %collective-permute-start.10 = (bf16[2,128,512]{2,1,0:T(8,128)(2,1)S(1)}, bf16[2,128,512]{2,1,0:T(8,128)(2,1)S(1)}, u32[]{:S(2)}, u32[]{:S(2)}) collective-permute-start(bf16[2,128,512]{2,1,0:T(8,128)(2,1)S(1)} %get-tuple-element.44), channel_id=1, source_target_pairs={{8,0},{12,4},{16,8},{20,12},{24,16},{28,20},{32,24},{36,28},{40,32... | collective-permute-start | bytes 786440 | tf_op jit(solution)/shard_map/ppermute | solution.py:18
  108.3 27.0 %collective-permute-start.11 = (bf16[2,128,512]{2,1,0:T(8,128)(2,1)S(1)}, bf16[2,128,512]{2,1,0:T(8,128)(2,1)S(1)}, u32[]{:S(2)}, u32[]{:S(2)}) collective-permute-start(bf16[2,128,512]{2,1,0:T(8,128)(2,1)S(1)} %get-tuple-element.43), channel_id=1, source_target_pairs={{4,0},{8,4},{12,8},{16,12},{20,16},{24,20},{28,24},{32,28},{36,32}... | collective-permute-start | bytes 786440 | tf_op jit(solution)/shard_map/ppermute | solution.py:18
  109.6 27.1 %collective-permute-start.12 = (bf16[2,128,512]{2,1,0:T(8,128)(2,1)S(1)}, bf16[2,128,512]{2,1,0:T(8,128)(2,1)S(1)}, u32[]{:S(2)}, u32[]{:S(2)}) collective-permute-start(bf16[2,128,512]{2,1,0:T(8,128)(2,1)S(1)} %get-tuple-element.42), channel_id=1, source_target_pairs={{0,4},{4,8},{8,12},{12,16},{16,20},{20,24},{24,28},{28,32},{32,36}... | collective-permute-start | bytes 786440 | tf_op jit(solution)/shard_map/ppermute | solution.py:18
  115.7 22.6 %collective-permute-start.13 = (bf16[2,128,512]{2,1,0:T(8,128)(2,1)S(1)}, bf16[2,128,512]{2,1,0:T(8,128)(2,1)S(1)}, u32[]{:S(2)}, u32[]{:S(2)}) collective-permute-start(bf16[2,128,512]{2,1,0:T(8,128)(2,1)S(1)} %get-tuple-element.41), channel_id=1, source_target_pairs={{0,8},{4,12},{8,16},{12,20},{16,24},{20,28},{24,32},{28,36},{32,40... | collective-permute-start | bytes 786440 | tf_op jit(solution)/shard_map/ppermute | solution.py:18
  124.2 14.0 %collective-permute-start.14 = (bf16[2,128,512]{2,1,0:T(8,128)(2,1)S(1)}, bf16[2,128,512]{2,1,0:T(8,128)(2,1)S(1)}, u32[]{:S(2)}, u32[]{:S(2)}) collective-permute-start(bf16[2,128,512]{2,1,0:T(8,128)(2,1)S(1)} %get-tuple-element.40), channel_id=1, source_target_pairs={{0,12},{4,16},{8,20},{12,24},{16,28},{20,32},{24,36},{28,40},{32,4... | collective-permute-start | bytes 786440 | tf_op jit(solution)/shard_map/ppermute | solution.py:18
  128.6 15.2 %collective-permute-start.15 = (bf16[2,128,512]{2,1,0:T(8,128)(2,1)S(1)}, bf16[2,128,512]{2,1,0:T(8,128)(2,1)S(1)}, u32[]{:S(2)}, u32[]{:S(2)}) collective-permute-start(bf16[2,128,512]{2,1,0:T(8,128)(2,1)S(1)} %get-tuple-element.39), channel_id=1, source_target_pairs={{0,16},{4,20},{8,24},{12,28},{16,32},{20,36},{24,40},{28,44},{32,4... | collective-permute-start | bytes 786440 | tf_op jit(solution)/shard_map/ppermute | solution.py:18
  135.3 19.0 %collective-permute-start.8 = (bf16[2,128,512]{2,1,0:T(8,128)(2,1)S(1)}, bf16[2,128,512]{2,1,0:T(8,128)(2,1)S(1)}, u32[]{:S(2)}, u32[]{:S(2)}) collective-permute-start(bf16[2,128,512]{2,1,0:T(8,128)(2,1)S(1)} %get-tuple-element.38), channel_id=1, source_target_pairs={{16,0},{20,4},{24,8},{28,12},{32,16},{36,20},{40,24},{44,28},{48,3... | collective-permute-start | bytes 786440 | tf_op jit(solution)/shard_map/ppermute | solution.py:18
  136.6 17.7 %collective-permute-start.9 = (bf16[2,128,512]{2,1,0:T(8,128)(2,1)S(1)}, bf16[2,128,512]{2,1,0:T(8,128)(2,1)S(1)}, u32[]{:S(2)}, u32[]{:S(2)}) collective-permute-start(bf16[2,128,512]{2,1,0:T(8,128)(2,1)S(1)} %get-tuple-element.45), channel_id=1, source_target_pairs={{12,0},{16,4},{20,8},{24,12},{28,16},{32,20},{36,24},{40,28},{44,3... | collective-permute-start | bytes 786440 | tf_op jit(solution)/shard_map/ppermute | solution.py:18
  155.5 70.8 %reduce-scatter.5.cloned.1.call-start = ((), (), s32[]{:S(2)}) async-start(), calls=%async_computation.3 | async-start | bytes 1310720 | tf_op jit(solution)/shard_map/reduce_scatter | solution.py:204
  155.5 1.6 copy-start.2
  159.0 89.1 %reduce-scatter.7.cloned.1.call-start = ((), (), s32[]{:S(2)}) async-start(), calls=%async_computation.5 | async-start | bytes 1310720
Sparse Core Ops, SparseCore 0:
  155.6 64.7 all-gather.1
Sparse Core Ops, SparseCore 1:
  159.0 34.0 reduce-scatter.4
  226.3 21.6 reduce-scatter.6

commit v13 on v11

--- a/solution.py
+++ b/solution.py
@@ -170,7 +170,6 @@
     position = lax.axis_index(blk)
     head_cols = key_weight.shape[1]
     model = encoder.shape[1]
-    near = lax.all_gather(encoder, "byx", axis=0, tiled=False)
     own_keys = jnp.dot(encoder, key_weight, preferred_element_type=jnp.float32).astype(jnp.bfloat16)
     own_values = jnp.dot(encoder, value_weight, preferred_element_type=jnp.float32).astype(
         jnp.bfloat16
@@ -183,6 +182,8 @@
         else:
             arrived.append(passed_along(own, blk, -offset, outer * inner))
     stock = jnp.stack(arrived, 0)
+    late_encoder, stock = lax.optimization_barrier((encoder, stock))
+    near = lax.all_gather(late_encoder, "byx", axis=0, tiled=False)
     slot_ids = (block_lists - (position - REACH)).astype(jnp.int32)
     attended, query_grad, owned, sending = attention(
         queries, out_grad, stock, slot_ids, list_counts.astype(jnp.int32)

time: 253 us -> 253 us (level)
  local copies, waits for them, and re-layouts: 15.3 us -> 12.2 us
  Pallas kernels: 49.4 us -> 52.3 us
    unnamed x19 -> x18, local copies, waits for them, and re-layouts: 10.1 us -> 5.97 us
    pallas_call x1, Pallas kernels: 49.4 us -> 52.3 us  [attention(): pl.pallas_call(attention_kernel, grid_spec=grid_spec, out_shape=[jax.Shap...]
  transfers between devices with their start and end apart: 20 -> 20, of which waited for: 10 -> 9; matrix products, arithmetic and copies ran while one was open for 9% -> 7% of each run, Pallas kernels for 20% -> 21%
where the time goes in v13:
time: 253 us; the launch traced here: 252 us
  waiting for transfers between devices  108 us (43%)
  Pallas kernels  52.3 us (21%)
  starting transfers between devices  51.1 us (20%)
  between operations  15.8 us (6%)
  local copies, waits for them, and re-layouts  12.2 us (5%)
  matrix products  8.67 us (3%)
  other arithmetic  4.08 us (2%)
    all_gather x1, waiting for transfers between devices, on_device(): group_grads = lax.all_gather(both_grads, 'byx', axis=0, tiled=True)  56.4 us
    pallas_call x1, Pallas kernels, attention(): pl.pallas_call(attention_kernel, grid_spec=grid_spec, out_shape=[jax.Shap...  52.3 us
    ppermute x16, starting transfers between devices, passed_along(): return lax.ppermute(value, axis, pairs)  50.9 us
    ppermute x16, waiting for transfers between devices, passed_along(): return lax.ppermute(value, axis, pairs)  31.2 us
    reduce_scatter x1, waiting for transfers between devices, on_device(): lax.psum_scatter(partial, 'bz', scatter_dimension=0, tiled=True)  20.1 us
    unnamed x18, local copies, waits for them, and re-layouts  5.97 us
  transfers between devices with their start and end apart: 20, of which 9 were waited for; matrix products, arithmetic and copies ran while one was open for 7% of the time, Pallas kernels for 21%

profile of v13, /device:TPU:0, one launch (start us, length us, event | category | flops | bytes accessed | tf_op | source)
XLA Modules:
  0.0 251.9 jit_solution(11055515519478152419)
XLA Ops:
  8.1 2.3 fusion.1
  10.5 0.4 fusion
  11.0 5.2 %collective-permute-start = (bf16[2,128,512]{2,1,0:T(8,128)(2,1)S(1)}, bf16[2,128,512]{2,1,0:T(8,128)(2,1)S(1)}, u32[]{:S(2)}, u32[]{:S(2)}) collective-permute-start(bf16[2,128,512]{2,1,0:T(8,128)(2,1)S(1)} %pad_maximum_fusion), channel_id=1, source_target_pairs={{0,16},{4,20},{8,24},{12,28},{16,32},{20,36},{24,40},{28,44},{32,4... | collective-permute-start | bytes 786440 | tf_op jit(solution)/shard_map/ppermute | solution.py:18
  16.2 5.1 %collective-permute-start.1 = (bf16[2,128,512]{2,1,0:T(8,128)(2,1)S(1)}, bf16[2,128,512]{2,1,0:T(8,128)(2,1)S(1)}, u32[]{:S(2)}, u32[]{:S(2)}) collective-permute-start(bf16[2,128,512]{2,1,0:T(8,128)(2,1)S(1)} %pad_maximum_fusion), channel_id=1, source_target_pairs={{0,12},{4,16},{8,20},{12,24},{16,28},{20,32},{24,36},{28,40},{32,4... | collective-permute-start | bytes 786440 | tf_op jit(solution)/shard_map/ppermute | solution.py:18
  21.2 2.9 %collective-permute-start.2 = (bf16[2,128,512]{2,1,0:T(8,128)(2,1)S(1)}, bf16[2,128,512]{2,1,0:T(8,128)(2,1)S(1)}, u32[]{:S(2)}, u32[]{:S(2)}) collective-permute-start(bf16[2,128,512]{2,1,0:T(8,128)(2,1)S(1)} %pad_maximum_fusion), channel_id=1, source_target_pairs={{0,8},{4,12},{8,16},{12,20},{16,24},{20,28},{24,32},{28,36},{32,40... | collective-permute-start | bytes 786440 | tf_op jit(solution)/shard_map/ppermute | solution.py:18
  24.1 4.0 %collective-permute-start.3 = (bf16[2,128,512]{2,1,0:T(8,128)(2,1)S(1)}, bf16[2,128,512]{2,1,0:T(8,128)(2,1)S(1)}, u32[]{:S(2)}, u32[]{:S(2)}) collective-permute-start(bf16[2,128,512]{2,1,0:T(8,128)(2,1)S(1)} %pad_maximum_fusion), channel_id=1, source_target_pairs={{0,4},{4,8},{8,12},{12,16},{16,20},{20,24},{24,28},{28,32},{32,36}... | collective-permute-start | bytes 786440 | tf_op jit(solution)/shard_map/ppermute | solution.py:18
  28.2 1.3 collective-permute-start.4
  29.5 1.3 collective-permute-start.5
  30.8 0.7 bitcast_dynamic-update-slice_fusion.8
  31.5 1.3 collective-permute-start.6
  32.8 0.7 bitcast_dynamic-update-slice_fusion.7
  33.5 5.1 %collective-permute-done.2 = bf16[2,128,512]{2,1,0:T(8,128)(2,1)S(1)} collective-permute-done((bf16[2,128,512]{2,1,0:T(8,128)(2,1)S(1)}, bf16[2,128,512]{2,1,0:T(8,128)(2,1)S(1)}, u32[]{:S(2)}, u32[]{:S(2)}) %collective-permute-start.2) | collective-permute-done | bytes 262176 | tf_op jit(solution)/shard_map/ppermute | solution.py:18
  38.7 1.3 collective-permute-start.7
  39.9 0.7 bitcast_dynamic-update-slice_fusion.6
  40.7 0.7 bitcast_dynamic-update-slice_fusion.5
  41.4 0.7 bitcast_dynamic-update-slice_fusion.4
  42.1 0.7 bitcast_dynamic-update-slice_fusion.3
  42.8 0.7 bitcast_dynamic-update-slice_fusion.2
  43.6 5.7 %collective-permute-done.6 = bf16[2,128,512]{2,1,0:T(8,128)(2,1)S(1)} collective-permute-done((bf16[2,128,512]{2,1,0:T(8,128)(2,1)S(1)}, bf16[2,128,512]{2,1,0:T(8,128)(2,1)S(1)}, u32[]{:S(2)}, u32[]{:S(2)}) %collective-permute-start.6) | collective-permute-done | bytes 262176 | tf_op jit(solution)/shard_map/ppermute | solution.py:18
  49.2 0.7 bitcast_dynamic-update-slice_fusion.1
  50.0 1.1 collective-permute-done.7
  51.1 0.7 bitcast_dynamic-update-slice_fusion.stock_ref
  51.8 1.0 copy.17
  53.0 0.6 broadcast_subtract_fusion.slots_ref
  53.6 52.3 %shard_map.110 = (bf16[2048,512]{1,0:T(8,128)(2,1)}, bf16[2048,512]{1,0:T(8,128)(2,1)}, f32[2,128,512]{2,1,0:T(8,128)}, bf16[9,2,128,512]{3,2,1,0:T(8,128)(2,1)}) custom-call(s32[16,5]{1,0:T(8,128)} %broadcast_subtract_fusion.slots_ref, s32[16]{0:T(128)} %counts_ref.1, bf16[2048,512]{1,0:T(8,128)(2,1)} %q_ref.1, bf16[2048,512]{1,0:T(8,128)(2,1)} %g_ref.1, ...), custom_call_target="tpu_custom_call" | custom-call | flops 9663676416 | bytes 15466496 | tf_op jit(solution)/shard_map/pallas_call | solution.py:149
  105.9 1.7 slice_bitcast_fusion.7
  107.6 6.8 %collective-permute-start.15 = (bf16[2,128,512]{2,1,0:T(8,128)(2,1)S(1)}, bf16[2,128,512]{2,1,0:T(8,128)(2,1)S(1)}, u32[]{:S(2)}, u32[]{:S(2)}) collective-permute-start(bf16[2,128,512]{2,1,0:T(8,128)(2,1)S(1)} %get-tuple-element.18), channel_id=1, source_target_pairs={{0,16},{4,20},{8,24},{12,28},{16,32},{20,36},{24,40},{28,44},{32,4... | collective-permute-start | bytes 786440 | tf_op jit(solution)/shard_map/ppermute | solution.py:18
  114.4 7.2 %collective-permute-start.14 = (bf16[2,128,512]{2,1,0:T(8,128)(2,1)S(1)}, bf16[2,128,512]{2,1,0:T(8,128)(2,1)S(1)}, u32[]{:S(2)}, u32[]{:S(2)}) collective-permute-start(bf16[2,128,512]{2,1,0:T(8,128)(2,1)S(1)} %get-tuple-element.19), channel_id=1, source_target_pairs={{0,12},{4,16},{8,20},{12,24},{16,28},{20,32},{24,36},{28,40},{32,4... | collective-permute-start | bytes 786440 | tf_op jit(solution)/shard_map/ppermute | solution.py:18
  121.6 8.1 %collective-permute-start.13 = (bf16[2,128,512]{2,1,0:T(8,128)(2,1)S(1)}, bf16[2,128,512]{2,1,0:T(8,128)(2,1)S(1)}, u32[]{:S(2)}, u32[]{:S(2)}) collective-permute-start(bf16[2,128,512]{2,1,0:T(8,128)(2,1)S(1)} %get-tuple-element.20), channel_id=1, source_target_pairs={{0,8},{4,12},{8,16},{12,20},{16,24},{20,28},{24,32},{28,36},{32,40... | collective-permute-start | bytes 786440 | tf_op jit(solution)/shard_map/ppermute | solution.py:18
  129.8 1.3 collective-permute-start.12
  131.1 1.3 collective-permute-start.11
  132.4 1.3 collective-permute-start.10
  133.7 1.3 collective-permute-start.9
  135.0 8.4 %collective-permute-done.13 = bf16[2,128,512]{2,1,0:T(8,128)(2,1)S(1)} collective-permute-done((bf16[2,128,512]{2,1,0:T(8,128)(2,1)S(1)}, bf16[2,128,512]{2,1,0:T(8,128)(2,1)S(1)}, u32[]{:S(2)}, u32[]{:S(2)}) %collective-permute-start.13) | collective-permute-done | bytes 262176 | tf_op jit(solution)/shard_map/ppermute | solution.py:18
  143.5 1.3 collective-permute-start.8
  144.8 1.6 collective-permute-done.10
  146.3 2.8 %collective-permute-done.9 = bf16[2,128,512]{2,1,0:T(8,128)(2,1)S(1)} collective-permute-done((bf16[2,128,512]{2,1,0:T(8,128)(2,1)S(1)}, bf16[2,128,512]{2,1,0:T(8,128)(2,1)S(1)}, u32[]{:S(2)}, u32[]{:S(2)}) %collective-permute-start.9) | collective-permute-done | bytes 262176 | tf_op jit(solution)/shard_map/ppermute | solution.py:18
  149.1 6.4 %collective-permute-done.8 = bf16[2,128,512]{2,1,0:T(8,128)(2,1)S(1)} collective-permute-done((bf16[2,128,512]{2,1,0:T(8,128)(2,1)S(1)}, bf16[2,128,512]{2,1,0:T(8,128)(2,1)S(1)}, u32[]{:S(2)}, u32[]{:S(2)}) %collective-permute-start.8) | collective-permute-done | bytes 262176 | tf_op jit(solution)/shard_map/ppermute | solution.py:18
  155.9 0.7 pad_maximum_fusion.1
  156.8 0.8 fusion.2
  157.6 0.8 copy-done.1
  158.3 1.8 convolution_add_fusion
  160.2 1.1 constant_dynamic-slice_fusion
  161.3 56.4 %all-gather.4.cloned.1.call-done = bf16[1024,1024]{1,0:T(8,128)(2,1)} async-done(((bf16[128,1024]{1,0:T(8,128)(2,1)}), bf16[1024,1024]{1,0:T(8,128)(2,1)}) %all-gather.4.cloned.1.call-update) | async-done | bytes 2097168 | tf_op jit(solution)/shard_map/all_gather | solution.py:204
  217.7 3.3 %fusion.4 = f32[256,1024]{1,0:T(8,128)} fusion(bf16[1024,256]{0,1:T(8,128)(2,1)S(1)} %bitcast.54, bf16[1024,1024]{1,0:T(8,128)(2,1)} %all-gather.4.cloned.1.call-done), kind=kOutput, calls=%fused_computation.31 | convolution fusion | flops 536870912 | bytes 3670016 | tf_op jit(solution)/shard_map/dot_general | solution.py:213
  221.1 1.6 convert_element_type.47
  222.7 20.1 %reduce-scatter.5.cloned.1.call-done = f32[64,1024]{1,0:T(8,128)} async-done(((f32[256,1024]{1,0:T(8,128)}), f32[64,1024]{1,0:T(8,128)}) %reduce-scatter.5.cloned.1.call-update) | async-done | bytes 262160 | tf_op jit(solution)/shard_map/reduce_scatter | solution.py:216
  242.8 1.7 fusion.3
  (32 shorter events, 0.8 us)
Async XLA Ops:
  8.0 2.4 copy-start
  8.0 2.5 copy-start.2
  8.0 152.2 %all-gather.6.cloned.1.call-start = ((), (), s32[]{:S(2)}) async-start(), calls=%async_computation.5 | async-start | bytes 4718592 | tf_op jit(solution)/shard_map/all_gather | solution.py:186
  11.0 18.5 %collective-permute-start = (bf16[2,128,512]{2,1,0:T(8,128)(2,1)S(1)}, bf16[2,128,512]{2,1,0:T(8,128)(2,1)S(1)}, u32[]{:S(2)}, u32[]{:S(2)}) collective-permute-start(bf16[2,128,512]{2,1,0:T(8,128)(2,1)S(1)} %pad_maximum_fusion), channel_id=1, source_target_pairs={{0,16},{4,20},{8,24},{12,28},{16,32},{20,36},{24,40},{28,44},{32,4... | collective-permute-start | bytes 786440 | tf_op jit(solution)/shard_map/ppermute | solution.py:18
  16.2 15.3 %collective-permute-start.1 = (bf16[2,128,512]{2,1,0:T(8,128)(2,1)S(1)}, bf16[2,128,512]{2,1,0:T(8,128)(2,1)S(1)}, u32[]{:S(2)}, u32[]{:S(2)}) collective-permute-start(bf16[2,128,512]{2,1,0:T(8,128)(2,1)S(1)} %pad_maximum_fusion), channel_id=1, source_target_pairs={{0,12},{4,16},{8,20},{12,24},{16,28},{20,32},{24,36},{28,40},{32,4... | collective-permute-start | bytes 786440 | tf_op jit(solution)/shard_map/ppermute | solution.py:18
  21.2 17.4 %collective-permute-start.2 = (bf16[2,128,512]{2,1,0:T(8,128)(2,1)S(1)}, bf16[2,128,512]{2,1,0:T(8,128)(2,1)S(1)}, u32[]{:S(2)}, u32[]{:S(2)}) collective-permute-start(bf16[2,128,512]{2,1,0:T(8,128)(2,1)S(1)} %pad_maximum_fusion), channel_id=1, source_target_pairs={{0,8},{4,12},{8,16},{12,20},{16,24},{20,28},{24,32},{28,36},{32,40... | collective-permute-start | bytes 786440 | tf_op jit(solution)/shard_map/ppermute | solution.py:18
  24.1 16.5 %collective-permute-start.3 = (bf16[2,128,512]{2,1,0:T(8,128)(2,1)S(1)}, bf16[2,128,512]{2,1,0:T(8,128)(2,1)S(1)}, u32[]{:S(2)}, u32[]{:S(2)}) collective-permute-start(bf16[2,128,512]{2,1,0:T(8,128)(2,1)S(1)} %pad_maximum_fusion), channel_id=1, source_target_pairs={{0,4},{4,8},{8,12},{12,16},{16,20},{20,24},{24,28},{28,32},{32,36}... | collective-permute-start | bytes 786440 | tf_op jit(solution)/shard_map/ppermute | solution.py:18
  28.2 13.9 %collective-permute-start.4 = (bf16[2,128,512]{2,1,0:T(8,128)(2,1)S(1)}, bf16[2,128,512]{2,1,0:T(8,128)(2,1)S(1)}, u32[]{:S(2)}, u32[]{:S(2)}) collective-permute-start(bf16[2,128,512]{2,1,0:T(8,128)(2,1)S(1)} %pad_maximum_fusion), channel_id=1, source_target_pairs={{4,0},{8,4},{12,8},{16,12},{20,16},{24,20},{28,24},{32,28},{36,32}... | collective-permute-start | bytes 786440 | tf_op jit(solution)/shard_map/ppermute | solution.py:18
  29.5 13.4 %collective-permute-start.5 = (bf16[2,128,512]{2,1,0:T(8,128)(2,1)S(1)}, bf16[2,128,512]{2,1,0:T(8,128)(2,1)S(1)}, u32[]{:S(2)}, u32[]{:S(2)}) collective-permute-start(bf16[2,128,512]{2,1,0:T(8,128)(2,1)S(1)} %pad_maximum_fusion), channel_id=1, source_target_pairs={{8,0},{12,4},{16,8},{20,12},{24,16},{28,20},{32,24},{36,28},{40,32... | collective-permute-start | bytes 786440 | tf_op jit(solution)/shard_map/ppermute | solution.py:18
  31.5 17.7 %collective-permute-start.6 = (bf16[2,128,512]{2,1,0:T(8,128)(2,1)S(1)}, bf16[2,128,512]{2,1,0:T(8,128)(2,1)S(1)}, u32[]{:S(2)}, u32[]{:S(2)}) collective-permute-start(bf16[2,128,512]{2,1,0:T(8,128)(2,1)S(1)} %pad_maximum_fusion), channel_id=1, source_target_pairs={{12,0},{16,4},{20,8},{24,12},{28,16},{32,20},{36,24},{40,28},{44,3... | collective-permute-start | bytes 786440 | tf_op jit(solution)/shard_map/ppermute | solution.py:18
  38.7 12.4 %collective-permute-start.7 = (bf16[2,128,512]{2,1,0:T(8,128)(2,1)S(1)}, bf16[2,128,512]{2,1,0:T(8,128)(2,1)S(1)}, u32[]{:S(2)}, u32[]{:S(2)}) collective-permute-start(bf16[2,128,512]{2,1,0:T(8,128)(2,1)S(1)} %pad_maximum_fusion), channel_id=1, source_target_pairs={{16,0},{20,4},{24,8},{28,12},{32,16},{36,20},{40,24},{44,28},{48,3... | collective-permute-start | bytes 786440 | tf_op jit(solution)/shard_map/ppermute | solution.py:18
  40.6 12.2 %copy-start.4 = (s32[16,5]{0,1:T(8,128)S(1)}, s32[16,5]{0,1:T(8,128)}, u32[]{:S(2)}) copy-start(s32[16,5]{0,1:T(8,128)} %param.12) | copy-start | bytes 964
  52.8 164.9 %all-gather.4.cloned.1.call-start = ((), (), s32[]{:S(2)}) async-start(), calls=%async_computation.3 | async-start | bytes 2359296 | tf_op jit(solution)/shard_map/all_gather | solution.py:204
  105.9 49.7 %copy-start.3 = (f32[2,128,512]{2,1,0:T(8,128)S(1)}, f32[2,128,512]{2,1,0:T(8,128)}, u32[]{:S(2)}) copy-start(f32[2,128,512]{2,1,0:T(8,128)} %get-tuple-element.14) | copy-start | bytes 1572868
  107.6 24.8 %collective-permute-start.15 = (bf16[2,128,512]{2,1,0:T(8,128)(2,1)S(1)}, bf16[2,128,512]{2,1,0:T(8,128)(2,1)S(1)}, u32[]{:S(2)}, u32[]{:S(2)}) collective-permute-start(bf16[2,128,512]{2,1,0:T(8,128)(2,1)S(1)} %get-tuple-element.18), channel_id=1, source_target_pairs={{0,16},{4,20},{8,24},{12,28},{16,32},{20,36},{24,40},{28,44},{32,4... | collective-permute-start | bytes 786440 | tf_op jit(solution)/shard_map/ppermute | solution.py:18
  114.4 19.3 %collective-permute-start.14 = (bf16[2,128,512]{2,1,0:T(8,128)(2,1)S(1)}, bf16[2,128,512]{2,1,0:T(8,128)(2,1)S(1)}, u32[]{:S(2)}, u32[]{:S(2)}) collective-permute-start(bf16[2,128,512]{2,1,0:T(8,128)(2,1)S(1)} %get-tuple-element.19), channel_id=1, source_target_pairs={{0,12},{4,16},{8,20},{12,24},{16,28},{20,32},{24,36},{28,40},{32,4... | collective-permute-start | bytes 786440 | tf_op jit(solution)/shard_map/ppermute | solution.py:18
  121.6 21.8 %collective-permute-start.13 = (bf16[2,128,512]{2,1,0:T(8,128)(2,1)S(1)}, bf16[2,128,512]{2,1,0:T(8,128)(2,1)S(1)}, u32[]{:S(2)}, u32[]{:S(2)}) collective-permute-start(bf16[2,128,512]{2,1,0:T(8,128)(2,1)S(1)} %get-tuple-element.20), channel_id=1, source_target_pairs={{0,8},{4,12},{8,16},{12,20},{16,24},{20,28},{24,32},{28,36},{32,40... | collective-permute-start | bytes 786440 | tf_op jit(solution)/shard_map/ppermute | solution.py:18
  129.8 15.0 %collective-permute-start.12 = (bf16[2,128,512]{2,1,0:T(8,128)(2,1)S(1)}, bf16[2,128,512]{2,1,0:T(8,128)(2,1)S(1)}, u32[]{:S(2)}, u32[]{:S(2)}) collective-permute-start(bf16[2,128,512]{2,1,0:T(8,128)(2,1)S(1)} %get-tuple-element.21), channel_id=1, source_target_pairs={{0,4},{4,8},{8,12},{12,16},{16,20},{20,24},{24,28},{28,32},{32,36}... | collective-permute-start | bytes 786440 | tf_op jit(solution)/shard_map/ppermute | solution.py:18
  131.1 13.7 %collective-permute-start.11 = (bf16[2,128,512]{2,1,0:T(8,128)(2,1)S(1)}, bf16[2,128,512]{2,1,0:T(8,128)(2,1)S(1)}, u32[]{:S(2)}, u32[]{:S(2)}) collective-permute-start(bf16[2,128,512]{2,1,0:T(8,128)(2,1)S(1)} %get-tuple-element.22), channel_id=1, source_target_pairs={{4,0},{8,4},{12,8},{16,12},{20,16},{24,20},{28,24},{32,28},{36,32}... | collective-permute-start | bytes 786440 | tf_op jit(solution)/shard_map/ppermute | solution.py:18
  132.4 13.9 %collective-permute-start.10 = (bf16[2,128,512]{2,1,0:T(8,128)(2,1)S(1)}, bf16[2,128,512]{2,1,0:T(8,128)(2,1)S(1)}, u32[]{:S(2)}, u32[]{:S(2)}) collective-permute-start(bf16[2,128,512]{2,1,0:T(8,128)(2,1)S(1)} %get-tuple-element.23), channel_id=1, source_target_pairs={{8,0},{12,4},{16,8},{20,12},{24,16},{28,20},{32,24},{36,28},{40,32... | collective-permute-start | bytes 786440 | tf_op jit(solution)/shard_map/ppermute | solution.py:18
  133.7 15.4 %collective-permute-start.9 = (bf16[2,128,512]{2,1,0:T(8,128)(2,1)S(1)}, bf16[2,128,512]{2,1,0:T(8,128)(2,1)S(1)}, u32[]{:S(2)}, u32[]{:S(2)}) collective-permute-start(bf16[2,128,512]{2,1,0:T(8,128)(2,1)S(1)} %get-tuple-element.24), channel_id=1, source_target_pairs={{12,0},{16,4},{20,8},{24,12},{28,16},{32,20},{36,24},{40,28},{44,3... | collective-permute-start | bytes 786440 | tf_op jit(solution)/shard_map/ppermute | solution.py:18
  143.5 12.1 %collective-permute-start.8 = (bf16[2,128,512]{2,1,0:T(8,128)(2,1)S(1)}, bf16[2,128,512]{2,1,0:T(8,128)(2,1)S(1)}, u32[]{:S(2)}, u32[]{:S(2)}) collective-permute-start(bf16[2,128,512]{2,1,0:T(8,128)(2,1)S(1)} %get-tuple-element.17), channel_id=1, source_target_pairs={{16,0},{20,4},{24,8},{28,12},{32,16},{36,20},{40,24},{44,28},{48,3... | collective-permute-start | bytes 786440 | tf_op jit(solution)/shard_map/ppermute | solution.py:18
  156.7 64.4 %reduce-scatter.3.cloned.1.call-start = ((), (), s32[]{:S(2)}) async-start(), calls=%async_computation.2 | async-start | bytes 1310720 | tf_op jit(solution)/shard_map/reduce_scatter | solution.py:200
  156.7 1.6 copy-start.1
  160.1 82.7 %reduce-scatter.5.cloned.1.call-start = ((), (), s32[]{:S(2)}) async-start(), calls=%async_computation.4 | async-start | bytes 1310720 | tf_op jit(solution)/shard_map/reduce_scatter | solution.py:216
Sparse Core Ops, SparseCore 0:
  53.0 103.2 all-gather.5
  158.9 58.7 all-gather.3
Sparse Core Ops, SparseCore 1:
  160.2 28.6 reduce-scatter.2
  221.1 21.6 reduce-scatter.4
